TPU v7x, 512 devices: a whole 4x8x8 slice. The times are simulated.
512 devices in a mesh: seq: 32 (over x, y), head: 8 (over z), doc: 2 (over core).
Axes of the slice: x: 4, y: 8, z: 8, core: 2. Of those that a mesh axis runs over, the one named last changes fastest.
Arguments:
- byte_states: bfloat16 [32768, 1024], P(('doc', 'seq')), parts along dimension 0, may hold values from -36 to 36
- conv_kernel: float32 [4, 1024], replicated, may hold values from -3 to 3
- mix_weight: bfloat16 [1024, 1024], replicated, may hold values from -0.1875 to 0.1875
- norm_gain: float32 [1024], replicated, may hold values from 0.1 to 1.9
- query_weight: bfloat16 [1024, 1024], P(None, 'head'), may hold values from -3 to 3
- key_weight: bfloat16 [1024, 1024], P(None, 'head'), may hold values from -3 to 3
- value_weight: bfloat16 [1024, 1024], P(None, 'head'), may hold values from -0.1875 to 0.1875
- boundaries: int32 [4096], P(('doc', 'seq')), parts along dimension 0, may hold values from 0 to 511, as said below
- span_counts: int32 [64], P(('doc', 'seq')), parts along dimension 0, may hold values from 16 to 64, as said below
- grad_attended: bfloat16 [4096, 1024], P(('doc', 'seq'), 'head'), parts along dimension 0, may hold values from -6 to 6
Outputs:
- attended: bfloat16 [4096, 1024], P(('doc', 'seq'), 'head'), parts along dimension 0
- grad_bytes: bfloat16 [32768, 1024], P(('doc', 'seq')), parts along dimension 0
There are 2 independent parts, one for each index of `doc`. A program takes and returns all parts, laid end to end along the dimension named above; an argument that names none is the same for every part. Nothing has to cross between parts.
Inputs may be any that keep to these rules, and one draw needn't show every extreme that they name: `span_counts`: number of spans starting in each shard; in every draw some shard has exactly 64. `boundaries`: in each shard's 64 slots the first span_counts entries are strictly increasing byte positions inside the shard, the first of them 0; the remaining slots hold 0.
All inputs are finite; a program needn't handle non-finite values.
Results may differ from a plain program's by a relative error of at most 0.017.
Values may be sent and summed in bfloat16 or wider, within the bound.
No kernel may reach another device: no remote copies, remote signals or barrier semaphores. Data moves between devices by JAX's collectives and lax.ppermute only.
A program may use at most 64 MiB of HBM per device.

v0:
```python
import math

import jax
import jax.numpy as jnp
from jax import lax
from jax.sharding import PartitionSpec as P

D = 1024
HD = 128
KCONV = 4


masked_score = -1e30


def passed_along(array, axis, by):
    devices = lax.axis_size(axis)
    pairs = [(i, i + by) for i in range(devices) if 0 <= i + by < devices]
    return lax.ppermute(array, axis, pairs)


def neighbour(rim_rows, offset_by):
    return passed_along(rim_rows, "seq", offset_by)


def per_device(
    byte_states,
    conv_kernel,
    mix_weight,
    norm_gain,
    query_weight,
    key_weight,
    value_weight,
    boundaries,
    span_counts,
    grad_attended,
):
    row_count = byte_states.shape[0]
    slot_count = boundaries.shape[0]
    head_width = query_weight.shape[1]
    local_heads = head_width // HD
    score_scale = 1.0 / math.sqrt(HD)
    shard_index = lax.axis_index("seq")
    first_slot = shard_index * slot_count
    own_ids = first_slot + jnp.arange(slot_count, dtype=jnp.int32)
    before_rim = neighbour(byte_states[row_count - (KCONV - 1) :].astype(jnp.float32), 1)
    extended = jnp.concatenate([before_rim.astype(jnp.bfloat16), byte_states], axis=0)
    span_depth = conv_kernel[0] * jnp.take(extended, boundaries + (KCONV - 1), axis=0).astype(
        jnp.float32
    )
    for offset in range(1, KCONV):
        tapped = jnp.take(extended, boundaries + (KCONV - 1 - offset), axis=0).astype(jnp.float32)
        span_depth = span_depth + conv_kernel[offset] * tapped
    span_depth = span_depth.astype(jnp.bfloat16)
    span_bytes = jnp.take(byte_states, boundaries, axis=0).astype(jnp.float32)
    live_mask = jnp.arange(slot_count, dtype=jnp.int32) < span_counts[0]
    live_half = live_mask.astype(jnp.bfloat16)
    span_state = span_bytes + jnp.dot(span_depth, mix_weight, preferred_element_type=jnp.float32)
    inverse_rms = lax.rsqrt(jnp.mean(span_state * span_state, axis=1) + 1e-05)
    normed = (span_state * inverse_rms[:, None] * norm_gain).astype(jnp.bfloat16)
    queries = jnp.dot(normed, query_weight, preferred_element_type=jnp.float32).astype(jnp.bfloat16)
    key_rows = jnp.dot(normed, key_weight, preferred_element_type=jnp.float32).astype(jnp.bfloat16)
    value_rows = jnp.dot(normed, value_weight, preferred_element_type=jnp.float32).astype(
        jnp.bfloat16
    )
    grad_rows = jnp.where(live_mask[:, None], grad_attended, jnp.zeros_like(grad_attended))
    query_heads = queries.reshape(slot_count, local_heads, HD)
    key_heads = key_rows.reshape(slot_count, local_heads, HD)
    value_heads = value_rows.reshape(slot_count, local_heads, HD)
    grad_heads = grad_rows.reshape(slot_count, local_heads, HD)
    piece_keys = lax.all_gather(key_rows, "seq", axis=0, tiled=True)
    piece_values = lax.all_gather(value_rows, "seq", axis=0, tiled=True)
    piece_live = lax.all_gather(live_half, "seq", axis=0, tiled=True)
    running_max = jnp.full((local_heads, slot_count), masked_score, jnp.float32)
    piece_rows = piece_keys.shape[0]
    key_ids = jnp.arange(piece_rows, dtype=jnp.int32)
    allowed = (key_ids[None, :] <= own_ids[:, None]) & (piece_live[None, :] > 0.5)
    scores = (
        jnp.einsum(
            "qhd,khd->hqk",
            query_heads,
            piece_keys.reshape(piece_rows, local_heads, HD),
            preferred_element_type=jnp.float32,
        )
        * score_scale
    )
    scores = jnp.where(allowed[None], scores, masked_score)
    new_max = jnp.maximum(running_max, jnp.max(scores, axis=2))
    softmax_part = jnp.exp(scores - new_max[:, :, None])
    new_sum = jnp.sum(softmax_part, axis=2)
    product = jnp.einsum(
        "hqk,khd->hqd",
        softmax_part.astype(jnp.bfloat16),
        piece_values.reshape(piece_rows, local_heads, HD),
        preferred_element_type=jnp.float32,
    )
    attention = jnp.transpose(product / new_sum[:, :, None], (1, 0, 2)).reshape(
        slot_count, head_width
    )
    attended = jnp.where(live_mask[:, None], attention, jnp.float32(0.0)).astype(jnp.bfloat16)
    log_rows = jnp.transpose(new_max + jnp.log(new_sum))
    delta_rows = jnp.sum(
        grad_heads.astype(jnp.float32)
        * attended.reshape(slot_count, local_heads, HD).astype(jnp.float32),
        axis=2,
    )
    own_logs = jnp.transpose(log_rows)
    own_deltas = jnp.transpose(delta_rows)
    all_logs, all_deltas = (
        lax.all_gather(log_rows, "seq", axis=0, tiled=True),
        lax.all_gather(delta_rows, "seq", axis=0, tiled=True),
    )
    piece_queries = lax.all_gather(queries, "seq", axis=0, tiled=True)
    piece_keys = lax.all_gather(key_rows, "seq", axis=0, tiled=True)
    piece_values = lax.all_gather(value_rows, "seq", axis=0, tiled=True)
    piece_grads = lax.all_gather(grad_rows, "seq", axis=0, tiled=True)
    piece_live = lax.all_gather(live_half, "seq", axis=0, tiled=True)
    piece_rows = piece_keys.shape[0]
    key_ids = jnp.arange(piece_rows, dtype=jnp.int32)
    key_part = piece_keys.reshape(piece_rows, local_heads, HD)
    allowed = (key_ids[None, :] <= own_ids[:, None]) & (piece_live[None, :] > 0.5)
    scores = (
        jnp.einsum("qhd,khd->hqk", query_heads, key_part, preferred_element_type=jnp.float32)
        * score_scale
    )
    scores = jnp.where(allowed[None], scores, masked_score)
    probs_full = jnp.exp(scores - own_logs[:, :, None])
    grad_probs = jnp.einsum(
        "qhd,khd->hqk",
        grad_heads,
        piece_values.reshape(piece_rows, local_heads, HD),
        preferred_element_type=jnp.float32,
    )
    grad_scores = (probs_full * (grad_probs - own_deltas[:, :, None])).astype(jnp.bfloat16)
    new_query = jnp.einsum(
        "hqk,khd->hqd", grad_scores, key_part, preferred_element_type=jnp.float32
    )
    piece_rows = piece_queries.shape[0]
    piece_ids = jnp.arange(piece_rows, dtype=jnp.int32)
    query_part = piece_queries.reshape(piece_rows, local_heads, HD)
    grad_part = piece_grads.reshape(piece_rows, local_heads, HD)
    piece_logs = jnp.transpose(all_logs)
    piece_deltas = jnp.transpose(all_deltas)
    allowed = (own_ids[None, :] <= piece_ids[:, None]) & live_mask[None, :]
    scores = (
        jnp.einsum("qhd,khd->hqk", query_part, key_heads, preferred_element_type=jnp.float32)
        * score_scale
    )
    scores = jnp.where(allowed[None], scores, masked_score)
    probs_full = jnp.exp(scores - piece_logs[:, :, None])
    grad_value = jnp.einsum(
        "hqk,qhd->hkd",
        probs_full.astype(jnp.bfloat16),
        grad_part,
        preferred_element_type=jnp.float32,
    )
    grad_probs = jnp.einsum(
        "qhd,khd->hqk", grad_part, value_heads, preferred_element_type=jnp.float32
    )
    grad_scores = (probs_full * (grad_probs - piece_deltas[:, :, None])).astype(jnp.bfloat16)
    grad_key = jnp.einsum(
        "hqk,qhd->hkd", grad_scores, query_part, preferred_element_type=jnp.float32
    )

    def to_rows(stacked):
        return jnp.transpose(stacked, (1, 0, 2)).reshape(slot_count, head_width)

    contract = (((1,), (1,)), ((), ()))
    query_grad_rows = (to_rows(new_query) * score_scale).astype(jnp.bfloat16)
    key_grad_rows = (to_rows(grad_key) * score_scale).astype(jnp.bfloat16)
    value_grad_rows = to_rows(grad_value).astype(jnp.bfloat16)
    partial_normed = lax.dot_general(
        query_grad_rows, query_weight, contract, preferred_element_type=jnp.float32
    )
    partial_normed = partial_normed + lax.dot_general(
        key_grad_rows, key_weight, contract, preferred_element_type=jnp.float32
    )
    partial_normed = partial_normed + lax.dot_general(
        value_grad_rows, value_weight, contract, preferred_element_type=jnp.float32
    )
    grad_normed = lax.psum(partial_normed.astype(jnp.bfloat16), "head").astype(jnp.float32)
    scaled_grad = norm_gain * grad_normed
    cubed = inverse_rms * inverse_rms * inverse_rms
    grad_state = (
        inverse_rms[:, None] * scaled_grad
        - span_state * cubed[:, None] * jnp.mean(scaled_grad * span_state, axis=1)[:, None]
    )
    grad_state = jnp.where(live_mask[:, None], grad_state, jnp.float32(0.0))
    mixed_grad = lax.dot_general(
        grad_state.astype(jnp.bfloat16), mix_weight, contract, preferred_element_type=jnp.float32
    )
    spread_mix = jnp.zeros((row_count, D), jnp.float32).at[boundaries].add(mixed_grad)
    residual_grad = jnp.zeros((row_count, D), jnp.float32).at[boundaries].add(grad_state)
    after_rim = neighbour(spread_mix[: KCONV - 1], -1)
    padded_grad = jnp.concatenate([spread_mix, after_rim], axis=0)
    conv_grad = conv_kernel[0] * spread_mix
    for offset in range(1, KCONV):
        conv_grad = conv_grad + conv_kernel[offset] * padded_grad[offset : offset + row_count]
    grad_bytes = (residual_grad + conv_grad).astype(jnp.bfloat16)
    return (attended, grad_bytes)


def solution(mesh):
    return jax.shard_map(
        per_device,
        mesh=mesh,
        in_specs=(
            P(("doc", "seq"), None),
            P(),
            P(),
            P(),
            P(None, "head"),
            P(None, "head"),
            P(None, "head"),
            P(("doc", "seq")),
            P(("doc", "seq")),
            P(("doc", "seq"), "head"),
        ),
        out_specs=(P(("doc", "seq"), "head"), P(("doc", "seq"), None)),
        check_vma=False,
    )
```

profile of v0, /device:TPU:56, one launch (start us, length us, event | category | flops | bytes accessed | tf_op | source)
XLA Modules:
  0.0 557.7 jit_solution(17123047837741712854)
XLA Ops:
  7.2 0.0 copy-start
  7.2 0.0 all-reduce.6.cloned.1.call-start
  7.2 0.9 slice.68
  8.1 2.6 collective-permute-start
  10.7 0.7 compare_select_fusion.1
  11.4 1.3 compare_and_fusion.4
  13.3 0.5 iota_add_fusion
  13.8 1.3 dynamic-slice
  15.8 0.2 dynamic-update-slice
  16.0 63.5 %all-reduce = bf16[2048]{0:T(1024)(128)(2,1)S(1)} all-reduce(bf16[2048]{0:T(1024)(128)(2,1)S(1)} %dynamic-update-slice), channel_id=1, replica_groups=mesh['seq'=32,'head'=8,'doc'=2] {'seq'}, use_global_device_ids=true, to_apply=%add | all-reduce | flops 2048 | bytes 8192
  79.5 0.6 broadcast_compare_fusion
  80.1 1.5 fusion.54
  81.6 0.0 copy-done.15
  81.6 0.5 iota_compare_fusion.2
  82.1 2.2 gather_fusion
  84.3 0.0 collective-permute-done
  84.3 1.5 pad_maximum_fusion
  85.8 1.4 gather_fusion.4
  87.2 1.4 gather_fusion.3
  88.5 1.3 gather_fusion.2
  89.9 1.4 gather_fusion.1
  91.2 0.0 copy-done
  91.2 1.9 multiply_reduce_fusion.1
  93.2 0.0 copy-start.12
  93.2 0.0 copy-start.14
  93.2 0.0 copy-done.9
  93.2 0.1 multiply_convert_fusion
  93.3 0.0 copy-done.8
  93.3 0.2 convolution_convert_fusion.1
  93.5 0.0 copy-done.6
  93.5 0.0 copy-start.11
  93.5 0.0 copy-start.13
  93.5 0.2 convolution_convert_fusion.2
  93.7 0.2 convolution_convert_fusion.3
  93.9 60.8 %all_gather.27 = bf16[2048,128]{1,0:T(8,128)(2,1)} all-gather(bf16[64,128]{1,0:T(8,128)(2,1)S(1)} %convolution_convert_fusion.3), channel_id=1, replica_groups=mesh['seq'=32,'head'=8,'doc'=2] {'seq'}, dimensions={0}, use_global_device_ids=true | all-gather | bytes 540672 | tf_op jit(solution)/shard_map/all_gather | solution.py:113
  154.7 48.0 %all_gather.25 = bf16[2048,128]{1,0:T(8,128)(2,1)S(1)} all-gather(bf16[64,128]{1,0:T(8,128)(2,1)S(1)} %convolution_convert_fusion.2), channel_id=1, replica_groups=mesh['seq'=32,'head'=8,'doc'=2] {'seq'}, dimensions={0}, use_global_device_ids=true | all-gather | bytes 540672 | tf_op jit(solution)/shard_map/all_gather | solution.py:71
  202.7 0.0 copy-start.2
  202.7 0.4 fusion.55
  203.1 47.6 %all_gather.26 = bf16[2048,128]{1,0:T(8,128)(2,1)S(1)} all-gather(bf16[64,128]{1,0:T(8,128)(2,1)S(1)} %convolution_convert_fusion.1), channel_id=1, replica_groups=mesh['seq'=32,'head'=8,'doc'=2] {'seq'}, dimensions={0}, use_global_device_ids=true | all-gather | bytes 540672 | tf_op jit(solution)/shard_map/all_gather | solution.py:72
  250.8 0.2 fusion.26
  251.0 0.1 fusion.53
  251.1 1.0 multiply_reduce_fusion.2
  252.2 48.0 %all_gather.29 = bf16[2048,128]{1,0:T(8,128)(2,1)S(1)} all-gather(bf16[64,128]{1,0:T(8,128)(2,1)S(1)} %get-tuple-element.8), channel_id=1, replica_groups=mesh['seq'=32,'head'=8,'doc'=2] {'seq'}, dimensions={0}, use_global_device_ids=true | all-gather | bytes 540672 | tf_op jit(solution)/shard_map/all_gather | solution.py:116
  300.2 1.7 fusion.19
  301.8 0.0 copy-start.4
  301.8 0.3 dynamic-update-slice.2
  302.1 1.8 fusion.56
  304.0 126.1 %all-reduce.3 = (f32[2048]{0:T(1024)S(1)}, f32[2048]{0:T(1024)S(1)}) all-reduce(f32[2048]{0:T(1024)S(1)} %get-tuple-element.5, f32[2048]{0:T(1024)S(1)} %dynamic-update-slice.2), channel_id=2, replica_groups=mesh['seq'=32,'head'=8,'doc'=2] {'seq'}, use_global_device_ids=true, to_apply=%add.1 | all-reduce | flops 4096 | bytes 32768
  430.1 2.2 fusion.5
  432.3 1.5 fusion.18
  433.7 1.2 convolution_add_fusion.1
  435.0 2.1 fusion.13
  437.1 0.0 all-reduce.6.cloned.1.call-update
  437.2 90.4 %all-reduce.6.cloned.1.call-done = bf16[64,1024]{1,0:T(8,128)(2,1)} async-done(((bf16[64,1024]{1,0:T(8,128)(2,1)}), bf16[64,1024]{1,0:T(8,128)(2,1)}) %all-reduce.6.cloned.1.call-update) | async-done | bytes 131088 | tf_op jit(solution)/shard_map/psum | solution.py:181
  527.6 1.0 multiply_reduce_fusion
  528.7 1.7 fusion.39
  530.3 2.6 scatter_custom_fusion
  533.0 0.8 slice.50
  533.7 3.5 collective-permute-start.1
  537.2 1.8 constant_dynamic-update-slice_fusion.1
  539.1 2.5 collective-permute-done.1
  541.6 2.2 fusion.8
  543.9 4.2 scatter_custom_fusion.1
  548.1 2.7 convert_element_type.113
  (31 shorter events, 0.1 us)
Async XLA Ops:
  7.2 84.1 %copy-start = (bf16[1024,1024]{1,0:T(8,128)(2,1)S(1)}, bf16[1024,1024]{1,0:T(8,128)(2,1)}, u32[]{:S(2)}) copy-start(bf16[1024,1024]{1,0:T(8,128)(2,1)} %param.14) | copy-start | bytes 6291460
  7.2 520.4 %all-reduce.6.cloned.1.call-start = ((), (), s32[]{:S(2)}) async-start(), calls=%async_computation | async-start | bytes 262144 | tf_op jit(solution)/shard_map/psum | solution.py:181
  8.1 76.2 %collective-permute-start = (bf16[3,1024]{1,0:T(4,128)(2,1)S(1)}, bf16[3,1024]{1,0:T(4,128)(2,1)S(1)}, u32[]{:S(2)}, u32[]{:S(2)}) collective-permute-start(bf16[3,1024]{1,0:T(4,128)(2,1)S(1)} %slice.68), channel_id=1, source_target_pairs={{0,16},{16,32},{32,48},{48,64},{64,80},{80,96},{96,112},{112,128},... | collective-permute-start | bytes 18440 | tf_op jit(solution)/shard_map/ppermute | solution.py:19
  11.4 70.2 %copy-start.15 = (s32[64]{0:T(128)}, s32[64]{0:T(128)S(1)}, u32[]{:S(2)}) copy-start(s32[64]{0:T(128)S(1)} %get-tuple-element.29) | copy-start | bytes 772
  89.9 3.4 copy-start.9
  91.2 2.1 copy-start.8
  91.2 2.3 copy-start.6
  91.2 2.5 copy-start.7
  93.2 109.5 %copy-start.12 = (pred[2048]{0:T(1024)(128)(4,1)S(1)}, pred[2048]{0:T(1024)(128)(4,1)}, u32[]{:S(2)}) copy-start(pred[2048]{0:T(1024)(128)(4,1)} %broadcast_compare_fusion) | copy-start | bytes 6148
  93.2 109.5 %copy-start.14 = (s32[64]{0:T(128)S(1)}, s32[64]{0:T(128)}, u32[]{:S(2)}) copy-start(s32[64]{0:T(128)} %iota_add_fusion) | copy-start | bytes 772
  93.5 157.6 %copy-start.11 = (bf16[64,128]{1,0:T(8,128)(2,1)S(1)}, bf16[64,128]{1,0:T(8,128)(2,1)}, u32[]{:S(2)}) copy-start(bf16[64,128]{1,0:T(8,128)(2,1)} %param.21) | copy-start | bytes 49156
  93.5 157.6 %copy-start.13 = (pred[64]{0:T(512)(128)(4,1)S(1)}, pred[64]{0:T(512)(128)(4,1)}, u32[]{:S(2)}) copy-start(pred[64]{0:T(512)(128)(4,1)} %iota_compare_fusion.2) | copy-start | bytes 196
  202.7 49.4 %copy-start.2 = (bf16[2048,128]{1,0:T(8,128)(2,1)}, bf16[2048,128]{1,0:T(8,128)(2,1)S(1)}, u32[]{:S(2)}) copy-start(bf16[2048,128]{1,0:T(8,128)(2,1)S(1)} %all_gather.25) | copy-start | bytes 1572868
  250.7 1.4 copy-start.3
  301.8 130.4 %copy-start.4 = (bf16[2048,128]{1,0:T(8,128)(2,1)S(1)}, bf16[2048,128]{1,0:T(8,128)(2,1)}, u32[]{:S(2)}) copy-start(bf16[2048,128]{1,0:T(8,128)(2,1)} %all_gather.27) | copy-start | bytes 1572868
  533.7 7.9 %copy-start.1 = (f32[512,1024]{1,0:T(8,128)S(1)}, f32[512,1024]{1,0:T(8,128)}, u32[]{:S(2)}) copy-start(f32[512,1024]{1,0:T(8,128)} %scatter_custom_fusion) | copy-start | bytes 6291460
  533.7 7.9 %copy-start.10 = (f32[1,1024]{1,0:T(1,128)S(1)}, f32[1,1024]{1,0:T(1,128)}, u32[]{:S(2)}) copy-start(f32[1,1024]{1,0:T(1,128)} %get-tuple-element.18) | copy-start | bytes 12292
  533.7 7.9 %collective-permute-start.1 = (f32[3,1024]{1,0:T(4,128)S(1)}, f32[3,1024]{1,0:T(4,128)S(1)}, u32[]{:S(2)}, u32[]{:S(2)}) collective-permute-start(f32[3,1024]{1,0:T(4,128)S(1)} %slice.50), channel_id=1, source_target_pairs={{16,0},{32,16},{48,32},{64,48},{80,64},{96,80},{112,96},{128,112},... | collective-permute-start | bytes 36872 | tf_op jit(solution)/shard_map/ppermute | solution.py:19
  541.6 2.2 copy-start.5
Sparse Core Ops, SparseCore 0:
  437.3 90.2 all-reduce.5
where the time goes:
time: 559 us; the launch traced here: 558 us
  blocking collectives  394 us (70%)
  waiting for transfers between devices  93 us (17%)
  other arithmetic  18.4 us (3%)
  matrix products  16.1 us (3%)
  between operations  15.6 us (3%)
  local copies, waits for them, and re-layouts  14.4 us (3%)
  starting transfers between devices  6.1 us (1%)
    unnamed x2, blocking collectives  190 us
    psum x1, waiting for transfers between devices, per_device(): lax.psum(partial_normed.astype(jnp.bfloat16), 'head').astype(jnp.float32)  90.4 us
    all_gather x1, blocking collectives, per_device(): piece_queries = lax.all_gather(queries, 'seq', axis=0, tiled=True)  60.8 us
    all_gather x1, blocking collectives, per_device(): piece_grads = lax.all_gather(grad_rows, 'seq', axis=0, tiled=True)  48 us
    all_gather x1, blocking collectives, per_device(): piece_keys = lax.all_gather(key_rows, 'seq', axis=0, tiled=True)  48 us
    all_gather x1, blocking collectives, per_device(): piece_values = lax.all_gather(value_rows, 'seq', axis=0, tiled=True)  47.6 us
  transfers between devices with their start and end apart: 3, of which 2 were waited for; matrix products, arithmetic and copies ran while one was open for 2% of the time, Pallas kernels for 0%

commit v1 on v0

v1 whole, which is shorter than its diff:
```python
import math

import jax
import jax.numpy as jnp
from jax import lax
from jax.sharding import PartitionSpec as P

D = 1024
HD = 128
KCONV = 4
CHUNK = 256


masked_score = -1e30


def passed_along(array, axis, by):
    devices = lax.axis_size(axis)
    pairs = [(i, i + by) for i in range(devices) if 0 <= i + by < devices]
    return lax.ppermute(array, axis, pairs)


def neighbour(rim_rows, offset_by):
    return passed_along(rim_rows, "seq", offset_by)


def gather_blocks(block, axis):
    devices = lax.axis_size(axis)
    me = lax.axis_index(axis)
    held = block[None]
    step = 1
    while step < devices:
        other = lax.ppermute(held, axis, [(i, i ^ step) for i in range(devices)])
        held = jnp.concatenate([held, other], axis=0)
        step *= 2
    order = jnp.arange(devices, dtype=jnp.int32) ^ me
    return jnp.take(held, order, axis=0)


def summed_over(partial, axis):
    devices = lax.axis_size(axis)
    sent = partial.astype(jnp.bfloat16)
    total = sent.astype(jnp.float32)
    for shift in range(1, devices):
        total = total + lax.ppermute(
            sent, axis, [(i, (i + shift) % devices) for i in range(devices)]
        ).astype(jnp.float32)
    return total


def per_device(
    byte_states,
    conv_kernel,
    mix_weight,
    norm_gain,
    query_weight,
    key_weight,
    value_weight,
    boundaries,
    span_counts,
    grad_attended,
):
    row_count = byte_states.shape[0]
    slot_count = boundaries.shape[0]
    head_width = query_weight.shape[1]
    score_scale = 1.0 / math.sqrt(HD)
    shard_index = lax.axis_index("seq")
    shards = lax.axis_size("seq")
    first_slot = shard_index * slot_count
    own_ids = first_slot + jnp.arange(slot_count, dtype=jnp.int32)
    before_rim = neighbour(byte_states[row_count - (KCONV - 1) :].astype(jnp.float32), 1)
    extended = jnp.concatenate([before_rim.astype(jnp.bfloat16), byte_states], axis=0)
    span_depth = conv_kernel[0] * jnp.take(extended, boundaries + (KCONV - 1), axis=0).astype(
        jnp.float32
    )
    for offset in range(1, KCONV):
        tapped = jnp.take(extended, boundaries + (KCONV - 1 - offset), axis=0).astype(jnp.float32)
        span_depth = span_depth + conv_kernel[offset] * tapped
    span_depth = span_depth.astype(jnp.bfloat16)
    span_bytes = jnp.take(byte_states, boundaries, axis=0).astype(jnp.float32)
    live_mask = jnp.arange(slot_count, dtype=jnp.int32) < span_counts[0]
    span_state = span_bytes + jnp.dot(span_depth, mix_weight, preferred_element_type=jnp.float32)
    inverse_rms = lax.rsqrt(jnp.mean(span_state * span_state, axis=1) + 1e-05)
    normed = (span_state * inverse_rms[:, None] * norm_gain).astype(jnp.bfloat16)
    queries = jnp.dot(normed, query_weight, preferred_element_type=jnp.float32).astype(jnp.bfloat16)
    key_rows = jnp.dot(normed, key_weight, preferred_element_type=jnp.float32).astype(jnp.bfloat16)
    value_rows = jnp.dot(normed, value_weight, preferred_element_type=jnp.float32).astype(
        jnp.bfloat16
    )
    grad_rows = jnp.where(live_mask[:, None], grad_attended, jnp.zeros_like(grad_attended))

    count_rows = jnp.broadcast_to(span_counts[0].astype(jnp.bfloat16), (16, head_width))
    packed = jnp.concatenate([queries, key_rows, value_rows, grad_rows, count_rows], axis=0)
    gathered = gather_blocks(packed, "seq")
    total_slots = shards * slot_count

    def piece(k):
        return gathered[:, k * slot_count : (k + 1) * slot_count].reshape(total_slots, head_width)

    all_queries, all_keys, all_values, all_grads = piece(0), piece(1), piece(2), piece(3)
    all_counts = gathered[:, 4 * slot_count, 0].astype(jnp.int32)
    all_live = (
        jnp.arange(slot_count, dtype=jnp.int32)[None, :] < all_counts[:, None]
    ).reshape(total_slots)
    slot_ids = jnp.arange(total_slots, dtype=jnp.int32)

    log_parts = []
    delta_parts = []
    attended_parts = []
    for chunk in range(total_slots // CHUNK):
        q0, q1 = chunk * CHUNK, (chunk + 1) * CHUNK
        q_ids = slot_ids[q0:q1]
        k_ids = slot_ids[:q1]
        allowed = (k_ids[None, :] <= q_ids[:, None]) & all_live[None, :q1]
        scores = (
            jnp.dot(all_queries[q0:q1], all_keys[:q1].T, preferred_element_type=jnp.float32)
            * score_scale
        )
        scores = jnp.where(allowed, scores, masked_score)
        row_max = jnp.max(scores, axis=1)
        softmax_part = jnp.exp(scores - row_max[:, None])
        row_sum = jnp.sum(softmax_part, axis=1)
        product = jnp.dot(
            softmax_part.astype(jnp.bfloat16), all_values[:q1], preferred_element_type=jnp.float32
        )
        attention = jnp.where(
            all_live[q0:q1, None], product / row_sum[:, None], jnp.float32(0.0)
        ).astype(jnp.bfloat16)
        log_parts.append(row_max + jnp.log(row_sum))
        delta_parts.append(
            jnp.sum(all_grads[q0:q1].astype(jnp.float32) * attention.astype(jnp.float32), axis=1)
        )
        attended_parts.append(attention)
    all_logs = jnp.concatenate(log_parts)
    all_deltas = jnp.concatenate(delta_parts)
    all_attended = jnp.concatenate(attended_parts, axis=0)
    attended = lax.dynamic_slice_in_dim(all_attended, first_slot, slot_count, axis=0)
    own_logs = lax.dynamic_slice_in_dim(all_logs, first_slot, slot_count)
    own_deltas = lax.dynamic_slice_in_dim(all_deltas, first_slot, slot_count)

    allowed = (slot_ids[None, :] <= own_ids[:, None]) & all_live[None, :]
    scores = jnp.dot(queries, all_keys.T, preferred_element_type=jnp.float32) * score_scale
    scores = jnp.where(allowed, scores, masked_score)
    probs_full = jnp.exp(scores - own_logs[:, None])
    grad_probs = jnp.dot(grad_rows, all_values.T, preferred_element_type=jnp.float32)
    grad_scores = (probs_full * (grad_probs - own_deltas[:, None])).astype(jnp.bfloat16)
    query_grad_rows = (
        jnp.dot(grad_scores, all_keys, preferred_element_type=jnp.float32) * score_scale
    ).astype(jnp.bfloat16)

    allowed = (own_ids[None, :] <= slot_ids[:, None]) & live_mask[None, :]
    scores = jnp.dot(all_queries, key_rows.T, preferred_element_type=jnp.float32) * score_scale
    scores = jnp.where(allowed, scores, masked_score)
    probs_full = jnp.exp(scores - all_logs[:, None])
    contract_rows = (((0,), (0,)), ((), ()))
    value_grad_rows = lax.dot_general(
        probs_full.astype(jnp.bfloat16), all_grads, contract_rows, preferred_element_type=jnp.float32
    ).astype(jnp.bfloat16)
    grad_probs = jnp.dot(all_grads, value_rows.T, preferred_element_type=jnp.float32)
    grad_scores = (probs_full * (grad_probs - all_deltas[:, None])).astype(jnp.bfloat16)
    key_grad_rows = (
        lax.dot_general(grad_scores, all_queries, contract_rows, preferred_element_type=jnp.float32)
        * score_scale
    ).astype(jnp.bfloat16)

    contract = (((1,), (1,)), ((), ()))
    partial_normed = lax.dot_general(
        query_grad_rows, query_weight, contract, preferred_element_type=jnp.float32
    )
    partial_normed = partial_normed + lax.dot_general(
        key_grad_rows, key_weight, contract, preferred_element_type=jnp.float32
    )
    partial_normed = partial_normed + lax.dot_general(
        value_grad_rows, value_weight, contract, preferred_element_type=jnp.float32
    )
    grad_normed = summed_over(partial_normed, "head")
    scaled_grad = norm_gain * grad_normed
    cubed = inverse_rms * inverse_rms * inverse_rms
    grad_state = (
        inverse_rms[:, None] * scaled_grad
        - span_state * cubed[:, None] * jnp.mean(scaled_grad * span_state, axis=1)[:, None]
    )
    grad_state = jnp.where(live_mask[:, None], grad_state, jnp.float32(0.0))
    mixed_grad = lax.dot_general(
        grad_state.astype(jnp.bfloat16), mix_weight, contract, preferred_element_type=jnp.float32
    )
    spread_mix = jnp.zeros((row_count, D), jnp.float32).at[boundaries].add(mixed_grad)
    residual_grad = jnp.zeros((row_count, D), jnp.float32).at[boundaries].add(grad_state)
    after_rim = neighbour(spread_mix[: KCONV - 1], -1)
    padded_grad = jnp.concatenate([spread_mix, after_rim], axis=0)
    conv_grad = conv_kernel[0] * spread_mix
    for offset in range(1, KCONV):
        conv_grad = conv_grad + conv_kernel[offset] * padded_grad[offset : offset + row_count]
    grad_bytes = (residual_grad + conv_grad).astype(jnp.bfloat16)
    return (attended, grad_bytes)


def solution(mesh):
    return jax.shard_map(
        per_device,
        mesh=mesh,
        in_specs=(
            P(("doc", "seq"), None),
            P(),
            P(),
            P(),
            P(None, "head"),
            P(None, "head"),
            P(None, "head"),
            P(("doc", "seq")),
            P(("doc", "seq")),
            P(("doc", "seq"), "head"),
        ),
        out_specs=(P(("doc", "seq"), "head"), P(("doc", "seq"), None)),
        check_vma=False,
    )
```

time: 559 us -> 227 us (0.41)
  the two profiles are of different devices: /device:TPU:56 before, /device:TPU:24 now
where the time goes in v1:
time: 227 us; the launch traced here: 226 us
  waiting for transfers between devices  60.2 us (27%)
  starting transfers between devices  55.4 us (24%)
  local copies, waits for them, and re-layouts  47.6 us (21%)
  other arithmetic  32.9 us (14%)
  matrix products  27 us (12%)
  between operations  2.79 us (1%)
    ppermute x5, waiting for transfers between devices, gather_blocks(): other = lax.ppermute(held, axis, [(i, i ^ step) for i in range(devices)])  47.1 us
    ppermute x7, starting transfers between devices, summed_over(): lax.ppermute(sent, axis, [(i, (i + shift) % devices) for i in range(devic...  32.4 us
    ppermute x5, starting transfers between devices, gather_blocks(): other = lax.ppermute(held, axis, [(i, i ^ step) for i in range(devices)])  16.3 us
    broadcast_in_dim x8, local copies, waits for them, and re-layouts, per_device(): jnp.where(all_live[q0:q1, None], product / row_sum[:, None], jnp.float32(...  10.1 us
    ppermute x7, waiting for transfers between devices, summed_over(): lax.ppermute(sent, axis, [(i, (i + shift) % devices) for i in range(devic...  10.1 us
    ppermute x2, starting transfers between devices, passed_along(): return lax.ppermute(array, axis, pairs)  6.74 us
    dot_general x8, matrix products, per_device(): jnp.dot(all_queries[q0:q1], all_keys[:q1].T, preferred_element_type=jnp.f...  6.57 us
    unnamed x172, local copies, waits for them, and re-layouts  5.54 us
  transfers between devices with their start and end apart: 14, of which 9 were waited for; matrix products, arithmetic and copies ran while one was open for 9% of the time, Pallas kernels for 0%

profile of v1, /device:TPU:24, one launch (start us, length us, event | category | flops | bytes accessed | tf_op | source)
XLA Modules:
  0.0 225.9 jit_solution(15847215689227087860)
XLA Ops:
  1.5 4.7 %collective-permute-start = (bf16[3,1024]{1,0:T(4,128)(2,1)S(1)}, bf16[3,1024]{1,0:T(4,128)(2,1)S(1)}, u32[]{:S(2)}, u32[]{:S(2)}) collective-permute-start(bf16[3,1024]{1,0:T(4,128)(2,1)S(1)} %slice.516), channel_id=1, source_target_pairs={{0,16},{16,32},{32,48},{48,64},{64,80},{80,96},{96,112},{112,128},... | collective-permute-start | bytes 18440 | tf_op jit(solution)/shard_map/ppermute | solution.py:20
  6.9 1.3 compare_and_fusion.4
  11.4 2.2 gather_fusion
  13.6 1.5 pad_maximum_fusion
  15.1 1.4 gather_fusion.5
  16.5 1.4 gather_fusion.4
  17.8 1.4 gather_fusion.3
  19.2 1.4 gather_fusion.2
  20.6 1.9 multiply_reduce_fusion.1
  25.7 1.9 collective-permute-start.1
  28.2 3.8 %collective-permute-done.1 = bf16[1,272,128]{2,1,0:T(8,128)(2,1)S(1)} collective-permute-done((bf16[1,272,128]{2,1,0:T(8,128)(2,1)S(1)}, bf16[1,272,128]{2,1,0:T(8,128)(2,1)S(1)}, u32[]{:S(2)}, u32[]{:S(2)}) %collective-permute-start.1) | collective-permute-done | bytes 69664 | tf_op jit(solution)/shard_map/ppermute | solution.py:33
  32.0 2.6 %collective-permute-start.2 = (bf16[2,272,128]{2,1,0:T(8,128)(2,1)S(1)}, bf16[2,272,128]{2,1,0:T(8,128)(2,1)S(1)}, u32[]{:S(2)}, u32[]{:S(2)}) collective-permute-start(bf16[2,272,128]{2,1,0:T(8,128)(2,1)S(1)} %pad_maximum_fusion.3), channel_id=1, source_target_pairs={{0,32},{16,48},{32,0},{48,16},{64,96},{80,112},{96,64},{112,80},{1... | collective-permute-start | bytes 417800 | tf_op jit(solution)/shard_map/ppermute | solution.py:33
  35.2 6.2 %collective-permute-done.2 = bf16[2,272,128]{2,1,0:T(8,128)(2,1)S(1)} collective-permute-done((bf16[2,272,128]{2,1,0:T(8,128)(2,1)S(1)}, bf16[2,272,128]{2,1,0:T(8,128)(2,1)S(1)}, u32[]{:S(2)}, u32[]{:S(2)}) %collective-permute-start.2) | collective-permute-done | bytes 139296 | tf_op jit(solution)/shard_map/ppermute | solution.py:33
  41.5 3.2 %collective-permute-start.3 = (bf16[4,272,128]{2,1,0:T(8,128)(2,1)S(1)}, bf16[4,272,128]{2,1,0:T(8,128)(2,1)S(1)}, u32[]{:S(2)}, u32[]{:S(2)}) collective-permute-start(bf16[4,272,128]{2,1,0:T(8,128)(2,1)S(1)} %pad_maximum_fusion.2), channel_id=1, source_target_pairs={{0,64},{16,80},{32,96},{48,112},{64,0},{80,16},{96,32},{112,48},{1... | collective-permute-start | bytes 835592 | tf_op jit(solution)/shard_map/ppermute | solution.py:33
  45.8 12.4 %collective-permute-done.3 = bf16[4,272,128]{2,1,0:T(8,128)(2,1)S(1)} collective-permute-done((bf16[4,272,128]{2,1,0:T(8,128)(2,1)S(1)}, bf16[4,272,128]{2,1,0:T(8,128)(2,1)S(1)}, u32[]{:S(2)}, u32[]{:S(2)}) %collective-permute-start.3) | collective-permute-done | bytes 278560 | tf_op jit(solution)/shard_map/ppermute | solution.py:33
  58.3 3.4 %collective-permute-start.4 = (bf16[8,272,128]{2,1,0:T(8,128)(2,1)S(1)}, bf16[8,272,128]{2,1,0:T(8,128)(2,1)S(1)}, u32[]{:S(2)}, u32[]{:S(2)}) collective-permute-start(bf16[8,272,128]{2,1,0:T(8,128)(2,1)S(1)} %pad_maximum_fusion.1), channel_id=1, source_target_pairs={{0,128},{16,144},{32,160},{48,176},{64,192},{80,208},{96,224},{112... | collective-permute-start | bytes 1671176 | tf_op jit(solution)/shard_map/ppermute | solution.py:33
  64.5 8.2 %collective-permute-done.4 = bf16[8,272,128]{2,1,0:T(8,128)(2,1)S(1)} collective-permute-done((bf16[8,272,128]{2,1,0:T(8,128)(2,1)S(1)}, bf16[8,272,128]{2,1,0:T(8,128)(2,1)S(1)}, u32[]{:S(2)}, u32[]{:S(2)}) %collective-permute-start.4) | collective-permute-done | bytes 557088 | tf_op jit(solution)/shard_map/ppermute | solution.py:33
  73.7 5.1 %collective-permute-start.5 = (bf16[16,272,128]{2,1,0:T(8,128)(2,1)S(1)}, bf16[16,272,128]{2,1,0:T(8,128)(2,1)S(1)}, u32[]{:S(2)}, u32[]{:S(2)}) collective-permute-start(bf16[16,272,128]{2,1,0:T(8,128)(2,1)S(1)} %get-tuple-element.45), channel_id=1, source_target_pairs={{0,256},{16,272},{32,288},{48,304},{64,320},{80,336},{96,352},{112... | collective-permute-start | bytes 3342344 | tf_op jit(solution)/shard_map/ppermute | solution.py:33
  84.0 16.5 %collective-permute-done.5 = bf16[16,272,128]{2,1,0:T(8,128)(2,1)S(1)} collective-permute-done((bf16[16,272,128]{2,1,0:T(8,128)(2,1)S(1)}, bf16[16,272,128]{2,1,0:T(8,128)(2,1)S(1)}, u32[]{:S(2)}, u32[]{:S(2)}) %collective-permute-start.5) | collective-permute-done | bytes 1114144 | tf_op jit(solution)/shard_map/ppermute | solution.py:33
  100.5 1.1 constant_dynamic-update-slice_fusion.10
  101.6 3.9 %gather_fusion.1 = bf16[32,272,128]{2,1,0:T(8,128)(2,1)} fusion(bf16[32,272,128]{2,1,0:T(8,128)(2,1)} %constant_dynamic-update-slice_fusion.10, s32[1024]{0:T(1024)S(1)} %pad_clamp_fusion), kind=kCustom, calls=%fused_computation.5 | custom fusion | bytes 4456576 | tf_op jit(solution)/shard_map/jit(_take)/gather | solution.py:37
  105.5 1.9 broadcast_select_fusion
  107.4 1.0 fusion.115
  115.3 1.1 fusion.116
  116.4 1.3 fusion.114
  118.3 1.3 broadcast_in_dim.247
  119.6 1.3 and.113
  120.9 1.3 broadcast_in_dim.251
  122.8 1.3 broadcast_in_dim.254
  124.1 1.3 and.119
  125.4 1.3 broadcast_in_dim.257
  127.4 1.3 broadcast_in_dim.260
  128.8 1.2 broadcast_in_dim.263
  130.1 1.2 broadcast_in_dim.266
  131.3 1.3 broadcast_in_dim.269
  132.6 1.1 fusion.124
  133.8 1.1 constant_dynamic-update-slice_fusion.23
  135.0 1.3 constant_dynamic-update-slice_fusion.24
  136.3 1.2 fusion.125
  137.8 1.1 fusion.126
  150.1 1.2 fusion.9
  151.2 1.7 fusion.52
  152.9 1.9 fusion.132
  154.8 1.4 fusion.11
  156.2 1.7 fusion.51
  158.0 1.9 convolution_add_fusion.1
  159.9 1.4 fusion.32
  161.3 11.0 %collective-permute-start.12 = (bf16[64,1024]{1,0:T(8,128)(2,1)S(1)}, bf16[64,1024]{1,0:T(8,128)(2,1)S(1)}, u32[]{:S(2)}, u32[]{:S(2)}) collective-permute-start(bf16[64,1024]{1,0:T(8,128)(2,1)S(1)} %fusion.32), channel_id=1, source_target_pairs={{0,14},{2,0},{4,2},{6,4},{8,6},{10,8},{12,10},{14,12},{1,15},{3,1}... | collective-permute-start | bytes 393224 | tf_op jit(solution)/shard_map/ppermute | solution.py:45
  172.3 2.4 %collective-permute-start.11 = (bf16[64,1024]{1,0:T(8,128)(2,1)S(1)}, bf16[64,1024]{1,0:T(8,128)(2,1)S(1)}, u32[]{:S(2)}, u32[]{:S(2)}) collective-permute-start(bf16[64,1024]{1,0:T(8,128)(2,1)S(1)} %fusion.32), channel_id=1, source_target_pairs={{0,12},{2,14},{4,0},{6,2},{8,4},{10,6},{12,8},{14,10},{1,13},{3,15... | collective-permute-start | bytes 393224 | tf_op jit(solution)/shard_map/ppermute | solution.py:45
  174.7 1.9 collective-permute-start.10
  176.7 7.9 %collective-permute-start.9 = (bf16[64,1024]{1,0:T(8,128)(2,1)S(1)}, bf16[64,1024]{1,0:T(8,128)(2,1)S(1)}, u32[]{:S(2)}, u32[]{:S(2)}) collective-permute-start(bf16[64,1024]{1,0:T(8,128)(2,1)S(1)} %fusion.32), channel_id=1, source_target_pairs={{0,8},{2,10},{4,12},{6,14},{8,0},{10,2},{12,4},{14,6},{1,9},{3,11}... | collective-permute-start | bytes 393224 | tf_op jit(solution)/shard_map/ppermute | solution.py:45
  184.6 1.9 collective-permute-start.8
  186.5 3.4 %collective-permute-start.7 = (bf16[64,1024]{1,0:T(8,128)(2,1)S(1)}, bf16[64,1024]{1,0:T(8,128)(2,1)S(1)}, u32[]{:S(2)}, u32[]{:S(2)}) collective-permute-start(bf16[64,1024]{1,0:T(8,128)(2,1)S(1)} %fusion.32), channel_id=1, source_target_pairs={{0,4},{2,6},{4,8},{6,10},{8,12},{10,14},{12,0},{14,2},{1,5},{3,7},... | collective-permute-start | bytes 393224 | tf_op jit(solution)/shard_map/ppermute | solution.py:45
  189.9 3.9 %collective-permute-start.6 = (bf16[64,1024]{1,0:T(8,128)(2,1)S(1)}, bf16[64,1024]{1,0:T(8,128)(2,1)S(1)}, u32[]{:S(2)}, u32[]{:S(2)}) collective-permute-start(bf16[64,1024]{1,0:T(8,128)(2,1)S(1)} %fusion.32), channel_id=1, source_target_pairs={{0,2},{2,4},{4,6},{6,8},{8,10},{10,12},{12,14},{14,0},{1,3},{3,5},... | collective-permute-start | bytes 393224 | tf_op jit(solution)/shard_map/ppermute | solution.py:45
  193.8 1.3 constant_dynamic-slice_fusion
  195.1 4.8 %collective-permute-done.8 = bf16[64,1024]{1,0:T(8,128)(2,1)S(1)} collective-permute-done((bf16[64,1024]{1,0:T(8,128)(2,1)S(1)}, bf16[64,1024]{1,0:T(8,128)(2,1)S(1)}, u32[]{:S(2)}, u32[]{:S(2)}) %collective-permute-start.8) | collective-permute-done | bytes 131104 | tf_op jit(solution)/shard_map/ppermute | solution.py:45
  199.9 4.4 %collective-permute-done.7 = bf16[64,1024]{1,0:T(8,128)(2,1)S(1)} collective-permute-done((bf16[64,1024]{1,0:T(8,128)(2,1)S(1)}, bf16[64,1024]{1,0:T(8,128)(2,1)S(1)}, u32[]{:S(2)}, u32[]{:S(2)}) %collective-permute-start.7) | collective-permute-done | bytes 131104 | tf_op jit(solution)/shard_map/ppermute | solution.py:45
  206.2 2.6 %scatter_custom_fusion = f32[512,1024]{1,0:T(8,128)} fusion(s32[64]{0:T(128)} %copy-done.62, f32[64,1024]{1,0:T(8,128)S(1)} %fusion.96, f32[]{:T(128)} %constant.25.clone.1), kind=kCustom, calls=%fused_computation.98 | custom fusion | flops 65536 | bytes 2097664 | tf_op jit(solution)/shard_map/scatter-add | solution.py:187
  209.7 2.1 collective-permute-start.13
  211.7 1.8 constant_dynamic-update-slice_fusion.27
  213.6 3.1 %collective-permute-done.13 = f32[3,1024]{1,0:T(4,128)S(1)} collective-permute-done((f32[3,1024]{1,0:T(4,128)S(1)}, f32[3,1024]{1,0:T(4,128)S(1)}, u32[]{:S(2)}, u32[]{:S(2)}) %collective-permute-start.13) | collective-permute-done | bytes 12320 | tf_op jit(solution)/shard_map/ppermute | solution.py:20
  216.7 2.2 fusion.14
  218.9 4.2 %scatter_custom_fusion.1 = f32[512,1024]{1,0:T(8,128)} fusion(f32[512,1024]{1,0:T(8,128)} %fusion.14, s32[64]{0:T(128)} %copy-done.62, f32[64,1024]{1,0:T(8,128)S(1)} %get-tuple-element.80, f32[64,1024]{1,0:T(8,128)S(1)} %get-tuple-element.4, f32[64]{0:T(128)S(1)} %broadcast_multiply_fusion, f32[64]{0:T(128)S(1)} %copy-done.56, f32[64]{0:T(128)S(1)} %copy-done.54, ...), kind=kCustom, calls=%fused_computation.256 | custom fusion | flops 393216 | bytes 2622272 | tf_op jit(solution)/shard_map/scatter-add | solution.py:188
  223.1 2.7 %convert_element_type.291 = bf16[512,1024]{1,0:T(8,128)(2,1)} convert(f32[512,1024]{1,0:T(8,128)} %scatter_custom_fusion.1) | non-fusion elementwise | flops 524288 | bytes 3145728 | tf_op jit(solution)/shard_map/convert_element_type | solution.py:194
  (276 shorter events, 40.9 us)
Async XLA Ops:
  0.6 20.0 %copy-start = (bf16[1024,1024]{1,0:T(8,128)(2,1)S(1)}, bf16[1024,1024]{1,0:T(8,128)(2,1)}, u32[]{:S(2)}) copy-start(bf16[1024,1024]{1,0:T(8,128)(2,1)} %param.14) | copy-start | bytes 6291460
  1.5 12.1 %collective-permute-start = (bf16[3,1024]{1,0:T(4,128)(2,1)S(1)}, bf16[3,1024]{1,0:T(4,128)(2,1)S(1)}, u32[]{:S(2)}, u32[]{:S(2)}) collective-permute-start(bf16[3,1024]{1,0:T(4,128)(2,1)S(1)} %slice.516), channel_id=1, source_target_pairs={{0,16},{16,32},{32,48},{48,64},{64,80},{80,96},{96,112},{112,128},... | collective-permute-start | bytes 18440 | tf_op jit(solution)/shard_map/ppermute | solution.py:20
  6.9 4.0 %copy-start.62 = (s32[64]{0:T(128)}, s32[64]{0:T(128)S(1)}, u32[]{:S(2)}) copy-start(s32[64]{0:T(128)S(1)} %get-tuple-element.77) | copy-start | bytes 772
  10.2 10.4 %copy-start.32 = (f32[1,1024]{1,0:T(1,128)}, f32[1,1024]{1,0:T(1,128)S(1)}, u32[]{:S(2)}) copy-start(f32[1,1024]{1,0:T(1,128)S(1)} %get-tuple-element.55) | copy-start | bytes 12292
  10.2 10.4 %copy-start.34 = (f32[1,1024]{1,0:T(1,128)}, f32[1,1024]{1,0:T(1,128)S(1)}, u32[]{:S(2)}) copy-start(f32[1,1024]{1,0:T(1,128)S(1)} %get-tuple-element.56) | copy-start | bytes 12292
  10.2 10.4 %copy-start.36 = (f32[1,1024]{1,0:T(1,128)}, f32[1,1024]{1,0:T(1,128)S(1)}, u32[]{:S(2)}) copy-start(f32[1,1024]{1,0:T(1,128)S(1)} %get-tuple-element.57) | copy-start | bytes 12292
  10.2 10.4 %copy-start.38 = (f32[1,1024]{1,0:T(1,128)}, f32[1,1024]{1,0:T(1,128)S(1)}, u32[]{:S(2)}) copy-start(f32[1,1024]{1,0:T(1,128)S(1)} %get-tuple-element.58) | copy-start | bytes 12292
  20.5 2.6 %copy-start.40 = (f32[1024]{0:T(1024)S(1)}, f32[1024]{0:T(1024)}, u32[]{:S(2)}) copy-start(f32[1024]{0:T(1024)} %param.15) | copy-start | bytes 12292
  20.5 2.7 %copy-start.6 = (bf16[1024,128]{1,0:T(8,128)(2,1)S(1)}, bf16[1024,128]{1,0:T(8,128)(2,1)}, u32[]{:S(2)}) copy-start(bf16[1024,128]{1,0:T(8,128)(2,1)} %param.16) | copy-start | bytes 786436
  20.5 3.5 %copy-start.5 = (bf16[1024,128]{1,0:T(8,128)(2,1)S(1)}, bf16[1024,128]{1,0:T(8,128)(2,1)}, u32[]{:S(2)}) copy-start(bf16[1024,128]{1,0:T(8,128)(2,1)} %param.17) | copy-start | bytes 786436
  20.6 4.3 %copy-start.7 = (bf16[1024,128]{1,0:T(8,128)(2,1)S(1)}, bf16[1024,128]{1,0:T(8,128)(2,1)}, u32[]{:S(2)}) copy-start(bf16[1024,128]{1,0:T(8,128)(2,1)} %param.18) | copy-start | bytes 786436
  20.6 5.0 %copy-start.23 = (bf16[64,128]{1,0:T(8,128)(2,1)S(1)}, bf16[64,128]{1,0:T(8,128)(2,1)}, u32[]{:S(2)}) copy-start(bf16[64,128]{1,0:T(8,128)(2,1)} %param.21) | copy-start | bytes 49156
  20.6 5.0 %copy-start.47 = (pred[64]{0:T(512)(128)(4,1)S(1)}, pred[64]{0:T(512)(128)(4,1)}, u32[]{:S(2)}) copy-start(pred[64]{0:T(512)(128)(4,1)} %iota_compare_fusion.4) | copy-start | bytes 196
  23.2 40.5 %copy-start.53 = (f32[64]{0:T(128)}, f32[64]{0:T(128)S(1)}, u32[]{:S(2)}) copy-start(f32[64]{0:T(128)S(1)} %get-tuple-element.68) | copy-start | bytes 772
  25.7 6.2 %collective-permute-start.1 = (bf16[1,272,128]{2,1,0:T(8,128)(2,1)S(1)}, bf16[1,272,128]{2,1,0:T(8,128)(2,1)S(1)}, u32[]{:S(2)}, u32[]{:S(2)}) collective-permute-start(bf16[1,272,128]{2,1,0:T(8,128)(2,1)S(1)} %bitcast.121), channel_id=1, source_target_pairs={{0,16},{16,0},{32,48},{48,32},{64,80},{80,64},{96,112},{112,96},{1... | collective-permute-start | bytes 208904 | tf_op jit(solution)/shard_map/ppermute | solution.py:33
  32.0 9.5 %collective-permute-start.2 = (bf16[2,272,128]{2,1,0:T(8,128)(2,1)S(1)}, bf16[2,272,128]{2,1,0:T(8,128)(2,1)S(1)}, u32[]{:S(2)}, u32[]{:S(2)}) collective-permute-start(bf16[2,272,128]{2,1,0:T(8,128)(2,1)S(1)} %pad_maximum_fusion.3), channel_id=1, source_target_pairs={{0,32},{16,48},{32,0},{48,16},{64,96},{80,112},{96,64},{112,80},{1... | collective-permute-start | bytes 417800 | tf_op jit(solution)/shard_map/ppermute | solution.py:33
  41.5 16.8 %collective-permute-start.3 = (bf16[4,272,128]{2,1,0:T(8,128)(2,1)S(1)}, bf16[4,272,128]{2,1,0:T(8,128)(2,1)S(1)}, u32[]{:S(2)}, u32[]{:S(2)}) collective-permute-start(bf16[4,272,128]{2,1,0:T(8,128)(2,1)S(1)} %pad_maximum_fusion.2), channel_id=1, source_target_pairs={{0,64},{16,80},{32,96},{48,112},{64,0},{80,16},{96,32},{112,48},{1... | collective-permute-start | bytes 835592 | tf_op jit(solution)/shard_map/ppermute | solution.py:33
  58.3 14.4 %collective-permute-start.4 = (bf16[8,272,128]{2,1,0:T(8,128)(2,1)S(1)}, bf16[8,272,128]{2,1,0:T(8,128)(2,1)S(1)}, u32[]{:S(2)}, u32[]{:S(2)}) collective-permute-start(bf16[8,272,128]{2,1,0:T(8,128)(2,1)S(1)} %pad_maximum_fusion.1), channel_id=1, source_target_pairs={{0,128},{16,144},{32,160},{48,176},{64,192},{80,208},{96,224},{112... | collective-permute-start | bytes 1671176 | tf_op jit(solution)/shard_map/ppermute | solution.py:33
  73.7 26.9 %collective-permute-start.5 = (bf16[16,272,128]{2,1,0:T(8,128)(2,1)S(1)}, bf16[16,272,128]{2,1,0:T(8,128)(2,1)S(1)}, u32[]{:S(2)}, u32[]{:S(2)}) collective-permute-start(bf16[16,272,128]{2,1,0:T(8,128)(2,1)S(1)} %get-tuple-element.45), channel_id=1, source_target_pairs={{0,256},{16,272},{32,288},{48,304},{64,320},{80,336},{96,352},{112... | collective-permute-start | bytes 3342344 | tf_op jit(solution)/shard_map/ppermute | solution.py:33
  128.8 8.9 %copy-start.60 = (pred[768]{0:T(1024)(128)(4,1)S(1)}, pred[768]{0:T(1024)(128)(4,1)}, u32[]{:S(2)}) copy-start(pred[768]{0:T(1024)(128)(4,1)} %and.116) | copy-start | bytes 2308
  132.6 5.2 %copy-start.21 = (bf16[12,64,128]{2,1,0:T(8,128)(2,1)S(1)}, bf16[12,64,128]{2,1,0:T(8,128)(2,1)}, u32[]{:S(2)}) copy-start(bf16[12,64,128]{2,1,0:T(8,128)(2,1)} %get-tuple-element.41) | copy-start | bytes 589828
  132.6 5.2 %copy-start.31 = (bf16[4,64,128]{2,1,0:T(8,128)(2,1)S(1)}, bf16[4,64,128]{2,1,0:T(8,128)(2,1)}, u32[]{:S(2)}) copy-start(bf16[4,64,128]{2,1,0:T(8,128)(2,1)} %get-tuple-element.28) | copy-start | bytes 196612
  133.8 5.4 %copy-start.19 = (bf16[16,64,128]{2,1,0:T(8,128)(2,1)S(1)}, bf16[16,64,128]{2,1,0:T(8,128)(2,1)}, u32[]{:S(2)}) copy-start(bf16[16,64,128]{2,1,0:T(8,128)(2,1)} %get-tuple-element.39) | copy-start | bytes 786436
  133.8 5.4 %copy-start.30 = (bf16[4,64,128]{2,1,0:T(8,128)(2,1)S(1)}, bf16[4,64,128]{2,1,0:T(8,128)(2,1)}, u32[]{:S(2)}) copy-start(bf16[4,64,128]{2,1,0:T(8,128)(2,1)} %get-tuple-element.27) | copy-start | bytes 196612
  133.8 5.4 %copy-start.55 = (s32[1024]{0:T(1024)S(1)}, s32[1024]{0:T(1024)}, u32[]{:S(2)}) copy-start(s32[1024]{0:T(1024)} %iota_add_fusion.3) | copy-start | bytes 12292
  133.8 5.4 %copy-start.59 = (pred[1024]{0:T(1024)(128)(4,1)S(1)}, pred[1024]{0:T(1024)(128)(4,1)}, u32[]{:S(2)}) copy-start(pred[1024]{0:T(1024)(128)(4,1)} %and.119) | copy-start | bytes 3076
  133.8 5.4 %copy-start.69 = (s32[256]{0:T(256)S(1)}, s32[256]{0:T(256)}, u32[]{:S(2)}) copy-start(s32[256]{0:T(256)} %iota_add_fusion.10) | copy-start | bytes 3076
  137.8 2.3 %copy-start.11 = (bf16[20,64,128]{2,1,0:T(8,128)(2,1)S(1)}, bf16[20,64,128]{2,1,0:T(8,128)(2,1)}, u32[]{:S(2)}) copy-start(bf16[20,64,128]{2,1,0:T(8,128)(2,1)} %get-tuple-element.37) | copy-start | bytes 983044
  137.8 2.3 %copy-start.29 = (bf16[4,64,128]{2,1,0:T(8,128)(2,1)S(1)}, bf16[4,64,128]{2,1,0:T(8,128)(2,1)}, u32[]{:S(2)}) copy-start(bf16[4,64,128]{2,1,0:T(8,128)(2,1)} %get-tuple-element.26) | copy-start | bytes 196612
  137.8 2.3 %copy-start.52 = (s32[1280]{0:T(1024)S(1)}, s32[1280]{0:T(1024)}, u32[]{:S(2)}) copy-start(s32[1280]{0:T(1024)} %iota_add_fusion.2) | copy-start | bytes 15364
  137.8 2.3 %copy-start.58 = (pred[1280]{0:T(1024)(128)(4,1)S(1)}, pred[1280]{0:T(1024)(128)(4,1)}, u32[]{:S(2)}) copy-start(pred[1280]{0:T(1024)(128)(4,1)} %and.122) | copy-start | bytes 3844
  137.8 2.3 %copy-start.71 = (s32[256]{0:T(256)S(1)}, s32[256]{0:T(256)}, u32[]{:S(2)}) copy-start(s32[256]{0:T(256)} %iota_add_fusion.9) | copy-start | bytes 3076
  143.3 1.7 copy-start.22
  143.3 1.7 copy-start.79
  144.1 1.8 copy-start.15
  144.1 1.9 copy-start.18
  144.2 1.9 copy-start.77
  144.7 1.8 copy-start.67
  145.0 1.7 copy-start.10
  145.0 1.7 copy-start.76
  148.5 2.8 %copy-start.24 = (bf16[64,128]{1,0:T(8,128)(2,1)S(1)}, bf16[64,128]{1,0:T(8,128)(2,1)}, u32[]{:S(2)}) copy-start(bf16[64,128]{1,0:T(8,128)(2,1)} %param.21) | copy-start | bytes 49156
  148.6 2.6 %copy-start.48 = (pred[64]{0:T(512)(128)(4,1)S(1)}, pred[64]{0:T(512)(128)(4,1)}, u32[]{:S(2)}) copy-start(pred[64]{0:T(512)(128)(4,1)} %iota_compare_fusion.4) | copy-start | bytes 196
  149.2 5.6 %copy-start.42 = (bf16[64,128]{1,0:T(8,128)(2,1)S(1)}, bf16[64,128]{1,0:T(8,128)(2,1)}, u32[]{:S(2)}) copy-start(bf16[64,128]{1,0:T(8,128)(2,1)} %get-tuple-element.84) | copy-start | bytes 49156
  149.2 5.6 %copy-start.68 = (f32[2048]{0:T(1024)S(1)}, f32[2048]{0:T(1024)}, u32[]{:S(2)}) copy-start(f32[2048]{0:T(1024)} %copy-done.67) | copy-start | bytes 24580
  149.2 5.6 %copy-start.75 = (s32[64]{0:T(128)S(1)}, s32[64]{0:T(128)}, u32[]{:S(2)}) copy-start(s32[64]{0:T(128)} %iota_add_fusion.14) | copy-start | bytes 772
  150.1 6.2 %copy-start.25 = (bf16[64,128]{1,0:T(8,128)(2,1)S(1)}, bf16[64,128]{1,0:T(8,128)(2,1)}, u32[]{:S(2)}) copy-start(bf16[64,128]{1,0:T(8,128)(2,1)} %get-tuple-element.86) | copy-start | bytes 49156
  151.2 5.0 %copy-start.46 = (f32[2048]{0:T(1024)S(1)}, f32[2048]{0:T(1024)}, u32[]{:S(2)}) copy-start(f32[2048]{0:T(1024)} %copy-done.45) | copy-start | bytes 24580
  156.2 48.9 %copy-start.41 = (f32[1024]{0:T(1024)S(1)}, f32[1024]{0:T(1024)}, u32[]{:S(2)}) copy-start(f32[1024]{0:T(1024)} %param.15) | copy-start | bytes 12292
  157.9 47.5 %copy-start.49 = (pred[64]{0:T(512)(128)(4,1)S(1)}, pred[64]{0:T(512)(128)(4,1)}, u32[]{:S(2)}) copy-start(pred[64]{0:T(512)(128)(4,1)} %iota_compare_fusion.4) | copy-start | bytes 196
  157.9 47.5 %copy-start.54 = (f32[64]{0:T(128)S(1)}, f32[64]{0:T(128)}, u32[]{:S(2)}) copy-start(f32[64]{0:T(128)} %copy-done.53) | copy-start | bytes 772
  158.0 47.5 %copy-start.56 = (f32[64]{0:T(128)S(1)}, f32[64]{0:T(128)}, u32[]{:S(2)}) copy-start(f32[64]{0:T(128)} %get-tuple-element.67) | copy-start | bytes 772
  161.3 25.2 %collective-permute-start.12 = (bf16[64,1024]{1,0:T(8,128)(2,1)S(1)}, bf16[64,1024]{1,0:T(8,128)(2,1)S(1)}, u32[]{:S(2)}, u32[]{:S(2)}) collective-permute-start(bf16[64,1024]{1,0:T(8,128)(2,1)S(1)} %fusion.32), channel_id=1, source_target_pairs={{0,14},{2,0},{4,2},{6,4},{8,6},{10,8},{12,10},{14,12},{1,15},{3,1}... | collective-permute-start | bytes 393224 | tf_op jit(solution)/shard_map/ppermute | solution.py:45
  172.3 17.6 %collective-permute-start.11 = (bf16[64,1024]{1,0:T(8,128)(2,1)S(1)}, bf16[64,1024]{1,0:T(8,128)(2,1)S(1)}, u32[]{:S(2)}, u32[]{:S(2)}) collective-permute-start(bf16[64,1024]{1,0:T(8,128)(2,1)S(1)} %fusion.32), channel_id=1, source_target_pairs={{0,12},{2,14},{4,0},{6,2},{8,4},{10,6},{12,8},{14,10},{1,13},{3,15... | collective-permute-start | bytes 393224 | tf_op jit(solution)/shard_map/ppermute | solution.py:45
  174.7 20.4 %collective-permute-start.10 = (bf16[64,1024]{1,0:T(8,128)(2,1)S(1)}, bf16[64,1024]{1,0:T(8,128)(2,1)S(1)}, u32[]{:S(2)}, u32[]{:S(2)}) collective-permute-start(bf16[64,1024]{1,0:T(8,128)(2,1)S(1)} %fusion.32), channel_id=1, source_target_pairs={{0,10},{2,12},{4,14},{6,0},{8,2},{10,4},{12,6},{14,8},{1,11},{3,13... | collective-permute-start | bytes 393224 | tf_op jit(solution)/shard_map/ppermute | solution.py:45
  176.7 18.4 %collective-permute-start.9 = (bf16[64,1024]{1,0:T(8,128)(2,1)S(1)}, bf16[64,1024]{1,0:T(8,128)(2,1)S(1)}, u32[]{:S(2)}, u32[]{:S(2)}) collective-permute-start(bf16[64,1024]{1,0:T(8,128)(2,1)S(1)} %fusion.32), channel_id=1, source_target_pairs={{0,8},{2,10},{4,12},{6,14},{8,0},{10,2},{12,4},{14,6},{1,9},{3,11}... | collective-permute-start | bytes 393224 | tf_op jit(solution)/shard_map/ppermute | solution.py:45
  184.6 15.4 %collective-permute-start.8 = (bf16[64,1024]{1,0:T(8,128)(2,1)S(1)}, bf16[64,1024]{1,0:T(8,128)(2,1)S(1)}, u32[]{:S(2)}, u32[]{:S(2)}) collective-permute-start(bf16[64,1024]{1,0:T(8,128)(2,1)S(1)} %fusion.32), channel_id=1, source_target_pairs={{0,6},{2,8},{4,10},{6,12},{8,14},{10,0},{12,2},{14,4},{1,7},{3,9},... | collective-permute-start | bytes 393224 | tf_op jit(solution)/shard_map/ppermute | solution.py:45
  186.5 17.9 %collective-permute-start.7 = (bf16[64,1024]{1,0:T(8,128)(2,1)S(1)}, bf16[64,1024]{1,0:T(8,128)(2,1)S(1)}, u32[]{:S(2)}, u32[]{:S(2)}) collective-permute-start(bf16[64,1024]{1,0:T(8,128)(2,1)S(1)} %fusion.32), channel_id=1, source_target_pairs={{0,4},{2,6},{4,8},{6,10},{8,12},{10,14},{12,0},{14,2},{1,5},{3,7},... | collective-permute-start | bytes 393224 | tf_op jit(solution)/shard_map/ppermute | solution.py:45
  189.9 15.3 %collective-permute-start.6 = (bf16[64,1024]{1,0:T(8,128)(2,1)S(1)}, bf16[64,1024]{1,0:T(8,128)(2,1)S(1)}, u32[]{:S(2)}, u32[]{:S(2)}) collective-permute-start(bf16[64,1024]{1,0:T(8,128)(2,1)S(1)} %fusion.32), channel_id=1, source_target_pairs={{0,2},{2,4},{4,6},{6,8},{8,10},{10,12},{12,14},{14,0},{1,3},{3,5},... | collective-permute-start | bytes 393224 | tf_op jit(solution)/shard_map/ppermute | solution.py:45
  209.6 7.0 %copy-start.1 = (f32[512,1024]{1,0:T(8,128)S(1)}, f32[512,1024]{1,0:T(8,128)}, u32[]{:S(2)}) copy-start(f32[512,1024]{1,0:T(8,128)} %scatter_custom_fusion) | copy-start | bytes 6291460
  209.6 7.0 %copy-start.33 = (f32[1,1024]{1,0:T(1,128)S(1)}, f32[1,1024]{1,0:T(1,128)}, u32[]{:S(2)}) copy-start(f32[1,1024]{1,0:T(1,128)} %copy-done.32) | copy-start | bytes 12292
  209.6 7.0 %copy-start.35 = (f32[1,1024]{1,0:T(1,128)S(1)}, f32[1,1024]{1,0:T(1,128)}, u32[]{:S(2)}) copy-start(f32[1,1024]{1,0:T(1,128)} %copy-done.34) | copy-start | bytes 12292
  209.6 7.0 %copy-start.37 = (f32[1,1024]{1,0:T(1,128)S(1)}, f32[1,1024]{1,0:T(1,128)}, u32[]{:S(2)}) copy-start(f32[1,1024]{1,0:T(1,128)} %copy-done.36) | copy-start | bytes 12292
  209.7 7.0 %copy-start.39 = (f32[1,1024]{1,0:T(1,128)S(1)}, f32[1,1024]{1,0:T(1,128)}, u32[]{:S(2)}) copy-start(f32[1,1024]{1,0:T(1,128)} %copy-done.38) | copy-start | bytes 12292
  209.7 7.0 %collective-permute-start.13 = (f32[3,1024]{1,0:T(4,128)S(1)}, f32[3,1024]{1,0:T(4,128)S(1)}, u32[]{:S(2)}, u32[]{:S(2)}) collective-permute-start(f32[3,1024]{1,0:T(4,128)S(1)} %slice.495), channel_id=1, source_target_pairs={{16,0},{32,16},{48,32},{64,48},{80,64},{96,80},{112,96},{128,112},... | collective-permute-start | bytes 36872 | tf_op jit(solution)/shard_map/ppermute | solution.py:20
  (30 other events, 37.7 us)

commit v2 on v1

--- a/solution.py
+++ b/solution.py
@@ -27,13 +27,18 @@
 def gather_blocks(block, axis):
     devices = lax.axis_size(axis)
     me = lax.axis_index(axis)
+    steps = [4, 16, 2, 1, 8] if devices == 32 else [1 << b for b in range(devices.bit_length() - 1)]
     held = block[None]
-    step = 1
-    while step < devices:
+    for step in steps:
         other = lax.ppermute(held, axis, [(i, i ^ step) for i in range(devices)])
         held = jnp.concatenate([held, other], axis=0)
-        step *= 2
-    order = jnp.arange(devices, dtype=jnp.int32) ^ me
+    offset = [0]
+    for step in steps:
+        offset = offset + [o ^ step for o in offset]
+    position = [0] * devices
+    for j, o in enumerate(offset):
+        position[o] = j
+    order = jnp.asarray(position, dtype=jnp.int32)[jnp.arange(devices, dtype=jnp.int32) ^ me]
     return jnp.take(held, order, axis=0)
 
 

time: 227 us -> 232 us (1.022)
  the two profiles are of different devices: /device:TPU:24 before, /device:TPU:60 now
where the time goes in v2:
time: 232 us; the launch traced here: 230 us
  waiting for transfers between devices  62.1 us (27%)
  starting transfers between devices  57.6 us (25%)
  local copies, waits for them, and re-layouts  48.1 us (21%)
  other arithmetic  33 us (14%)
  matrix products  26.9 us (12%)
  between operations  2.79 us (1%)
    ppermute x5, waiting for transfers between devices, gather_blocks(): other = lax.ppermute(held, axis, [(i, i ^ step) for i in range(devices)])  48.4 us
    ppermute x7, starting transfers between devices, summed_over(): lax.ppermute(sent, axis, [(i, (i + shift) % devices) for i in range(devic...  32.3 us
    ppermute x5, starting transfers between devices, gather_blocks(): other = lax.ppermute(held, axis, [(i, i ^ step) for i in range(devices)])  19.9 us
    ppermute x7, waiting for transfers between devices, summed_over(): lax.ppermute(sent, axis, [(i, (i + shift) % devices) for i in range(devic...  10.7 us
    broadcast_in_dim x8, local copies, waits for them, and re-layouts, per_device(): jnp.where(all_live[q0:q1, None], product / row_sum[:, None], jnp.float32(...  10.1 us
    dot_general x8, matrix products, per_device(): jnp.dot(all_queries[q0:q1], all_keys[:q1].T, preferred_element_type=jnp.f...  6.55 us
    unnamed x174, local copies, waits for them, and re-layouts  5.53 us
    slice x6, local copies, waits for them, and re-layouts, per_device(): all_keys[:q1]  5.45 us
  transfers between devices with their start and end apart: 14, of which 9 were waited for; matrix products, arithmetic and copies ran while one was open for 9% of the time, Pallas kernels for 0%

profile of v2, /device:TPU:60, one launch (start us, length us, event | category | flops | bytes accessed | tf_op | source)
XLA Modules:
  0.0 230.4 jit_solution(15457735523199878944)
XLA Ops:
  1.5 2.3 collective-permute-start
  4.5 1.2 compare_and_fusion.4
  10.7 2.2 gather_fusion.1
  12.9 1.5 pad_maximum_fusion
  14.4 1.4 gather_fusion.6
  15.8 1.4 gather_fusion.5
  17.1 1.4 gather_fusion.4
  18.5 1.4 gather_fusion.3
  20.0 1.9 multiply_reduce_fusion.1
  25.0 7.1 %collective-permute-start.1 = (bf16[1,272,128]{2,1,0:T(8,128)(2,1)S(1)}, bf16[1,272,128]{2,1,0:T(8,128)(2,1)S(1)}, u32[]{:S(2)}, u32[]{:S(2)}) collective-permute-start(bf16[1,272,128]{2,1,0:T(8,128)(2,1)S(1)} %bitcast.125), channel_id=1, source_target_pairs={{0,64},{16,80},{32,96},{48,112},{64,0},{80,16},{96,32},{112,48},{1... | collective-permute-start | bytes 208904 | tf_op jit(solution)/shard_map/ppermute | solution.py:33
  32.7 3.2 %collective-permute-done.1 = bf16[1,272,128]{2,1,0:T(8,128)(2,1)S(1)} collective-permute-done((bf16[1,272,128]{2,1,0:T(8,128)(2,1)S(1)}, bf16[1,272,128]{2,1,0:T(8,128)(2,1)S(1)}, u32[]{:S(2)}, u32[]{:S(2)}) %collective-permute-start.1) | collective-permute-done | bytes 69664 | tf_op jit(solution)/shard_map/ppermute | solution.py:33
  36.0 2.4 %collective-permute-start.2 = (bf16[2,272,128]{2,1,0:T(8,128)(2,1)S(1)}, bf16[2,272,128]{2,1,0:T(8,128)(2,1)S(1)}, u32[]{:S(2)}, u32[]{:S(2)}) collective-permute-start(bf16[2,272,128]{2,1,0:T(8,128)(2,1)S(1)} %pad_maximum_fusion.3), channel_id=1, source_target_pairs={{0,256},{16,272},{32,288},{48,304},{64,320},{80,336},{96,352},{112... | collective-permute-start | bytes 417800 | tf_op jit(solution)/shard_map/ppermute | solution.py:33
  39.0 5.4 %collective-permute-done.2 = bf16[2,272,128]{2,1,0:T(8,128)(2,1)S(1)} collective-permute-done((bf16[2,272,128]{2,1,0:T(8,128)(2,1)S(1)}, bf16[2,272,128]{2,1,0:T(8,128)(2,1)S(1)}, u32[]{:S(2)}, u32[]{:S(2)}) %collective-permute-start.2) | collective-permute-done | bytes 139296 | tf_op jit(solution)/shard_map/ppermute | solution.py:33
  44.4 3.6 %collective-permute-start.3 = (bf16[4,272,128]{2,1,0:T(8,128)(2,1)S(1)}, bf16[4,272,128]{2,1,0:T(8,128)(2,1)S(1)}, u32[]{:S(2)}, u32[]{:S(2)}) collective-permute-start(bf16[4,272,128]{2,1,0:T(8,128)(2,1)S(1)} %pad_maximum_fusion.2), channel_id=1, source_target_pairs={{0,32},{16,48},{32,0},{48,16},{64,96},{80,112},{96,64},{112,80},{1... | collective-permute-start | bytes 835592 | tf_op jit(solution)/shard_map/ppermute | solution.py:33
  50.5 8.2 %collective-permute-done.3 = bf16[4,272,128]{2,1,0:T(8,128)(2,1)S(1)} collective-permute-done((bf16[4,272,128]{2,1,0:T(8,128)(2,1)S(1)}, bf16[4,272,128]{2,1,0:T(8,128)(2,1)S(1)}, u32[]{:S(2)}, u32[]{:S(2)}) %collective-permute-start.3) | collective-permute-done | bytes 278560 | tf_op jit(solution)/shard_map/ppermute | solution.py:33
  58.8 1.9 collective-permute-start.4
  63.4 10.7 %collective-permute-done.4 = bf16[8,272,128]{2,1,0:T(8,128)(2,1)S(1)} collective-permute-done((bf16[8,272,128]{2,1,0:T(8,128)(2,1)S(1)}, bf16[8,272,128]{2,1,0:T(8,128)(2,1)S(1)}, u32[]{:S(2)}, u32[]{:S(2)}) %collective-permute-start.4) | collective-permute-done | bytes 557088 | tf_op jit(solution)/shard_map/ppermute | solution.py:33
  75.1 4.9 %collective-permute-start.5 = (bf16[16,272,128]{2,1,0:T(8,128)(2,1)S(1)}, bf16[16,272,128]{2,1,0:T(8,128)(2,1)S(1)}, u32[]{:S(2)}, u32[]{:S(2)}) collective-permute-start(bf16[16,272,128]{2,1,0:T(8,128)(2,1)S(1)} %get-tuple-element.45), channel_id=1, source_target_pairs={{0,128},{16,144},{32,160},{48,176},{64,192},{80,208},{96,224},{112... | collective-permute-start | bytes 3342344 | tf_op jit(solution)/shard_map/ppermute | solution.py:33
  82.9 20.8 %collective-permute-done.5 = bf16[16,272,128]{2,1,0:T(8,128)(2,1)S(1)} collective-permute-done((bf16[16,272,128]{2,1,0:T(8,128)(2,1)S(1)}, bf16[16,272,128]{2,1,0:T(8,128)(2,1)S(1)}, u32[]{:S(2)}, u32[]{:S(2)}) %collective-permute-start.5) | collective-permute-done | bytes 1114144 | tf_op jit(solution)/shard_map/ppermute | solution.py:33
  103.7 1.1 constant_dynamic-update-slice_fusion.10
  104.8 3.9 %gather_fusion.2 = bf16[32,272,128]{2,1,0:T(8,128)(2,1)} fusion(bf16[32,272,128]{2,1,0:T(8,128)(2,1)} %constant_dynamic-update-slice_fusion.10, s32[1024]{0:T(1024)S(1)} %pad_clamp_fusion), kind=kCustom, calls=%fused_computation.6 | custom fusion | bytes 4456576 | tf_op jit(solution)/shard_map/jit(_take)/gather | solution.py:42
  108.6 1.9 broadcast_select_fusion
  118.4 1.1 fusion.117
  119.6 1.3 fusion.115
  121.5 1.2 broadcast_in_dim.248
  122.7 1.3 and.113
  124.0 1.2 broadcast_in_dim.252
  125.9 1.3 broadcast_in_dim.255
  127.1 1.3 and.119
  128.4 1.2 broadcast_in_dim.258
  130.3 1.3 broadcast_in_dim.261
  131.7 1.3 broadcast_in_dim.264
  133.1 1.3 broadcast_in_dim.267
  134.4 1.3 broadcast_in_dim.270
  135.7 1.1 fusion.125
  137.0 1.1 constant_dynamic-update-slice_fusion.23
  138.1 1.3 constant_dynamic-update-slice_fusion.24
  139.4 1.2 fusion.126
  140.9 1.1 fusion.127
  153.1 1.2 fusion.9
  154.3 1.7 fusion.52
  156.0 1.9 fusion.133
  157.9 1.4 fusion.11
  159.3 1.7 fusion.51
  161.0 1.9 convolution_add_fusion.1
  162.9 1.4 fusion.32
  164.4 10.9 %collective-permute-start.12 = (bf16[64,1024]{1,0:T(8,128)(2,1)S(1)}, bf16[64,1024]{1,0:T(8,128)(2,1)S(1)}, u32[]{:S(2)}, u32[]{:S(2)}) collective-permute-start(bf16[64,1024]{1,0:T(8,128)(2,1)S(1)} %fusion.32), channel_id=1, source_target_pairs={{0,14},{2,0},{4,2},{6,4},{8,6},{10,8},{12,10},{14,12},{1,15},{3,1}... | collective-permute-start | bytes 393224 | tf_op jit(solution)/shard_map/ppermute | solution.py:50
  175.3 2.5 %collective-permute-start.11 = (bf16[64,1024]{1,0:T(8,128)(2,1)S(1)}, bf16[64,1024]{1,0:T(8,128)(2,1)S(1)}, u32[]{:S(2)}, u32[]{:S(2)}) collective-permute-start(bf16[64,1024]{1,0:T(8,128)(2,1)S(1)} %fusion.32), channel_id=1, source_target_pairs={{0,12},{2,14},{4,0},{6,2},{8,4},{10,6},{12,8},{14,10},{1,13},{3,15... | collective-permute-start | bytes 393224 | tf_op jit(solution)/shard_map/ppermute | solution.py:50
  177.8 1.9 collective-permute-start.10
  179.7 7.8 %collective-permute-start.9 = (bf16[64,1024]{1,0:T(8,128)(2,1)S(1)}, bf16[64,1024]{1,0:T(8,128)(2,1)S(1)}, u32[]{:S(2)}, u32[]{:S(2)}) collective-permute-start(bf16[64,1024]{1,0:T(8,128)(2,1)S(1)} %fusion.32), channel_id=1, source_target_pairs={{0,8},{2,10},{4,12},{6,14},{8,0},{10,2},{12,4},{14,6},{1,9},{3,11}... | collective-permute-start | bytes 393224 | tf_op jit(solution)/shard_map/ppermute | solution.py:50
  187.6 1.9 collective-permute-start.8
  189.5 3.4 %collective-permute-start.7 = (bf16[64,1024]{1,0:T(8,128)(2,1)S(1)}, bf16[64,1024]{1,0:T(8,128)(2,1)S(1)}, u32[]{:S(2)}, u32[]{:S(2)}) collective-permute-start(bf16[64,1024]{1,0:T(8,128)(2,1)S(1)} %fusion.32), channel_id=1, source_target_pairs={{0,4},{2,6},{4,8},{6,10},{8,12},{10,14},{12,0},{14,2},{1,5},{3,7},... | collective-permute-start | bytes 393224 | tf_op jit(solution)/shard_map/ppermute | solution.py:50
  192.9 3.9 %collective-permute-start.6 = (bf16[64,1024]{1,0:T(8,128)(2,1)S(1)}, bf16[64,1024]{1,0:T(8,128)(2,1)S(1)}, u32[]{:S(2)}, u32[]{:S(2)}) collective-permute-start(bf16[64,1024]{1,0:T(8,128)(2,1)S(1)} %fusion.32), channel_id=1, source_target_pairs={{0,2},{2,4},{4,6},{6,8},{8,10},{10,12},{12,14},{14,0},{1,3},{3,5},... | collective-permute-start | bytes 393224 | tf_op jit(solution)/shard_map/ppermute | solution.py:50
  196.8 1.3 constant_dynamic-slice_fusion
  198.1 6.3 %collective-permute-done.8 = bf16[64,1024]{1,0:T(8,128)(2,1)S(1)} collective-permute-done((bf16[64,1024]{1,0:T(8,128)(2,1)S(1)}, bf16[64,1024]{1,0:T(8,128)(2,1)S(1)}, u32[]{:S(2)}, u32[]{:S(2)}) %collective-permute-start.8) | collective-permute-done | bytes 131104 | tf_op jit(solution)/shard_map/ppermute | solution.py:50
  204.4 2.0 collective-permute-done.7
  206.4 2.3 %collective-permute-done.6 = bf16[64,1024]{1,0:T(8,128)(2,1)S(1)} collective-permute-done((bf16[64,1024]{1,0:T(8,128)(2,1)S(1)}, bf16[64,1024]{1,0:T(8,128)(2,1)S(1)}, u32[]{:S(2)}, u32[]{:S(2)}) %collective-permute-start.6) | collective-permute-done | bytes 131104 | tf_op jit(solution)/shard_map/ppermute | solution.py:50
  209.9 2.7 %scatter_custom_fusion = f32[512,1024]{1,0:T(8,128)} fusion(s32[64]{0:T(128)} %copy-done.63, f32[64,1024]{1,0:T(8,128)S(1)} %fusion.96, f32[]{:T(128)} %constant.24.clone.1), kind=kCustom, calls=%fused_computation.99 | custom fusion | flops 65536 | bytes 2097664 | tf_op jit(solution)/shard_map/scatter-add | solution.py:192
  213.3 3.0 %collective-permute-start.13 = (f32[3,1024]{1,0:T(4,128)S(1)}, f32[3,1024]{1,0:T(4,128)S(1)}, u32[]{:S(2)}, u32[]{:S(2)}) collective-permute-start(f32[3,1024]{1,0:T(4,128)S(1)} %slice.497), channel_id=1, source_target_pairs={{16,0},{32,16},{48,32},{64,48},{80,64},{96,80},{112,96},{128,112},... | collective-permute-start | bytes 36872 | tf_op jit(solution)/shard_map/ppermute | solution.py:20
  216.3 1.8 constant_dynamic-update-slice_fusion.27
  218.2 3.0 %collective-permute-done.13 = f32[3,1024]{1,0:T(4,128)S(1)} collective-permute-done((f32[3,1024]{1,0:T(4,128)S(1)}, f32[3,1024]{1,0:T(4,128)S(1)}, u32[]{:S(2)}, u32[]{:S(2)}) %collective-permute-start.13) | collective-permute-done | bytes 12320 | tf_op jit(solution)/shard_map/ppermute | solution.py:20
  221.2 2.2 fusion.14
  223.5 4.2 %scatter_custom_fusion.1 = f32[512,1024]{1,0:T(8,128)} fusion(f32[512,1024]{1,0:T(8,128)} %fusion.14, s32[64]{0:T(128)} %copy-done.63, f32[64,1024]{1,0:T(8,128)S(1)} %get-tuple-element.80, f32[64,1024]{1,0:T(8,128)S(1)} %get-tuple-element.4, f32[64]{0:T(128)S(1)} %broadcast_multiply_fusion, f32[64]{0:T(128)S(1)} %copy-done.57, f32[64]{0:T(128)S(1)} %copy-done.55, ...), kind=kCustom, calls=%fused_computation.260 | custom fusion | flops 393216 | bytes 2622272 | tf_op jit(solution)/shard_map/scatter-add | solution.py:193
  227.7 2.7 %convert_element_type.291 = bf16[512,1024]{1,0:T(8,128)(2,1)} convert(f32[512,1024]{1,0:T(8,128)} %scatter_custom_fusion.1) | non-fusion elementwise | flops 524288 | bytes 3145728 | tf_op jit(solution)/shard_map/convert_element_type | solution.py:199
  (280 shorter events, 41.9 us)
Async XLA Ops:
  0.6 19.3 %copy-start = (bf16[1024,1024]{1,0:T(8,128)(2,1)S(1)}, bf16[1024,1024]{1,0:T(8,128)(2,1)}, u32[]{:S(2)}) copy-start(bf16[1024,1024]{1,0:T(8,128)(2,1)} %param.15) | copy-start | bytes 6291460
  1.5 11.4 %collective-permute-start = (bf16[3,1024]{1,0:T(4,128)(2,1)S(1)}, bf16[3,1024]{1,0:T(4,128)(2,1)S(1)}, u32[]{:S(2)}, u32[]{:S(2)}) collective-permute-start(bf16[3,1024]{1,0:T(4,128)(2,1)S(1)} %slice.518), channel_id=1, source_target_pairs={{0,16},{16,32},{32,48},{48,64},{64,80},{80,96},{96,112},{112,128},... | collective-permute-start | bytes 18440 | tf_op jit(solution)/shard_map/ppermute | solution.py:20
  4.5 5.6 %copy-start.63 = (s32[64]{0:T(128)}, s32[64]{0:T(128)S(1)}, u32[]{:S(2)}) copy-start(s32[64]{0:T(128)S(1)} %get-tuple-element.77) | copy-start | bytes 772
  9.4 10.4 %copy-start.33 = (f32[1,1024]{1,0:T(1,128)}, f32[1,1024]{1,0:T(1,128)S(1)}, u32[]{:S(2)}) copy-start(f32[1,1024]{1,0:T(1,128)S(1)} %get-tuple-element.55) | copy-start | bytes 12292
  9.4 10.4 %copy-start.35 = (f32[1,1024]{1,0:T(1,128)}, f32[1,1024]{1,0:T(1,128)S(1)}, u32[]{:S(2)}) copy-start(f32[1,1024]{1,0:T(1,128)S(1)} %get-tuple-element.56) | copy-start | bytes 12292
  9.4 10.4 %copy-start.37 = (f32[1,1024]{1,0:T(1,128)}, f32[1,1024]{1,0:T(1,128)S(1)}, u32[]{:S(2)}) copy-start(f32[1,1024]{1,0:T(1,128)S(1)} %get-tuple-element.57) | copy-start | bytes 12292
  9.4 10.4 %copy-start.39 = (f32[1,1024]{1,0:T(1,128)}, f32[1,1024]{1,0:T(1,128)S(1)}, u32[]{:S(2)}) copy-start(f32[1,1024]{1,0:T(1,128)S(1)} %get-tuple-element.58) | copy-start | bytes 12292
  19.9 2.6 %copy-start.41 = (f32[1024]{0:T(1024)S(1)}, f32[1024]{0:T(1024)}, u32[]{:S(2)}) copy-start(f32[1024]{0:T(1024)} %param.16) | copy-start | bytes 12292
  19.9 2.7 %copy-start.7 = (bf16[1024,128]{1,0:T(8,128)(2,1)S(1)}, bf16[1024,128]{1,0:T(8,128)(2,1)}, u32[]{:S(2)}) copy-start(bf16[1024,128]{1,0:T(8,128)(2,1)} %param.17) | copy-start | bytes 786436
  19.9 3.5 %copy-start.6 = (bf16[1024,128]{1,0:T(8,128)(2,1)S(1)}, bf16[1024,128]{1,0:T(8,128)(2,1)}, u32[]{:S(2)}) copy-start(bf16[1024,128]{1,0:T(8,128)(2,1)} %param.18) | copy-start | bytes 786436
  19.9 4.2 %copy-start.8 = (bf16[1024,128]{1,0:T(8,128)(2,1)S(1)}, bf16[1024,128]{1,0:T(8,128)(2,1)}, u32[]{:S(2)}) copy-start(bf16[1024,128]{1,0:T(8,128)(2,1)} %param.19) | copy-start | bytes 786436
  19.9 5.0 %copy-start.24 = (bf16[64,128]{1,0:T(8,128)(2,1)S(1)}, bf16[64,128]{1,0:T(8,128)(2,1)}, u32[]{:S(2)}) copy-start(bf16[64,128]{1,0:T(8,128)(2,1)} %param.22) | copy-start | bytes 49156
  19.9 5.0 %copy-start.48 = (pred[64]{0:T(512)(128)(4,1)S(1)}, pred[64]{0:T(512)(128)(4,1)}, u32[]{:S(2)}) copy-start(pred[64]{0:T(512)(128)(4,1)} %iota_compare_fusion.4) | copy-start | bytes 196
  19.9 28.7 %copy-start.1 = (s32[32]{0:T(128)S(1)}, s32[32]{0:T(128)}, u32[]{:S(2)}) copy-start(s32[32]{0:T(128)} %constant.27.clone) | copy-start | bytes 388
  22.4 36.3 %copy-start.54 = (f32[64]{0:T(128)}, f32[64]{0:T(128)S(1)}, u32[]{:S(2)}) copy-start(f32[64]{0:T(128)S(1)} %get-tuple-element.68) | copy-start | bytes 772
  25.0 10.9 %collective-permute-start.1 = (bf16[1,272,128]{2,1,0:T(8,128)(2,1)S(1)}, bf16[1,272,128]{2,1,0:T(8,128)(2,1)S(1)}, u32[]{:S(2)}, u32[]{:S(2)}) collective-permute-start(bf16[1,272,128]{2,1,0:T(8,128)(2,1)S(1)} %bitcast.125), channel_id=1, source_target_pairs={{0,64},{16,80},{32,96},{48,112},{64,0},{80,16},{96,32},{112,48},{1... | collective-permute-start | bytes 208904 | tf_op jit(solution)/shard_map/ppermute | solution.py:33
  36.0 8.5 %collective-permute-start.2 = (bf16[2,272,128]{2,1,0:T(8,128)(2,1)S(1)}, bf16[2,272,128]{2,1,0:T(8,128)(2,1)S(1)}, u32[]{:S(2)}, u32[]{:S(2)}) collective-permute-start(bf16[2,272,128]{2,1,0:T(8,128)(2,1)S(1)} %pad_maximum_fusion.3), channel_id=1, source_target_pairs={{0,256},{16,272},{32,288},{48,304},{64,320},{80,336},{96,352},{112... | collective-permute-start | bytes 417800 | tf_op jit(solution)/shard_map/ppermute | solution.py:33
  44.4 14.3 %collective-permute-start.3 = (bf16[4,272,128]{2,1,0:T(8,128)(2,1)S(1)}, bf16[4,272,128]{2,1,0:T(8,128)(2,1)S(1)}, u32[]{:S(2)}, u32[]{:S(2)}) collective-permute-start(bf16[4,272,128]{2,1,0:T(8,128)(2,1)S(1)} %pad_maximum_fusion.2), channel_id=1, source_target_pairs={{0,32},{16,48},{32,0},{48,16},{64,96},{80,112},{96,64},{112,80},{1... | collective-permute-start | bytes 835592 | tf_op jit(solution)/shard_map/ppermute | solution.py:33
  58.8 15.4 %collective-permute-start.4 = (bf16[8,272,128]{2,1,0:T(8,128)(2,1)S(1)}, bf16[8,272,128]{2,1,0:T(8,128)(2,1)S(1)}, u32[]{:S(2)}, u32[]{:S(2)}) collective-permute-start(bf16[8,272,128]{2,1,0:T(8,128)(2,1)S(1)} %pad_maximum_fusion.1), channel_id=1, source_target_pairs={{0,16},{16,0},{32,48},{48,32},{64,80},{80,64},{96,112},{112,96},{1... | collective-permute-start | bytes 1671176 | tf_op jit(solution)/shard_map/ppermute | solution.py:33
  75.1 28.6 %collective-permute-start.5 = (bf16[16,272,128]{2,1,0:T(8,128)(2,1)S(1)}, bf16[16,272,128]{2,1,0:T(8,128)(2,1)S(1)}, u32[]{:S(2)}, u32[]{:S(2)}) collective-permute-start(bf16[16,272,128]{2,1,0:T(8,128)(2,1)S(1)} %get-tuple-element.45), channel_id=1, source_target_pairs={{0,128},{16,144},{32,160},{48,176},{64,192},{80,208},{96,224},{112... | collective-permute-start | bytes 3342344 | tf_op jit(solution)/shard_map/ppermute | solution.py:33
  131.7 9.2 %copy-start.61 = (pred[768]{0:T(1024)(128)(4,1)S(1)}, pred[768]{0:T(1024)(128)(4,1)}, u32[]{:S(2)}) copy-start(pred[768]{0:T(1024)(128)(4,1)} %and.116) | copy-start | bytes 2308
  135.7 5.2 %copy-start.22 = (bf16[12,64,128]{2,1,0:T(8,128)(2,1)S(1)}, bf16[12,64,128]{2,1,0:T(8,128)(2,1)}, u32[]{:S(2)}) copy-start(bf16[12,64,128]{2,1,0:T(8,128)(2,1)} %get-tuple-element.41) | copy-start | bytes 589828
  135.7 5.2 %copy-start.32 = (bf16[4,64,128]{2,1,0:T(8,128)(2,1)S(1)}, bf16[4,64,128]{2,1,0:T(8,128)(2,1)}, u32[]{:S(2)}) copy-start(bf16[4,64,128]{2,1,0:T(8,128)(2,1)} %get-tuple-element.28) | copy-start | bytes 196612
  136.9 5.4 %copy-start.20 = (bf16[16,64,128]{2,1,0:T(8,128)(2,1)S(1)}, bf16[16,64,128]{2,1,0:T(8,128)(2,1)}, u32[]{:S(2)}) copy-start(bf16[16,64,128]{2,1,0:T(8,128)(2,1)} %get-tuple-element.39) | copy-start | bytes 786436
  136.9 5.4 %copy-start.31 = (bf16[4,64,128]{2,1,0:T(8,128)(2,1)S(1)}, bf16[4,64,128]{2,1,0:T(8,128)(2,1)}, u32[]{:S(2)}) copy-start(bf16[4,64,128]{2,1,0:T(8,128)(2,1)} %get-tuple-element.27) | copy-start | bytes 196612
  136.9 5.4 %copy-start.56 = (s32[1024]{0:T(1024)S(1)}, s32[1024]{0:T(1024)}, u32[]{:S(2)}) copy-start(s32[1024]{0:T(1024)} %get-tuple-element.121) | copy-start | bytes 12292
  136.9 5.4 %copy-start.60 = (pred[1024]{0:T(1024)(128)(4,1)S(1)}, pred[1024]{0:T(1024)(128)(4,1)}, u32[]{:S(2)}) copy-start(pred[1024]{0:T(1024)(128)(4,1)} %and.119) | copy-start | bytes 3076
  136.9 5.4 %copy-start.71 = (s32[256]{0:T(256)S(1)}, s32[256]{0:T(256)}, u32[]{:S(2)}) copy-start(s32[256]{0:T(256)} %iota_add_fusion.10) | copy-start | bytes 3076
  140.9 2.3 copy-start.12
  140.9 2.3 copy-start.30
  140.9 2.3 copy-start.53
  140.9 2.3 copy-start.59
  140.9 2.3 copy-start.70
  146.4 1.7 copy-start.23
  147.2 1.8 copy-start.16
  147.2 1.9 copy-start.19
  147.2 1.9 copy-start.78
  147.8 1.8 copy-start.68
  148.1 1.7 copy-start.11
  148.1 1.7 copy-start.77
  151.6 2.7 %copy-start.25 = (bf16[64,128]{1,0:T(8,128)(2,1)S(1)}, bf16[64,128]{1,0:T(8,128)(2,1)}, u32[]{:S(2)}) copy-start(bf16[64,128]{1,0:T(8,128)(2,1)} %param.22) | copy-start | bytes 49156
  151.7 2.6 %copy-start.49 = (pred[64]{0:T(512)(128)(4,1)S(1)}, pred[64]{0:T(512)(128)(4,1)}, u32[]{:S(2)}) copy-start(pred[64]{0:T(512)(128)(4,1)} %iota_compare_fusion.4) | copy-start | bytes 196
  152.3 5.5 %copy-start.43 = (bf16[64,128]{1,0:T(8,128)(2,1)S(1)}, bf16[64,128]{1,0:T(8,128)(2,1)}, u32[]{:S(2)}) copy-start(bf16[64,128]{1,0:T(8,128)(2,1)} %get-tuple-element.84) | copy-start | bytes 49156
  152.3 5.5 %copy-start.69 = (f32[2048]{0:T(1024)S(1)}, f32[2048]{0:T(1024)}, u32[]{:S(2)}) copy-start(f32[2048]{0:T(1024)} %copy-done.68) | copy-start | bytes 24580
  152.3 5.5 %copy-start.76 = (s32[64]{0:T(128)S(1)}, s32[64]{0:T(128)}, u32[]{:S(2)}) copy-start(s32[64]{0:T(128)} %iota_add_fusion.14) | copy-start | bytes 772
  153.1 6.1 %copy-start.26 = (bf16[64,128]{1,0:T(8,128)(2,1)S(1)}, bf16[64,128]{1,0:T(8,128)(2,1)}, u32[]{:S(2)}) copy-start(bf16[64,128]{1,0:T(8,128)(2,1)} %get-tuple-element.86) | copy-start | bytes 49156
  154.3 5.0 %copy-start.47 = (f32[2048]{0:T(1024)S(1)}, f32[2048]{0:T(1024)}, u32[]{:S(2)}) copy-start(f32[2048]{0:T(1024)} %copy-done.46) | copy-start | bytes 24580
  159.3 49.5 %copy-start.42 = (f32[1024]{0:T(1024)S(1)}, f32[1024]{0:T(1024)}, u32[]{:S(2)}) copy-start(f32[1024]{0:T(1024)} %param.16) | copy-start | bytes 12292
  161.0 48.1 %copy-start.50 = (pred[64]{0:T(512)(128)(4,1)S(1)}, pred[64]{0:T(512)(128)(4,1)}, u32[]{:S(2)}) copy-start(pred[64]{0:T(512)(128)(4,1)} %iota_compare_fusion.4) | copy-start | bytes 196
  161.0 48.1 %copy-start.55 = (f32[64]{0:T(128)S(1)}, f32[64]{0:T(128)}, u32[]{:S(2)}) copy-start(f32[64]{0:T(128)} %copy-done.54) | copy-start | bytes 772
  161.0 48.1 %copy-start.57 = (f32[64]{0:T(128)S(1)}, f32[64]{0:T(128)}, u32[]{:S(2)}) copy-start(f32[64]{0:T(128)} %get-tuple-element.67) | copy-start | bytes 772
  164.4 25.1 %collective-permute-start.12 = (bf16[64,1024]{1,0:T(8,128)(2,1)S(1)}, bf16[64,1024]{1,0:T(8,128)(2,1)S(1)}, u32[]{:S(2)}, u32[]{:S(2)}) collective-permute-start(bf16[64,1024]{1,0:T(8,128)(2,1)S(1)} %fusion.32), channel_id=1, source_target_pairs={{0,14},{2,0},{4,2},{6,4},{8,6},{10,8},{12,10},{14,12},{1,15},{3,1}... | collective-permute-start | bytes 393224 | tf_op jit(solution)/shard_map/ppermute | solution.py:50
  175.3 17.6 %collective-permute-start.11 = (bf16[64,1024]{1,0:T(8,128)(2,1)S(1)}, bf16[64,1024]{1,0:T(8,128)(2,1)S(1)}, u32[]{:S(2)}, u32[]{:S(2)}) collective-permute-start(bf16[64,1024]{1,0:T(8,128)(2,1)S(1)} %fusion.32), channel_id=1, source_target_pairs={{0,12},{2,14},{4,0},{6,2},{8,4},{10,6},{12,8},{14,10},{1,13},{3,15... | collective-permute-start | bytes 393224 | tf_op jit(solution)/shard_map/ppermute | solution.py:50
  177.8 20.3 %collective-permute-start.10 = (bf16[64,1024]{1,0:T(8,128)(2,1)S(1)}, bf16[64,1024]{1,0:T(8,128)(2,1)S(1)}, u32[]{:S(2)}, u32[]{:S(2)}) collective-permute-start(bf16[64,1024]{1,0:T(8,128)(2,1)S(1)} %fusion.32), channel_id=1, source_target_pairs={{0,10},{2,12},{4,14},{6,0},{8,2},{10,4},{12,6},{14,8},{1,11},{3,13... | collective-permute-start | bytes 393224 | tf_op jit(solution)/shard_map/ppermute | solution.py:50
  179.7 18.4 %collective-permute-start.9 = (bf16[64,1024]{1,0:T(8,128)(2,1)S(1)}, bf16[64,1024]{1,0:T(8,128)(2,1)S(1)}, u32[]{:S(2)}, u32[]{:S(2)}) collective-permute-start(bf16[64,1024]{1,0:T(8,128)(2,1)S(1)} %fusion.32), channel_id=1, source_target_pairs={{0,8},{2,10},{4,12},{6,14},{8,0},{10,2},{12,4},{14,6},{1,9},{3,11}... | collective-permute-start | bytes 393224 | tf_op jit(solution)/shard_map/ppermute | solution.py:50
  187.6 16.9 %collective-permute-start.8 = (bf16[64,1024]{1,0:T(8,128)(2,1)S(1)}, bf16[64,1024]{1,0:T(8,128)(2,1)S(1)}, u32[]{:S(2)}, u32[]{:S(2)}) collective-permute-start(bf16[64,1024]{1,0:T(8,128)(2,1)S(1)} %fusion.32), channel_id=1, source_target_pairs={{0,6},{2,8},{4,10},{6,12},{8,14},{10,0},{12,2},{14,4},{1,7},{3,9},... | collective-permute-start | bytes 393224 | tf_op jit(solution)/shard_map/ppermute | solution.py:50
  189.5 16.9 %collective-permute-start.7 = (bf16[64,1024]{1,0:T(8,128)(2,1)S(1)}, bf16[64,1024]{1,0:T(8,128)(2,1)S(1)}, u32[]{:S(2)}, u32[]{:S(2)}) collective-permute-start(bf16[64,1024]{1,0:T(8,128)(2,1)S(1)} %fusion.32), channel_id=1, source_target_pairs={{0,4},{2,6},{4,8},{6,10},{8,12},{10,14},{12,0},{14,2},{1,5},{3,7},... | collective-permute-start | bytes 393224 | tf_op jit(solution)/shard_map/ppermute | solution.py:50
  192.9 15.9 %collective-permute-start.6 = (bf16[64,1024]{1,0:T(8,128)(2,1)S(1)}, bf16[64,1024]{1,0:T(8,128)(2,1)S(1)}, u32[]{:S(2)}, u32[]{:S(2)}) collective-permute-start(bf16[64,1024]{1,0:T(8,128)(2,1)S(1)} %fusion.32), channel_id=1, source_target_pairs={{0,2},{2,4},{4,6},{6,8},{8,10},{10,12},{12,14},{14,0},{1,3},{3,5},... | collective-permute-start | bytes 393224 | tf_op jit(solution)/shard_map/ppermute | solution.py:50
  213.3 7.9 %copy-start.2 = (f32[512,1024]{1,0:T(8,128)S(1)}, f32[512,1024]{1,0:T(8,128)}, u32[]{:S(2)}) copy-start(f32[512,1024]{1,0:T(8,128)} %scatter_custom_fusion) | copy-start | bytes 6291460
  213.3 7.9 %copy-start.34 = (f32[1,1024]{1,0:T(1,128)S(1)}, f32[1,1024]{1,0:T(1,128)}, u32[]{:S(2)}) copy-start(f32[1,1024]{1,0:T(1,128)} %copy-done.33) | copy-start | bytes 12292
  213.3 7.9 %copy-start.36 = (f32[1,1024]{1,0:T(1,128)S(1)}, f32[1,1024]{1,0:T(1,128)}, u32[]{:S(2)}) copy-start(f32[1,1024]{1,0:T(1,128)} %copy-done.35) | copy-start | bytes 12292
  213.3 7.9 %copy-start.38 = (f32[1,1024]{1,0:T(1,128)S(1)}, f32[1,1024]{1,0:T(1,128)}, u32[]{:S(2)}) copy-start(f32[1,1024]{1,0:T(1,128)} %copy-done.37) | copy-start | bytes 12292
  213.3 7.9 %copy-start.40 = (f32[1,1024]{1,0:T(1,128)S(1)}, f32[1,1024]{1,0:T(1,128)}, u32[]{:S(2)}) copy-start(f32[1,1024]{1,0:T(1,128)} %copy-done.39) | copy-start | bytes 12292
  213.3 7.9 %collective-permute-start.13 = (f32[3,1024]{1,0:T(4,128)S(1)}, f32[3,1024]{1,0:T(4,128)S(1)}, u32[]{:S(2)}, u32[]{:S(2)}) collective-permute-start(f32[3,1024]{1,0:T(4,128)S(1)} %slice.497), channel_id=1, source_target_pairs={{16,0},{32,16},{48,32},{64,48},{80,64},{96,80},{112,96},{128,112},... | collective-permute-start | bytes 36872 | tf_op jit(solution)/shard_map/ppermute | solution.py:20
  (31 other events, 39.3 us)

commit v3 on v1

--- a/solution.py
+++ b/solution.py
@@ -3,12 +3,13 @@
 import jax
 import jax.numpy as jnp
 from jax import lax
+from jax.experimental import pallas as pl
 from jax.sharding import PartitionSpec as P
 
 D = 1024
 HD = 128
 KCONV = 4
-CHUNK = 256
+QBLOCK = 256
 
 
 masked_score = -1e30
@@ -46,6 +47,52 @@
             sent, axis, [(i, (i + shift) % devices) for i in range(devices)]
         ).astype(jnp.float32)
     return total
+
+
+def forward_kernel(q_ref, k_ref, v_ref, g_ref, live_row_ref, live_col_ref, att_ref, log_ref, delta_ref):
+    block = pl.program_id(0)
+    rows = q_ref.shape[0]
+    keys = k_ref.shape[0]
+    scale = 1.0 / math.sqrt(HD)
+    scores = lax.dot_general(
+        q_ref[...], k_ref[...], (((1,), (1,)), ((), ())), preferred_element_type=jnp.float32
+    ) * scale
+    q_ids = block * rows + lax.broadcasted_iota(jnp.int32, (rows, keys), 0)
+    k_ids = lax.broadcasted_iota(jnp.int32, (rows, keys), 1)
+    allowed = (k_ids <= q_ids) & (live_row_ref[...] > 0.5)
+    scores = jnp.where(allowed, scores, masked_score)
+    row_max = jnp.max(scores, axis=1, keepdims=True)
+    softmax_part = jnp.exp(scores - row_max)
+    row_sum = jnp.sum(softmax_part, axis=1, keepdims=True)
+    product = jnp.dot(
+        softmax_part.astype(jnp.bfloat16), v_ref[...], preferred_element_type=jnp.float32
+    )
+    attention = jnp.where(live_col_ref[...] > 0.5, product / row_sum, 0.0).astype(jnp.bfloat16)
+    att_ref[...] = attention
+    log_ref[...] = row_max + jnp.log(row_sum)
+    delta_ref[...] = jnp.sum(
+        g_ref[...].astype(jnp.float32) * attention.astype(jnp.float32), axis=1, keepdims=True
+    )
+
+
+def forward_all(queries, keys, values, grads, live):
+    slots, width = queries.shape
+    live_f = live.astype(jnp.float32)
+    row_spec = pl.BlockSpec((QBLOCK, width), lambda i: (i, 0))
+    full_spec = pl.BlockSpec((slots, width), lambda i: (0, 0))
+    col_spec = pl.BlockSpec((QBLOCK, 1), lambda i: (i, 0))
+    return pl.pallas_call(
+        forward_kernel,
+        grid=(slots // QBLOCK,),
+        in_specs=[row_spec, full_spec, full_spec, row_spec,
+                  pl.BlockSpec((1, slots), lambda i: (0, 0)), col_spec],
+        out_specs=[row_spec, col_spec, col_spec],
+        out_shape=[
+            jax.ShapeDtypeStruct((slots, width), jnp.bfloat16),
+            jax.ShapeDtypeStruct((slots, 1), jnp.float32),
+            jax.ShapeDtypeStruct((slots, 1), jnp.float32),
+        ],
+    )(queries, keys, values, grads, live_f.reshape(1, slots), live_f.reshape(slots, 1))
 
 
 def per_device(
@@ -104,36 +151,11 @@
     ).reshape(total_slots)
     slot_ids = jnp.arange(total_slots, dtype=jnp.int32)
 
-    log_parts = []
-    delta_parts = []
-    attended_parts = []
-    for chunk in range(total_slots // CHUNK):
-        q0, q1 = chunk * CHUNK, (chunk + 1) * CHUNK
-        q_ids = slot_ids[q0:q1]
-        k_ids = slot_ids[:q1]
-        allowed = (k_ids[None, :] <= q_ids[:, None]) & all_live[None, :q1]
-        scores = (
-            jnp.dot(all_queries[q0:q1], all_keys[:q1].T, preferred_element_type=jnp.float32)
-            * score_scale
-        )
-        scores = jnp.where(allowed, scores, masked_score)
-        row_max = jnp.max(scores, axis=1)
-        softmax_part = jnp.exp(scores - row_max[:, None])
-        row_sum = jnp.sum(softmax_part, axis=1)
-        product = jnp.dot(
-            softmax_part.astype(jnp.bfloat16), all_values[:q1], preferred_element_type=jnp.float32
-        )
-        attention = jnp.where(
-            all_live[q0:q1, None], product / row_sum[:, None], jnp.float32(0.0)
-        ).astype(jnp.bfloat16)
-        log_parts.append(row_max + jnp.log(row_sum))
-        delta_parts.append(
-            jnp.sum(all_grads[q0:q1].astype(jnp.float32) * attention.astype(jnp.float32), axis=1)
-        )
-        attended_parts.append(attention)
-    all_logs = jnp.concatenate(log_parts)
-    all_deltas = jnp.concatenate(delta_parts)
-    all_attended = jnp.concatenate(attended_parts, axis=0)
+    all_attended, all_logs, all_deltas = forward_all(
+        all_queries, all_keys, all_values, all_grads, all_live
+    )
+    all_logs = all_logs.reshape(total_slots)
+    all_deltas = all_deltas.reshape(total_slots)
     attended = lax.dynamic_slice_in_dim(all_attended, first_slot, slot_count, axis=0)
     own_logs = lax.dynamic_slice_in_dim(all_logs, first_slot, slot_count)
     own_deltas = lax.dynamic_slice_in_dim(all_deltas, first_slot, slot_count)

time: 227 us -> 206 us (0.907)
  the two profiles are of different devices: /device:TPU:24 before, /device:TPU:28 now
where the time goes in v3:
time: 206 us; the launch traced here: 205 us
  waiting for transfers between devices  71.8 us (35%)
  starting transfers between devices  51.4 us (25%)
  local copies, waits for them, and re-layouts  30.1 us (15%)
  other arithmetic  22.2 us (11%)
  matrix products  14.5 us (7%)
  Pallas kernels  12.9 us (6%)
    ppermute x5, waiting for transfers between devices, gather_blocks(): other = lax.ppermute(held, axis, [(i, i ^ step) for i in range(devices)])  58.7 us
    ppermute x7, starting transfers between devices, summed_over(): lax.ppermute(sent, axis, [(i, (i + shift) % devices) for i in range(devic...  32.3 us
    pallas_call x1, Pallas kernels, forward_all(): pl.pallas_call(forward_kernel, grid=(slots // QBLOCK,), in_specs=[row_spe...  12.9 us
    ppermute x5, starting transfers between devices, gather_blocks(): other = lax.ppermute(held, axis, [(i, i ^ step) for i in range(devices)])  12.3 us
    ppermute x7, waiting for transfers between devices, summed_over(): lax.ppermute(sent, axis, [(i, (i + shift) % devices) for i in range(devic...  10 us
    ppermute x2, starting transfers between devices, passed_along(): return lax.ppermute(array, axis, pairs)  6.74 us
    unnamed x39, local copies, waits for them, and re-layouts  4.86 us
    scatter-add x1, other arithmetic, per_device(): jnp.zeros((row_count, D), jnp.float32).at[boundaries].add(grad_state)  4.2 us
  transfers between devices with their start and end apart: 14, of which 9 were waited for; matrix products, arithmetic and copies ran while one was open for 6% of the time, Pallas kernels for 0%

profile of v3, /device:TPU:28, one launch (start us, length us, event | category | flops | bytes accessed | tf_op | source)
XLA Modules:
  0.0 204.7 jit_solution(8559774235495916301)
XLA Ops:
  0.6 0.9 slice.98
  1.5 4.7 %collective-permute-start = (bf16[3,1024]{1,0:T(4,128)(2,1)S(1)}, bf16[3,1024]{1,0:T(4,128)(2,1)S(1)}, u32[]{:S(2)}, u32[]{:S(2)}) collective-permute-start(bf16[3,1024]{1,0:T(4,128)(2,1)S(1)} %slice.98), channel_id=1, source_target_pairs={{0,16},{16,32},{32,48},{48,64},{64,80},{80,96},{96,112},{112,128},... | collective-permute-start | bytes 18440 | tf_op jit(solution)/shard_map/ppermute | solution.py:21
  6.2 0.7 compare_select_fusion.1
  6.9 1.3 compare_and_fusion.4
  8.1 1.5 fusion.51
  10.9 2.2 %gather_fusion = bf16[64,1024]{1,0:T(8,128)(2,1)S(1)} fusion(bf16[512,1024]{1,0:T(8,128)(2,1)} %param.12, s32[1024]{0:T(1024)S(1)} %get-tuple-element.58), kind=kCustom, calls=%fused_computation.4 | custom fusion | bytes 262400 | tf_op jit(solution)/shard_map/jit(_take)/gather | solution.py:127
  13.1 1.5 pad_maximum_fusion
  14.6 1.4 gather_fusion.5
  15.9 1.4 gather_fusion.4
  17.3 1.4 gather_fusion.3
  18.7 1.3 gather_fusion.2
  20.1 1.9 multiply_reduce_fusion.1
  22.8 1.9 collective-permute-start.1
  24.7 4.3 %collective-permute-done.1 = bf16[1,272,128]{2,1,0:T(8,128)(2,1)S(1)} collective-permute-done((bf16[1,272,128]{2,1,0:T(8,128)(2,1)S(1)}, bf16[1,272,128]{2,1,0:T(8,128)(2,1)S(1)}, u32[]{:S(2)}, u32[]{:S(2)}) %collective-permute-start.1) | collective-permute-done | bytes 69664 | tf_op jit(solution)/shard_map/ppermute | solution.py:34
  29.0 1.9 collective-permute-start.2
  31.0 7.6 %collective-permute-done.2 = bf16[2,272,128]{2,1,0:T(8,128)(2,1)S(1)} collective-permute-done((bf16[2,272,128]{2,1,0:T(8,128)(2,1)S(1)}, bf16[2,272,128]{2,1,0:T(8,128)(2,1)S(1)}, u32[]{:S(2)}, u32[]{:S(2)}) %collective-permute-start.2) | collective-permute-done | bytes 139296 | tf_op jit(solution)/shard_map/ppermute | solution.py:34
  38.6 2.9 %collective-permute-start.3 = (bf16[4,272,128]{2,1,0:T(8,128)(2,1)S(1)}, bf16[4,272,128]{2,1,0:T(8,128)(2,1)S(1)}, u32[]{:S(2)}, u32[]{:S(2)}) collective-permute-start(bf16[4,272,128]{2,1,0:T(8,128)(2,1)S(1)} %pad_maximum_fusion.2), channel_id=1, source_target_pairs={{0,64},{16,80},{32,96},{48,112},{64,0},{80,16},{96,32},{112,48},{1... | collective-permute-start | bytes 835592 | tf_op jit(solution)/shard_map/ppermute | solution.py:34
  41.5 13.8 %collective-permute-done.3 = bf16[4,272,128]{2,1,0:T(8,128)(2,1)S(1)} collective-permute-done((bf16[4,272,128]{2,1,0:T(8,128)(2,1)S(1)}, bf16[4,272,128]{2,1,0:T(8,128)(2,1)S(1)}, u32[]{:S(2)}, u32[]{:S(2)}) %collective-permute-start.3) | collective-permute-done | bytes 278560 | tf_op jit(solution)/shard_map/ppermute | solution.py:34
  55.4 3.1 %collective-permute-start.4 = (bf16[8,272,128]{2,1,0:T(8,128)(2,1)S(1)}, bf16[8,272,128]{2,1,0:T(8,128)(2,1)S(1)}, u32[]{:S(2)}, u32[]{:S(2)}) collective-permute-start(bf16[8,272,128]{2,1,0:T(8,128)(2,1)S(1)} %pad_maximum_fusion.1), channel_id=1, source_target_pairs={{0,128},{16,144},{32,160},{48,176},{64,192},{80,208},{96,224},{112... | collective-permute-start | bytes 1671176 | tf_op jit(solution)/shard_map/ppermute | solution.py:34
  58.5 0.7 constant_dynamic-update-slice_fusion.9
  59.8 0.8 constant_dynamic-update-slice_fusion.7
  60.6 0.9 constant_dynamic-update-slice_fusion.6
  61.5 8.3 %collective-permute-done.4 = bf16[8,272,128]{2,1,0:T(8,128)(2,1)S(1)} collective-permute-done((bf16[8,272,128]{2,1,0:T(8,128)(2,1)S(1)}, bf16[8,272,128]{2,1,0:T(8,128)(2,1)S(1)}, u32[]{:S(2)}, u32[]{:S(2)}) %collective-permute-start.4) | collective-permute-done | bytes 557088 | tf_op jit(solution)/shard_map/ppermute | solution.py:34
  69.8 1.1 constant_dynamic-update-slice_fusion.5
  70.9 2.4 %collective-permute-start.5 = (bf16[16,272,128]{2,1,0:T(8,128)(2,1)}, bf16[16,272,128]{2,1,0:T(8,128)(2,1)}, u32[]{:S(2)}, u32[]{:S(2)}) collective-permute-start(bf16[16,272,128]{2,1,0:T(8,128)(2,1)} %get-tuple-element.21), channel_id=1, source_target_pairs={{0,256},{16,272},{32,288},{48,304},{64,320},{80,336},{96,352},{112... | collective-permute-start | bytes 3342344 | tf_op jit(solution)/shard_map/ppermute | solution.py:34
  73.4 24.7 %collective-permute-done.5 = bf16[16,272,128]{2,1,0:T(8,128)(2,1)} collective-permute-done((bf16[16,272,128]{2,1,0:T(8,128)(2,1)}, bf16[16,272,128]{2,1,0:T(8,128)(2,1)}, u32[]{:S(2)}, u32[]{:S(2)}) %collective-permute-start.5) | collective-permute-done | bytes 1114144 | tf_op jit(solution)/shard_map/ppermute | solution.py:34
  98.1 2.3 %constant_dynamic-update-slice_fusion.10 = bf16[32,272,128]{2,1,0:T(8,128)(2,1)} fusion(bf16[32,272,128]{2,1,0:T(8,128)(2,1)} %get-tuple-element.22, bf16[16,272,128]{2,1,0:T(8,128)(2,1)} %collective-permute-done.5), kind=kLoop, calls=%fused_computation.87 | loop fusion | bytes 2228224 | tf_op jit(solution)/shard_map/concatenate | solution.py:35
  100.4 3.8 %gather_fusion.1 = bf16[32,272,128]{2,1,0:T(8,128)(2,1)} fusion(bf16[32,272,128]{2,1,0:T(8,128)(2,1)} %constant_dynamic-update-slice_fusion.10, s32[1024]{0:T(1024)S(1)} %pad_clamp_fusion), kind=kCustom, calls=%fused_computation.5 | custom fusion | bytes 4456576 | tf_op jit(solution)/shard_map/jit(_take)/gather | solution.py:38
  104.2 1.9 broadcast_select_fusion
  106.1 1.4 fusion.50
  108.3 0.7 reshape.156.live_row_ref
  109.0 2.0 reshape.237.live_col_ref
  111.0 12.9 %shard_map.113 = (bf16[2048,128]{1,0:T(8,128)(2,1)}, f32[2048,1]{1,0:T(8,128)}, f32[2048,1]{1,0:T(8,128)}) custom-call(bf16[2048,128]{1,0:T(8,128)(2,1)} %bitcast.42, bf16[2048,128]{1,0:T(8,128)(2,1)} %bitcast.47, bf16[2048,128]{1,0:T(8,128)(2,1)} %bitcast.45, bf16[2048,128]{1,0:T(8,128)(2,1)} %bitcast.39, f32[1,2048]{1,0:T(1,128)} %reshape.156.live_row_ref, ...), custom_call_target="tpu_custom_call" | custom-call | tf_op jit(solution)/shard_map/pallas_call | solution.py:84
  123.9 0.9 dynamic-slice_reduce_fusion.1
  124.8 0.9 dynamic-slice_reduce_fusion
  125.6 1.6 reduce.3
  127.2 1.6 reduce.4
  128.9 2.2 %fusion.5 = f32[64,2048]{1,0:T(8,128)} fusion(bf16[64,128]{1,0:T(8,128)(2,1)S(1)} %get-tuple-element.52, bf16[2048,128]{1,0:T(8,128)(2,1)} %bitcast.48, f32[64]{0:T(128)S(1)} %dynamic-slice_reduce_fusion.1, s32[64]{0:T(128)S(1)} %iota_add_fusion, pred[2048]{0:T(1024)(128)(4,1)S(1)} %lt.104), kind=kOutput, calls=%fused_computation.17 | convolution fusion | flops 34209792 | bytes 1067520 | tf_op jit(solution)/shard_map/dot_general | solution.py:164
  131.2 1.8 fusion.19
  133.0 1.8 fusion.52
  134.9 1.1 fusion.7
  136.0 1.5 fusion.18
  137.5 1.2 convolution_add_fusion.1
  138.8 1.5 fusion.15
  140.3 10.9 %collective-permute-start.12 = (bf16[64,1024]{1,0:T(8,128)(2,1)S(1)}, bf16[64,1024]{1,0:T(8,128)(2,1)S(1)}, u32[]{:S(2)}, u32[]{:S(2)}) collective-permute-start(bf16[64,1024]{1,0:T(8,128)(2,1)S(1)} %fusion.15), channel_id=1, source_target_pairs={{0,14},{2,0},{4,2},{6,4},{8,6},{10,8},{12,10},{14,12},{1,15},{3,1}... | collective-permute-start | bytes 393224 | tf_op jit(solution)/shard_map/ppermute | solution.py:46
  151.2 2.5 %collective-permute-start.11 = (bf16[64,1024]{1,0:T(8,128)(2,1)S(1)}, bf16[64,1024]{1,0:T(8,128)(2,1)S(1)}, u32[]{:S(2)}, u32[]{:S(2)}) collective-permute-start(bf16[64,1024]{1,0:T(8,128)(2,1)S(1)} %fusion.15), channel_id=1, source_target_pairs={{0,12},{2,14},{4,0},{6,2},{8,4},{10,6},{12,8},{14,10},{1,13},{3,15... | collective-permute-start | bytes 393224 | tf_op jit(solution)/shard_map/ppermute | solution.py:46
  153.7 1.9 collective-permute-start.10
  155.6 7.8 %collective-permute-start.9 = (bf16[64,1024]{1,0:T(8,128)(2,1)S(1)}, bf16[64,1024]{1,0:T(8,128)(2,1)S(1)}, u32[]{:S(2)}, u32[]{:S(2)}) collective-permute-start(bf16[64,1024]{1,0:T(8,128)(2,1)S(1)} %fusion.15), channel_id=1, source_target_pairs={{0,8},{2,10},{4,12},{6,14},{8,0},{10,2},{12,4},{14,6},{1,9},{3,11}... | collective-permute-start | bytes 393224 | tf_op jit(solution)/shard_map/ppermute | solution.py:46
  163.4 1.9 collective-permute-start.8
  165.4 3.4 %collective-permute-start.7 = (bf16[64,1024]{1,0:T(8,128)(2,1)S(1)}, bf16[64,1024]{1,0:T(8,128)(2,1)S(1)}, u32[]{:S(2)}, u32[]{:S(2)}) collective-permute-start(bf16[64,1024]{1,0:T(8,128)(2,1)S(1)} %fusion.15), channel_id=1, source_target_pairs={{0,4},{2,6},{4,8},{6,10},{8,12},{10,14},{12,0},{14,2},{1,5},{3,7},... | collective-permute-start | bytes 393224 | tf_op jit(solution)/shard_map/ppermute | solution.py:46
  168.8 3.9 %collective-permute-start.6 = (bf16[64,1024]{1,0:T(8,128)(2,1)S(1)}, bf16[64,1024]{1,0:T(8,128)(2,1)S(1)}, u32[]{:S(2)}, u32[]{:S(2)}) collective-permute-start(bf16[64,1024]{1,0:T(8,128)(2,1)S(1)} %fusion.15), channel_id=1, source_target_pairs={{0,2},{2,4},{4,6},{6,8},{8,10},{10,12},{12,14},{14,0},{1,3},{3,5},... | collective-permute-start | bytes 393224 | tf_op jit(solution)/shard_map/ppermute | solution.py:46
  172.7 1.3 constant_dynamic-slice_fusion
  174.0 4.9 %collective-permute-done.8 = bf16[64,1024]{1,0:T(8,128)(2,1)S(1)} collective-permute-done((bf16[64,1024]{1,0:T(8,128)(2,1)S(1)}, bf16[64,1024]{1,0:T(8,128)(2,1)S(1)}, u32[]{:S(2)}, u32[]{:S(2)}) %collective-permute-start.8) | collective-permute-done | bytes 131104 | tf_op jit(solution)/shard_map/ppermute | solution.py:46
  178.9 4.4 %collective-permute-done.7 = bf16[64,1024]{1,0:T(8,128)(2,1)S(1)} collective-permute-done((bf16[64,1024]{1,0:T(8,128)(2,1)S(1)}, bf16[64,1024]{1,0:T(8,128)(2,1)S(1)}, u32[]{:S(2)}, u32[]{:S(2)}) %collective-permute-start.7) | collective-permute-done | bytes 131104 | tf_op jit(solution)/shard_map/ppermute | solution.py:46
  183.3 0.8 collective-permute-done.6
  184.3 0.8 fusion.32
  185.1 2.6 %scatter_custom_fusion = f32[512,1024]{1,0:T(8,128)} fusion(s32[64]{0:T(128)} %copy-done.16, f32[64,1024]{1,0:T(8,128)S(1)} %fusion.32, f32[]{:T(128)} %constant.45.clone.1), kind=kCustom, calls=%fused_computation.44 | custom fusion | flops 65536 | bytes 2097664 | tf_op jit(solution)/shard_map/scatter-add | solution.py:209
  187.7 0.8 slice.77
  188.5 2.1 %collective-permute-start.13 = (f32[3,1024]{1,0:T(4,128)S(1)}, f32[3,1024]{1,0:T(4,128)S(1)}, u32[]{:S(2)}, u32[]{:S(2)}) collective-permute-start(f32[3,1024]{1,0:T(4,128)S(1)} %slice.77), channel_id=1, source_target_pairs={{16,0},{32,16},{48,32},{64,48},{80,64},{96,80},{112,96},{128,112},... | collective-permute-start | bytes 36872 | tf_op jit(solution)/shard_map/ppermute | solution.py:21
  190.6 1.8 constant_dynamic-update-slice_fusion.17
  192.4 3.1 %collective-permute-done.13 = f32[3,1024]{1,0:T(4,128)S(1)} collective-permute-done((f32[3,1024]{1,0:T(4,128)S(1)}, f32[3,1024]{1,0:T(4,128)S(1)}, u32[]{:S(2)}, u32[]{:S(2)}) %collective-permute-start.13) | collective-permute-done | bytes 12320 | tf_op jit(solution)/shard_map/ppermute | solution.py:21
  195.6 2.2 %fusion.10 = f32[512,1024]{1,0:T(8,128)} fusion(f32[515,1024]{1,0:T(8,128)S(1)} %constant_dynamic-update-slice_fusion.16, f32[512,1024]{1,0:T(8,128)S(1)} %copy-done.1, f32[1024]{0:T(1024)S(1)} %bitcast.59, f32[1024]{0:T(1024)S(1)} %bitcast.61, f32[1024]{0:T(1024)S(1)} %bitcast.57, f32[1024]{0:T(1024)S(1)} %bitcast.55), kind=kLoop, calls=%fused_computation.24 | loop fusion | flops 3670016 | bytes 10502144 | tf_op jit(solution)/shard_map/add | solution.py:215
  197.8 4.2 %scatter_custom_fusion.1 = f32[512,1024]{1,0:T(8,128)} fusion(f32[512,1024]{1,0:T(8,128)} %fusion.10, s32[64]{0:T(128)} %copy-done.16, f32[64,1024]{1,0:T(8,128)S(1)} %get-tuple-element.50, f32[64,1024]{1,0:T(8,128)S(1)} %get-tuple-element.10, f32[64]{0:T(128)S(1)} %broadcast_multiply_fusion, f32[64]{0:T(128)S(1)} %get-tuple-element.35, ...), kind=kCustom, calls=%fused_computation.131 | custom fusion | flops 393216 | bytes 2622272 | tf_op jit(solution)/shard_map/scatter-add | solution.py:210
  202.0 2.7 %convert_element_type.160 = bf16[512,1024]{1,0:T(8,128)(2,1)} convert(f32[512,1024]{1,0:T(8,128)} %scatter_custom_fusion.1) | non-fusion elementwise | flops 524288 | bytes 3145728 | tf_op jit(solution)/shard_map/convert_element_type | solution.py:216
  (64 shorter events, 3.3 us)
Async XLA Ops:
  0.6 19.4 %copy-start = (bf16[1024,1024]{1,0:T(8,128)(2,1)S(1)}, bf16[1024,1024]{1,0:T(8,128)(2,1)}, u32[]{:S(2)}) copy-start(bf16[1024,1024]{1,0:T(8,128)(2,1)} %param.14) | copy-start | bytes 6291460
  1.5 11.5 %collective-permute-start = (bf16[3,1024]{1,0:T(4,128)(2,1)S(1)}, bf16[3,1024]{1,0:T(4,128)(2,1)S(1)}, u32[]{:S(2)}, u32[]{:S(2)}) collective-permute-start(bf16[3,1024]{1,0:T(4,128)(2,1)S(1)} %slice.98), channel_id=1, source_target_pairs={{0,16},{16,32},{32,48},{48,64},{64,80},{80,96},{96,112},{112,128},... | collective-permute-start | bytes 18440 | tf_op jit(solution)/shard_map/ppermute | solution.py:21
  6.9 3.4 %copy-start.16 = (s32[64]{0:T(128)}, s32[64]{0:T(128)S(1)}, u32[]{:S(2)}) copy-start(s32[64]{0:T(128)S(1)} %get-tuple-element.47) | copy-start | bytes 772
  20.0 2.0 copy-start.12
  20.0 2.1 %copy-start.5 = (bf16[1024,128]{1,0:T(8,128)(2,1)S(1)}, bf16[1024,128]{1,0:T(8,128)(2,1)}, u32[]{:S(2)}) copy-start(bf16[1024,128]{1,0:T(8,128)(2,1)} %param.16) | copy-start | bytes 786436
  20.0 2.3 %copy-start.4 = (bf16[1024,128]{1,0:T(8,128)(2,1)S(1)}, bf16[1024,128]{1,0:T(8,128)(2,1)}, u32[]{:S(2)}) copy-start(bf16[1024,128]{1,0:T(8,128)(2,1)} %param.17) | copy-start | bytes 786436
  20.0 2.5 %copy-start.6 = (bf16[1024,128]{1,0:T(8,128)(2,1)S(1)}, bf16[1024,128]{1,0:T(8,128)(2,1)}, u32[]{:S(2)}) copy-start(bf16[1024,128]{1,0:T(8,128)(2,1)} %param.18) | copy-start | bytes 786436
  20.0 2.7 %copy-start.7 = (bf16[64,128]{1,0:T(8,128)(2,1)S(1)}, bf16[64,128]{1,0:T(8,128)(2,1)}, u32[]{:S(2)}) copy-start(bf16[64,128]{1,0:T(8,128)(2,1)} %param.21) | copy-start | bytes 49156
  20.0 2.7 %copy-start.14 = (pred[64]{0:T(512)(128)(4,1)S(1)}, pred[64]{0:T(512)(128)(4,1)}, u32[]{:S(2)}) copy-start(pred[64]{0:T(512)(128)(4,1)} %iota_compare_fusion.3) | copy-start | bytes 196
  22.8 6.2 %collective-permute-start.1 = (bf16[1,272,128]{2,1,0:T(8,128)(2,1)S(1)}, bf16[1,272,128]{2,1,0:T(8,128)(2,1)S(1)}, u32[]{:S(2)}, u32[]{:S(2)}) collective-permute-start(bf16[1,272,128]{2,1,0:T(8,128)(2,1)S(1)} %bitcast.50), channel_id=1, source_target_pairs={{0,16},{16,0},{32,48},{48,32},{64,80},{80,64},{96,112},{112,96},{1... | collective-permute-start | bytes 208904 | tf_op jit(solution)/shard_map/ppermute | solution.py:34
  29.0 9.5 %collective-permute-start.2 = (bf16[2,272,128]{2,1,0:T(8,128)(2,1)S(1)}, bf16[2,272,128]{2,1,0:T(8,128)(2,1)S(1)}, u32[]{:S(2)}, u32[]{:S(2)}) collective-permute-start(bf16[2,272,128]{2,1,0:T(8,128)(2,1)S(1)} %pad_maximum_fusion.3), channel_id=1, source_target_pairs={{0,32},{16,48},{32,0},{48,16},{64,96},{80,112},{96,64},{112,80},{1... | collective-permute-start | bytes 417800 | tf_op jit(solution)/shard_map/ppermute | solution.py:34
  38.6 16.8 %collective-permute-start.3 = (bf16[4,272,128]{2,1,0:T(8,128)(2,1)S(1)}, bf16[4,272,128]{2,1,0:T(8,128)(2,1)S(1)}, u32[]{:S(2)}, u32[]{:S(2)}) collective-permute-start(bf16[4,272,128]{2,1,0:T(8,128)(2,1)S(1)} %pad_maximum_fusion.2), channel_id=1, source_target_pairs={{0,64},{16,80},{32,96},{48,112},{64,0},{80,16},{96,32},{112,48},{1... | collective-permute-start | bytes 835592 | tf_op jit(solution)/shard_map/ppermute | solution.py:34
  55.4 14.4 %collective-permute-start.4 = (bf16[8,272,128]{2,1,0:T(8,128)(2,1)S(1)}, bf16[8,272,128]{2,1,0:T(8,128)(2,1)S(1)}, u32[]{:S(2)}, u32[]{:S(2)}) collective-permute-start(bf16[8,272,128]{2,1,0:T(8,128)(2,1)S(1)} %pad_maximum_fusion.1), channel_id=1, source_target_pairs={{0,128},{16,144},{32,160},{48,176},{64,192},{80,208},{96,224},{112... | collective-permute-start | bytes 1671176 | tf_op jit(solution)/shard_map/ppermute | solution.py:34
  70.9 27.2 %collective-permute-start.5 = (bf16[16,272,128]{2,1,0:T(8,128)(2,1)}, bf16[16,272,128]{2,1,0:T(8,128)(2,1)}, u32[]{:S(2)}, u32[]{:S(2)}) collective-permute-start(bf16[16,272,128]{2,1,0:T(8,128)(2,1)} %get-tuple-element.21), channel_id=1, source_target_pairs={{0,256},{16,272},{32,288},{48,304},{64,320},{80,336},{96,352},{112... | collective-permute-start | bytes 3342344 | tf_op jit(solution)/shard_map/ppermute | solution.py:34
  123.9 7.3 %copy-start.15 = (pred[64]{0:T(512)(128)(4,1)S(1)}, pred[64]{0:T(512)(128)(4,1)}, u32[]{:S(2)}) copy-start(pred[64]{0:T(512)(128)(4,1)} %iota_compare_fusion.3) | copy-start | bytes 196
  127.2 7.7 %copy-start.3 = (bf16[32,64,128]{2,1,0:T(8,128)(2,1)S(1)}, bf16[32,64,128]{2,1,0:T(8,128)(2,1)}, u32[]{:S(2)}) copy-start(bf16[32,64,128]{2,1,0:T(8,128)(2,1)} %get-tuple-element.20) | copy-start | bytes 1572868
  128.9 7.1 %copy-start.2 = (bf16[32,64,128]{2,1,0:T(8,128)(2,1)S(1)}, bf16[32,64,128]{2,1,0:T(8,128)(2,1)}, u32[]{:S(2)}) copy-start(bf16[32,64,128]{2,1,0:T(8,128)(2,1)} %get-tuple-element.17) | copy-start | bytes 1572868
  136.0 48.0 %copy-start.13 = (f32[1024]{0:T(1024)S(1)}, f32[1024]{0:T(1024)}, u32[]{:S(2)}) copy-start(f32[1024]{0:T(1024)} %param.15) | copy-start | bytes 12292
  140.3 25.1 %collective-permute-start.12 = (bf16[64,1024]{1,0:T(8,128)(2,1)S(1)}, bf16[64,1024]{1,0:T(8,128)(2,1)S(1)}, u32[]{:S(2)}, u32[]{:S(2)}) collective-permute-start(bf16[64,1024]{1,0:T(8,128)(2,1)S(1)} %fusion.15), channel_id=1, source_target_pairs={{0,14},{2,0},{4,2},{6,4},{8,6},{10,8},{12,10},{14,12},{1,15},{3,1}... | collective-permute-start | bytes 393224 | tf_op jit(solution)/shard_map/ppermute | solution.py:46
  151.2 17.6 %collective-permute-start.11 = (bf16[64,1024]{1,0:T(8,128)(2,1)S(1)}, bf16[64,1024]{1,0:T(8,128)(2,1)S(1)}, u32[]{:S(2)}, u32[]{:S(2)}) collective-permute-start(bf16[64,1024]{1,0:T(8,128)(2,1)S(1)} %fusion.15), channel_id=1, source_target_pairs={{0,12},{2,14},{4,0},{6,2},{8,4},{10,6},{12,8},{14,10},{1,13},{3,15... | collective-permute-start | bytes 393224 | tf_op jit(solution)/shard_map/ppermute | solution.py:46
  153.7 20.3 %collective-permute-start.10 = (bf16[64,1024]{1,0:T(8,128)(2,1)S(1)}, bf16[64,1024]{1,0:T(8,128)(2,1)S(1)}, u32[]{:S(2)}, u32[]{:S(2)}) collective-permute-start(bf16[64,1024]{1,0:T(8,128)(2,1)S(1)} %fusion.15), channel_id=1, source_target_pairs={{0,10},{2,12},{4,14},{6,0},{8,2},{10,4},{12,6},{14,8},{1,11},{3,13... | collective-permute-start | bytes 393224 | tf_op jit(solution)/shard_map/ppermute | solution.py:46
  155.6 18.4 %collective-permute-start.9 = (bf16[64,1024]{1,0:T(8,128)(2,1)S(1)}, bf16[64,1024]{1,0:T(8,128)(2,1)S(1)}, u32[]{:S(2)}, u32[]{:S(2)}) collective-permute-start(bf16[64,1024]{1,0:T(8,128)(2,1)S(1)} %fusion.15), channel_id=1, source_target_pairs={{0,8},{2,10},{4,12},{6,14},{8,0},{10,2},{12,4},{14,6},{1,9},{3,11}... | collective-permute-start | bytes 393224 | tf_op jit(solution)/shard_map/ppermute | solution.py:46
  163.4 15.5 %collective-permute-start.8 = (bf16[64,1024]{1,0:T(8,128)(2,1)S(1)}, bf16[64,1024]{1,0:T(8,128)(2,1)S(1)}, u32[]{:S(2)}, u32[]{:S(2)}) collective-permute-start(bf16[64,1024]{1,0:T(8,128)(2,1)S(1)} %fusion.15), channel_id=1, source_target_pairs={{0,6},{2,8},{4,10},{6,12},{8,14},{10,0},{12,2},{14,4},{1,7},{3,9},... | collective-permute-start | bytes 393224 | tf_op jit(solution)/shard_map/ppermute | solution.py:46
  165.4 17.9 %collective-permute-start.7 = (bf16[64,1024]{1,0:T(8,128)(2,1)S(1)}, bf16[64,1024]{1,0:T(8,128)(2,1)S(1)}, u32[]{:S(2)}, u32[]{:S(2)}) collective-permute-start(bf16[64,1024]{1,0:T(8,128)(2,1)S(1)} %fusion.15), channel_id=1, source_target_pairs={{0,4},{2,6},{4,8},{6,10},{8,12},{10,14},{12,0},{14,2},{1,5},{3,7},... | collective-permute-start | bytes 393224 | tf_op jit(solution)/shard_map/ppermute | solution.py:46
  168.8 15.3 %collective-permute-start.6 = (bf16[64,1024]{1,0:T(8,128)(2,1)S(1)}, bf16[64,1024]{1,0:T(8,128)(2,1)S(1)}, u32[]{:S(2)}, u32[]{:S(2)}) collective-permute-start(bf16[64,1024]{1,0:T(8,128)(2,1)S(1)} %fusion.15), channel_id=1, source_target_pairs={{0,2},{2,4},{4,6},{6,8},{8,10},{10,12},{12,14},{14,0},{1,3},{3,5},... | collective-permute-start | bytes 393224 | tf_op jit(solution)/shard_map/ppermute | solution.py:46
  188.5 7.0 %copy-start.1 = (f32[512,1024]{1,0:T(8,128)S(1)}, f32[512,1024]{1,0:T(8,128)}, u32[]{:S(2)}) copy-start(f32[512,1024]{1,0:T(8,128)} %scatter_custom_fusion) | copy-start | bytes 6291460
  188.5 7.0 %copy-start.8 = (f32[1,1024]{1,0:T(1,128)S(1)}, f32[1,1024]{1,0:T(1,128)}, u32[]{:S(2)}) copy-start(f32[1,1024]{1,0:T(1,128)} %get-tuple-element.31) | copy-start | bytes 12292
  188.5 7.0 %copy-start.9 = (f32[1,1024]{1,0:T(1,128)S(1)}, f32[1,1024]{1,0:T(1,128)}, u32[]{:S(2)}) copy-start(f32[1,1024]{1,0:T(1,128)} %get-tuple-element.32) | copy-start | bytes 12292
  188.5 7.0 %copy-start.10 = (f32[1,1024]{1,0:T(1,128)S(1)}, f32[1,1024]{1,0:T(1,128)}, u32[]{:S(2)}) copy-start(f32[1,1024]{1,0:T(1,128)} %get-tuple-element.33) | copy-start | bytes 12292
  188.5 7.0 %copy-start.11 = (f32[1,1024]{1,0:T(1,128)S(1)}, f32[1,1024]{1,0:T(1,128)}, u32[]{:S(2)}) copy-start(f32[1,1024]{1,0:T(1,128)} %get-tuple-element.34) | copy-start | bytes 12292
  188.5 7.0 %collective-permute-start.13 = (f32[3,1024]{1,0:T(4,128)S(1)}, f32[3,1024]{1,0:T(4,128)S(1)}, u32[]{:S(2)}, u32[]{:S(2)}) collective-permute-start(f32[3,1024]{1,0:T(4,128)S(1)} %slice.77), channel_id=1, source_target_pairs={{16,0},{32,16},{48,32},{64,48},{80,64},{96,80},{112,96},{128,112},... | collective-permute-start | bytes 36872 | tf_op jit(solution)/shard_map/ppermute | solution.py:21

commit v4 on v3

--- a/solution.py
+++ b/solution.py
@@ -40,12 +40,13 @@
 
 def summed_over(partial, axis):
     devices = lax.axis_size(axis)
-    sent = partial.astype(jnp.bfloat16)
-    total = sent.astype(jnp.float32)
-    for shift in range(1, devices):
-        total = total + lax.ppermute(
-            sent, axis, [(i, (i + shift) % devices) for i in range(devices)]
-        ).astype(jnp.float32)
+    total = partial
+    step = 1
+    while step < devices:
+        sent = total.astype(jnp.bfloat16)
+        got = lax.ppermute(sent, axis, [(i, i ^ step) for i in range(devices)])
+        total = sent.astype(jnp.float32) + got.astype(jnp.float32)
+        step *= 2
     return total
 
 

time: 206 us -> 193 us (0.937)
  the two profiles are of different devices: /device:TPU:28 before, /device:TPU:30 now
where the time goes in v4:
time: 193 us; the launch traced here: 192 us
  waiting for transfers between devices  70.2 us (36%)
  starting transfers between devices  40.5 us (21%)
  local copies, waits for them, and re-layouts  30.1 us (16%)
  other arithmetic  22.1 us (11%)
  matrix products  14.5 us (8%)
  Pallas kernels  12.9 us (7%)
    ppermute x5, waiting for transfers between devices, gather_blocks(): other = lax.ppermute(held, axis, [(i, i ^ step) for i in range(devices)])  58.3 us
    ppermute x3, starting transfers between devices, summed_over(): got = lax.ppermute(sent, axis, [(i, i ^ step) for i in range(devices)])  21.1 us
    pallas_call x1, Pallas kernels, forward_all(): pl.pallas_call(forward_kernel, grid=(slots // QBLOCK,), in_specs=[row_spe...  12.9 us
    ppermute x5, starting transfers between devices, gather_blocks(): other = lax.ppermute(held, axis, [(i, i ^ step) for i in range(devices)])  12.7 us
    ppermute x3, waiting for transfers between devices, summed_over(): got = lax.ppermute(sent, axis, [(i, i ^ step) for i in range(devices)])  8.87 us
    ppermute x2, starting transfers between devices, passed_along(): return lax.ppermute(array, axis, pairs)  6.72 us
    unnamed x33, local copies, waits for them, and re-layouts  4.84 us
    scatter-add x1, other arithmetic, per_device(): jnp.zeros((row_count, D), jnp.float32).at[boundaries].add(grad_state)  4.24 us
  transfers between devices with their start and end apart: 10, of which 9 were waited for; matrix products, arithmetic and copies ran while one was open for 6% of the time, Pallas kernels for 0%

profile of v4, /device:TPU:30, one launch (start us, length us, event | category | flops | bytes accessed | tf_op | source)
XLA Modules:
  0.0 192.1 jit_solution(15976059741150064919)
XLA Ops:
  0.6 0.9 slice.98
  1.5 4.7 %collective-permute-start = (bf16[3,1024]{1,0:T(4,128)(2,1)S(1)}, bf16[3,1024]{1,0:T(4,128)(2,1)S(1)}, u32[]{:S(2)}, u32[]{:S(2)}) collective-permute-start(bf16[3,1024]{1,0:T(4,128)(2,1)S(1)} %slice.98), channel_id=1, source_target_pairs={{0,16},{16,32},{32,48},{48,64},{64,80},{80,96},{96,112},{112,128},... | collective-permute-start | bytes 18440 | tf_op jit(solution)/shard_map/ppermute | solution.py:21
  6.2 0.7 compare_select_fusion.1
  6.9 1.2 compare_and_fusion.4
  8.1 1.5 fusion.51
  10.3 0.5 iota_compare_fusion.3
  10.8 2.2 %gather_fusion = bf16[64,1024]{1,0:T(8,128)(2,1)S(1)} fusion(bf16[512,1024]{1,0:T(8,128)(2,1)} %param.12, s32[1024]{0:T(1024)S(1)} %get-tuple-element.56), kind=kCustom, calls=%fused_computation.4 | custom fusion | bytes 262400 | tf_op jit(solution)/shard_map/jit(_take)/gather | solution.py:128
  13.0 1.5 pad_maximum_fusion
  14.5 1.4 gather_fusion.5
  15.9 1.4 gather_fusion.4
  17.2 1.4 gather_fusion.3
  18.6 1.4 gather_fusion.2
  20.0 1.9 multiply_reduce_fusion.1
  22.4 0.2 constant_dynamic-update-slice_fusion.2
  22.7 1.9 collective-permute-start.1
  24.7 4.3 %collective-permute-done.1 = bf16[1,272,128]{2,1,0:T(8,128)(2,1)S(1)} collective-permute-done((bf16[1,272,128]{2,1,0:T(8,128)(2,1)S(1)}, bf16[1,272,128]{2,1,0:T(8,128)(2,1)S(1)}, u32[]{:S(2)}, u32[]{:S(2)}) %collective-permute-start.1) | collective-permute-done | bytes 69664 | tf_op jit(solution)/shard_map/ppermute | solution.py:34
  29.0 1.9 collective-permute-start.2
  30.9 7.6 %collective-permute-done.2 = bf16[2,272,128]{2,1,0:T(8,128)(2,1)S(1)} collective-permute-done((bf16[2,272,128]{2,1,0:T(8,128)(2,1)S(1)}, bf16[2,272,128]{2,1,0:T(8,128)(2,1)S(1)}, u32[]{:S(2)}, u32[]{:S(2)}) %collective-permute-start.2) | collective-permute-done | bytes 139296 | tf_op jit(solution)/shard_map/ppermute | solution.py:34
  38.5 2.8 %collective-permute-start.3 = (bf16[4,272,128]{2,1,0:T(8,128)(2,1)S(1)}, bf16[4,272,128]{2,1,0:T(8,128)(2,1)S(1)}, u32[]{:S(2)}, u32[]{:S(2)}) collective-permute-start(bf16[4,272,128]{2,1,0:T(8,128)(2,1)S(1)} %pad_maximum_fusion.2), channel_id=1, source_target_pairs={{0,64},{16,80},{32,96},{48,112},{64,0},{80,16},{96,32},{112,48},{1... | collective-permute-start | bytes 835592 | tf_op jit(solution)/shard_map/ppermute | solution.py:34
  41.3 13.9 %collective-permute-done.3 = bf16[4,272,128]{2,1,0:T(8,128)(2,1)S(1)} collective-permute-done((bf16[4,272,128]{2,1,0:T(8,128)(2,1)S(1)}, bf16[4,272,128]{2,1,0:T(8,128)(2,1)S(1)}, u32[]{:S(2)}, u32[]{:S(2)}) %collective-permute-start.3) | collective-permute-done | bytes 278560 | tf_op jit(solution)/shard_map/ppermute | solution.py:34
  55.3 2.7 %collective-permute-start.4 = (bf16[8,272,128]{2,1,0:T(8,128)(2,1)S(1)}, bf16[8,272,128]{2,1,0:T(8,128)(2,1)S(1)}, u32[]{:S(2)}, u32[]{:S(2)}) collective-permute-start(bf16[8,272,128]{2,1,0:T(8,128)(2,1)S(1)} %pad_maximum_fusion.1), channel_id=1, source_target_pairs={{0,128},{16,144},{32,160},{48,176},{64,192},{80,208},{96,224},{112... | collective-permute-start | bytes 1671176 | tf_op jit(solution)/shard_map/ppermute | solution.py:34
  58.0 0.7 constant_dynamic-update-slice_fusion.9
  58.7 0.7 constant_dynamic-update-slice_fusion.8
  59.4 0.7 constant_dynamic-update-slice_fusion.7
  60.1 0.9 constant_dynamic-update-slice_fusion.6
  61.0 8.7 %collective-permute-done.4 = bf16[8,272,128]{2,1,0:T(8,128)(2,1)S(1)} collective-permute-done((bf16[8,272,128]{2,1,0:T(8,128)(2,1)S(1)}, bf16[8,272,128]{2,1,0:T(8,128)(2,1)S(1)}, u32[]{:S(2)}, u32[]{:S(2)}) %collective-permute-start.4) | collective-permute-done | bytes 557088 | tf_op jit(solution)/shard_map/ppermute | solution.py:34
  69.7 1.1 constant_dynamic-update-slice_fusion.5
  70.8 3.3 %collective-permute-start.5 = (bf16[16,272,128]{2,1,0:T(8,128)(2,1)}, bf16[16,272,128]{2,1,0:T(8,128)(2,1)}, u32[]{:S(2)}, u32[]{:S(2)}) collective-permute-start(bf16[16,272,128]{2,1,0:T(8,128)(2,1)} %get-tuple-element.19), channel_id=1, source_target_pairs={{0,256},{16,272},{32,288},{48,304},{64,320},{80,336},{96,352},{112... | collective-permute-start | bytes 3342344 | tf_op jit(solution)/shard_map/ppermute | solution.py:34
  74.2 23.8 %collective-permute-done.5 = bf16[16,272,128]{2,1,0:T(8,128)(2,1)} collective-permute-done((bf16[16,272,128]{2,1,0:T(8,128)(2,1)}, bf16[16,272,128]{2,1,0:T(8,128)(2,1)}, u32[]{:S(2)}, u32[]{:S(2)}) %collective-permute-start.5) | collective-permute-done | bytes 1114144 | tf_op jit(solution)/shard_map/ppermute | solution.py:34
  98.0 2.3 %constant_dynamic-update-slice_fusion.10 = bf16[32,272,128]{2,1,0:T(8,128)(2,1)} fusion(bf16[32,272,128]{2,1,0:T(8,128)(2,1)} %get-tuple-element.20, bf16[16,272,128]{2,1,0:T(8,128)(2,1)} %collective-permute-done.5), kind=kLoop, calls=%fused_computation.89 | loop fusion | bytes 2228224 | tf_op jit(solution)/shard_map/concatenate | solution.py:35
  100.3 3.8 %gather_fusion.1 = bf16[32,272,128]{2,1,0:T(8,128)(2,1)} fusion(bf16[32,272,128]{2,1,0:T(8,128)(2,1)} %constant_dynamic-update-slice_fusion.10, s32[1024]{0:T(1024)S(1)} %pad_clamp_fusion), kind=kCustom, calls=%fused_computation.5 | custom fusion | bytes 4456576 | tf_op jit(solution)/shard_map/jit(_take)/gather | solution.py:38
  104.2 1.9 broadcast_select_fusion
  106.1 1.4 fusion.50
  107.5 0.7 fusion.43
  108.2 0.7 reshape.156.live_row_ref
  108.9 2.0 %reshape.237.live_col_ref = f32[2048,1]{1,0:T(8,128)} reshape(f32[32,64]{1,0:T(8,128)S(1)} %get-tuple-element.36) | data formatting | bytes 16384 | tf_op jit(solution)/shard_map/convert_element_type | solution.py:81
  110.9 12.9 %shard_map.113 = (bf16[2048,128]{1,0:T(8,128)(2,1)}, f32[2048,1]{1,0:T(8,128)}, f32[2048,1]{1,0:T(8,128)}) custom-call(bf16[2048,128]{1,0:T(8,128)(2,1)} %bitcast.42, bf16[2048,128]{1,0:T(8,128)(2,1)} %bitcast.47, bf16[2048,128]{1,0:T(8,128)(2,1)} %bitcast.45, bf16[2048,128]{1,0:T(8,128)(2,1)} %bitcast.39, f32[1,2048]{1,0:T(1,128)} %reshape.156.live_row_ref, ...), custom_call_target="tpu_custom_call" | custom-call | tf_op jit(solution)/shard_map/pallas_call | solution.py:85
  123.8 0.9 dynamic-slice_reduce_fusion.1
  124.7 0.9 dynamic-slice_reduce_fusion
  125.6 1.6 reduce.3
  127.2 1.6 reduce.4
  128.9 2.2 %fusion.5 = f32[64,2048]{1,0:T(8,128)} fusion(bf16[64,128]{1,0:T(8,128)(2,1)S(1)} %get-tuple-element.50, bf16[2048,128]{1,0:T(8,128)(2,1)} %bitcast.48, f32[64]{0:T(128)S(1)} %dynamic-slice_reduce_fusion.1, s32[64]{0:T(128)S(1)} %iota_add_fusion, pred[2048]{0:T(1024)(128)(4,1)S(1)} %lt.104), kind=kOutput, calls=%fused_computation.17 | convolution fusion | flops 34209792 | bytes 1067520 | tf_op jit(solution)/shard_map/dot_general | solution.py:165
  131.1 1.8 fusion.19
  133.0 1.9 fusion.52
  134.8 1.1 fusion.7
  136.0 1.5 fusion.18
  137.5 1.2 convolution_add_fusion.1
  138.7 1.5 fusion.15
  140.2 4.3 %collective-permute-start.6 = (bf16[64,1024]{1,0:T(8,128)(2,1)S(1)}, bf16[64,1024]{1,0:T(8,128)(2,1)S(1)}, u32[]{:S(2)}, u32[]{:S(2)}) collective-permute-start(bf16[64,1024]{1,0:T(8,128)(2,1)S(1)} %fusion.15), channel_id=1, source_target_pairs={{0,2},{2,0},{4,6},{6,4},{8,10},{10,8},{12,14},{14,12},{1,3},{3,1},... | collective-permute-start | bytes 393224 | tf_op jit(solution)/shard_map/ppermute | solution.py:47
  144.5 2.9 %collective-permute-done.6 = bf16[64,1024]{1,0:T(8,128)(2,1)S(1)} collective-permute-done((bf16[64,1024]{1,0:T(8,128)(2,1)S(1)}, bf16[64,1024]{1,0:T(8,128)(2,1)S(1)}, u32[]{:S(2)}, u32[]{:S(2)}) %collective-permute-start.6) | collective-permute-done | bytes 131104 | tf_op jit(solution)/shard_map/ppermute | solution.py:47
  147.5 6.3 %collective-permute-start.7 = (bf16[64,1024]{1,0:T(8,128)(2,1)S(1)}, bf16[64,1024]{1,0:T(8,128)(2,1)S(1)}, u32[]{:S(2)}, u32[]{:S(2)}) collective-permute-start(bf16[64,1024]{1,0:T(8,128)(2,1)S(1)} %add_convert_fusion.1), channel_id=1, source_target_pairs={{0,4},{2,6},{4,0},{6,2},{8,12},{10,14},{12,8},{14,10},{1,5},{3,7},... | collective-permute-start | bytes 393224 | tf_op jit(solution)/shard_map/ppermute | solution.py:47
  153.8 4.3 %collective-permute-done.7 = bf16[64,1024]{1,0:T(8,128)(2,1)S(1)} collective-permute-done((bf16[64,1024]{1,0:T(8,128)(2,1)S(1)}, bf16[64,1024]{1,0:T(8,128)(2,1)S(1)}, u32[]{:S(2)}, u32[]{:S(2)}) %collective-permute-start.7) | collective-permute-done | bytes 131104 | tf_op jit(solution)/shard_map/ppermute | solution.py:47
  158.1 10.5 %collective-permute-start.8 = (bf16[64,1024]{1,0:T(8,128)(2,1)S(1)}, bf16[64,1024]{1,0:T(8,128)(2,1)S(1)}, u32[]{:S(2)}, u32[]{:S(2)}) collective-permute-start(bf16[64,1024]{1,0:T(8,128)(2,1)S(1)} %add_convert_fusion), channel_id=1, source_target_pairs={{0,8},{2,10},{4,12},{6,14},{8,0},{10,2},{12,4},{14,6},{1,9},{3,11}... | collective-permute-start | bytes 393224 | tf_op jit(solution)/shard_map/ppermute | solution.py:47
  168.7 1.3 constant_dynamic-slice_fusion
  170.0 1.6 collective-permute-done.8
  171.7 0.8 fusion.32
  172.5 2.6 %scatter_custom_fusion = f32[512,1024]{1,0:T(8,128)} fusion(s32[64]{0:T(128)} %copy-done.13, f32[64,1024]{1,0:T(8,128)S(1)} %fusion.32, f32[]{:T(128)} %constant.45.clone.1), kind=kCustom, calls=%fused_computation.44 | custom fusion | flops 65536 | bytes 2097664 | tf_op jit(solution)/shard_map/scatter-add | solution.py:210
  175.2 0.8 slice.77
  175.9 2.0 %collective-permute-start.9 = (f32[3,1024]{1,0:T(4,128)S(1)}, f32[3,1024]{1,0:T(4,128)S(1)}, u32[]{:S(2)}, u32[]{:S(2)}) collective-permute-start(f32[3,1024]{1,0:T(4,128)S(1)} %slice.77), channel_id=1, source_target_pairs={{16,0},{32,16},{48,32},{64,48},{80,64},{96,80},{112,96},{128,112},... | collective-permute-start | bytes 36872 | tf_op jit(solution)/shard_map/ppermute | solution.py:21
  178.0 1.8 constant_dynamic-update-slice_fusion.17
  179.8 3.1 %collective-permute-done.9 = f32[3,1024]{1,0:T(4,128)S(1)} collective-permute-done((f32[3,1024]{1,0:T(4,128)S(1)}, f32[3,1024]{1,0:T(4,128)S(1)}, u32[]{:S(2)}, u32[]{:S(2)}) %collective-permute-start.9) | collective-permute-done | bytes 12320 | tf_op jit(solution)/shard_map/ppermute | solution.py:21
  182.9 2.2 %fusion.10 = f32[512,1024]{1,0:T(8,128)} fusion(f32[515,1024]{1,0:T(8,128)S(1)} %constant_dynamic-update-slice_fusion.16, f32[512,1024]{1,0:T(8,128)S(1)} %copy-done.1, f32[1024]{0:T(1024)S(1)} %bitcast.59, f32[1024]{0:T(1024)S(1)} %bitcast.61, f32[1024]{0:T(1024)S(1)} %bitcast.57, f32[1024]{0:T(1024)S(1)} %bitcast.55), kind=kLoop, calls=%fused_computation.24 | loop fusion | flops 3670016 | bytes 10502144 | tf_op jit(solution)/shard_map/add | solution.py:216
  185.1 4.2 %scatter_custom_fusion.1 = f32[512,1024]{1,0:T(8,128)} fusion(f32[512,1024]{1,0:T(8,128)} %fusion.10, s32[64]{0:T(128)} %copy-done.13, f32[64,1024]{1,0:T(8,128)S(1)} %get-tuple-element.48, bf16[64,1024]{1,0:T(8,128)(2,1)S(1)} %collective-permute-done.8, bf16[64,1024]{1,0:T(8,128)(2,1)S(1)} %add_convert_fusion, f32[64]{0:T(128)S(1)} %broadcast_multiply_fusion, ...), kind=kCustom, calls=%fused_computation.133 | custom fusion | flops 655360 | bytes 2626368 | tf_op jit(solution)/shard_map/scatter-add | solution.py:211
  189.4 2.7 %convert_element_type.160 = bf16[512,1024]{1,0:T(8,128)(2,1)} convert(f32[512,1024]{1,0:T(8,128)} %scatter_custom_fusion.1) | non-fusion elementwise | flops 524288 | bytes 3145728 | tf_op jit(solution)/shard_map/convert_element_type | solution.py:217
  (52 shorter events, 1.2 us)
Async XLA Ops:
  0.6 19.3 %copy-start = (bf16[1024,1024]{1,0:T(8,128)(2,1)S(1)}, bf16[1024,1024]{1,0:T(8,128)(2,1)}, u32[]{:S(2)}) copy-start(bf16[1024,1024]{1,0:T(8,128)(2,1)} %param.14) | copy-start | bytes 6291460
  1.5 11.5 %collective-permute-start = (bf16[3,1024]{1,0:T(4,128)(2,1)S(1)}, bf16[3,1024]{1,0:T(4,128)(2,1)S(1)}, u32[]{:S(2)}, u32[]{:S(2)}) collective-permute-start(bf16[3,1024]{1,0:T(4,128)(2,1)S(1)} %slice.98), channel_id=1, source_target_pairs={{0,16},{16,32},{32,48},{48,64},{64,80},{80,96},{96,112},{112,128},... | collective-permute-start | bytes 18440 | tf_op jit(solution)/shard_map/ppermute | solution.py:21
  6.9 3.4 %copy-start.13 = (s32[64]{0:T(128)}, s32[64]{0:T(128)S(1)}, u32[]{:S(2)}) copy-start(s32[64]{0:T(128)S(1)} %get-tuple-element.45) | copy-start | bytes 772
  18.6 3.3 %copy-start.7 = (f32[1024]{0:T(1024)S(1)}, f32[1024]{0:T(1024)}, u32[]{:S(2)}) copy-start(f32[1024]{0:T(1024)} %param.15) | copy-start | bytes 12292
  19.9 2.1 %copy-start.5 = (bf16[1024,128]{1,0:T(8,128)(2,1)S(1)}, bf16[1024,128]{1,0:T(8,128)(2,1)}, u32[]{:S(2)}) copy-start(bf16[1024,128]{1,0:T(8,128)(2,1)} %param.16) | copy-start | bytes 786436
  19.9 2.3 %copy-start.4 = (bf16[1024,128]{1,0:T(8,128)(2,1)S(1)}, bf16[1024,128]{1,0:T(8,128)(2,1)}, u32[]{:S(2)}) copy-start(bf16[1024,128]{1,0:T(8,128)(2,1)} %param.17) | copy-start | bytes 786436
  19.9 2.5 %copy-start.6 = (bf16[1024,128]{1,0:T(8,128)(2,1)S(1)}, bf16[1024,128]{1,0:T(8,128)(2,1)}, u32[]{:S(2)}) copy-start(bf16[1024,128]{1,0:T(8,128)(2,1)} %param.18) | copy-start | bytes 786436
  19.9 2.7 %copy-start.8 = (bf16[64,128]{1,0:T(8,128)(2,1)S(1)}, bf16[64,128]{1,0:T(8,128)(2,1)}, u32[]{:S(2)}) copy-start(bf16[64,128]{1,0:T(8,128)(2,1)} %param.21) | copy-start | bytes 49156
  20.0 2.7 %copy-start.11 = (pred[64]{0:T(512)(128)(4,1)S(1)}, pred[64]{0:T(512)(128)(4,1)}, u32[]{:S(2)}) copy-start(pred[64]{0:T(512)(128)(4,1)} %iota_compare_fusion.3) | copy-start | bytes 196
  22.7 6.2 %collective-permute-start.1 = (bf16[1,272,128]{2,1,0:T(8,128)(2,1)S(1)}, bf16[1,272,128]{2,1,0:T(8,128)(2,1)S(1)}, u32[]{:S(2)}, u32[]{:S(2)}) collective-permute-start(bf16[1,272,128]{2,1,0:T(8,128)(2,1)S(1)} %bitcast.50), channel_id=1, source_target_pairs={{0,16},{16,0},{32,48},{48,32},{64,80},{80,64},{96,112},{112,96},{1... | collective-permute-start | bytes 208904 | tf_op jit(solution)/shard_map/ppermute | solution.py:34
  29.0 9.5 %collective-permute-start.2 = (bf16[2,272,128]{2,1,0:T(8,128)(2,1)S(1)}, bf16[2,272,128]{2,1,0:T(8,128)(2,1)S(1)}, u32[]{:S(2)}, u32[]{:S(2)}) collective-permute-start(bf16[2,272,128]{2,1,0:T(8,128)(2,1)S(1)} %pad_maximum_fusion.3), channel_id=1, source_target_pairs={{0,32},{16,48},{32,0},{48,16},{64,96},{80,112},{96,64},{112,80},{1... | collective-permute-start | bytes 417800 | tf_op jit(solution)/shard_map/ppermute | solution.py:34
  38.5 16.8 %collective-permute-start.3 = (bf16[4,272,128]{2,1,0:T(8,128)(2,1)S(1)}, bf16[4,272,128]{2,1,0:T(8,128)(2,1)S(1)}, u32[]{:S(2)}, u32[]{:S(2)}) collective-permute-start(bf16[4,272,128]{2,1,0:T(8,128)(2,1)S(1)} %pad_maximum_fusion.2), channel_id=1, source_target_pairs={{0,64},{16,80},{32,96},{48,112},{64,0},{80,16},{96,32},{112,48},{1... | collective-permute-start | bytes 835592 | tf_op jit(solution)/shard_map/ppermute | solution.py:34
  55.3 14.4 %collective-permute-start.4 = (bf16[8,272,128]{2,1,0:T(8,128)(2,1)S(1)}, bf16[8,272,128]{2,1,0:T(8,128)(2,1)S(1)}, u32[]{:S(2)}, u32[]{:S(2)}) collective-permute-start(bf16[8,272,128]{2,1,0:T(8,128)(2,1)S(1)} %pad_maximum_fusion.1), channel_id=1, source_target_pairs={{0,128},{16,144},{32,160},{48,176},{64,192},{80,208},{96,224},{112... | collective-permute-start | bytes 1671176 | tf_op jit(solution)/shard_map/ppermute | solution.py:34
  70.8 27.2 %collective-permute-start.5 = (bf16[16,272,128]{2,1,0:T(8,128)(2,1)}, bf16[16,272,128]{2,1,0:T(8,128)(2,1)}, u32[]{:S(2)}, u32[]{:S(2)}) collective-permute-start(bf16[16,272,128]{2,1,0:T(8,128)(2,1)} %get-tuple-element.19), channel_id=1, source_target_pairs={{0,256},{16,272},{32,288},{48,304},{64,320},{80,336},{96,352},{112... | collective-permute-start | bytes 3342344 | tf_op jit(solution)/shard_map/ppermute | solution.py:34
  123.8 7.3 %copy-start.9 = (bf16[64,128]{1,0:T(8,128)(2,1)S(1)}, bf16[64,128]{1,0:T(8,128)(2,1)}, u32[]{:S(2)}) copy-start(bf16[64,128]{1,0:T(8,128)(2,1)} %param.21) | copy-start | bytes 49156
  123.8 7.3 %copy-start.12 = (pred[64]{0:T(512)(128)(4,1)S(1)}, pred[64]{0:T(512)(128)(4,1)}, u32[]{:S(2)}) copy-start(pred[64]{0:T(512)(128)(4,1)} %iota_compare_fusion.3) | copy-start | bytes 196
  127.2 7.7 %copy-start.3 = (bf16[32,64,128]{2,1,0:T(8,128)(2,1)S(1)}, bf16[32,64,128]{2,1,0:T(8,128)(2,1)}, u32[]{:S(2)}) copy-start(bf16[32,64,128]{2,1,0:T(8,128)(2,1)} %get-tuple-element.18) | copy-start | bytes 1572868
  128.9 7.1 %copy-start.2 = (bf16[32,64,128]{2,1,0:T(8,128)(2,1)S(1)}, bf16[32,64,128]{2,1,0:T(8,128)(2,1)}, u32[]{:S(2)}) copy-start(bf16[32,64,128]{2,1,0:T(8,128)(2,1)} %get-tuple-element.15) | copy-start | bytes 1572868
  140.2 7.2 %collective-permute-start.6 = (bf16[64,1024]{1,0:T(8,128)(2,1)S(1)}, bf16[64,1024]{1,0:T(8,128)(2,1)S(1)}, u32[]{:S(2)}, u32[]{:S(2)}) collective-permute-start(bf16[64,1024]{1,0:T(8,128)(2,1)S(1)} %fusion.15), channel_id=1, source_target_pairs={{0,2},{2,0},{4,6},{6,4},{8,10},{10,8},{12,14},{14,12},{1,3},{3,1},... | collective-permute-start | bytes 393224 | tf_op jit(solution)/shard_map/ppermute | solution.py:47
  147.5 10.6 %collective-permute-start.7 = (bf16[64,1024]{1,0:T(8,128)(2,1)S(1)}, bf16[64,1024]{1,0:T(8,128)(2,1)S(1)}, u32[]{:S(2)}, u32[]{:S(2)}) collective-permute-start(bf16[64,1024]{1,0:T(8,128)(2,1)S(1)} %add_convert_fusion.1), channel_id=1, source_target_pairs={{0,4},{2,6},{4,0},{6,2},{8,12},{10,14},{12,8},{14,10},{1,5},{3,7},... | collective-permute-start | bytes 393224 | tf_op jit(solution)/shard_map/ppermute | solution.py:47
  158.1 13.4 %collective-permute-start.8 = (bf16[64,1024]{1,0:T(8,128)(2,1)S(1)}, bf16[64,1024]{1,0:T(8,128)(2,1)S(1)}, u32[]{:S(2)}, u32[]{:S(2)}) collective-permute-start(bf16[64,1024]{1,0:T(8,128)(2,1)S(1)} %add_convert_fusion), channel_id=1, source_target_pairs={{0,8},{2,10},{4,12},{6,14},{8,0},{10,2},{12,4},{14,6},{1,9},{3,11}... | collective-permute-start | bytes 393224 | tf_op jit(solution)/shard_map/ppermute | solution.py:47
  175.9 7.0 %copy-start.1 = (f32[512,1024]{1,0:T(8,128)S(1)}, f32[512,1024]{1,0:T(8,128)}, u32[]{:S(2)}) copy-start(f32[512,1024]{1,0:T(8,128)} %scatter_custom_fusion) | copy-start | bytes 6291460
  175.9 7.0 %copy-start.10 = (f32[1,1024]{1,0:T(1,128)S(1)}, f32[1,1024]{1,0:T(1,128)}, u32[]{:S(2)}) copy-start(f32[1,1024]{1,0:T(1,128)} %get-tuple-element.32) | copy-start | bytes 12292
  175.9 7.0 %collective-permute-start.9 = (f32[3,1024]{1,0:T(4,128)S(1)}, f32[3,1024]{1,0:T(4,128)S(1)}, u32[]{:S(2)}, u32[]{:S(2)}) collective-permute-start(f32[3,1024]{1,0:T(4,128)S(1)} %slice.77), channel_id=1, source_target_pairs={{16,0},{32,16},{48,32},{64,48},{80,64},{96,80},{112,96},{128,112},... | collective-permute-start | bytes 36872 | tf_op jit(solution)/shard_map/ppermute | solution.py:21

commit v5 on v4

--- a/solution.py
+++ b/solution.py
@@ -27,15 +27,13 @@
 
 def gather_blocks(block, axis):
     devices = lax.axis_size(axis)
-    me = lax.axis_index(axis)
     held = block[None]
     step = 1
     while step < devices:
         other = lax.ppermute(held, axis, [(i, i ^ step) for i in range(devices)])
         held = jnp.concatenate([held, other], axis=0)
         step *= 2
-    order = jnp.arange(devices, dtype=jnp.int32) ^ me
-    return jnp.take(held, order, axis=0)
+    return held
 
 
 def summed_over(partial, axis):
@@ -50,17 +48,14 @@
     return total
 
 
-def forward_kernel(q_ref, k_ref, v_ref, g_ref, live_row_ref, live_col_ref, att_ref, log_ref, delta_ref):
-    block = pl.program_id(0)
-    rows = q_ref.shape[0]
-    keys = k_ref.shape[0]
+def forward_kernel(
+    q_ref, k_ref, v_ref, g_ref, live_row_ref, live_col_ref, id_row_ref, id_col_ref, att_ref, log_ref, delta_ref
+):
     scale = 1.0 / math.sqrt(HD)
     scores = lax.dot_general(
         q_ref[...], k_ref[...], (((1,), (1,)), ((), ())), preferred_element_type=jnp.float32
     ) * scale
-    q_ids = block * rows + lax.broadcasted_iota(jnp.int32, (rows, keys), 0)
-    k_ids = lax.broadcasted_iota(jnp.int32, (rows, keys), 1)
-    allowed = (k_ids <= q_ids) & (live_row_ref[...] > 0.5)
+    allowed = (id_row_ref[...] <= id_col_ref[...]) & (live_row_ref[...] > 0.5)
     scores = jnp.where(allowed, scores, masked_score)
     row_max = jnp.max(scores, axis=1, keepdims=True)
     softmax_part = jnp.exp(scores - row_max)
@@ -76,7 +71,7 @@
     )
 
 
-def forward_all(queries, keys, values, grads, live):
+def forward_all(queries, keys, values, grads, live, ids):
     slots, width = queries.shape
     live_f = live.astype(jnp.float32)
     row_spec = pl.BlockSpec((QBLOCK, width), lambda i: (i, 0))
@@ -86,6 +81,7 @@
         forward_kernel,
         grid=(slots // QBLOCK,),
         in_specs=[row_spec, full_spec, full_spec, row_spec,
+                  pl.BlockSpec((1, slots), lambda i: (0, 0)), col_spec,
                   pl.BlockSpec((1, slots), lambda i: (0, 0)), col_spec],
         out_specs=[row_spec, col_spec, col_spec],
         out_shape=[
@@ -93,7 +89,10 @@
             jax.ShapeDtypeStruct((slots, 1), jnp.float32),
             jax.ShapeDtypeStruct((slots, 1), jnp.float32),
         ],
-    )(queries, keys, values, grads, live_f.reshape(1, slots), live_f.reshape(slots, 1))
+    )(
+        queries, keys, values, grads, live_f.reshape(1, slots), live_f.reshape(slots, 1),
+        ids.reshape(1, slots), ids.reshape(slots, 1),
+    )
 
 
 def per_device(
@@ -150,16 +149,19 @@
     all_live = (
         jnp.arange(slot_count, dtype=jnp.int32)[None, :] < all_counts[:, None]
     ).reshape(total_slots)
-    slot_ids = jnp.arange(total_slots, dtype=jnp.int32)
+    held_shards = jnp.arange(shards, dtype=jnp.int32) ^ shard_index
+    slot_ids = (
+        held_shards[:, None] * slot_count + jnp.arange(slot_count, dtype=jnp.int32)[None, :]
+    ).reshape(total_slots)
 
     all_attended, all_logs, all_deltas = forward_all(
-        all_queries, all_keys, all_values, all_grads, all_live
+        all_queries, all_keys, all_values, all_grads, all_live, slot_ids
     )
     all_logs = all_logs.reshape(total_slots)
     all_deltas = all_deltas.reshape(total_slots)
-    attended = lax.dynamic_slice_in_dim(all_attended, first_slot, slot_count, axis=0)
-    own_logs = lax.dynamic_slice_in_dim(all_logs, first_slot, slot_count)
-    own_deltas = lax.dynamic_slice_in_dim(all_deltas, first_slot, slot_count)
+    attended = all_attended[:slot_count]
+    own_logs = all_logs[:slot_count]
+    own_deltas = all_deltas[:slot_count]
 
     allowed = (slot_ids[None, :] <= own_ids[:, None]) & all_live[None, :]
     scores = jnp.dot(queries, all_keys.T, preferred_element_type=jnp.float32) * score_scale

time: 193 us -> 190 us (0.984)
  waiting for transfers between devices: 70.2 us -> 67.4 us
    gather x1 -> x0, local copies, waits for them, and re-layouts: 3.82 us -> none  [gather_blocks(): return jnp.take(held, order, axis=0)]
    dynamic_slice x3 -> x0, local copies, waits for them, and re-layouts: 3.07 us -> none  [the longest x1 1.33 us: per_device(): lax.dynamic_slice_in_dim(all_attended, first_slot, slot_count, axis=0)]
    slice x0 -> x3, local copies, waits for them, and re-layouts: none -> 3.06 us  [the longest x1 1.32 us: per_device(): attended = all_attended[:slot_count]]
    ppermute x5, waiting for transfers between devices: 58.3 us -> 55.4 us  [gather_blocks(): other = lax.ppermute(held, axis, [(i, i ^ step) for i in range(devices)])]
    add x0 -> x3, local copies, waits for them, and re-layouts: none -> 2.79 us  [per_device(): held_shards[:, None] * slot_count]
    unnamed x33 -> x37, local copies, waits for them, and re-layouts: 4.84 us -> 4.89 us
  transfers between devices with their start and end apart: 10 -> 10, of which waited for: 9 -> 9; matrix products, arithmetic and copies ran while one was open for 6% -> 8% of each run, Pallas kernels for 0% -> 0%
where the time goes in v5:
time: 190 us; the launch traced here: 189 us
  waiting for transfers between devices  67.4 us (35%)
  starting transfers between devices  40.5 us (21%)
  local copies, waits for them, and re-layouts  30.5 us (16%)
  other arithmetic  21.2 us (11%)
  matrix products  14.5 us (8%)
  Pallas kernels  13 us (7%)
    ppermute x5, waiting for transfers between devices, gather_blocks(): other = lax.ppermute(held, axis, [(i, i ^ step) for i in range(devices)])  55.4 us
    ppermute x3, starting transfers between devices, summed_over(): got = lax.ppermute(sent, axis, [(i, i ^ step) for i in range(devices)])  21.1 us
    pallas_call x1, Pallas kernels, forward_all(): pl.pallas_call(forward_kernel, grid=(slots // QBLOCK,), in_specs=[row_spe...  13 us
    ppermute x5, starting transfers between devices, gather_blocks(): other = lax.ppermute(held, axis, [(i, i ^ step) for i in range(devices)])  12.7 us
    ppermute x3, waiting for transfers between devices, summed_over(): got = lax.ppermute(sent, axis, [(i, i ^ step) for i in range(devices)])  8.87 us
    ppermute x2, starting transfers between devices, passed_along(): return lax.ppermute(array, axis, pairs)  6.72 us
    unnamed x37, local copies, waits for them, and re-layouts  4.89 us
    scatter-add x1, other arithmetic, per_device(): jnp.zeros((row_count, D), jnp.float32).at[boundaries].add(grad_state)  4.25 us
  transfers between devices with their start and end apart: 10, of which 9 were waited for; matrix products, arithmetic and copies ran while one was open for 8% of the time, Pallas kernels for 0%

profile of v5, /device:TPU:30, one launch (start us, length us, event | category | flops | bytes accessed | tf_op | source)
XLA Modules:
  0.0 188.7 jit_solution(15340794577122217462)
XLA Ops:
  0.6 0.9 slice.112
  1.5 4.7 %collective-permute-start = (bf16[3,1024]{1,0:T(4,128)(2,1)S(1)}, bf16[3,1024]{1,0:T(4,128)(2,1)S(1)}, u32[]{:S(2)}, u32[]{:S(2)}) collective-permute-start(bf16[3,1024]{1,0:T(4,128)(2,1)S(1)} %slice.112), channel_id=1, source_target_pairs={{0,16},{16,32},{32,48},{48,64},{64,80},{80,96},{96,112},{112,128},... | collective-permute-start | bytes 18440 | tf_op jit(solution)/shard_map/ppermute | solution.py:21
  6.2 0.7 compare_select_fusion.1
  6.9 1.2 compare_and_fusion.4
  8.1 1.5 fusion.48
  10.2 0.6 iota_compare_fusion.1
  10.8 2.2 %gather_fusion = bf16[64,1024]{1,0:T(8,128)(2,1)S(1)} fusion(bf16[512,1024]{1,0:T(8,128)(2,1)} %param.12, s32[1024]{0:T(1024)S(1)} %get-tuple-element.56), kind=kCustom, calls=%fused_computation.4 | custom fusion | bytes 262400 | tf_op jit(solution)/shard_map/jit(_take)/gather | solution.py:127
  13.0 1.5 pad_maximum_fusion
  14.5 1.4 gather_fusion.4
  15.9 1.4 gather_fusion.3
  17.3 1.3 gather_fusion.2
  18.6 1.4 gather_fusion.1
  20.0 1.9 %multiply_reduce_fusion.1 = (f32[64]{0:T(128)S(1)}, f32[64,1024]{1,0:T(8,128)S(1)}) fusion(bf16[1024,1024]{1,0:T(8,128)(2,1)S(1)} %copy-done, bf16[64,1024]{1,0:T(8,128)(2,1)} %gather_fusion.4, bf16[64,1024]{1,0:T(8,128)(2,1)} %gather_fusion.3, bf16[64,1024]{1,0:T(8,128)(2,1)} %gather_fusion.2, bf16[64,1024]{1,0:T(8,128)(2,1)} %gather_fusion.1, ...), kind=kOutput, calls=%fused_computation.55 | convolution fusion | flops 135593920 | bytes 3031616 | tf_op jit(solution)/shard_map/dot_general | solution.py:129
  22.2 0.2 constant_dynamic-update-slice_fusion.3
  22.8 1.9 %collective-permute-start.1 = (bf16[1,272,128]{2,1,0:T(8,128)(2,1)S(1)}, bf16[1,272,128]{2,1,0:T(8,128)(2,1)S(1)}, u32[]{:S(2)}, u32[]{:S(2)}) collective-permute-start(bf16[1,272,128]{2,1,0:T(8,128)(2,1)S(1)} %bitcast.48), channel_id=1, source_target_pairs={{0,16},{16,0},{32,48},{48,32},{64,80},{80,64},{96,112},{112,96},{1... | collective-permute-start | bytes 208904 | tf_op jit(solution)/shard_map/ppermute | solution.py:33
  24.7 4.3 %collective-permute-done.1 = bf16[1,272,128]{2,1,0:T(8,128)(2,1)S(1)} collective-permute-done((bf16[1,272,128]{2,1,0:T(8,128)(2,1)S(1)}, bf16[1,272,128]{2,1,0:T(8,128)(2,1)S(1)}, u32[]{:S(2)}, u32[]{:S(2)}) %collective-permute-start.1) | collective-permute-done | bytes 69664 | tf_op jit(solution)/shard_map/ppermute | solution.py:33
  29.0 1.9 %collective-permute-start.2 = (bf16[2,272,128]{2,1,0:T(8,128)(2,1)S(1)}, bf16[2,272,128]{2,1,0:T(8,128)(2,1)S(1)}, u32[]{:S(2)}, u32[]{:S(2)}) collective-permute-start(bf16[2,272,128]{2,1,0:T(8,128)(2,1)S(1)} %pad_maximum_fusion.3), channel_id=1, source_target_pairs={{0,32},{16,48},{32,0},{48,16},{64,96},{80,112},{96,64},{112,80},{1... | collective-permute-start | bytes 417800 | tf_op jit(solution)/shard_map/ppermute | solution.py:33
  30.9 7.6 %collective-permute-done.2 = bf16[2,272,128]{2,1,0:T(8,128)(2,1)S(1)} collective-permute-done((bf16[2,272,128]{2,1,0:T(8,128)(2,1)S(1)}, bf16[2,272,128]{2,1,0:T(8,128)(2,1)S(1)}, u32[]{:S(2)}, u32[]{:S(2)}) %collective-permute-start.2) | collective-permute-done | bytes 139296 | tf_op jit(solution)/shard_map/ppermute | solution.py:33
  38.5 2.8 %collective-permute-start.3 = (bf16[4,272,128]{2,1,0:T(8,128)(2,1)S(1)}, bf16[4,272,128]{2,1,0:T(8,128)(2,1)S(1)}, u32[]{:S(2)}, u32[]{:S(2)}) collective-permute-start(bf16[4,272,128]{2,1,0:T(8,128)(2,1)S(1)} %pad_maximum_fusion.2), channel_id=1, source_target_pairs={{0,64},{16,80},{32,96},{48,112},{64,0},{80,16},{96,32},{112,48},{1... | collective-permute-start | bytes 835592 | tf_op jit(solution)/shard_map/ppermute | solution.py:33
  41.3 13.9 %collective-permute-done.3 = bf16[4,272,128]{2,1,0:T(8,128)(2,1)S(1)} collective-permute-done((bf16[4,272,128]{2,1,0:T(8,128)(2,1)S(1)}, bf16[4,272,128]{2,1,0:T(8,128)(2,1)S(1)}, u32[]{:S(2)}, u32[]{:S(2)}) %collective-permute-start.3) | collective-permute-done | bytes 278560 | tf_op jit(solution)/shard_map/ppermute | solution.py:33
  55.3 2.7 %collective-permute-start.4 = (bf16[8,272,128]{2,1,0:T(8,128)(2,1)S(1)}, bf16[8,272,128]{2,1,0:T(8,128)(2,1)S(1)}, u32[]{:S(2)}, u32[]{:S(2)}) collective-permute-start(bf16[8,272,128]{2,1,0:T(8,128)(2,1)S(1)} %pad_maximum_fusion.1), channel_id=1, source_target_pairs={{0,128},{16,144},{32,160},{48,176},{64,192},{80,208},{96,224},{112... | collective-permute-start | bytes 1671176 | tf_op jit(solution)/shard_map/ppermute | solution.py:33
  58.1 0.7 constant_dynamic-update-slice_fusion.9
  58.8 0.7 constant_dynamic-update-slice_fusion.8
  59.4 0.7 constant_dynamic-update-slice_fusion.7
  60.2 0.9 constant_dynamic-update-slice_fusion.6
  61.1 8.6 %collective-permute-done.4 = bf16[8,272,128]{2,1,0:T(8,128)(2,1)S(1)} collective-permute-done((bf16[8,272,128]{2,1,0:T(8,128)(2,1)S(1)}, bf16[8,272,128]{2,1,0:T(8,128)(2,1)S(1)}, u32[]{:S(2)}, u32[]{:S(2)}) %collective-permute-start.4) | collective-permute-done | bytes 557088 | tf_op jit(solution)/shard_map/ppermute | solution.py:33
  69.7 1.1 constant_dynamic-update-slice_fusion.5
  70.9 3.3 %collective-permute-start.5 = (bf16[16,272,128]{2,1,0:T(8,128)(2,1)}, bf16[16,272,128]{2,1,0:T(8,128)(2,1)}, u32[]{:S(2)}, u32[]{:S(2)}) collective-permute-start(bf16[16,272,128]{2,1,0:T(8,128)(2,1)} %get-tuple-element.19), channel_id=1, source_target_pairs={{0,256},{16,272},{32,288},{48,304},{64,320},{80,336},{96,352},{112... | collective-permute-start | bytes 3342344 | tf_op jit(solution)/shard_map/ppermute | solution.py:33
  74.2 0.7 add.155.id_row_ref
  74.9 2.0 %add.188.id_col_ref = s32[2048,1]{1,0:T(8,128)} reshape(s32[32,64]{1,0:T(8,128)S(1)} %iota_add_fusion) | data formatting | bytes 16384 | tf_op jit(solution)/shard_map/add | solution.py:154
  77.0 21.0 %collective-permute-done.5 = bf16[16,272,128]{2,1,0:T(8,128)(2,1)} collective-permute-done((bf16[16,272,128]{2,1,0:T(8,128)(2,1)}, bf16[16,272,128]{2,1,0:T(8,128)(2,1)}, u32[]{:S(2)}, u32[]{:S(2)}) %collective-permute-start.5) | collective-permute-done | bytes 1114144 | tf_op jit(solution)/shard_map/ppermute | solution.py:33
  98.0 2.3 %constant_dynamic-update-slice_fusion.10 = bf16[32,272,128]{2,1,0:T(8,128)(2,1)} fusion(bf16[32,272,128]{2,1,0:T(8,128)(2,1)} %get-tuple-element.20, bf16[16,272,128]{2,1,0:T(8,128)(2,1)} %collective-permute-done.5), kind=kLoop, calls=%fused_computation.83 | loop fusion | bytes 2228224 | tf_op jit(solution)/shard_map/concatenate | solution.py:34
  100.4 2.9 %fusion.47 = (bf16[32,64,128]{2,1,0:T(8,128)(2,1)}, bf16[32,64,128]{2,1,0:T(8,128)(2,1)}, bf16[32,64,128]{2,1,0:T(8,128)(2,1)}, bf16[32,64,128]{2,1,0:T(8,128)(2,1)}) fusion(bf16[32,272,128]{2,1,0:T(8,128)(2,1)} %constant_dynamic-update-slice_fusion.10), kind=kLoop, calls=%fused_computation.124 | loop fusion | bytes 4194304 | tf_op jit(solution)/shard_map/slice | solution.py:145
  103.2 1.5 fusion.41
  104.8 0.7 reshape.190.live_row_ref
  105.5 2.0 %reshape.263.live_col_ref = f32[2048,1]{1,0:T(8,128)} reshape(f32[32,64]{1,0:T(8,128)S(1)} %get-tuple-element.36) | data formatting | bytes 16384 | tf_op jit(solution)/shard_map/convert_element_type | solution.py:76
  107.5 13.0 %shard_map.113 = (bf16[2048,128]{1,0:T(8,128)(2,1)}, f32[2048,1]{1,0:T(8,128)}, f32[2048,1]{1,0:T(8,128)}) custom-call(bf16[2048,128]{1,0:T(8,128)(2,1)} %bitcast.40, bf16[2048,128]{1,0:T(8,128)(2,1)} %bitcast.45, bf16[2048,128]{1,0:T(8,128)(2,1)} %bitcast.43, bf16[2048,128]{1,0:T(8,128)(2,1)} %bitcast.37, f32[1,2048]{1,0:T(1,128)} %reshape.190.live_row_ref, ...), custom_call_target="tpu_custom_call" | custom-call | tf_op jit(solution)/shard_map/pallas_call | solution.py:80
  120.4 0.9 slice_reduce_fusion.1
  121.3 0.9 slice_reduce_fusion
  122.2 1.6 reduce.3
  123.8 1.6 reduce.4
  125.5 2.2 %fusion.5 = f32[64,2048]{1,0:T(8,128)} fusion(bf16[64,128]{1,0:T(8,128)(2,1)S(1)} %get-tuple-element.50, bf16[2048,128]{1,0:T(8,128)(2,1)} %bitcast.46, f32[64]{0:T(128)S(1)} %slice_reduce_fusion.1, s32[2048]{0:T(1024)S(1)} %add.157, s32[64]{0:T(128)S(1)} %iota_add_fusion.1, pred[2048]{0:T(1024)(128)(4,1)S(1)} %lt.76), kind=kOutput, calls=%fused_computation.16 | convolution fusion | flops 34209792 | bytes 1075712 | tf_op jit(solution)/shard_map/dot_general | solution.py:167
  127.7 1.8 fusion.19
  129.6 1.9 fusion.49
  131.4 1.1 fusion.7
  132.5 1.5 fusion.18
  134.0 1.2 convolution_add_fusion.1
  135.3 1.5 fusion.15
  136.8 4.3 %collective-permute-start.6 = (bf16[64,1024]{1,0:T(8,128)(2,1)S(1)}, bf16[64,1024]{1,0:T(8,128)(2,1)S(1)}, u32[]{:S(2)}, u32[]{:S(2)}) collective-permute-start(bf16[64,1024]{1,0:T(8,128)(2,1)S(1)} %fusion.15), channel_id=1, source_target_pairs={{0,2},{2,0},{4,6},{6,4},{8,10},{10,8},{12,14},{14,12},{1,3},{3,1},... | collective-permute-start | bytes 393224 | tf_op jit(solution)/shard_map/ppermute | solution.py:45
  141.1 2.9 %collective-permute-done.6 = bf16[64,1024]{1,0:T(8,128)(2,1)S(1)} collective-permute-done((bf16[64,1024]{1,0:T(8,128)(2,1)S(1)}, bf16[64,1024]{1,0:T(8,128)(2,1)S(1)}, u32[]{:S(2)}, u32[]{:S(2)}) %collective-permute-start.6) | collective-permute-done | bytes 131104 | tf_op jit(solution)/shard_map/ppermute | solution.py:45
  144.0 6.3 %collective-permute-start.7 = (bf16[64,1024]{1,0:T(8,128)(2,1)S(1)}, bf16[64,1024]{1,0:T(8,128)(2,1)S(1)}, u32[]{:S(2)}, u32[]{:S(2)}) collective-permute-start(bf16[64,1024]{1,0:T(8,128)(2,1)S(1)} %add_convert_fusion.1), channel_id=1, source_target_pairs={{0,4},{2,6},{4,0},{6,2},{8,12},{10,14},{12,8},{14,10},{1,5},{3,7},... | collective-permute-start | bytes 393224 | tf_op jit(solution)/shard_map/ppermute | solution.py:45
  150.3 4.3 %collective-permute-done.7 = bf16[64,1024]{1,0:T(8,128)(2,1)S(1)} collective-permute-done((bf16[64,1024]{1,0:T(8,128)(2,1)S(1)}, bf16[64,1024]{1,0:T(8,128)(2,1)S(1)}, u32[]{:S(2)}, u32[]{:S(2)}) %collective-permute-start.7) | collective-permute-done | bytes 131104 | tf_op jit(solution)/shard_map/ppermute | solution.py:45
  154.7 10.5 %collective-permute-start.8 = (bf16[64,1024]{1,0:T(8,128)(2,1)S(1)}, bf16[64,1024]{1,0:T(8,128)(2,1)S(1)}, u32[]{:S(2)}, u32[]{:S(2)}) collective-permute-start(bf16[64,1024]{1,0:T(8,128)(2,1)S(1)} %add_convert_fusion), channel_id=1, source_target_pairs={{0,8},{2,10},{4,12},{6,14},{8,0},{10,2},{12,4},{14,6},{1,9},{3,11}... | collective-permute-start | bytes 393224 | tf_op jit(solution)/shard_map/ppermute | solution.py:45
  165.2 1.3 slice.67
  166.5 1.6 collective-permute-done.8
  168.3 0.8 fusion.30
  169.1 2.7 %scatter_custom_fusion = f32[512,1024]{1,0:T(8,128)} fusion(s32[64]{0:T(128)} %copy-done.13, f32[64,1024]{1,0:T(8,128)S(1)} %fusion.30, f32[]{:T(128)} %constant.31.clone.1), kind=kCustom, calls=%fused_computation.42 | custom fusion | flops 65536 | bytes 2097664 | tf_op jit(solution)/shard_map/scatter-add | solution.py:212
  171.7 0.8 slice.89
  172.5 2.0 %collective-permute-start.9 = (f32[3,1024]{1,0:T(4,128)S(1)}, f32[3,1024]{1,0:T(4,128)S(1)}, u32[]{:S(2)}, u32[]{:S(2)}) collective-permute-start(f32[3,1024]{1,0:T(4,128)S(1)} %slice.89), channel_id=1, source_target_pairs={{16,0},{32,16},{48,32},{64,48},{80,64},{96,80},{112,96},{128,112},... | collective-permute-start | bytes 36872 | tf_op jit(solution)/shard_map/ppermute | solution.py:21
  174.6 1.8 constant_dynamic-update-slice_fusion.17
  176.4 3.1 %collective-permute-done.9 = f32[3,1024]{1,0:T(4,128)S(1)} collective-permute-done((f32[3,1024]{1,0:T(4,128)S(1)}, f32[3,1024]{1,0:T(4,128)S(1)}, u32[]{:S(2)}, u32[]{:S(2)}) %collective-permute-start.9) | collective-permute-done | bytes 12320 | tf_op jit(solution)/shard_map/ppermute | solution.py:21
  179.5 2.2 %fusion.10 = f32[512,1024]{1,0:T(8,128)} fusion(f32[515,1024]{1,0:T(8,128)S(1)} %constant_dynamic-update-slice_fusion.16, f32[512,1024]{1,0:T(8,128)S(1)} %copy-done.1, f32[1024]{0:T(1024)S(1)} %bitcast.57, f32[1024]{0:T(1024)S(1)} %bitcast.59, f32[1024]{0:T(1024)S(1)} %bitcast.55, f32[1024]{0:T(1024)S(1)} %bitcast.53), kind=kLoop, calls=%fused_computation.22 | loop fusion | flops 3670016 | bytes 10502144 | tf_op jit(solution)/shard_map/add | solution.py:218
  181.7 4.2 %scatter_custom_fusion.1 = f32[512,1024]{1,0:T(8,128)} fusion(f32[512,1024]{1,0:T(8,128)} %fusion.10, s32[64]{0:T(128)} %copy-done.13, f32[64,1024]{1,0:T(8,128)S(1)} %get-tuple-element.48, bf16[64,1024]{1,0:T(8,128)(2,1)S(1)} %collective-permute-done.8, bf16[64,1024]{1,0:T(8,128)(2,1)S(1)} %add_convert_fusion, f32[64]{0:T(128)S(1)} %broadcast_multiply_fusion, ...), kind=kCustom, calls=%fused_computation.123 | custom fusion | flops 655360 | bytes 2626368 | tf_op jit(solution)/shard_map/scatter-add | solution.py:213
  186.0 2.7 %convert_element_type.160 = bf16[512,1024]{1,0:T(8,128)(2,1)} convert(f32[512,1024]{1,0:T(8,128)} %scatter_custom_fusion.1) | non-fusion elementwise | flops 524288 | bytes 3145728 | tf_op jit(solution)/shard_map/convert_element_type | solution.py:219
  (56 shorter events, 1.3 us)
Async XLA Ops:
  0.6 19.3 %copy-start = (bf16[1024,1024]{1,0:T(8,128)(2,1)S(1)}, bf16[1024,1024]{1,0:T(8,128)(2,1)}, u32[]{:S(2)}) copy-start(bf16[1024,1024]{1,0:T(8,128)(2,1)} %param.14) | copy-start | bytes 6291460
  1.5 11.5 %collective-permute-start = (bf16[3,1024]{1,0:T(4,128)(2,1)S(1)}, bf16[3,1024]{1,0:T(4,128)(2,1)S(1)}, u32[]{:S(2)}, u32[]{:S(2)}) collective-permute-start(bf16[3,1024]{1,0:T(4,128)(2,1)S(1)} %slice.112), channel_id=1, source_target_pairs={{0,16},{16,32},{32,48},{48,64},{64,80},{80,96},{96,112},{112,128},... | collective-permute-start | bytes 18440 | tf_op jit(solution)/shard_map/ppermute | solution.py:21
  6.9 3.4 %copy-start.13 = (s32[64]{0:T(128)}, s32[64]{0:T(128)S(1)}, u32[]{:S(2)}) copy-start(s32[64]{0:T(128)S(1)} %get-tuple-element.45) | copy-start | bytes 772
  18.6 3.3 %copy-start.7 = (f32[1024]{0:T(1024)S(1)}, f32[1024]{0:T(1024)}, u32[]{:S(2)}) copy-start(f32[1024]{0:T(1024)} %param.15) | copy-start | bytes 12292
  20.0 2.1 %copy-start.5 = (bf16[1024,128]{1,0:T(8,128)(2,1)S(1)}, bf16[1024,128]{1,0:T(8,128)(2,1)}, u32[]{:S(2)}) copy-start(bf16[1024,128]{1,0:T(8,128)(2,1)} %param.16) | copy-start | bytes 786436
  20.0 2.3 %copy-start.4 = (bf16[1024,128]{1,0:T(8,128)(2,1)S(1)}, bf16[1024,128]{1,0:T(8,128)(2,1)}, u32[]{:S(2)}) copy-start(bf16[1024,128]{1,0:T(8,128)(2,1)} %param.17) | copy-start | bytes 786436
  20.0 2.5 %copy-start.6 = (bf16[1024,128]{1,0:T(8,128)(2,1)S(1)}, bf16[1024,128]{1,0:T(8,128)(2,1)}, u32[]{:S(2)}) copy-start(bf16[1024,128]{1,0:T(8,128)(2,1)} %param.18) | copy-start | bytes 786436
  20.0 2.7 %copy-start.8 = (bf16[64,128]{1,0:T(8,128)(2,1)S(1)}, bf16[64,128]{1,0:T(8,128)(2,1)}, u32[]{:S(2)}) copy-start(bf16[64,128]{1,0:T(8,128)(2,1)} %param.21) | copy-start | bytes 49156
  20.0 2.7 %copy-start.11 = (pred[64]{0:T(512)(128)(4,1)S(1)}, pred[64]{0:T(512)(128)(4,1)}, u32[]{:S(2)}) copy-start(pred[64]{0:T(512)(128)(4,1)} %iota_compare_fusion.1) | copy-start | bytes 196
  22.8 6.2 %collective-permute-start.1 = (bf16[1,272,128]{2,1,0:T(8,128)(2,1)S(1)}, bf16[1,272,128]{2,1,0:T(8,128)(2,1)S(1)}, u32[]{:S(2)}, u32[]{:S(2)}) collective-permute-start(bf16[1,272,128]{2,1,0:T(8,128)(2,1)S(1)} %bitcast.48), channel_id=1, source_target_pairs={{0,16},{16,0},{32,48},{48,32},{64,80},{80,64},{96,112},{112,96},{1... | collective-permute-start | bytes 208904 | tf_op jit(solution)/shard_map/ppermute | solution.py:33
  29.0 9.5 %collective-permute-start.2 = (bf16[2,272,128]{2,1,0:T(8,128)(2,1)S(1)}, bf16[2,272,128]{2,1,0:T(8,128)(2,1)S(1)}, u32[]{:S(2)}, u32[]{:S(2)}) collective-permute-start(bf16[2,272,128]{2,1,0:T(8,128)(2,1)S(1)} %pad_maximum_fusion.3), channel_id=1, source_target_pairs={{0,32},{16,48},{32,0},{48,16},{64,96},{80,112},{96,64},{112,80},{1... | collective-permute-start | bytes 417800 | tf_op jit(solution)/shard_map/ppermute | solution.py:33
  38.5 16.8 %collective-permute-start.3 = (bf16[4,272,128]{2,1,0:T(8,128)(2,1)S(1)}, bf16[4,272,128]{2,1,0:T(8,128)(2,1)S(1)}, u32[]{:S(2)}, u32[]{:S(2)}) collective-permute-start(bf16[4,272,128]{2,1,0:T(8,128)(2,1)S(1)} %pad_maximum_fusion.2), channel_id=1, source_target_pairs={{0,64},{16,80},{32,96},{48,112},{64,0},{80,16},{96,32},{112,48},{1... | collective-permute-start | bytes 835592 | tf_op jit(solution)/shard_map/ppermute | solution.py:33
  55.3 14.4 %collective-permute-start.4 = (bf16[8,272,128]{2,1,0:T(8,128)(2,1)S(1)}, bf16[8,272,128]{2,1,0:T(8,128)(2,1)S(1)}, u32[]{:S(2)}, u32[]{:S(2)}) collective-permute-start(bf16[8,272,128]{2,1,0:T(8,128)(2,1)S(1)} %pad_maximum_fusion.1), channel_id=1, source_target_pairs={{0,128},{16,144},{32,160},{48,176},{64,192},{80,208},{96,224},{112... | collective-permute-start | bytes 1671176 | tf_op jit(solution)/shard_map/ppermute | solution.py:33
  70.9 27.2 %collective-permute-start.5 = (bf16[16,272,128]{2,1,0:T(8,128)(2,1)}, bf16[16,272,128]{2,1,0:T(8,128)(2,1)}, u32[]{:S(2)}, u32[]{:S(2)}) collective-permute-start(bf16[16,272,128]{2,1,0:T(8,128)(2,1)} %get-tuple-element.19), channel_id=1, source_target_pairs={{0,256},{16,272},{32,288},{48,304},{64,320},{80,336},{96,352},{112... | collective-permute-start | bytes 3342344 | tf_op jit(solution)/shard_map/ppermute | solution.py:33
  77.0 48.4 %copy-start.14 = (s32[64]{0:T(128)}, s32[64]{0:T(128)S(1)}, u32[]{:S(2)}) copy-start(s32[64]{0:T(128)S(1)} %iota_add_fusion.1) | copy-start | bytes 772
  120.4 7.3 %copy-start.9 = (bf16[64,128]{1,0:T(8,128)(2,1)S(1)}, bf16[64,128]{1,0:T(8,128)(2,1)}, u32[]{:S(2)}) copy-start(bf16[64,128]{1,0:T(8,128)(2,1)} %param.21) | copy-start | bytes 49156
  120.4 7.3 %copy-start.12 = (pred[64]{0:T(512)(128)(4,1)S(1)}, pred[64]{0:T(512)(128)(4,1)}, u32[]{:S(2)}) copy-start(pred[64]{0:T(512)(128)(4,1)} %iota_compare_fusion.1) | copy-start | bytes 196
  123.8 7.7 %copy-start.3 = (bf16[32,64,128]{2,1,0:T(8,128)(2,1)S(1)}, bf16[32,64,128]{2,1,0:T(8,128)(2,1)}, u32[]{:S(2)}) copy-start(bf16[32,64,128]{2,1,0:T(8,128)(2,1)} %get-tuple-element.18) | copy-start | bytes 1572868
  125.5 7.1 %copy-start.2 = (bf16[32,64,128]{2,1,0:T(8,128)(2,1)S(1)}, bf16[32,64,128]{2,1,0:T(8,128)(2,1)}, u32[]{:S(2)}) copy-start(bf16[32,64,128]{2,1,0:T(8,128)(2,1)} %get-tuple-element.15) | copy-start | bytes 1572868
  127.7 3.7 %copy-start.15 = (s32[64]{0:T(128)S(1)}, s32[64]{0:T(128)}, u32[]{:S(2)}) copy-start(s32[64]{0:T(128)} %copy-done.14) | copy-start | bytes 772
  136.8 7.2 %collective-permute-start.6 = (bf16[64,1024]{1,0:T(8,128)(2,1)S(1)}, bf16[64,1024]{1,0:T(8,128)(2,1)S(1)}, u32[]{:S(2)}, u32[]{:S(2)}) collective-permute-start(bf16[64,1024]{1,0:T(8,128)(2,1)S(1)} %fusion.15), channel_id=1, source_target_pairs={{0,2},{2,0},{4,6},{6,4},{8,10},{10,8},{12,14},{14,12},{1,3},{3,1},... | collective-permute-start | bytes 393224 | tf_op jit(solution)/shard_map/ppermute | solution.py:45
  144.0 10.6 %collective-permute-start.7 = (bf16[64,1024]{1,0:T(8,128)(2,1)S(1)}, bf16[64,1024]{1,0:T(8,128)(2,1)S(1)}, u32[]{:S(2)}, u32[]{:S(2)}) collective-permute-start(bf16[64,1024]{1,0:T(8,128)(2,1)S(1)} %add_convert_fusion.1), channel_id=1, source_target_pairs={{0,4},{2,6},{4,0},{6,2},{8,12},{10,14},{12,8},{14,10},{1,5},{3,7},... | collective-permute-start | bytes 393224 | tf_op jit(solution)/shard_map/ppermute | solution.py:45
  154.7 13.4 %collective-permute-start.8 = (bf16[64,1024]{1,0:T(8,128)(2,1)S(1)}, bf16[64,1024]{1,0:T(8,128)(2,1)S(1)}, u32[]{:S(2)}, u32[]{:S(2)}) collective-permute-start(bf16[64,1024]{1,0:T(8,128)(2,1)S(1)} %add_convert_fusion), channel_id=1, source_target_pairs={{0,8},{2,10},{4,12},{6,14},{8,0},{10,2},{12,4},{14,6},{1,9},{3,11}... | collective-permute-start | bytes 393224 | tf_op jit(solution)/shard_map/ppermute | solution.py:45
  172.5 7.0 %copy-start.1 = (f32[512,1024]{1,0:T(8,128)S(1)}, f32[512,1024]{1,0:T(8,128)}, u32[]{:S(2)}) copy-start(f32[512,1024]{1,0:T(8,128)} %scatter_custom_fusion) | copy-start | bytes 6291460
  172.5 7.0 %copy-start.10 = (f32[1,1024]{1,0:T(1,128)S(1)}, f32[1,1024]{1,0:T(1,128)}, u32[]{:S(2)}) copy-start(f32[1,1024]{1,0:T(1,128)} %get-tuple-element.32) | copy-start | bytes 12292
  172.5 7.0 %collective-permute-start.9 = (f32[3,1024]{1,0:T(4,128)S(1)}, f32[3,1024]{1,0:T(4,128)S(1)}, u32[]{:S(2)}, u32[]{:S(2)}) collective-permute-start(f32[3,1024]{1,0:T(4,128)S(1)} %slice.89), channel_id=1, source_target_pairs={{16,0},{32,16},{48,32},{64,48},{80,64},{96,80},{112,96},{128,112},... | collective-permute-start | bytes 36872 | tf_op jit(solution)/shard_map/ppermute | solution.py:21

commit v6 on v5

--- a/solution.py
+++ b/solution.py
@@ -25,15 +25,41 @@
     return passed_along(rim_rows, "seq", offset_by)
 
 
-def gather_blocks(block, axis):
+def gather_blocks(block, axis, inner):
     devices = lax.axis_size(axis)
+    me = lax.axis_index(axis)
     held = block[None]
     step = 1
-    while step < devices:
+    while step < inner:
         other = lax.ppermute(held, axis, [(i, i ^ step) for i in range(devices)])
         held = jnp.concatenate([held, other], axis=0)
         step *= 2
-    return held
+    sources = jnp.arange(inner, dtype=jnp.int32) ^ me
+    outer = devices // inner
+    if outer == 1:
+        return held, sources
+
+    def shifted(array, by):
+        return lax.ppermute(array, axis, [(i, (i + by) % devices) for i in range(devices)])
+
+    parts = [held]
+    origins = [sources]
+    from_below = shifted(held, inner)
+    from_above = shifted(held, -inner) if outer > 2 else None
+    parts.append(from_below)
+    origins.append((sources - inner) % devices)
+    if outer > 2:
+        parts.append(from_above)
+        origins.append((sources + inner) % devices)
+    if outer == 4:
+        half = inner // 2
+        parts.append(shifted(from_below[:half], inner))
+        origins.append((sources[:half] - 2 * inner) % devices)
+        parts.append(shifted(from_above[half:], -inner))
+        origins.append((sources[half:] + 2 * inner) % devices)
+    else:
+        assert outer <= 3
+    return jnp.concatenate(parts, axis=0), jnp.concatenate(origins)
 
 
 def summed_over(partial, axis):
@@ -138,7 +164,7 @@
 
     count_rows = jnp.broadcast_to(span_counts[0].astype(jnp.bfloat16), (16, head_width))
     packed = jnp.concatenate([queries, key_rows, value_rows, grad_rows, count_rows], axis=0)
-    gathered = gather_blocks(packed, "seq")
+    gathered, held_shards = gather_blocks(packed, "seq", 8 if shards == 32 else shards)
     total_slots = shards * slot_count
 
     def piece(k):
@@ -149,7 +175,6 @@
     all_live = (
         jnp.arange(slot_count, dtype=jnp.int32)[None, :] < all_counts[:, None]
     ).reshape(total_slots)
-    held_shards = jnp.arange(shards, dtype=jnp.int32) ^ shard_index
     slot_ids = (
         held_shards[:, None] * slot_count + jnp.arange(slot_count, dtype=jnp.int32)[None, :]
     ).reshape(total_slots)

time: 190 us -> 174 us (0.916)
  waiting for transfers between devices: 67.4 us -> 50.4 us
  starting transfers between devices: 40.5 us -> 48.5 us
  local copies, waits for them, and re-layouts: 30.5 us -> 24.7 us
    ppermute x5 -> x3, waiting for transfers between devices: 55.4 us -> 22.8 us  [gather_blocks(): other = lax.ppermute(held, axis, [(i, i ^ step) for i in range(devices)])]
    ppermute x0 -> x4, waiting for transfers between devices: none -> 15.6 us  [shifted(): lax.ppermute(array, axis, [(i, (i + by) % devices) for i in range(devices)])]
    ppermute x0 -> x4, starting transfers between devices: none -> 11.7 us  [shifted(): lax.ppermute(array, axis, [(i, (i + by) % devices) for i in range(devices)])]
    ppermute x5 -> x3, starting transfers between devices: 12.7 us -> 6.65 us  [gather_blocks(): other = lax.ppermute(held, axis, [(i, i ^ step) for i in range(devices)])]
    concatenate x2, local copies, waits for them, and re-layouts: 3.46 us -> 0.12 us  [gather_blocks(): return (jnp.concatenate(parts, axis=0), jnp.concatenate(origins))]
    ppermute x3, starting transfers between devices: 21.1 us -> 23.4 us  [summed_over(): got = lax.ppermute(sent, axis, [(i, i ^ step) for i in range(devices)])]
    unnamed x37 -> x42, local copies, waits for them, and re-layouts: 4.89 us -> 3.83 us
  transfers between devices with their start and end apart: 10 -> 12, of which waited for: 9 -> 10; matrix products, arithmetic and copies ran while one was open for 8% -> 8% of each run, Pallas kernels for 0% -> 0%
where the time goes in v6:
time: 174 us; the launch traced here: 173 us
  waiting for transfers between devices  50.4 us (29%)
  starting transfers between devices  48.5 us (28%)
  local copies, waits for them, and re-layouts  24.7 us (14%)
  other arithmetic  20.4 us (12%)
  matrix products  14.5 us (8%)
  Pallas kernels  13 us (7%)
  between operations  1.77 us (1%)
    ppermute x3, starting transfers between devices, summed_over(): got = lax.ppermute(sent, axis, [(i, i ^ step) for i in range(devices)])  23.4 us
    ppermute x3, waiting for transfers between devices, gather_blocks(): other = lax.ppermute(held, axis, [(i, i ^ step) for i in range(devices)])  22.8 us
    ppermute x4, waiting for transfers between devices, shifted(): lax.ppermute(array, axis, [(i, (i + by) % devices) for i in range(devices)])  15.6 us
    pallas_call x1, Pallas kernels, forward_all(): pl.pallas_call(forward_kernel, grid=(slots // QBLOCK,), in_specs=[row_spe...  13 us
    ppermute x4, starting transfers between devices, shifted(): lax.ppermute(array, axis, [(i, (i + by) % devices) for i in range(devices)])  11.7 us
    ppermute x3, waiting for transfers between devices, summed_over(): got = lax.ppermute(sent, axis, [(i, i ^ step) for i in range(devices)])  8.87 us
    ppermute x2, starting transfers between devices, passed_along(): return lax.ppermute(array, axis, pairs)  6.72 us
    ppermute x3, starting transfers between devices, gather_blocks(): other = lax.ppermute(held, axis, [(i, i ^ step) for i in range(devices)])  6.65 us
  transfers between devices with their start and end apart: 12, of which 10 were waited for; matrix products, arithmetic and copies ran while one was open for 8% of the time, Pallas kernels for 0%

profile of v6, /device:TPU:30, one launch (start us, length us, event | category | flops | bytes accessed | tf_op | source)
XLA Modules:
  0.0 173.2 jit_solution(5118624150554661033)
XLA Ops:
  0.6 0.9 slice.132
  1.5 4.7 %collective-permute-start = (bf16[3,1024]{1,0:T(4,128)(2,1)S(1)}, bf16[3,1024]{1,0:T(4,128)(2,1)S(1)}, u32[]{:S(2)}, u32[]{:S(2)}) collective-permute-start(bf16[3,1024]{1,0:T(4,128)(2,1)S(1)} %slice.132), channel_id=1, source_target_pairs={{0,16},{16,32},{32,48},{48,64},{64,80},{80,96},{96,112},{112,128},... | collective-permute-start | bytes 18440 | tf_op jit(solution)/shard_map/ppermute | solution.py:21
  6.2 0.7 compare_select_fusion.1
  6.9 1.2 compare_and_fusion.4
  8.1 1.5 fusion.52
  10.3 0.6 iota_compare_fusion.1
  10.8 2.2 %gather_fusion = bf16[64,1024]{1,0:T(8,128)(2,1)S(1)} fusion(bf16[512,1024]{1,0:T(8,128)(2,1)} %param.12, s32[1024]{0:T(1024)S(1)} %get-tuple-element.48), kind=kCustom, calls=%fused_computation.4 | custom fusion | bytes 262400 | tf_op jit(solution)/shard_map/jit(_take)/gather | solution.py:153
  13.0 1.5 pad_maximum_fusion
  14.5 1.4 gather_fusion.4
  15.9 1.4 gather_fusion.3
  17.2 1.3 gather_fusion.2
  18.6 1.4 gather_fusion.1
  20.0 1.9 %multiply_reduce_fusion.1 = (f32[64]{0:T(128)S(1)}, f32[64,1024]{1,0:T(8,128)S(1)}) fusion(bf16[1024,1024]{1,0:T(8,128)(2,1)S(1)} %copy-done, bf16[64,1024]{1,0:T(8,128)(2,1)} %gather_fusion.4, bf16[64,1024]{1,0:T(8,128)(2,1)} %gather_fusion.3, bf16[64,1024]{1,0:T(8,128)(2,1)} %gather_fusion.2, bf16[64,1024]{1,0:T(8,128)(2,1)} %gather_fusion.1, ...), kind=kOutput, calls=%fused_computation.55 | convolution fusion | flops 135593920 | bytes 3031616 | tf_op jit(solution)/shard_map/dot_general | solution.py:155
  22.2 0.2 constant_dynamic-update-slice_fusion.3
  22.4 0.2 constant_dynamic-update-slice_fusion.2
  22.7 1.9 %collective-permute-start.1 = (bf16[1,272,128]{2,1,0:T(8,128)(2,1)S(1)}, bf16[1,272,128]{2,1,0:T(8,128)(2,1)S(1)}, u32[]{:S(2)}, u32[]{:S(2)}) collective-permute-start(bf16[1,272,128]{2,1,0:T(8,128)(2,1)S(1)} %bitcast.47), channel_id=1, source_target_pairs={{0,16},{16,0},{32,48},{48,32},{64,80},{80,64},{96,112},{112,96},{1... | collective-permute-start | bytes 208904 | tf_op jit(solution)/shard_map/ppermute | solution.py:34
  24.7 4.3 %collective-permute-done.1 = bf16[1,272,128]{2,1,0:T(8,128)(2,1)S(1)} collective-permute-done((bf16[1,272,128]{2,1,0:T(8,128)(2,1)S(1)}, bf16[1,272,128]{2,1,0:T(8,128)(2,1)S(1)}, u32[]{:S(2)}, u32[]{:S(2)}) %collective-permute-start.1) | collective-permute-done | bytes 69664 | tf_op jit(solution)/shard_map/ppermute | solution.py:34
  28.9 1.9 %collective-permute-start.2 = (bf16[2,272,128]{2,1,0:T(8,128)(2,1)S(1)}, bf16[2,272,128]{2,1,0:T(8,128)(2,1)S(1)}, u32[]{:S(2)}, u32[]{:S(2)}) collective-permute-start(bf16[2,272,128]{2,1,0:T(8,128)(2,1)S(1)} %pad_maximum_fusion.3), channel_id=1, source_target_pairs={{0,32},{16,48},{32,0},{48,16},{64,96},{80,112},{96,64},{112,80},{1... | collective-permute-start | bytes 417800 | tf_op jit(solution)/shard_map/ppermute | solution.py:34
  31.0 7.4 %collective-permute-done.2 = bf16[2,272,128]{2,1,0:T(8,128)(2,1)S(1)} collective-permute-done((bf16[2,272,128]{2,1,0:T(8,128)(2,1)S(1)}, bf16[2,272,128]{2,1,0:T(8,128)(2,1)S(1)}, u32[]{:S(2)}, u32[]{:S(2)}) %collective-permute-start.2) | collective-permute-done | bytes 139296 | tf_op jit(solution)/shard_map/ppermute | solution.py:34
  38.5 2.8 %collective-permute-start.3 = (bf16[4,272,128]{2,1,0:T(8,128)(2,1)S(1)}, bf16[4,272,128]{2,1,0:T(8,128)(2,1)S(1)}, u32[]{:S(2)}, u32[]{:S(2)}) collective-permute-start(bf16[4,272,128]{2,1,0:T(8,128)(2,1)S(1)} %pad_maximum_fusion.2), channel_id=1, source_target_pairs={{0,64},{16,80},{32,96},{48,112},{64,0},{80,16},{96,32},{112,48},{1... | collective-permute-start | bytes 835592 | tf_op jit(solution)/shard_map/ppermute | solution.py:34
  41.4 0.7 add.197.id_row_ref
  42.0 2.0 %add.230.id_col_ref = s32[2048,1]{1,0:T(8,128)} reshape(s32[32,64]{1,0:T(8,128)S(1)} %iota_add_fusion) | data formatting | bytes 16384 | tf_op jit(solution)/shard_map/add | solution.py:179
  44.1 11.1 %collective-permute-done.3 = bf16[4,272,128]{2,1,0:T(8,128)(2,1)S(1)} collective-permute-done((bf16[4,272,128]{2,1,0:T(8,128)(2,1)S(1)}, bf16[4,272,128]{2,1,0:T(8,128)(2,1)S(1)}, u32[]{:S(2)}, u32[]{:S(2)}) %collective-permute-start.3) | collective-permute-done | bytes 278560 | tf_op jit(solution)/shard_map/ppermute | solution.py:34
  55.2 0.7 copy-done.4
  56.0 2.4 %collective-permute-start.4 = (bf16[8,272,128]{2,1,0:T(8,128)(2,1)S(1)}, bf16[8,272,128]{2,1,0:T(8,128)(2,1)S(1)}, u32[]{:S(2)}, u32[]{:S(2)}) collective-permute-start(bf16[8,272,128]{2,1,0:T(8,128)(2,1)S(1)} %pad_maximum_fusion.1), channel_id=1, source_target_pairs={{0,128},{16,144},{32,160},{48,176},{64,192},{80,208},{96,224},{112... | collective-permute-start | bytes 1671176 | tf_op jit(solution)/shard_map/ppermute | solution.py:43
  58.4 3.5 %collective-permute-start.5 = (bf16[8,272,128]{2,1,0:T(8,128)(2,1)S(1)}, bf16[8,272,128]{2,1,0:T(8,128)(2,1)S(1)}, u32[]{:S(2)}, u32[]{:S(2)}) collective-permute-start(bf16[8,272,128]{2,1,0:T(8,128)(2,1)S(1)} %pad_maximum_fusion.1), channel_id=1, source_target_pairs={{0,384},{16,400},{32,416},{48,432},{64,448},{80,464},{96,480},{112... | collective-permute-start | bytes 1671176 | tf_op jit(solution)/shard_map/ppermute | solution.py:43
  62.0 8.4 %collective-permute-done.4 = bf16[8,272,128]{2,1,0:T(8,128)(2,1)S(1)} collective-permute-done((bf16[8,272,128]{2,1,0:T(8,128)(2,1)S(1)}, bf16[8,272,128]{2,1,0:T(8,128)(2,1)S(1)}, u32[]{:S(2)}, u32[]{:S(2)}) %collective-permute-start.4) | collective-permute-done | bytes 557088 | tf_op jit(solution)/shard_map/ppermute | solution.py:43
  70.4 3.6 %collective-permute-start.6 = (bf16[4,272,128]{2,1,0:T(8,128)(2,1)S(1)}, bf16[4,272,128]{2,1,0:T(8,128)(2,1)S(1)}, u32[]{:S(2)}, u32[]{:S(2)}) collective-permute-start(bf16[4,272,128]{2,1,0:T(8,128)(2,1)S(1)} %slice.100), channel_id=1, source_target_pairs={{0,128},{16,144},{32,160},{48,176},{64,192},{80,208},{96,224},{112... | collective-permute-start | bytes 835592 | tf_op jit(solution)/shard_map/ppermute | solution.py:43
  74.0 1.0 constant_dynamic-update-slice_fusion.9
  75.1 2.2 %collective-permute-start.7 = (bf16[4,272,128]{2,1,0:T(8,128)(2,1)S(1)}, bf16[4,272,128]{2,1,0:T(8,128)(2,1)S(1)}, u32[]{:S(2)}, u32[]{:S(2)}) collective-permute-start(bf16[4,272,128]{2,1,0:T(8,128)(2,1)S(1)} %slice.101), channel_id=1, source_target_pairs={{0,384},{16,400},{32,416},{48,432},{64,448},{80,464},{96,480},{112... | collective-permute-start | bytes 835592 | tf_op jit(solution)/shard_map/ppermute | solution.py:43
  77.5 1.4 collective-permute-done.6
  78.9 5.8 %collective-permute-done.7 = bf16[4,272,128]{2,1,0:T(8,128)(2,1)S(1)} collective-permute-done((bf16[4,272,128]{2,1,0:T(8,128)(2,1)S(1)}, bf16[4,272,128]{2,1,0:T(8,128)(2,1)S(1)}, u32[]{:S(2)}, u32[]{:S(2)}) %collective-permute-start.7) | collective-permute-done | bytes 278560 | tf_op jit(solution)/shard_map/ppermute | solution.py:43
  84.7 1.5 fusion.51
  86.2 0.7 fusion.41
  86.9 0.7 reshape.218.live_row_ref
  87.6 2.0 %reshape.291.live_col_ref = f32[2048,1]{1,0:T(8,128)} reshape(f32[32,64]{1,0:T(8,128)S(1)} %get-tuple-element.26) | data formatting | bytes 16384 | tf_op jit(solution)/shard_map/convert_element_type | solution.py:102
  89.6 13.0 %shard_map.113 = (bf16[2048,128]{1,0:T(8,128)(2,1)}, f32[2048,1]{1,0:T(8,128)}, f32[2048,1]{1,0:T(8,128)}) custom-call(bf16[2048,128]{1,0:T(8,128)(2,1)} %bitcast.39, bf16[2048,128]{1,0:T(8,128)(2,1)} %bitcast.44, bf16[2048,128]{1,0:T(8,128)(2,1)} %bitcast.42, bf16[2048,128]{1,0:T(8,128)(2,1)} %bitcast.36, f32[1,2048]{1,0:T(1,128)} %reshape.218.live_row_ref, ...), custom_call_target="tpu_custom_call" | custom-call | tf_op jit(solution)/shard_map/pallas_call | solution.py:106
  102.6 0.9 slice_reduce_fusion.1
  103.5 0.9 slice_reduce_fusion
  104.3 1.6 reduce.3
  105.9 1.6 reduce.4
  107.6 2.2 %fusion.5 = f32[64,2048]{1,0:T(8,128)} fusion(bf16[64,128]{1,0:T(8,128)(2,1)S(1)} %get-tuple-element.42, bf16[2048,128]{1,0:T(8,128)(2,1)} %bitcast.45, f32[64]{0:T(128)S(1)} %slice_reduce_fusion.1, s32[2048]{0:T(1024)S(1)} %add.199, s32[64]{0:T(128)S(1)} %iota_add_fusion.1, pred[2048]{0:T(1024)(128)(4,1)S(1)} %lt.100), kind=kOutput, calls=%fused_computation.16 | convolution fusion | flops 34209792 | bytes 1075712 | tf_op jit(solution)/shard_map/dot_general | solution.py:192
  109.9 1.8 %fusion.19 = bf16[64,128]{1,0:T(8,128)(2,1)S(1)} fusion(bf16[2048,128]{1,0:T(8,128)(2,1)} %bitcast.46, f32[64,2048]{1,0:T(8,128)} %fusion.5, bf16[2048,128]{1,0:T(8,128)(2,1)} %bitcast.43, f32[64]{0:T(128)S(1)} %slice_reduce_fusion, bf16[64,128]{1,0:T(8,128)(2,1)S(1)} %copy-done.10, pred[64]{0:T(512)(128)(4,1)S(1)} %copy-done.13), kind=kOutput, calls=%fused_computation.36 | convolution fusion | flops 67526656 | bytes 1605952 | tf_op jit(solution)/shard_map/dot_general | solution.py:198
  111.7 1.9 %fusion.53 = f32[64,1024]{1,0:T(8,128)} fusion(bf16[64,128]{1,0:T(8,128)(2,1)S(1)} %fusion.19, bf16[1024,128]{1,0:T(8,128)(2,1)} %param.16), kind=kOutput, calls=%fused_computation.140 | convolution fusion | flops 16777216 | bytes 540672 | tf_op jit(solution)/shard_map/dot_general | solution.py:217
  113.6 1.1 fusion.7
  114.7 1.5 fusion.18
  116.2 1.2 convolution_add_fusion.1
  117.4 1.5 fusion.15
  118.9 4.3 %collective-permute-start.8 = (bf16[64,1024]{1,0:T(8,128)(2,1)S(1)}, bf16[64,1024]{1,0:T(8,128)(2,1)S(1)}, u32[]{:S(2)}, u32[]{:S(2)}) collective-permute-start(bf16[64,1024]{1,0:T(8,128)(2,1)S(1)} %fusion.15), channel_id=1, source_target_pairs={{0,2},{2,0},{4,6},{6,4},{8,10},{10,8},{12,14},{14,12},{1,3},{3,1},... | collective-permute-start | bytes 393224 | tf_op jit(solution)/shard_map/ppermute | solution.py:71
  123.2 2.9 %collective-permute-done.8 = bf16[64,1024]{1,0:T(8,128)(2,1)S(1)} collective-permute-done((bf16[64,1024]{1,0:T(8,128)(2,1)S(1)}, bf16[64,1024]{1,0:T(8,128)(2,1)S(1)}, u32[]{:S(2)}, u32[]{:S(2)}) %collective-permute-start.8) | collective-permute-done | bytes 131104 | tf_op jit(solution)/shard_map/ppermute | solution.py:71
  126.2 6.9 %collective-permute-start.9 = (bf16[64,1024]{1,0:T(8,128)(2,1)S(1)}, bf16[64,1024]{1,0:T(8,128)(2,1)S(1)}, u32[]{:S(2)}, u32[]{:S(2)}) collective-permute-start(bf16[64,1024]{1,0:T(8,128)(2,1)S(1)} %add_convert_fusion.1), channel_id=1, source_target_pairs={{0,4},{2,6},{4,0},{6,2},{8,12},{10,14},{12,8},{14,10},{1,5},{3,7},... | collective-permute-start | bytes 393224 | tf_op jit(solution)/shard_map/ppermute | solution.py:71
  133.0 4.3 %collective-permute-done.9 = bf16[64,1024]{1,0:T(8,128)(2,1)S(1)} collective-permute-done((bf16[64,1024]{1,0:T(8,128)(2,1)S(1)}, bf16[64,1024]{1,0:T(8,128)(2,1)S(1)}, u32[]{:S(2)}, u32[]{:S(2)}) %collective-permute-start.9) | collective-permute-done | bytes 131104 | tf_op jit(solution)/shard_map/ppermute | solution.py:71
  137.4 12.3 %collective-permute-start.10 = (bf16[64,1024]{1,0:T(8,128)(2,1)S(1)}, bf16[64,1024]{1,0:T(8,128)(2,1)S(1)}, u32[]{:S(2)}, u32[]{:S(2)}) collective-permute-start(bf16[64,1024]{1,0:T(8,128)(2,1)S(1)} %add_convert_fusion), channel_id=1, source_target_pairs={{0,8},{2,10},{4,12},{6,14},{8,0},{10,2},{12,4},{14,6},{1,9},{3,11}... | collective-permute-start | bytes 393224 | tf_op jit(solution)/shard_map/ppermute | solution.py:71
  149.7 1.3 slice.83
  151.1 1.6 collective-permute-done.10
  152.8 0.8 fusion.30
  153.6 2.7 %scatter_custom_fusion = f32[512,1024]{1,0:T(8,128)} fusion(s32[64]{0:T(128)} %copy-done.14, f32[64,1024]{1,0:T(8,128)S(1)} %fusion.30, f32[]{:T(128)} %constant.85.clone.1), kind=kCustom, calls=%fused_computation.42 | custom fusion | flops 65536 | bytes 2097664 | tf_op jit(solution)/shard_map/scatter-add | solution.py:237
  156.2 0.8 slice.107
  157.0 2.0 %collective-permute-start.11 = (f32[3,1024]{1,0:T(4,128)S(1)}, f32[3,1024]{1,0:T(4,128)S(1)}, u32[]{:S(2)}, u32[]{:S(2)}) collective-permute-start(f32[3,1024]{1,0:T(4,128)S(1)} %slice.107), channel_id=1, source_target_pairs={{16,0},{32,16},{48,32},{64,48},{80,64},{96,80},{112,96},{128,112},... | collective-permute-start | bytes 36872 | tf_op jit(solution)/shard_map/ppermute | solution.py:21
  159.1 1.8 %constant_dynamic-update-slice_fusion.14 = f32[515,1024]{1,0:T(8,128)S(1)} fusion(f32[512,1024]{1,0:T(8,128)} %scatter_custom_fusion), kind=kLoop, calls=%fused_computation.89 | loop fusion | bytes 4194304
  160.9 3.1 %collective-permute-done.11 = f32[3,1024]{1,0:T(4,128)S(1)} collective-permute-done((f32[3,1024]{1,0:T(4,128)S(1)}, f32[3,1024]{1,0:T(4,128)S(1)}, u32[]{:S(2)}, u32[]{:S(2)}) %collective-permute-start.11) | collective-permute-done | bytes 12320 | tf_op jit(solution)/shard_map/ppermute | solution.py:21
  164.0 2.2 %fusion.10 = f32[512,1024]{1,0:T(8,128)} fusion(f32[515,1024]{1,0:T(8,128)S(1)} %constant_dynamic-update-slice_fusion.13, f32[512,1024]{1,0:T(8,128)S(1)} %copy-done.1, f32[1024]{0:T(1024)S(1)} %bitcast.56, f32[1024]{0:T(1024)S(1)} %bitcast.58, f32[1024]{0:T(1024)S(1)} %bitcast.54, f32[1024]{0:T(1024)S(1)} %bitcast.52), kind=kLoop, calls=%fused_computation.22 | loop fusion | flops 3670016 | bytes 10502144 | tf_op jit(solution)/shard_map/add | solution.py:243
  166.2 4.2 %scatter_custom_fusion.1 = f32[512,1024]{1,0:T(8,128)} fusion(f32[512,1024]{1,0:T(8,128)} %fusion.10, s32[64]{0:T(128)} %copy-done.14, f32[64,1024]{1,0:T(8,128)S(1)} %get-tuple-element.40, bf16[64,1024]{1,0:T(8,128)(2,1)S(1)} %collective-permute-done.10, bf16[64,1024]{1,0:T(8,128)(2,1)S(1)} %add_convert_fusion, f32[64]{0:T(128)S(1)} %broadcast_multiply_fusion.1, ...), kind=kCustom, calls=%fused_computation.137 | custom fusion | flops 655360 | bytes 2626368 | tf_op jit(solution)/shard_map/scatter-add | solution.py:238
  170.5 2.7 %convert_element_type.160 = bf16[512,1024]{1,0:T(8,128)(2,1)} convert(f32[512,1024]{1,0:T(8,128)} %scatter_custom_fusion.1) | non-fusion elementwise | flops 524288 | bytes 3145728 | tf_op jit(solution)/shard_map/convert_element_type | solution.py:244
  (70 shorter events, 1.6 us)
Async XLA Ops:
  0.6 19.3 %copy-start = (bf16[1024,1024]{1,0:T(8,128)(2,1)S(1)}, bf16[1024,1024]{1,0:T(8,128)(2,1)}, u32[]{:S(2)}) copy-start(bf16[1024,1024]{1,0:T(8,128)(2,1)} %param.14) | copy-start | bytes 6291460
  1.5 11.5 %collective-permute-start = (bf16[3,1024]{1,0:T(4,128)(2,1)S(1)}, bf16[3,1024]{1,0:T(4,128)(2,1)S(1)}, u32[]{:S(2)}, u32[]{:S(2)}) collective-permute-start(bf16[3,1024]{1,0:T(4,128)(2,1)S(1)} %slice.132), channel_id=1, source_target_pairs={{0,16},{16,32},{32,48},{48,64},{64,80},{80,96},{96,112},{112,128},... | collective-permute-start | bytes 18440 | tf_op jit(solution)/shard_map/ppermute | solution.py:21
  6.9 3.4 %copy-start.14 = (s32[64]{0:T(128)}, s32[64]{0:T(128)S(1)}, u32[]{:S(2)}) copy-start(s32[64]{0:T(128)S(1)} %get-tuple-element.37) | copy-start | bytes 772
  18.6 3.3 %copy-start.8 = (f32[1024]{0:T(1024)S(1)}, f32[1024]{0:T(1024)}, u32[]{:S(2)}) copy-start(f32[1024]{0:T(1024)} %param.15) | copy-start | bytes 12292
  19.9 2.1 %copy-start.6 = (bf16[1024,128]{1,0:T(8,128)(2,1)S(1)}, bf16[1024,128]{1,0:T(8,128)(2,1)}, u32[]{:S(2)}) copy-start(bf16[1024,128]{1,0:T(8,128)(2,1)} %param.16) | copy-start | bytes 786436
  19.9 2.3 %copy-start.5 = (bf16[1024,128]{1,0:T(8,128)(2,1)S(1)}, bf16[1024,128]{1,0:T(8,128)(2,1)}, u32[]{:S(2)}) copy-start(bf16[1024,128]{1,0:T(8,128)(2,1)} %param.17) | copy-start | bytes 786436
  19.9 2.5 %copy-start.7 = (bf16[1024,128]{1,0:T(8,128)(2,1)S(1)}, bf16[1024,128]{1,0:T(8,128)(2,1)}, u32[]{:S(2)}) copy-start(bf16[1024,128]{1,0:T(8,128)(2,1)} %param.18) | copy-start | bytes 786436
  19.9 2.7 %copy-start.9 = (bf16[64,128]{1,0:T(8,128)(2,1)S(1)}, bf16[64,128]{1,0:T(8,128)(2,1)}, u32[]{:S(2)}) copy-start(bf16[64,128]{1,0:T(8,128)(2,1)} %param.21) | copy-start | bytes 49156
  20.0 2.7 %copy-start.12 = (pred[64]{0:T(512)(128)(4,1)S(1)}, pred[64]{0:T(512)(128)(4,1)}, u32[]{:S(2)}) copy-start(pred[64]{0:T(512)(128)(4,1)} %iota_compare_fusion.1) | copy-start | bytes 196
  22.7 6.2 %collective-permute-start.1 = (bf16[1,272,128]{2,1,0:T(8,128)(2,1)S(1)}, bf16[1,272,128]{2,1,0:T(8,128)(2,1)S(1)}, u32[]{:S(2)}, u32[]{:S(2)}) collective-permute-start(bf16[1,272,128]{2,1,0:T(8,128)(2,1)S(1)} %bitcast.47), channel_id=1, source_target_pairs={{0,16},{16,0},{32,48},{48,32},{64,80},{80,64},{96,112},{112,96},{1... | collective-permute-start | bytes 208904 | tf_op jit(solution)/shard_map/ppermute | solution.py:34
  28.9 9.5 %collective-permute-start.2 = (bf16[2,272,128]{2,1,0:T(8,128)(2,1)S(1)}, bf16[2,272,128]{2,1,0:T(8,128)(2,1)S(1)}, u32[]{:S(2)}, u32[]{:S(2)}) collective-permute-start(bf16[2,272,128]{2,1,0:T(8,128)(2,1)S(1)} %pad_maximum_fusion.3), channel_id=1, source_target_pairs={{0,32},{16,48},{32,0},{48,16},{64,96},{80,112},{96,64},{112,80},{1... | collective-permute-start | bytes 417800 | tf_op jit(solution)/shard_map/ppermute | solution.py:34
  38.5 16.8 %collective-permute-start.3 = (bf16[4,272,128]{2,1,0:T(8,128)(2,1)S(1)}, bf16[4,272,128]{2,1,0:T(8,128)(2,1)S(1)}, u32[]{:S(2)}, u32[]{:S(2)}) collective-permute-start(bf16[4,272,128]{2,1,0:T(8,128)(2,1)S(1)} %pad_maximum_fusion.2), channel_id=1, source_target_pairs={{0,64},{16,80},{32,96},{48,112},{64,0},{80,16},{96,32},{112,48},{1... | collective-permute-start | bytes 835592 | tf_op jit(solution)/shard_map/ppermute | solution.py:34
  55.2 0.7 copy-start.4
  56.0 14.4 %collective-permute-start.4 = (bf16[8,272,128]{2,1,0:T(8,128)(2,1)S(1)}, bf16[8,272,128]{2,1,0:T(8,128)(2,1)S(1)}, u32[]{:S(2)}, u32[]{:S(2)}) collective-permute-start(bf16[8,272,128]{2,1,0:T(8,128)(2,1)S(1)} %pad_maximum_fusion.1), channel_id=1, source_target_pairs={{0,128},{16,144},{32,160},{48,176},{64,192},{80,208},{96,224},{112... | collective-permute-start | bytes 1671176 | tf_op jit(solution)/shard_map/ppermute | solution.py:43
  58.4 49.2 %copy-start.15 = (s32[64]{0:T(128)}, s32[64]{0:T(128)S(1)}, u32[]{:S(2)}) copy-start(s32[64]{0:T(128)S(1)} %iota_add_fusion.1) | copy-start | bytes 772
  58.4 16.6 %collective-permute-start.5 = (bf16[8,272,128]{2,1,0:T(8,128)(2,1)S(1)}, bf16[8,272,128]{2,1,0:T(8,128)(2,1)S(1)}, u32[]{:S(2)}, u32[]{:S(2)}) collective-permute-start(bf16[8,272,128]{2,1,0:T(8,128)(2,1)S(1)} %pad_maximum_fusion.1), channel_id=1, source_target_pairs={{0,384},{16,400},{32,416},{48,432},{64,448},{80,464},{96,480},{112... | collective-permute-start | bytes 1671176 | tf_op jit(solution)/shard_map/ppermute | solution.py:43
  70.4 8.4 %collective-permute-start.6 = (bf16[4,272,128]{2,1,0:T(8,128)(2,1)S(1)}, bf16[4,272,128]{2,1,0:T(8,128)(2,1)S(1)}, u32[]{:S(2)}, u32[]{:S(2)}) collective-permute-start(bf16[4,272,128]{2,1,0:T(8,128)(2,1)S(1)} %slice.100), channel_id=1, source_target_pairs={{0,128},{16,144},{32,160},{48,176},{64,192},{80,208},{96,224},{112... | collective-permute-start | bytes 835592 | tf_op jit(solution)/shard_map/ppermute | solution.py:43
  75.1 9.7 %collective-permute-start.7 = (bf16[4,272,128]{2,1,0:T(8,128)(2,1)S(1)}, bf16[4,272,128]{2,1,0:T(8,128)(2,1)S(1)}, u32[]{:S(2)}, u32[]{:S(2)}) collective-permute-start(bf16[4,272,128]{2,1,0:T(8,128)(2,1)S(1)} %slice.101), channel_id=1, source_target_pairs={{0,384},{16,400},{32,416},{48,432},{64,448},{80,464},{96,480},{112... | collective-permute-start | bytes 835592 | tf_op jit(solution)/shard_map/ppermute | solution.py:43
  102.6 7.3 %copy-start.10 = (bf16[64,128]{1,0:T(8,128)(2,1)S(1)}, bf16[64,128]{1,0:T(8,128)(2,1)}, u32[]{:S(2)}) copy-start(bf16[64,128]{1,0:T(8,128)(2,1)} %param.21) | copy-start | bytes 49156
  102.6 7.3 %copy-start.13 = (pred[64]{0:T(512)(128)(4,1)S(1)}, pred[64]{0:T(512)(128)(4,1)}, u32[]{:S(2)}) copy-start(pred[64]{0:T(512)(128)(4,1)} %iota_compare_fusion.1) | copy-start | bytes 196
  105.9 7.7 %copy-start.3 = (bf16[32,64,128]{2,1,0:T(8,128)(2,1)S(1)}, bf16[32,64,128]{2,1,0:T(8,128)(2,1)}, u32[]{:S(2)}) copy-start(bf16[32,64,128]{2,1,0:T(8,128)(2,1)} %get-tuple-element.18) | copy-start | bytes 1572868
  107.6 7.1 %copy-start.2 = (bf16[32,64,128]{2,1,0:T(8,128)(2,1)S(1)}, bf16[32,64,128]{2,1,0:T(8,128)(2,1)}, u32[]{:S(2)}) copy-start(bf16[32,64,128]{2,1,0:T(8,128)(2,1)} %get-tuple-element.15) | copy-start | bytes 1572868
  109.9 3.7 %copy-start.16 = (s32[64]{0:T(128)S(1)}, s32[64]{0:T(128)}, u32[]{:S(2)}) copy-start(s32[64]{0:T(128)} %copy-done.15) | copy-start | bytes 772
  118.9 7.2 %collective-permute-start.8 = (bf16[64,1024]{1,0:T(8,128)(2,1)S(1)}, bf16[64,1024]{1,0:T(8,128)(2,1)S(1)}, u32[]{:S(2)}, u32[]{:S(2)}) collective-permute-start(bf16[64,1024]{1,0:T(8,128)(2,1)S(1)} %fusion.15), channel_id=1, source_target_pairs={{0,2},{2,0},{4,6},{6,4},{8,10},{10,8},{12,14},{14,12},{1,3},{3,1},... | collective-permute-start | bytes 393224 | tf_op jit(solution)/shard_map/ppermute | solution.py:71
  126.2 11.2 %collective-permute-start.9 = (bf16[64,1024]{1,0:T(8,128)(2,1)S(1)}, bf16[64,1024]{1,0:T(8,128)(2,1)S(1)}, u32[]{:S(2)}, u32[]{:S(2)}) collective-permute-start(bf16[64,1024]{1,0:T(8,128)(2,1)S(1)} %add_convert_fusion.1), channel_id=1, source_target_pairs={{0,4},{2,6},{4,0},{6,2},{8,12},{10,14},{12,8},{14,10},{1,5},{3,7},... | collective-permute-start | bytes 393224 | tf_op jit(solution)/shard_map/ppermute | solution.py:71
  137.4 15.2 %collective-permute-start.10 = (bf16[64,1024]{1,0:T(8,128)(2,1)S(1)}, bf16[64,1024]{1,0:T(8,128)(2,1)S(1)}, u32[]{:S(2)}, u32[]{:S(2)}) collective-permute-start(bf16[64,1024]{1,0:T(8,128)(2,1)S(1)} %add_convert_fusion), channel_id=1, source_target_pairs={{0,8},{2,10},{4,12},{6,14},{8,0},{10,2},{12,4},{14,6},{1,9},{3,11}... | collective-permute-start | bytes 393224 | tf_op jit(solution)/shard_map/ppermute | solution.py:71
  157.0 7.0 %copy-start.1 = (f32[512,1024]{1,0:T(8,128)S(1)}, f32[512,1024]{1,0:T(8,128)}, u32[]{:S(2)}) copy-start(f32[512,1024]{1,0:T(8,128)} %scatter_custom_fusion) | copy-start | bytes 6291460
  157.0 7.0 %copy-start.11 = (f32[1,1024]{1,0:T(1,128)S(1)}, f32[1,1024]{1,0:T(1,128)}, u32[]{:S(2)}) copy-start(f32[1,1024]{1,0:T(1,128)} %get-tuple-element.22) | copy-start | bytes 12292
  157.0 7.0 %collective-permute-start.11 = (f32[3,1024]{1,0:T(4,128)S(1)}, f32[3,1024]{1,0:T(4,128)S(1)}, u32[]{:S(2)}, u32[]{:S(2)}) collective-permute-start(f32[3,1024]{1,0:T(4,128)S(1)} %slice.107), channel_id=1, source_target_pairs={{16,0},{32,16},{48,32},{64,48},{80,64},{96,80},{112,96},{128,112},... | collective-permute-start | bytes 36872 | tf_op jit(solution)/shard_map/ppermute | solution.py:21

commit v7 on v6

--- a/solution.py
+++ b/solution.py
@@ -4,12 +4,14 @@
 import jax.numpy as jnp
 from jax import lax
 from jax.experimental import pallas as pl
+from jax.experimental.pallas import tpu as pltpu
 from jax.sharding import PartitionSpec as P
 
 D = 1024
 HD = 128
 KCONV = 4
 QBLOCK = 256
+BLOCKS_PER_STEP = 4
 
 
 masked_score = -1e30
@@ -74,22 +76,26 @@
     return total
 
 
-def forward_kernel(
-    q_ref, k_ref, v_ref, g_ref, live_row_ref, live_col_ref, id_row_ref, id_col_ref, att_ref, log_ref, delta_ref
-):
+def forward_kernel(shards_ref, q_ref, k_ref, v_ref, g_ref, key_code_ref, att_ref, log_ref, delta_ref):
+    rows = q_ref.shape[0]
+    block_rows = rows // BLOCKS_PER_STEP
+    first = pl.program_id(0) * BLOCKS_PER_STEP
+    row = lax.broadcasted_iota(jnp.int32, (rows, 1), 0)
+    q_ids = row % block_rows
+    for t in range(BLOCKS_PER_STEP):
+        q_ids = q_ids + jnp.where(row // block_rows == t, shards_ref[first + t] * block_rows, 0)
     scale = 1.0 / math.sqrt(HD)
     scores = lax.dot_general(
         q_ref[...], k_ref[...], (((1,), (1,)), ((), ())), preferred_element_type=jnp.float32
     ) * scale
-    allowed = (id_row_ref[...] <= id_col_ref[...]) & (live_row_ref[...] > 0.5)
-    scores = jnp.where(allowed, scores, masked_score)
+    scores = jnp.where(key_code_ref[...] <= q_ids, scores, masked_score)
     row_max = jnp.max(scores, axis=1, keepdims=True)
     softmax_part = jnp.exp(scores - row_max)
     row_sum = jnp.sum(softmax_part, axis=1, keepdims=True)
     product = jnp.dot(
         softmax_part.astype(jnp.bfloat16), v_ref[...], preferred_element_type=jnp.float32
     )
-    attention = jnp.where(live_col_ref[...] > 0.5, product / row_sum, 0.0).astype(jnp.bfloat16)
+    attention = (product / row_sum).astype(jnp.bfloat16)
     att_ref[...] = attention
     log_ref[...] = row_max + jnp.log(row_sum)
     delta_ref[...] = jnp.sum(
@@ -97,28 +103,27 @@
     )
 
 
-def forward_all(queries, keys, values, grads, live, ids):
+def forward_all(queries, keys, values, grads, key_code, held_shards):
     slots, width = queries.shape
-    live_f = live.astype(jnp.float32)
-    row_spec = pl.BlockSpec((QBLOCK, width), lambda i: (i, 0))
-    full_spec = pl.BlockSpec((slots, width), lambda i: (0, 0))
-    col_spec = pl.BlockSpec((QBLOCK, 1), lambda i: (i, 0))
+    row_spec = pl.BlockSpec((QBLOCK, width), lambda i, shards: (i, 0))
+    full_spec = pl.BlockSpec((slots, width), lambda i, shards: (0, 0))
+    col_spec = pl.BlockSpec((QBLOCK, 1), lambda i, shards: (i, 0))
+    grid_spec = pltpu.PrefetchScalarGridSpec(
+        num_scalar_prefetch=1,
+        grid=(slots // QBLOCK,),
+        in_specs=[row_spec, full_spec, full_spec, row_spec,
+                  pl.BlockSpec((1, slots), lambda i, shards: (0, 0))],
+        out_specs=[row_spec, col_spec, col_spec],
+    )
     return pl.pallas_call(
         forward_kernel,
-        grid=(slots // QBLOCK,),
-        in_specs=[row_spec, full_spec, full_spec, row_spec,
-                  pl.BlockSpec((1, slots), lambda i: (0, 0)), col_spec,
-                  pl.BlockSpec((1, slots), lambda i: (0, 0)), col_spec],
-        out_specs=[row_spec, col_spec, col_spec],
+        grid_spec=grid_spec,
         out_shape=[
             jax.ShapeDtypeStruct((slots, width), jnp.bfloat16),
             jax.ShapeDtypeStruct((slots, 1), jnp.float32),
             jax.ShapeDtypeStruct((slots, 1), jnp.float32),
         ],
-    )(
-        queries, keys, values, grads, live_f.reshape(1, slots), live_f.reshape(slots, 1),
-        ids.reshape(1, slots), ids.reshape(slots, 1),
-    )
+    )(held_shards, queries, keys, values, grads, key_code.reshape(1, slots))
 
 
 def per_device(
@@ -143,14 +148,14 @@
     own_ids = first_slot + jnp.arange(slot_count, dtype=jnp.int32)
     before_rim = neighbour(byte_states[row_count - (KCONV - 1) :].astype(jnp.float32), 1)
     extended = jnp.concatenate([before_rim.astype(jnp.bfloat16), byte_states], axis=0)
-    span_depth = conv_kernel[0] * jnp.take(extended, boundaries + (KCONV - 1), axis=0).astype(
-        jnp.float32
-    )
+    tap_rows = (boundaries[None, :] + jnp.arange(KCONV - 1, -1, -1, dtype=jnp.int32)[:, None])
+    tapped = jnp.take(extended, tap_rows.reshape(-1), axis=0).astype(jnp.float32)
+    tapped = tapped.reshape(KCONV, slot_count, D)
+    span_depth = conv_kernel[0] * tapped[0]
     for offset in range(1, KCONV):
-        tapped = jnp.take(extended, boundaries + (KCONV - 1 - offset), axis=0).astype(jnp.float32)
-        span_depth = span_depth + conv_kernel[offset] * tapped
+        span_depth = span_depth + conv_kernel[offset] * tapped[offset]
     span_depth = span_depth.astype(jnp.bfloat16)
-    span_bytes = jnp.take(byte_states, boundaries, axis=0).astype(jnp.float32)
+    span_bytes = tapped[0]
     live_mask = jnp.arange(slot_count, dtype=jnp.int32) < span_counts[0]
     span_state = span_bytes + jnp.dot(span_depth, mix_weight, preferred_element_type=jnp.float32)
     inverse_rms = lax.rsqrt(jnp.mean(span_state * span_state, axis=1) + 1e-05)
@@ -180,11 +185,12 @@
     ).reshape(total_slots)
 
     all_attended, all_logs, all_deltas = forward_all(
-        all_queries, all_keys, all_values, all_grads, all_live, slot_ids
+        all_queries, all_keys, all_values, all_grads,
+        jnp.where(all_live, slot_ids, total_slots), held_shards,
     )
     all_logs = all_logs.reshape(total_slots)
     all_deltas = all_deltas.reshape(total_slots)
-    attended = all_attended[:slot_count]
+    attended = jnp.where(live_mask[:, None], all_attended[:slot_count], jnp.bfloat16(0.0))
     own_logs = all_logs[:slot_count]
     own_deltas = all_deltas[:slot_count]
 

time: 174 us -> 164 us (0.943)
  local copies, waits for them, and re-layouts: 24.7 us -> 11 us
  waiting for transfers between devices: 50.4 us -> 52.3 us
    gather x5 -> x1, local copies, waits for them, and re-layouts: 7.58 us -> 1.96 us  [per_device(): jnp.take(extended, tap_rows.reshape(-1), axis=0).astype(jnp.float32)]
    add x3 -> x1, local copies, waits for them, and re-layouts: 2.74 us -> 0.07 us  [per_device(): held_shards[:, None] * slot_count]
    convert_element_type x2 -> x0, local copies, waits for them, and re-layouts: 2.67 us -> none  [forward_all(): live_f = live.astype(jnp.float32)]
    ppermute x3, waiting for transfers between devices: 22.8 us -> 25.4 us  [gather_blocks(): other = lax.ppermute(held, axis, [(i, i ^ step) for i in range(devices)])]
    slice x2 -> x1, local copies, waits for them, and re-layouts: 2.8 us -> 0.89 us  [per_device(): span_depth = conv_kernel[0] * tapped[0]]
    unnamed x42 -> x30, local copies, waits for them, and re-layouts: 3.83 us -> 2.16 us
  transfers between devices with their start and end apart: 12 -> 12, of which waited for: 10 -> 11; matrix products, arithmetic and copies ran while one was open for 8% -> 4% of each run, Pallas kernels for 0% -> 0%
where the time goes in v7:
time: 164 us; the launch traced here: 162 us
  waiting for transfers between devices  52.3 us (32%)
  starting transfers between devices  49.1 us (30%)
  other arithmetic  21.7 us (13%)
  matrix products  13.8 us (8%)
  Pallas kernels  12.6 us (8%)
  local copies, waits for them, and re-layouts  11 us (7%)
  between operations  1.73 us (1%)
    ppermute x3, waiting for transfers between devices, gather_blocks(): other = lax.ppermute(held, axis, [(i, i ^ step) for i in range(devices)])  25.4 us
    ppermute x3, starting transfers between devices, summed_over(): got = lax.ppermute(sent, axis, [(i, i ^ step) for i in range(devices)])  23.7 us
    ppermute x4, waiting for transfers between devices, shifted(): lax.ppermute(array, axis, [(i, (i + by) % devices) for i in range(devices)])  15.1 us
    pallas_call x1, Pallas kernels, forward_all(): pl.pallas_call(forward_kernel, grid_spec=grid_spec, out_shape=[jax.ShapeD...  12.6 us
    ppermute x4, starting transfers between devices, shifted(): lax.ppermute(array, axis, [(i, (i + by) % devices) for i in range(devices)])  11.7 us
    ppermute x3, waiting for transfers between devices, summed_over(): got = lax.ppermute(sent, axis, [(i, i ^ step) for i in range(devices)])  8.77 us
    ppermute x3, starting transfers between devices, gather_blocks(): other = lax.ppermute(held, axis, [(i, i ^ step) for i in range(devices)])  7.06 us
    ppermute x2, starting transfers between devices, passed_along(): return lax.ppermute(array, axis, pairs)  6.72 us
  transfers between devices with their start and end apart: 12, of which 11 were waited for; matrix products, arithmetic and copies ran while one was open for 4% of the time, Pallas kernels for 0%

profile of v7, /device:TPU:30, one launch (start us, length us, event | category | flops | bytes accessed | tf_op | source)
XLA Modules:
  0.0 162.4 jit_solution(10809667528384205161)
XLA Ops:
  0.6 0.9 slice.172
  1.5 4.7 %collective-permute-start = (bf16[3,1024]{1,0:T(4,128)(2,1)S(1)}, bf16[3,1024]{1,0:T(4,128)(2,1)S(1)}, u32[]{:S(2)}, u32[]{:S(2)}) collective-permute-start(bf16[3,1024]{1,0:T(4,128)(2,1)S(1)} %slice.172), channel_id=1, source_target_pairs={{0,16},{16,32},{32,48},{48,64},{64,80},{80,96},{96,112},{112,128},... | collective-permute-start | bytes 18440 | tf_op jit(solution)/shard_map/ppermute | solution.py:23
  6.2 0.7 broadcast_add_fusion
  7.0 0.1 add.209
  7.0 0.1 add.206
  7.1 0.9 fusion.47
  8.7 1.5 pad_maximum_fusion
  10.2 2.0 %gather_fusion = bf16[256,1024]{1,0:T(8,128)(2,1)} fusion(bf16[515,1024]{1,0:T(8,128)(2,1)S(1)} %pad_maximum_fusion, s32[1024]{0:T(1024)S(1)} %pad_clamp_fusion), kind=kCustom, calls=%fused_computation | custom fusion | bytes 1049600 | tf_op jit(solution)/shard_map/jit(_take)/gather | solution.py:152
  12.2 1.2 select_convert_fusion
  13.5 0.6 multiply_reduce_fusion.1
  14.1 0.1 multiply_convert_fusion
  14.2 0.2 constant_dynamic-update-slice_fusion.4
  14.4 0.2 constant_dynamic-update-slice_fusion.3
  14.6 0.2 constant_dynamic-update-slice_fusion.2
  14.8 0.1 constant_dynamic-update-slice_fusion.1
  14.9 1.9 %collective-permute-start.1 = (bf16[1,272,128]{2,1,0:T(8,128)(2,1)S(1)}, bf16[1,272,128]{2,1,0:T(8,128)(2,1)S(1)}, u32[]{:S(2)}, u32[]{:S(2)}) collective-permute-start(bf16[1,272,128]{2,1,0:T(8,128)(2,1)S(1)} %bitcast.48), channel_id=1, source_target_pairs={{0,16},{16,0},{32,48},{48,32},{64,80},{80,64},{96,112},{112,96},{1... | collective-permute-start | bytes 208904 | tf_op jit(solution)/shard_map/ppermute | solution.py:36
  16.8 4.3 %collective-permute-done.1 = bf16[1,272,128]{2,1,0:T(8,128)(2,1)S(1)} collective-permute-done((bf16[1,272,128]{2,1,0:T(8,128)(2,1)S(1)}, bf16[1,272,128]{2,1,0:T(8,128)(2,1)S(1)}, u32[]{:S(2)}, u32[]{:S(2)}) %collective-permute-start.1) | collective-permute-done | bytes 69664 | tf_op jit(solution)/shard_map/ppermute | solution.py:36
  21.1 1.9 %collective-permute-start.2 = (bf16[2,272,128]{2,1,0:T(8,128)(2,1)S(1)}, bf16[2,272,128]{2,1,0:T(8,128)(2,1)S(1)}, u32[]{:S(2)}, u32[]{:S(2)}) collective-permute-start(bf16[2,272,128]{2,1,0:T(8,128)(2,1)S(1)} %pad_maximum_fusion.3), channel_id=1, source_target_pairs={{0,32},{16,48},{32,0},{48,16},{64,96},{80,112},{96,64},{112,80},{1... | collective-permute-start | bytes 417800 | tf_op jit(solution)/shard_map/ppermute | solution.py:36
  23.0 0.1 and_select_fusion
  23.1 7.5 %collective-permute-done.2 = bf16[2,272,128]{2,1,0:T(8,128)(2,1)S(1)} collective-permute-done((bf16[2,272,128]{2,1,0:T(8,128)(2,1)S(1)}, bf16[2,272,128]{2,1,0:T(8,128)(2,1)S(1)}, u32[]{:S(2)}, u32[]{:S(2)}) %collective-permute-start.2) | collective-permute-done | bytes 139296 | tf_op jit(solution)/shard_map/ppermute | solution.py:36
  30.6 3.2 %collective-permute-start.3 = (bf16[4,272,128]{2,1,0:T(8,128)(2,1)S(1)}, bf16[4,272,128]{2,1,0:T(8,128)(2,1)S(1)}, u32[]{:S(2)}, u32[]{:S(2)}) collective-permute-start(bf16[4,272,128]{2,1,0:T(8,128)(2,1)S(1)} %pad_maximum_fusion.2), channel_id=1, source_target_pairs={{0,64},{16,80},{32,96},{48,112},{64,0},{80,16},{96,32},{112,48},{1... | collective-permute-start | bytes 835592 | tf_op jit(solution)/shard_map/ppermute | solution.py:36
  34.0 13.6 %collective-permute-done.3 = bf16[4,272,128]{2,1,0:T(8,128)(2,1)S(1)} collective-permute-done((bf16[4,272,128]{2,1,0:T(8,128)(2,1)S(1)}, bf16[4,272,128]{2,1,0:T(8,128)(2,1)S(1)}, u32[]{:S(2)}, u32[]{:S(2)}) %collective-permute-start.3) | collective-permute-done | bytes 278560 | tf_op jit(solution)/shard_map/ppermute | solution.py:36
  47.7 2.4 %collective-permute-start.4 = (bf16[8,272,128]{2,1,0:T(8,128)(2,1)S(1)}, bf16[8,272,128]{2,1,0:T(8,128)(2,1)S(1)}, u32[]{:S(2)}, u32[]{:S(2)}) collective-permute-start(bf16[8,272,128]{2,1,0:T(8,128)(2,1)S(1)} %pad_maximum_fusion.1), channel_id=1, source_target_pairs={{0,128},{16,144},{32,160},{48,176},{64,192},{80,208},{96,224},{112... | collective-permute-start | bytes 1671176 | tf_op jit(solution)/shard_map/ppermute | solution.py:45
  50.0 0.6 iota_add_fusion.1
  50.6 3.4 %collective-permute-start.5 = (bf16[8,272,128]{2,1,0:T(8,128)(2,1)S(1)}, bf16[8,272,128]{2,1,0:T(8,128)(2,1)S(1)}, u32[]{:S(2)}, u32[]{:S(2)}) collective-permute-start(bf16[8,272,128]{2,1,0:T(8,128)(2,1)S(1)} %pad_maximum_fusion.1), channel_id=1, source_target_pairs={{0,384},{16,400},{32,416},{48,432},{64,448},{80,464},{96,480},{112... | collective-permute-start | bytes 1671176 | tf_op jit(solution)/shard_map/ppermute | solution.py:45
  54.1 7.7 %collective-permute-done.4 = bf16[8,272,128]{2,1,0:T(8,128)(2,1)S(1)} collective-permute-done((bf16[8,272,128]{2,1,0:T(8,128)(2,1)S(1)}, bf16[8,272,128]{2,1,0:T(8,128)(2,1)S(1)}, u32[]{:S(2)}, u32[]{:S(2)}) %collective-permute-start.4) | collective-permute-done | bytes 557088 | tf_op jit(solution)/shard_map/ppermute | solution.py:45
  61.8 3.6 %collective-permute-start.6 = (bf16[4,272,128]{2,1,0:T(8,128)(2,1)S(1)}, bf16[4,272,128]{2,1,0:T(8,128)(2,1)S(1)}, u32[]{:S(2)}, u32[]{:S(2)}) collective-permute-start(bf16[4,272,128]{2,1,0:T(8,128)(2,1)S(1)} %slice.117), channel_id=1, source_target_pairs={{0,128},{16,144},{32,160},{48,176},{64,192},{80,208},{96,224},{112... | collective-permute-start | bytes 835592 | tf_op jit(solution)/shard_map/ppermute | solution.py:45
  65.5 0.2 collective-permute-done.5
  65.7 2.2 %collective-permute-start.7 = (bf16[4,272,128]{2,1,0:T(8,128)(2,1)S(1)}, bf16[4,272,128]{2,1,0:T(8,128)(2,1)S(1)}, u32[]{:S(2)}, u32[]{:S(2)}) collective-permute-start(bf16[4,272,128]{2,1,0:T(8,128)(2,1)S(1)} %slice.118), channel_id=1, source_target_pairs={{0,384},{16,400},{32,416},{48,432},{64,448},{80,464},{96,480},{112... | collective-permute-start | bytes 835592 | tf_op jit(solution)/shard_map/ppermute | solution.py:45
  68.2 2.1 %collective-permute-done.6 = bf16[4,272,128]{2,1,0:T(8,128)(2,1)S(1)} collective-permute-done((bf16[4,272,128]{2,1,0:T(8,128)(2,1)S(1)}, bf16[4,272,128]{2,1,0:T(8,128)(2,1)S(1)}, u32[]{:S(2)}, u32[]{:S(2)}) %collective-permute-start.6) | collective-permute-done | bytes 278560 | tf_op jit(solution)/shard_map/ppermute | solution.py:45
  70.3 5.1 %collective-permute-done.7 = bf16[4,272,128]{2,1,0:T(8,128)(2,1)S(1)} collective-permute-done((bf16[4,272,128]{2,1,0:T(8,128)(2,1)S(1)}, bf16[4,272,128]{2,1,0:T(8,128)(2,1)S(1)}, u32[]{:S(2)}, u32[]{:S(2)}) %collective-permute-start.7) | collective-permute-done | bytes 278560 | tf_op jit(solution)/shard_map/ppermute | solution.py:45
  75.4 1.5 fusion.46
  76.9 0.7 fusion.38
  77.7 0.7 select_n.92.key_code_ref
  78.4 12.6 %shard_map.113 = (bf16[2048,128]{1,0:T(8,128)(2,1)}, f32[2048,1]{1,0:T(8,128)}, f32[2048,1]{1,0:T(8,128)}) custom-call(s32[32]{0:T(128)} %copy-done.9, bf16[2048,128]{1,0:T(8,128)(2,1)} %bitcast.40, bf16[2048,128]{1,0:T(8,128)(2,1)} %bitcast.45, bf16[2048,128]{1,0:T(8,128)(2,1)} %bitcast.43, bf16[2048,128]{1,0:T(8,128)(2,1)} %bitcast.37, ...), custom_call_target="tpu_custom_call" | custom-call | tf_op jit(solution)/shard_map/pallas_call | solution.py:118
  91.0 0.9 slice_reduce_fusion.1
  91.9 0.9 slice_reduce_fusion
  92.8 1.6 reduce.3
  94.3 1.6 reduce.4
  96.0 0.1 lt.104
  96.1 2.2 %fusion.5 = f32[64,2048]{1,0:T(8,128)} fusion(bf16[64,128]{1,0:T(8,128)(2,1)S(1)} %get-tuple-element.25, bf16[2048,128]{1,0:T(8,128)(2,1)} %bitcast.46, f32[64]{0:T(128)S(1)} %slice_reduce_fusion.1, s32[2048]{0:T(1024)S(1)} %add.221, s32[64]{0:T(128)} %iota_add_fusion.1, pred[2048]{0:T(1024)(128)(4,1)S(1)} %lt.104), kind=kOutput, calls=%fused_computation.12 | convolution fusion | flops 34209792 | bytes 1075712 | tf_op jit(solution)/shard_map/dot_general | solution.py:198
  98.4 1.8 %fusion.19 = bf16[64,128]{1,0:T(8,128)(2,1)S(1)} fusion(bf16[2048,128]{1,0:T(8,128)(2,1)} %bitcast.47, f32[64,2048]{1,0:T(8,128)} %fusion.5, bf16[2048,128]{1,0:T(8,128)(2,1)} %bitcast.44, f32[64]{0:T(128)S(1)} %slice_reduce_fusion, bf16[64,128]{1,0:T(8,128)(2,1)S(1)} %copy-done.8, pred[64]{0:T(512)(128)(4,1)S(1)} %iota_compare_fusion.1), kind=kOutput, calls=%fused_computation.32 | convolution fusion | flops 67526656 | bytes 1605952 | tf_op jit(solution)/shard_map/dot_general | solution.py:204
  100.2 1.9 %fusion.48 = f32[64,1024]{1,0:T(8,128)} fusion(bf16[64,128]{1,0:T(8,128)(2,1)S(1)} %fusion.19, bf16[1024,128]{1,0:T(8,128)(2,1)} %param.14), kind=kOutput, calls=%fused_computation.127 | convolution fusion | flops 16777216 | bytes 540672 | tf_op jit(solution)/shard_map/dot_general | solution.py:223
  102.1 1.8 %fusion.7 = f32[2048,64]{0,1:T(8,128)} fusion(bf16[2048,128]{1,0:T(8,128)(2,1)S(1)} %bitcast.41, bf16[64,128]{1,0:T(8,128)(2,1)S(1)} %get-tuple-element.27, f32[2048]{0:T(1024)S(1)} %reduce.3, s32[2048]{0:T(1024)S(1)} %add.221, s32[64]{0:T(128)} %iota_add_fusion.1, pred[64]{0:T(512)(128)(4,1)S(1)} %iota_compare_fusion.1), kind=kOutput, calls=%fused_computation.14 | convolution fusion | flops 34209792 | bytes 1081664 | tf_op jit(solution)/shard_map/dot_general | solution.py:208
  103.9 1.5 fusion.18
  105.3 1.2 convolution_add_fusion.1
  106.6 1.5 fusion.15
  108.1 4.3 %collective-permute-start.8 = (bf16[64,1024]{1,0:T(8,128)(2,1)S(1)}, bf16[64,1024]{1,0:T(8,128)(2,1)S(1)}, u32[]{:S(2)}, u32[]{:S(2)}) collective-permute-start(bf16[64,1024]{1,0:T(8,128)(2,1)S(1)} %fusion.15), channel_id=1, source_target_pairs={{0,2},{2,0},{4,6},{6,4},{8,10},{10,8},{12,14},{14,12},{1,3},{3,1},... | collective-permute-start | bytes 393224 | tf_op jit(solution)/shard_map/ppermute | solution.py:73
  112.4 2.9 %collective-permute-done.8 = bf16[64,1024]{1,0:T(8,128)(2,1)S(1)} collective-permute-done((bf16[64,1024]{1,0:T(8,128)(2,1)S(1)}, bf16[64,1024]{1,0:T(8,128)(2,1)S(1)}, u32[]{:S(2)}, u32[]{:S(2)}) %collective-permute-start.8) | collective-permute-done | bytes 131104 | tf_op jit(solution)/shard_map/ppermute | solution.py:73
  115.4 7.1 %collective-permute-start.9 = (bf16[64,1024]{1,0:T(8,128)(2,1)S(1)}, bf16[64,1024]{1,0:T(8,128)(2,1)S(1)}, u32[]{:S(2)}, u32[]{:S(2)}) collective-permute-start(bf16[64,1024]{1,0:T(8,128)(2,1)S(1)} %add_convert_fusion.1), channel_id=1, source_target_pairs={{0,4},{2,6},{4,0},{6,2},{8,12},{10,14},{12,8},{14,10},{1,5},{3,7},... | collective-permute-start | bytes 393224 | tf_op jit(solution)/shard_map/ppermute | solution.py:73
  122.5 4.3 %collective-permute-done.9 = bf16[64,1024]{1,0:T(8,128)(2,1)S(1)} collective-permute-done((bf16[64,1024]{1,0:T(8,128)(2,1)S(1)}, bf16[64,1024]{1,0:T(8,128)(2,1)S(1)}, u32[]{:S(2)}, u32[]{:S(2)}) %collective-permute-start.9) | collective-permute-done | bytes 131104 | tf_op jit(solution)/shard_map/ppermute | solution.py:73
  126.9 12.3 %collective-permute-start.10 = (bf16[64,1024]{1,0:T(8,128)(2,1)S(1)}, bf16[64,1024]{1,0:T(8,128)(2,1)S(1)}, u32[]{:S(2)}, u32[]{:S(2)}) collective-permute-start(bf16[64,1024]{1,0:T(8,128)(2,1)S(1)} %add_convert_fusion), channel_id=1, source_target_pairs={{0,8},{2,10},{4,12},{6,14},{8,0},{10,2},{12,4},{14,6},{1,9},{3,11}... | collective-permute-start | bytes 393224 | tf_op jit(solution)/shard_map/ppermute | solution.py:73
  139.1 1.4 slice_select_fusion
  140.5 1.5 collective-permute-done.10
  142.1 0.2 multiply_reduce_fusion
  142.2 0.8 fusion.32
  143.0 2.5 %scatter_custom_fusion = f32[512,1024]{1,0:T(8,128)} fusion(s32[64]{0:T(128)S(1)} %compare_select_fusion.2, f32[64,1024]{1,0:T(8,128)S(1)} %fusion.32, f32[]{:T(128)} %constant.83.clone.1), kind=kCustom, calls=%fused_computation.38 | custom fusion | flops 65536 | bytes 2097156 | tf_op jit(solution)/shard_map/scatter-add | solution.py:243
  145.5 0.8 slice.124
  146.3 2.0 %collective-permute-start.11 = (f32[3,1024]{1,0:T(4,128)S(1)}, f32[3,1024]{1,0:T(4,128)S(1)}, u32[]{:S(2)}, u32[]{:S(2)}) collective-permute-start(f32[3,1024]{1,0:T(4,128)S(1)} %slice.124), channel_id=1, source_target_pairs={{16,0},{32,16},{48,32},{64,48},{80,64},{96,80},{112,96},{128,112},... | collective-permute-start | bytes 36872 | tf_op jit(solution)/shard_map/ppermute | solution.py:23
  148.4 1.8 %constant_dynamic-update-slice_fusion.14 = f32[515,1024]{1,0:T(8,128)S(1)} fusion(f32[512,1024]{1,0:T(8,128)} %scatter_custom_fusion), kind=kLoop, calls=%fused_computation.84 | loop fusion | bytes 4194304
  150.2 3.1 %collective-permute-done.11 = f32[3,1024]{1,0:T(4,128)S(1)} collective-permute-done((f32[3,1024]{1,0:T(4,128)S(1)}, f32[3,1024]{1,0:T(4,128)S(1)}, u32[]{:S(2)}, u32[]{:S(2)}) %collective-permute-start.11) | collective-permute-done | bytes 12320 | tf_op jit(solution)/shard_map/ppermute | solution.py:23
  153.3 2.2 %fusion.10 = f32[512,1024]{1,0:T(8,128)} fusion(f32[515,1024]{1,0:T(8,128)S(1)} %constant_dynamic-update-slice_fusion.13, f32[512,1024]{1,0:T(8,128)S(1)} %copy-done.1, f32[1024]{0:T(1024)S(1)} %bitcast.57, f32[1024]{0:T(1024)S(1)} %bitcast.59, f32[1024]{0:T(1024)S(1)} %bitcast.55, f32[1024]{0:T(1024)S(1)} %bitcast.53), kind=kLoop, calls=%fused_computation.18 | loop fusion | flops 3670016 | bytes 10502144 | tf_op jit(solution)/shard_map/add | solution.py:249
  155.5 4.1 %scatter_custom_fusion.1 = f32[512,1024]{1,0:T(8,128)} fusion(f32[512,1024]{1,0:T(8,128)} %fusion.10, s32[64]{0:T(128)S(1)} %compare_select_fusion.2, f32[64,1024]{1,0:T(8,128)S(1)} %get-tuple-element.23, bf16[64,1024]{1,0:T(8,128)(2,1)S(1)} %collective-permute-done.10, bf16[64,1024]{1,0:T(8,128)(2,1)S(1)} %add_convert_fusion, ...), kind=kCustom, calls=%fused_computation.124 | custom fusion | flops 655360 | bytes 2627584 | tf_op jit(solution)/shard_map/scatter-add | solution.py:244
  159.7 2.7 %convert_element_type.115 = bf16[512,1024]{1,0:T(8,128)(2,1)} convert(f32[512,1024]{1,0:T(8,128)} %scatter_custom_fusion.1) | non-fusion elementwise | flops 524288 | bytes 3145728 | tf_op jit(solution)/shard_map/convert_element_type | solution.py:250
  (55 shorter events, 1.0 us)
Async XLA Ops:
  0.6 12.8 %copy-start = (bf16[1024,1024]{1,0:T(8,128)(2,1)S(1)}, bf16[1024,1024]{1,0:T(8,128)(2,1)}, u32[]{:S(2)}) copy-start(bf16[1024,1024]{1,0:T(8,128)(2,1)} %param.12) | copy-start | bytes 6291460
  1.5 7.2 %collective-permute-start = (bf16[3,1024]{1,0:T(4,128)(2,1)S(1)}, bf16[3,1024]{1,0:T(4,128)(2,1)S(1)}, u32[]{:S(2)}, u32[]{:S(2)}) collective-permute-start(bf16[3,1024]{1,0:T(4,128)(2,1)S(1)} %slice.172), channel_id=1, source_target_pairs={{0,16},{16,32},{32,48},{48,64},{64,80},{80,96},{96,112},{112,128},... | collective-permute-start | bytes 18440 | tf_op jit(solution)/shard_map/ppermute | solution.py:23
  12.2 1.9 %copy-start.7 = (f32[1024]{0:T(1024)S(1)}, f32[1024]{0:T(1024)}, u32[]{:S(2)}) copy-start(f32[1024]{0:T(1024)} %param.13) | copy-start | bytes 12292
  12.2 2.0 %copy-start.5 = (bf16[1024,128]{1,0:T(8,128)(2,1)S(1)}, bf16[1024,128]{1,0:T(8,128)(2,1)}, u32[]{:S(2)}) copy-start(bf16[1024,128]{1,0:T(8,128)(2,1)} %param.14) | copy-start | bytes 786436
  13.4 1.0 copy-start.4
  13.4 1.1 copy-start.6
  13.5 1.3 copy-start.8
  14.9 6.2 %collective-permute-start.1 = (bf16[1,272,128]{2,1,0:T(8,128)(2,1)S(1)}, bf16[1,272,128]{2,1,0:T(8,128)(2,1)S(1)}, u32[]{:S(2)}, u32[]{:S(2)}) collective-permute-start(bf16[1,272,128]{2,1,0:T(8,128)(2,1)S(1)} %bitcast.48), channel_id=1, source_target_pairs={{0,16},{16,0},{32,48},{48,32},{64,80},{80,64},{96,112},{112,96},{1... | collective-permute-start | bytes 208904 | tf_op jit(solution)/shard_map/ppermute | solution.py:36
  21.1 9.5 %collective-permute-start.2 = (bf16[2,272,128]{2,1,0:T(8,128)(2,1)S(1)}, bf16[2,272,128]{2,1,0:T(8,128)(2,1)S(1)}, u32[]{:S(2)}, u32[]{:S(2)}) collective-permute-start(bf16[2,272,128]{2,1,0:T(8,128)(2,1)S(1)} %pad_maximum_fusion.3), channel_id=1, source_target_pairs={{0,32},{16,48},{32,0},{48,16},{64,96},{80,112},{96,64},{112,80},{1... | collective-permute-start | bytes 417800 | tf_op jit(solution)/shard_map/ppermute | solution.py:36
  30.6 17.0 %collective-permute-start.3 = (bf16[4,272,128]{2,1,0:T(8,128)(2,1)S(1)}, bf16[4,272,128]{2,1,0:T(8,128)(2,1)S(1)}, u32[]{:S(2)}, u32[]{:S(2)}) collective-permute-start(bf16[4,272,128]{2,1,0:T(8,128)(2,1)S(1)} %pad_maximum_fusion.2), channel_id=1, source_target_pairs={{0,64},{16,80},{32,96},{48,112},{64,0},{80,16},{96,32},{112,48},{1... | collective-permute-start | bytes 835592 | tf_op jit(solution)/shard_map/ppermute | solution.py:36
  33.9 34.1 %copy-start.9 = (s32[32]{0:T(128)}, s32[32]{0:T(128)S(1)}, u32[]{:S(2)}) copy-start(s32[32]{0:T(128)S(1)} %concatenate.31.shards_ref) | copy-start | bytes 388
  47.7 14.2 %collective-permute-start.4 = (bf16[8,272,128]{2,1,0:T(8,128)(2,1)S(1)}, bf16[8,272,128]{2,1,0:T(8,128)(2,1)S(1)}, u32[]{:S(2)}, u32[]{:S(2)}) collective-permute-start(bf16[8,272,128]{2,1,0:T(8,128)(2,1)S(1)} %pad_maximum_fusion.1), channel_id=1, source_target_pairs={{0,128},{16,144},{32,160},{48,176},{64,192},{80,208},{96,224},{112... | collective-permute-start | bytes 1671176 | tf_op jit(solution)/shard_map/ppermute | solution.py:45
  50.6 15.1 %collective-permute-start.5 = (bf16[8,272,128]{2,1,0:T(8,128)(2,1)S(1)}, bf16[8,272,128]{2,1,0:T(8,128)(2,1)S(1)}, u32[]{:S(2)}, u32[]{:S(2)}) collective-permute-start(bf16[8,272,128]{2,1,0:T(8,128)(2,1)S(1)} %pad_maximum_fusion.1), channel_id=1, source_target_pairs={{0,384},{16,400},{32,416},{48,432},{64,448},{80,464},{96,480},{112... | collective-permute-start | bytes 1671176 | tf_op jit(solution)/shard_map/ppermute | solution.py:45
  61.8 8.4 %collective-permute-start.6 = (bf16[4,272,128]{2,1,0:T(8,128)(2,1)S(1)}, bf16[4,272,128]{2,1,0:T(8,128)(2,1)S(1)}, u32[]{:S(2)}, u32[]{:S(2)}) collective-permute-start(bf16[4,272,128]{2,1,0:T(8,128)(2,1)S(1)} %slice.117), channel_id=1, source_target_pairs={{0,128},{16,144},{32,160},{48,176},{64,192},{80,208},{96,224},{112... | collective-permute-start | bytes 835592 | tf_op jit(solution)/shard_map/ppermute | solution.py:45
  65.7 9.7 %collective-permute-start.7 = (bf16[4,272,128]{2,1,0:T(8,128)(2,1)S(1)}, bf16[4,272,128]{2,1,0:T(8,128)(2,1)S(1)}, u32[]{:S(2)}, u32[]{:S(2)}) collective-permute-start(bf16[4,272,128]{2,1,0:T(8,128)(2,1)S(1)} %slice.118), channel_id=1, source_target_pairs={{0,384},{16,400},{32,416},{48,432},{64,448},{80,464},{96,480},{112... | collective-permute-start | bytes 835592 | tf_op jit(solution)/shard_map/ppermute | solution.py:45
  94.3 7.7 %copy-start.3 = (bf16[32,64,128]{2,1,0:T(8,128)(2,1)S(1)}, bf16[32,64,128]{2,1,0:T(8,128)(2,1)}, u32[]{:S(2)}) copy-start(bf16[32,64,128]{2,1,0:T(8,128)(2,1)} %get-tuple-element.11) | copy-start | bytes 1572868
  96.1 7.7 %copy-start.2 = (bf16[32,64,128]{2,1,0:T(8,128)(2,1)S(1)}, bf16[32,64,128]{2,1,0:T(8,128)(2,1)}, u32[]{:S(2)}) copy-start(bf16[32,64,128]{2,1,0:T(8,128)(2,1)} %get-tuple-element.8) | copy-start | bytes 1572868
  103.9 18.6 %copy-start.10 = (s32[64]{0:T(128)S(1)}, s32[64]{0:T(128)}, u32[]{:S(2)}) copy-start(s32[64]{0:T(128)} %param.17) | copy-start | bytes 772
  108.1 7.2 %collective-permute-start.8 = (bf16[64,1024]{1,0:T(8,128)(2,1)S(1)}, bf16[64,1024]{1,0:T(8,128)(2,1)S(1)}, u32[]{:S(2)}, u32[]{:S(2)}) collective-permute-start(bf16[64,1024]{1,0:T(8,128)(2,1)S(1)} %fusion.15), channel_id=1, source_target_pairs={{0,2},{2,0},{4,6},{6,4},{8,10},{10,8},{12,14},{14,12},{1,3},{3,1},... | collective-permute-start | bytes 393224 | tf_op jit(solution)/shard_map/ppermute | solution.py:73
  115.4 11.5 %collective-permute-start.9 = (bf16[64,1024]{1,0:T(8,128)(2,1)S(1)}, bf16[64,1024]{1,0:T(8,128)(2,1)S(1)}, u32[]{:S(2)}, u32[]{:S(2)}) collective-permute-start(bf16[64,1024]{1,0:T(8,128)(2,1)S(1)} %add_convert_fusion.1), channel_id=1, source_target_pairs={{0,4},{2,6},{4,0},{6,2},{8,12},{10,14},{12,8},{14,10},{1,5},{3,7},... | collective-permute-start | bytes 393224 | tf_op jit(solution)/shard_map/ppermute | solution.py:73
  126.9 15.2 %collective-permute-start.10 = (bf16[64,1024]{1,0:T(8,128)(2,1)S(1)}, bf16[64,1024]{1,0:T(8,128)(2,1)S(1)}, u32[]{:S(2)}, u32[]{:S(2)}) collective-permute-start(bf16[64,1024]{1,0:T(8,128)(2,1)S(1)} %add_convert_fusion), channel_id=1, source_target_pairs={{0,8},{2,10},{4,12},{6,14},{8,0},{10,2},{12,4},{14,6},{1,9},{3,11}... | collective-permute-start | bytes 393224 | tf_op jit(solution)/shard_map/ppermute | solution.py:73
  146.3 7.0 %copy-start.1 = (f32[512,1024]{1,0:T(8,128)S(1)}, f32[512,1024]{1,0:T(8,128)}, u32[]{:S(2)}) copy-start(f32[512,1024]{1,0:T(8,128)} %scatter_custom_fusion) | copy-start | bytes 6291460
  146.3 7.0 %collective-permute-start.11 = (f32[3,1024]{1,0:T(4,128)S(1)}, f32[3,1024]{1,0:T(4,128)S(1)}, u32[]{:S(2)}, u32[]{:S(2)}) collective-permute-start(f32[3,1024]{1,0:T(4,128)S(1)} %slice.124), channel_id=1, source_target_pairs={{16,0},{32,16},{48,32},{64,48},{80,64},{96,80},{112,96},{128,112},... | collective-permute-start | bytes 36872 | tf_op jit(solution)/shard_map/ppermute | solution.py:23

commit v8 on v7

--- a/solution.py
+++ b/solution.py
@@ -240,14 +240,28 @@
     mixed_grad = lax.dot_general(
         grad_state.astype(jnp.bfloat16), mix_weight, contract, preferred_element_type=jnp.float32
     )
-    spread_mix = jnp.zeros((row_count, D), jnp.float32).at[boundaries].add(mixed_grad)
-    residual_grad = jnp.zeros((row_count, D), jnp.float32).at[boundaries].add(grad_state)
-    after_rim = neighbour(spread_mix[: KCONV - 1], -1)
-    padded_grad = jnp.concatenate([spread_mix, after_rim], axis=0)
-    conv_grad = conv_kernel[0] * spread_mix
-    for offset in range(1, KCONV):
-        conv_grad = conv_grad + conv_kernel[offset] * padded_grad[offset : offset + row_count]
-    grad_bytes = (residual_grad + conv_grad).astype(jnp.bfloat16)
+    mixed_grad = mixed_grad.astype(jnp.float32)
+    contributions = jnp.concatenate(
+        [grad_state + conv_kernel[0] * mixed_grad]
+        + [conv_kernel[offset] * mixed_grad for offset in range(1, KCONV)],
+        axis=0,
+    )
+    target_rows = (
+        boundaries[None, :] - jnp.arange(KCONV, dtype=jnp.int32)[:, None]
+    ).reshape(KCONV * slot_count)
+    exact = lax.Precision.HIGHEST
+    rim_rows = jnp.arange(-(KCONV - 1), 0, dtype=jnp.int32)
+    rim_pick = (rim_rows[:, None] == target_rows[None, :]).astype(jnp.float32)
+    before_rows = jnp.dot(rim_pick, contributions, precision=exact)
+    after_rim = neighbour(before_rows, -1)
+    row_pick = (
+        jnp.arange(row_count, dtype=jnp.int32)[:, None] == target_rows[None, :]
+    ).astype(jnp.float32)
+    local_grad = jnp.dot(row_pick, contributions, precision=exact)
+    tail = jnp.concatenate(
+        [jnp.zeros((row_count - (KCONV - 1), D), jnp.float32), after_rim], axis=0
+    )
+    grad_bytes = (local_grad + tail).astype(jnp.bfloat16)
     return (attended, grad_bytes)
 
 

time: 164 us -> 153 us (0.933)
  other arithmetic: 21.7 us -> 9.53 us
  local copies, waits for them, and re-layouts: 11 us -> 8.46 us
  waiting for transfers between devices: 52.3 us -> 54.4 us
  matrix products: 13.8 us -> 15.7 us
    scatter-add x2 -> x0, other arithmetic: 6.67 us -> none  [the longest x1 4.13 us: per_device(): jnp.zeros((row_count, D), jnp.float32).at[boundaries].add(grad_state)]
    add x2 -> x1, other arithmetic: 2.97 us -> 0.01 us  [per_device(): rim_rows = jnp.arange(-(KCONV - 1), 0, dtype=jnp.int32)]
    convert_element_type x1 -> x0, other arithmetic: 2.72 us -> none  [per_device(): grad_bytes = (residual_grad + conv_grad).astype(jnp.bfloat16)]
    dot_general x0 -> x2, matrix products: none -> 2.52 us  [the longest x1 2.05 us: per_device(): local_grad = jnp.dot(row_pick, contributions, precision=exact)]
    unnamed x30 -> x25, local copies, waits for them, and re-layouts: 2.16 us -> 0.31 us
  transfers between devices with their start and end apart: 12 -> 12, of which waited for: 11 -> 10; matrix products, arithmetic and copies ran while one was open for 4% -> 3% of each run, Pallas kernels for 0% -> 0%
where the time goes in v8:
time: 153 us; the launch traced here: 151 us
  waiting for transfers between devices  54.4 us (36%)
  starting transfers between devices  49 us (32%)
  matrix products  15.7 us (10%)
  Pallas kernels  12.6 us (8%)
  other arithmetic  9.53 us (6%)
  local copies, waits for them, and re-layouts  8.46 us (6%)
  between operations  1.73 us (1%)
    ppermute x3, waiting for transfers between devices, gather_blocks(): other = lax.ppermute(held, axis, [(i, i ^ step) for i in range(devices)])  25.4 us
    ppermute x3, starting transfers between devices, summed_over(): got = lax.ppermute(sent, axis, [(i, i ^ step) for i in range(devices)])  23.7 us
    ppermute x4, waiting for transfers between devices, shifted(): lax.ppermute(array, axis, [(i, (i + by) % devices) for i in range(devices)])  15.4 us
    pallas_call x1, Pallas kernels, forward_all(): pl.pallas_call(forward_kernel, grid_spec=grid_spec, out_shape=[jax.ShapeD...  12.6 us
    ppermute x4, starting transfers between devices, shifted(): lax.ppermute(array, axis, [(i, (i + by) % devices) for i in range(devices)])  11.7 us
    ppermute x3, waiting for transfers between devices, summed_over(): got = lax.ppermute(sent, axis, [(i, i ^ step) for i in range(devices)])  10.1 us
    ppermute x3, starting transfers between devices, gather_blocks(): other = lax.ppermute(held, axis, [(i, i ^ step) for i in range(devices)])  7.07 us
    ppermute x2, starting transfers between devices, passed_along(): return lax.ppermute(array, axis, pairs)  6.6 us
  transfers between devices with their start and end apart: 12, of which 10 were waited for; matrix products, arithmetic and copies ran while one was open for 3% of the time, Pallas kernels for 0%

profile of v8, /device:TPU:30, one launch (start us, length us, event | category | flops | bytes accessed | tf_op | source)
XLA Modules:
  0.0 151.5 jit_solution(336286521000716069)
XLA Ops:
  0.6 0.9 slice.139
  1.5 4.7 %collective-permute-start = (bf16[3,1024]{1,0:T(4,128)(2,1)S(1)}, bf16[3,1024]{1,0:T(4,128)(2,1)S(1)}, u32[]{:S(2)}, u32[]{:S(2)}) collective-permute-start(bf16[3,1024]{1,0:T(4,128)(2,1)S(1)} %slice.139), channel_id=1, source_target_pairs={{0,16},{16,32},{32,48},{48,64},{64,80},{80,96},{96,112},{112,128},... | collective-permute-start | bytes 18440 | tf_op jit(solution)/shard_map/ppermute | solution.py:23
  6.2 0.7 iota_subtract_fusion
  7.0 0.1 add.205
  7.0 0.1 add.202
  7.1 0.9 fusion.49
  8.7 1.5 pad_maximum_fusion
  10.2 2.0 %gather_fusion = bf16[256,1024]{1,0:T(8,128)(2,1)} fusion(bf16[515,1024]{1,0:T(8,128)(2,1)S(1)} %pad_maximum_fusion, s32[1024]{0:T(1024)S(1)} %pad_clamp_fusion), kind=kCustom, calls=%fused_computation | custom fusion | bytes 1049600 | tf_op jit(solution)/shard_map/jit(_take)/gather | solution.py:152
  12.2 1.2 select_convert_fusion
  13.5 0.6 multiply_reduce_fusion.1
  14.1 0.1 multiply_convert_fusion
  14.2 0.2 constant_dynamic-update-slice_fusion.4
  14.4 0.2 constant_dynamic-update-slice_fusion.3
  14.6 0.2 constant_dynamic-update-slice_fusion.2
  14.8 0.1 constant_dynamic-update-slice_fusion.1
  14.9 1.9 %collective-permute-start.1 = (bf16[1,272,128]{2,1,0:T(8,128)(2,1)S(1)}, bf16[1,272,128]{2,1,0:T(8,128)(2,1)S(1)}, u32[]{:S(2)}, u32[]{:S(2)}) collective-permute-start(bf16[1,272,128]{2,1,0:T(8,128)(2,1)S(1)} %bitcast.48), channel_id=1, source_target_pairs={{0,16},{16,0},{32,48},{48,32},{64,80},{80,64},{96,112},{112,96},{1... | collective-permute-start | bytes 208904 | tf_op jit(solution)/shard_map/ppermute | solution.py:36
  16.8 4.3 %collective-permute-done.1 = bf16[1,272,128]{2,1,0:T(8,128)(2,1)S(1)} collective-permute-done((bf16[1,272,128]{2,1,0:T(8,128)(2,1)S(1)}, bf16[1,272,128]{2,1,0:T(8,128)(2,1)S(1)}, u32[]{:S(2)}, u32[]{:S(2)}) %collective-permute-start.1) | collective-permute-done | bytes 69664 | tf_op jit(solution)/shard_map/ppermute | solution.py:36
  21.1 1.9 %collective-permute-start.2 = (bf16[2,272,128]{2,1,0:T(8,128)(2,1)S(1)}, bf16[2,272,128]{2,1,0:T(8,128)(2,1)S(1)}, u32[]{:S(2)}, u32[]{:S(2)}) collective-permute-start(bf16[2,272,128]{2,1,0:T(8,128)(2,1)S(1)} %pad_maximum_fusion.8), channel_id=1, source_target_pairs={{0,32},{16,48},{32,0},{48,16},{64,96},{80,112},{96,64},{112,80},{1... | collective-permute-start | bytes 417800 | tf_op jit(solution)/shard_map/ppermute | solution.py:36
  23.0 0.1 and_select_fusion
  23.1 7.5 %collective-permute-done.2 = bf16[2,272,128]{2,1,0:T(8,128)(2,1)S(1)} collective-permute-done((bf16[2,272,128]{2,1,0:T(8,128)(2,1)S(1)}, bf16[2,272,128]{2,1,0:T(8,128)(2,1)S(1)}, u32[]{:S(2)}, u32[]{:S(2)}) %collective-permute-start.2) | collective-permute-done | bytes 139296 | tf_op jit(solution)/shard_map/ppermute | solution.py:36
  30.6 3.2 %collective-permute-start.3 = (bf16[4,272,128]{2,1,0:T(8,128)(2,1)S(1)}, bf16[4,272,128]{2,1,0:T(8,128)(2,1)S(1)}, u32[]{:S(2)}, u32[]{:S(2)}) collective-permute-start(bf16[4,272,128]{2,1,0:T(8,128)(2,1)S(1)} %pad_maximum_fusion.7), channel_id=1, source_target_pairs={{0,64},{16,80},{32,96},{48,112},{64,0},{80,16},{96,32},{112,48},{1... | collective-permute-start | bytes 835592 | tf_op jit(solution)/shard_map/ppermute | solution.py:36
  33.9 0.1 concatenate.34.shards_ref
  34.0 13.6 %collective-permute-done.3 = bf16[4,272,128]{2,1,0:T(8,128)(2,1)S(1)} collective-permute-done((bf16[4,272,128]{2,1,0:T(8,128)(2,1)S(1)}, bf16[4,272,128]{2,1,0:T(8,128)(2,1)S(1)}, u32[]{:S(2)}, u32[]{:S(2)}) %collective-permute-start.3) | collective-permute-done | bytes 278560 | tf_op jit(solution)/shard_map/ppermute | solution.py:36
  47.6 2.4 %collective-permute-start.4 = (bf16[8,272,128]{2,1,0:T(8,128)(2,1)S(1)}, bf16[8,272,128]{2,1,0:T(8,128)(2,1)S(1)}, u32[]{:S(2)}, u32[]{:S(2)}) collective-permute-start(bf16[8,272,128]{2,1,0:T(8,128)(2,1)S(1)} %pad_maximum_fusion.6), channel_id=1, source_target_pairs={{0,128},{16,144},{32,160},{48,176},{64,192},{80,208},{96,224},{112... | collective-permute-start | bytes 1671176 | tf_op jit(solution)/shard_map/ppermute | solution.py:45
  50.1 3.5 %collective-permute-start.5 = (bf16[8,272,128]{2,1,0:T(8,128)(2,1)S(1)}, bf16[8,272,128]{2,1,0:T(8,128)(2,1)S(1)}, u32[]{:S(2)}, u32[]{:S(2)}) collective-permute-start(bf16[8,272,128]{2,1,0:T(8,128)(2,1)S(1)} %pad_maximum_fusion.6), channel_id=1, source_target_pairs={{0,384},{16,400},{32,416},{48,432},{64,448},{80,464},{96,480},{112... | collective-permute-start | bytes 1671176 | tf_op jit(solution)/shard_map/ppermute | solution.py:45
  53.6 8.2 %collective-permute-done.4 = bf16[8,272,128]{2,1,0:T(8,128)(2,1)S(1)} collective-permute-done((bf16[8,272,128]{2,1,0:T(8,128)(2,1)S(1)}, bf16[8,272,128]{2,1,0:T(8,128)(2,1)S(1)}, u32[]{:S(2)}, u32[]{:S(2)}) %collective-permute-start.4) | collective-permute-done | bytes 557088 | tf_op jit(solution)/shard_map/ppermute | solution.py:45
  61.8 3.6 %collective-permute-start.6 = (bf16[4,272,128]{2,1,0:T(8,128)(2,1)S(1)}, bf16[4,272,128]{2,1,0:T(8,128)(2,1)S(1)}, u32[]{:S(2)}, u32[]{:S(2)}) collective-permute-start(bf16[4,272,128]{2,1,0:T(8,128)(2,1)S(1)} %slice.101), channel_id=1, source_target_pairs={{0,128},{16,144},{32,160},{48,176},{64,192},{80,208},{96,224},{112... | collective-permute-start | bytes 835592 | tf_op jit(solution)/shard_map/ppermute | solution.py:45
  65.5 2.2 %collective-permute-start.7 = (bf16[4,272,128]{2,1,0:T(8,128)(2,1)S(1)}, bf16[4,272,128]{2,1,0:T(8,128)(2,1)S(1)}, u32[]{:S(2)}, u32[]{:S(2)}) collective-permute-start(bf16[4,272,128]{2,1,0:T(8,128)(2,1)S(1)} %slice.102), channel_id=1, source_target_pairs={{0,384},{16,400},{32,416},{48,432},{64,448},{80,464},{96,480},{112... | collective-permute-start | bytes 835592 | tf_op jit(solution)/shard_map/ppermute | solution.py:45
  67.8 0.1 constant_dynamic-update-slice_fusion.8
  67.9 0.1 constant_dynamic-update-slice_fusion.7
  67.9 2.3 %collective-permute-done.6 = bf16[4,272,128]{2,1,0:T(8,128)(2,1)S(1)} collective-permute-done((bf16[4,272,128]{2,1,0:T(8,128)(2,1)S(1)}, bf16[4,272,128]{2,1,0:T(8,128)(2,1)S(1)}, u32[]{:S(2)}, u32[]{:S(2)}) %collective-permute-start.6) | collective-permute-done | bytes 278560 | tf_op jit(solution)/shard_map/ppermute | solution.py:45
  70.3 4.9 %collective-permute-done.7 = bf16[4,272,128]{2,1,0:T(8,128)(2,1)S(1)} collective-permute-done((bf16[4,272,128]{2,1,0:T(8,128)(2,1)S(1)}, bf16[4,272,128]{2,1,0:T(8,128)(2,1)S(1)}, u32[]{:S(2)}, u32[]{:S(2)}) %collective-permute-start.7) | collective-permute-done | bytes 278560 | tf_op jit(solution)/shard_map/ppermute | solution.py:45
  75.2 1.4 fusion.48
  76.6 0.7 fusion.36
  77.3 0.1 iota_compare_fusion.2
  77.4 0.1 iota_add_fusion
  77.5 0.7 select_n.88.key_code_ref
  78.2 12.6 %shard_map.113 = (bf16[2048,128]{1,0:T(8,128)(2,1)}, f32[2048,1]{1,0:T(8,128)}, f32[2048,1]{1,0:T(8,128)}) custom-call(s32[32]{0:T(128)} %copy-done.8, bf16[2048,128]{1,0:T(8,128)(2,1)} %bitcast.40, bf16[2048,128]{1,0:T(8,128)(2,1)} %bitcast.45, bf16[2048,128]{1,0:T(8,128)(2,1)} %bitcast.43, bf16[2048,128]{1,0:T(8,128)(2,1)} %bitcast.37, ...), custom_call_target="tpu_custom_call" | custom-call | tf_op jit(solution)/shard_map/pallas_call | solution.py:118
  90.8 0.9 slice_reduce_fusion.1
  91.6 0.9 slice_reduce_fusion
  92.5 1.6 %reduce.3 = f32[2048]{0:T(1024)S(1)} reduce(f32[2048,1]{1,0:T(8,128)} %get-tuple-element.6, f32[]{:T(128)} %constant.95), dimensions={1}, to_apply=%get-tuple-element.6.reduce_sub_computation | reduce | bytes 16388 | tf_op jit(solution)/shard_map/pallas_call | solution.py:118
  94.1 1.6 %reduce.4 = f32[2048]{0:T(1024)S(1)} reduce(f32[2048,1]{1,0:T(8,128)} %get-tuple-element.7, f32[]{:T(128)} %constant.95), dimensions={1}, to_apply=%get-tuple-element.7.reduce_sub_computation | reduce | bytes 16388 | tf_op jit(solution)/shard_map/pallas_call | solution.py:118
  95.8 0.1 lt.99
  95.9 2.2 %fusion.5 = f32[64,2048]{1,0:T(8,128)} fusion(bf16[64,128]{1,0:T(8,128)(2,1)S(1)} %get-tuple-element.31, bf16[2048,128]{1,0:T(8,128)(2,1)} %bitcast.46, f32[64]{0:T(128)S(1)} %slice_reduce_fusion.1, s32[2048]{0:T(1024)S(1)} %add.216, s32[64]{0:T(128)S(1)} %iota_add_fusion.2, pred[2048]{0:T(1024)(128)(4,1)S(1)} %lt.99), kind=kOutput, calls=%fused_computation.10 | convolution fusion | flops 34209792 | bytes 1075712 | tf_op jit(solution)/shard_map/dot_general | solution.py:198
  98.1 1.8 %fusion.16 = bf16[64,128]{1,0:T(8,128)(2,1)S(1)} fusion(bf16[2048,128]{1,0:T(8,128)(2,1)} %bitcast.47, f32[64,2048]{1,0:T(8,128)} %fusion.5, bf16[2048,128]{1,0:T(8,128)(2,1)} %bitcast.44, f32[64]{0:T(128)S(1)} %slice_reduce_fusion, bf16[64,128]{1,0:T(8,128)(2,1)S(1)} %copy-done.6, pred[64]{0:T(512)(128)(4,1)S(1)} %iota_compare_fusion.3), kind=kOutput, calls=%fused_computation.25 | convolution fusion | flops 67526656 | bytes 1605952 | tf_op jit(solution)/shard_map/dot_general | solution.py:204
  100.0 1.9 %fusion.50 = f32[64,1024]{1,0:T(8,128)} fusion(bf16[64,128]{1,0:T(8,128)(2,1)S(1)} %fusion.16, bf16[1024,128]{1,0:T(8,128)(2,1)} %param.14), kind=kOutput, calls=%fused_computation.130 | convolution fusion | flops 16777216 | bytes 540672 | tf_op jit(solution)/shard_map/dot_general | solution.py:223
  101.8 1.1 fusion.7
  103.0 1.5 fusion.15
  104.4 1.2 convolution_add_fusion.1
  105.7 1.5 fusion.12
  107.2 4.3 %collective-permute-start.8 = (bf16[64,1024]{1,0:T(8,128)(2,1)S(1)}, bf16[64,1024]{1,0:T(8,128)(2,1)S(1)}, u32[]{:S(2)}, u32[]{:S(2)}) collective-permute-start(bf16[64,1024]{1,0:T(8,128)(2,1)S(1)} %fusion.12), channel_id=1, source_target_pairs={{0,2},{2,0},{4,6},{6,4},{8,10},{10,8},{12,14},{14,12},{1,3},{3,1},... | collective-permute-start | bytes 393224 | tf_op jit(solution)/shard_map/ppermute | solution.py:73
  111.5 2.9 %collective-permute-done.8 = bf16[64,1024]{1,0:T(8,128)(2,1)S(1)} collective-permute-done((bf16[64,1024]{1,0:T(8,128)(2,1)S(1)}, bf16[64,1024]{1,0:T(8,128)(2,1)S(1)}, u32[]{:S(2)}, u32[]{:S(2)}) %collective-permute-start.8) | collective-permute-done | bytes 131104 | tf_op jit(solution)/shard_map/ppermute | solution.py:73
  114.5 7.1 %collective-permute-start.9 = (bf16[64,1024]{1,0:T(8,128)(2,1)S(1)}, bf16[64,1024]{1,0:T(8,128)(2,1)S(1)}, u32[]{:S(2)}, u32[]{:S(2)}) collective-permute-start(bf16[64,1024]{1,0:T(8,128)(2,1)S(1)} %add_convert_fusion.2), channel_id=1, source_target_pairs={{0,4},{2,6},{4,0},{6,2},{8,12},{10,14},{12,8},{14,10},{1,5},{3,7},... | collective-permute-start | bytes 393224 | tf_op jit(solution)/shard_map/ppermute | solution.py:73
  121.6 4.3 %collective-permute-done.9 = bf16[64,1024]{1,0:T(8,128)(2,1)S(1)} collective-permute-done((bf16[64,1024]{1,0:T(8,128)(2,1)S(1)}, bf16[64,1024]{1,0:T(8,128)(2,1)S(1)}, u32[]{:S(2)}, u32[]{:S(2)}) %collective-permute-start.9) | collective-permute-done | bytes 131104 | tf_op jit(solution)/shard_map/ppermute | solution.py:73
  125.9 12.2 %collective-permute-start.10 = (bf16[64,1024]{1,0:T(8,128)(2,1)S(1)}, bf16[64,1024]{1,0:T(8,128)(2,1)S(1)}, u32[]{:S(2)}, u32[]{:S(2)}) collective-permute-start(bf16[64,1024]{1,0:T(8,128)(2,1)S(1)} %add_convert_fusion.1), channel_id=1, source_target_pairs={{0,8},{2,10},{4,12},{6,14},{8,0},{10,2},{12,4},{14,6},{1,9},{3,11}... | collective-permute-start | bytes 393224 | tf_op jit(solution)/shard_map/ppermute | solution.py:73
  138.2 0.1 sub.71
  138.3 2.8 %collective-permute-done.10 = bf16[64,1024]{1,0:T(8,128)(2,1)S(1)} collective-permute-done((bf16[64,1024]{1,0:T(8,128)(2,1)S(1)}, bf16[64,1024]{1,0:T(8,128)(2,1)S(1)}, u32[]{:S(2)}, u32[]{:S(2)}) %collective-permute-start.10) | collective-permute-done | bytes 131104 | tf_op jit(solution)/shard_map/ppermute | solution.py:73
  141.1 0.2 multiply_reduce_fusion
  141.3 0.8 multiply_add_fusion
  142.1 0.5 fusion.17
  142.6 1.9 %collective-permute-start.11 = (f32[3,1024]{1,0:T(4,128)S(1)}, f32[3,1024]{1,0:T(4,128)S(1)}, u32[]{:S(2)}, u32[]{:S(2)}) collective-permute-start(f32[3,1024]{1,0:T(4,128)S(1)} %fusion.17), channel_id=1, source_target_pairs={{16,0},{32,16},{48,32},{64,48},{80,64},{96,80},{112,96},{128,112},... | collective-permute-start | bytes 36872 | tf_op jit(solution)/shard_map/ppermute | solution.py:23
  144.5 1.4 slice_select_fusion
  145.9 3.5 %collective-permute-done.11 = f32[3,1024]{1,0:T(4,128)S(1)} collective-permute-done((f32[3,1024]{1,0:T(4,128)S(1)}, f32[3,1024]{1,0:T(4,128)S(1)}, u32[]{:S(2)}, u32[]{:S(2)}) %collective-permute-start.11) | collective-permute-done | bytes 12320 | tf_op jit(solution)/shard_map/ppermute | solution.py:23
  149.4 2.1 %add_convert_fusion = bf16[512,1024]{1,0:T(8,128)(2,1)} fusion(f32[3,1024]{1,0:T(4,128)S(1)} %collective-permute-done.11, f32[64,1024]{1,0:T(8,128)S(1)} %get-tuple-element.13, f32[64,1024]{1,0:T(8,128)S(1)} %get-tuple-element.14, f32[64,1024]{1,0:T(8,128)S(1)} %get-tuple-element.15, f32[64,1024]{1,0:T(8,128)S(1)} %get-tuple-element.12, s32[256]{0:T(256)S(1)} %sub.71), kind=kOutput, calls=%fused_computation.15 | convolution fusion | flops 1612578816 | bytes 2110464 | tf_op jit(solution)/shard_map/dot_general | solution.py:260
  (47 shorter events, 0.6 us)
Async XLA Ops:
  0.6 12.8 %copy-start = (bf16[1024,1024]{1,0:T(8,128)(2,1)S(1)}, bf16[1024,1024]{1,0:T(8,128)(2,1)}, u32[]{:S(2)}) copy-start(bf16[1024,1024]{1,0:T(8,128)(2,1)} %param.12) | copy-start | bytes 6291460
  1.5 7.2 %collective-permute-start = (bf16[3,1024]{1,0:T(4,128)(2,1)S(1)}, bf16[3,1024]{1,0:T(4,128)(2,1)S(1)}, u32[]{:S(2)}, u32[]{:S(2)}) collective-permute-start(bf16[3,1024]{1,0:T(4,128)(2,1)S(1)} %slice.139), channel_id=1, source_target_pairs={{0,16},{16,32},{32,48},{48,64},{64,80},{80,96},{96,112},{112,128},... | collective-permute-start | bytes 18440 | tf_op jit(solution)/shard_map/ppermute | solution.py:23
  12.2 1.9 %copy-start.7 = (f32[1024]{0:T(1024)S(1)}, f32[1024]{0:T(1024)}, u32[]{:S(2)}) copy-start(f32[1024]{0:T(1024)} %param.13) | copy-start | bytes 12292
  12.2 2.0 %copy-start.4 = (bf16[1024,128]{1,0:T(8,128)(2,1)S(1)}, bf16[1024,128]{1,0:T(8,128)(2,1)}, u32[]{:S(2)}) copy-start(bf16[1024,128]{1,0:T(8,128)(2,1)} %param.14) | copy-start | bytes 786436
  12.2 2.2 %copy-start.3 = (bf16[1024,128]{1,0:T(8,128)(2,1)S(1)}, bf16[1024,128]{1,0:T(8,128)(2,1)}, u32[]{:S(2)}) copy-start(bf16[1024,128]{1,0:T(8,128)(2,1)} %param.15) | copy-start | bytes 786436
  13.4 1.1 copy-start.5
  13.5 1.3 copy-start.6
  14.9 6.2 %collective-permute-start.1 = (bf16[1,272,128]{2,1,0:T(8,128)(2,1)S(1)}, bf16[1,272,128]{2,1,0:T(8,128)(2,1)S(1)}, u32[]{:S(2)}, u32[]{:S(2)}) collective-permute-start(bf16[1,272,128]{2,1,0:T(8,128)(2,1)S(1)} %bitcast.48), channel_id=1, source_target_pairs={{0,16},{16,0},{32,48},{48,32},{64,80},{80,64},{96,112},{112,96},{1... | collective-permute-start | bytes 208904 | tf_op jit(solution)/shard_map/ppermute | solution.py:36
  21.1 9.5 %collective-permute-start.2 = (bf16[2,272,128]{2,1,0:T(8,128)(2,1)S(1)}, bf16[2,272,128]{2,1,0:T(8,128)(2,1)S(1)}, u32[]{:S(2)}, u32[]{:S(2)}) collective-permute-start(bf16[2,272,128]{2,1,0:T(8,128)(2,1)S(1)} %pad_maximum_fusion.8), channel_id=1, source_target_pairs={{0,32},{16,48},{32,0},{48,16},{64,96},{80,112},{96,64},{112,80},{1... | collective-permute-start | bytes 417800 | tf_op jit(solution)/shard_map/ppermute | solution.py:36
  30.6 17.0 %collective-permute-start.3 = (bf16[4,272,128]{2,1,0:T(8,128)(2,1)S(1)}, bf16[4,272,128]{2,1,0:T(8,128)(2,1)S(1)}, u32[]{:S(2)}, u32[]{:S(2)}) collective-permute-start(bf16[4,272,128]{2,1,0:T(8,128)(2,1)S(1)} %pad_maximum_fusion.7), channel_id=1, source_target_pairs={{0,64},{16,80},{32,96},{48,112},{64,0},{80,16},{96,32},{112,48},{1... | collective-permute-start | bytes 835592 | tf_op jit(solution)/shard_map/ppermute | solution.py:36
  33.9 33.9 %copy-start.8 = (s32[32]{0:T(128)}, s32[32]{0:T(128)S(1)}, u32[]{:S(2)}) copy-start(s32[32]{0:T(128)S(1)} %concatenate.34.shards_ref) | copy-start | bytes 388
  47.6 14.2 %collective-permute-start.4 = (bf16[8,272,128]{2,1,0:T(8,128)(2,1)S(1)}, bf16[8,272,128]{2,1,0:T(8,128)(2,1)S(1)}, u32[]{:S(2)}, u32[]{:S(2)}) collective-permute-start(bf16[8,272,128]{2,1,0:T(8,128)(2,1)S(1)} %pad_maximum_fusion.6), channel_id=1, source_target_pairs={{0,128},{16,144},{32,160},{48,176},{64,192},{80,208},{96,224},{112... | collective-permute-start | bytes 1671176 | tf_op jit(solution)/shard_map/ppermute | solution.py:45
  50.1 15.4 %collective-permute-start.5 = (bf16[8,272,128]{2,1,0:T(8,128)(2,1)S(1)}, bf16[8,272,128]{2,1,0:T(8,128)(2,1)S(1)}, u32[]{:S(2)}, u32[]{:S(2)}) collective-permute-start(bf16[8,272,128]{2,1,0:T(8,128)(2,1)S(1)} %pad_maximum_fusion.6), channel_id=1, source_target_pairs={{0,384},{16,400},{32,416},{48,432},{64,448},{80,464},{96,480},{112... | collective-permute-start | bytes 1671176 | tf_op jit(solution)/shard_map/ppermute | solution.py:45
  61.8 8.4 %collective-permute-start.6 = (bf16[4,272,128]{2,1,0:T(8,128)(2,1)S(1)}, bf16[4,272,128]{2,1,0:T(8,128)(2,1)S(1)}, u32[]{:S(2)}, u32[]{:S(2)}) collective-permute-start(bf16[4,272,128]{2,1,0:T(8,128)(2,1)S(1)} %slice.101), channel_id=1, source_target_pairs={{0,128},{16,144},{32,160},{48,176},{64,192},{80,208},{96,224},{112... | collective-permute-start | bytes 835592 | tf_op jit(solution)/shard_map/ppermute | solution.py:45
  65.5 9.7 %collective-permute-start.7 = (bf16[4,272,128]{2,1,0:T(8,128)(2,1)S(1)}, bf16[4,272,128]{2,1,0:T(8,128)(2,1)S(1)}, u32[]{:S(2)}, u32[]{:S(2)}) collective-permute-start(bf16[4,272,128]{2,1,0:T(8,128)(2,1)S(1)} %slice.102), channel_id=1, source_target_pairs={{0,384},{16,400},{32,416},{48,432},{64,448},{80,464},{96,480},{112... | collective-permute-start | bytes 835592 | tf_op jit(solution)/shard_map/ppermute | solution.py:45
  94.1 7.7 %copy-start.2 = (bf16[32,64,128]{2,1,0:T(8,128)(2,1)S(1)}, bf16[32,64,128]{2,1,0:T(8,128)(2,1)}, u32[]{:S(2)}) copy-start(bf16[32,64,128]{2,1,0:T(8,128)(2,1)} %get-tuple-element.11) | copy-start | bytes 1572868
  95.9 7.1 %copy-start.1 = (bf16[32,64,128]{2,1,0:T(8,128)(2,1)S(1)}, bf16[32,64,128]{2,1,0:T(8,128)(2,1)}, u32[]{:S(2)}) copy-start(bf16[32,64,128]{2,1,0:T(8,128)(2,1)} %get-tuple-element.8) | copy-start | bytes 1572868
  107.2 7.3 %collective-permute-start.8 = (bf16[64,1024]{1,0:T(8,128)(2,1)S(1)}, bf16[64,1024]{1,0:T(8,128)(2,1)S(1)}, u32[]{:S(2)}, u32[]{:S(2)}) collective-permute-start(bf16[64,1024]{1,0:T(8,128)(2,1)S(1)} %fusion.12), channel_id=1, source_target_pairs={{0,2},{2,0},{4,6},{6,4},{8,10},{10,8},{12,14},{14,12},{1,3},{3,1},... | collective-permute-start | bytes 393224 | tf_op jit(solution)/shard_map/ppermute | solution.py:73
  114.5 11.4 %collective-permute-start.9 = (bf16[64,1024]{1,0:T(8,128)(2,1)S(1)}, bf16[64,1024]{1,0:T(8,128)(2,1)S(1)}, u32[]{:S(2)}, u32[]{:S(2)}) collective-permute-start(bf16[64,1024]{1,0:T(8,128)(2,1)S(1)} %add_convert_fusion.2), channel_id=1, source_target_pairs={{0,4},{2,6},{4,0},{6,2},{8,12},{10,14},{12,8},{14,10},{1,5},{3,7},... | collective-permute-start | bytes 393224 | tf_op jit(solution)/shard_map/ppermute | solution.py:73
  125.9 15.2 %collective-permute-start.10 = (bf16[64,1024]{1,0:T(8,128)(2,1)S(1)}, bf16[64,1024]{1,0:T(8,128)(2,1)S(1)}, u32[]{:S(2)}, u32[]{:S(2)}) collective-permute-start(bf16[64,1024]{1,0:T(8,128)(2,1)S(1)} %add_convert_fusion.1), channel_id=1, source_target_pairs={{0,8},{2,10},{4,12},{6,14},{8,0},{10,2},{12,4},{14,6},{1,9},{3,11}... | collective-permute-start | bytes 393224 | tf_op jit(solution)/shard_map/ppermute | solution.py:73
  142.6 6.8 %collective-permute-start.11 = (f32[3,1024]{1,0:T(4,128)S(1)}, f32[3,1024]{1,0:T(4,128)S(1)}, u32[]{:S(2)}, u32[]{:S(2)}) collective-permute-start(f32[3,1024]{1,0:T(4,128)S(1)} %fusion.17), channel_id=1, source_target_pairs={{16,0},{32,16},{48,32},{64,48},{80,64},{96,80},{112,96},{128,112},... | collective-permute-start | bytes 36872 | tf_op jit(solution)/shard_map/ppermute | solution.py:23

commit v9 on v8

--- a/solution.py
+++ b/solution.py
@@ -76,18 +76,24 @@
     return total
 
 
-def forward_kernel(shards_ref, q_ref, k_ref, v_ref, g_ref, key_code_ref, att_ref, log_ref, delta_ref):
+def forward_kernel(
+    shards_ref, q_ref, k_ref, v_ref, g_ref, key_code_ref, own_code_ref,
+    att_ref, log_ref, delta_ref, gq_ref, gk_ref, gv_ref,
+):
     rows = q_ref.shape[0]
     block_rows = rows // BLOCKS_PER_STEP
-    first = pl.program_id(0) * BLOCKS_PER_STEP
+    step = pl.program_id(0)
+    first = step * BLOCKS_PER_STEP
     row = lax.broadcasted_iota(jnp.int32, (rows, 1), 0)
     q_ids = row % block_rows
     for t in range(BLOCKS_PER_STEP):
         q_ids = q_ids + jnp.where(row // block_rows == t, shards_ref[first + t] * block_rows, 0)
     scale = 1.0 / math.sqrt(HD)
-    scores = lax.dot_general(
-        q_ref[...], k_ref[...], (((1,), (1,)), ((), ())), preferred_element_type=jnp.float32
-    ) * scale
+    by_rows = (((1,), (1,)), ((), ()))
+    by_cols = (((0,), (0,)), ((), ()))
+    queries = q_ref[...]
+    grads = g_ref[...]
+    scores = lax.dot_general(queries, k_ref[...], by_rows, preferred_element_type=jnp.float32) * scale
     scores = jnp.where(key_code_ref[...] <= q_ids, scores, masked_score)
     row_max = jnp.max(scores, axis=1, keepdims=True)
     softmax_part = jnp.exp(scores - row_max)
@@ -96,25 +102,53 @@
         softmax_part.astype(jnp.bfloat16), v_ref[...], preferred_element_type=jnp.float32
     )
     attention = (product / row_sum).astype(jnp.bfloat16)
+    log_total = row_max + jnp.log(row_sum)
+    delta = jnp.sum(grads.astype(jnp.float32) * attention.astype(jnp.float32), axis=1, keepdims=True)
     att_ref[...] = attention
-    log_ref[...] = row_max + jnp.log(row_sum)
-    delta_ref[...] = jnp.sum(
-        g_ref[...].astype(jnp.float32) * attention.astype(jnp.float32), axis=1, keepdims=True
-    )
-
-
-def forward_all(queries, keys, values, grads, key_code, held_shards):
+    log_ref[...] = log_total
+    delta_ref[...] = delta
+
+    own = block_rows
+
+    @pl.when(step == 0)
+    def _():
+        probs = jnp.exp(scores[:own] - log_total[:own])
+        grad_probs = lax.dot_general(
+            grads[:own], v_ref[...], by_rows, preferred_element_type=jnp.float32
+        )
+        grad_scores = (probs * (grad_probs - delta[:own])).astype(jnp.bfloat16)
+        gq_ref[...] = jnp.dot(grad_scores, k_ref[...], preferred_element_type=jnp.float32)
+        gk_ref[...] = jnp.zeros_like(gk_ref)
+        gv_ref[...] = jnp.zeros_like(gv_ref)
+
+    own_scores = lax.dot_general(
+        queries, k_ref[:own], by_rows, preferred_element_type=jnp.float32
+    ) * scale
+    own_scores = jnp.where(own_code_ref[...] <= q_ids, own_scores, masked_score)
+    probs = jnp.exp(own_scores - log_total)
+    gv_ref[...] += lax.dot_general(
+        probs.astype(jnp.bfloat16), grads, by_cols, preferred_element_type=jnp.float32
+    )
+    grad_probs = lax.dot_general(grads, v_ref[:own], by_rows, preferred_element_type=jnp.float32)
+    grad_scores = (probs * (grad_probs - delta)).astype(jnp.bfloat16)
+    gk_ref[...] += lax.dot_general(grad_scores, queries, by_cols, preferred_element_type=jnp.float32)
+
+
+def attention_all(queries, keys, values, grads, key_code, held_shards, own_rows):
     slots, width = queries.shape
     row_spec = pl.BlockSpec((QBLOCK, width), lambda i, shards: (i, 0))
     full_spec = pl.BlockSpec((slots, width), lambda i, shards: (0, 0))
     col_spec = pl.BlockSpec((QBLOCK, 1), lambda i, shards: (i, 0))
+    own_spec = pl.BlockSpec((own_rows, width), lambda i, shards: (0, 0))
     grid_spec = pltpu.PrefetchScalarGridSpec(
         num_scalar_prefetch=1,
         grid=(slots // QBLOCK,),
         in_specs=[row_spec, full_spec, full_spec, row_spec,
-                  pl.BlockSpec((1, slots), lambda i, shards: (0, 0))],
-        out_specs=[row_spec, col_spec, col_spec],
-    )
+                  pl.BlockSpec((1, slots), lambda i, shards: (0, 0)),
+                  pl.BlockSpec((1, own_rows), lambda i, shards: (0, 0))],
+        out_specs=[row_spec, col_spec, col_spec, own_spec, own_spec, own_spec],
+    )
+    own_grad = jax.ShapeDtypeStruct((own_rows, width), jnp.float32)
     return pl.pallas_call(
         forward_kernel,
         grid_spec=grid_spec,
@@ -122,8 +156,10 @@
             jax.ShapeDtypeStruct((slots, width), jnp.bfloat16),
             jax.ShapeDtypeStruct((slots, 1), jnp.float32),
             jax.ShapeDtypeStruct((slots, 1), jnp.float32),
+            own_grad, own_grad, own_grad,
         ],
-    )(held_shards, queries, keys, values, grads, key_code.reshape(1, slots))
+    )(held_shards, queries, keys, values, grads, key_code.reshape(1, slots),
+      key_code[:own_rows].reshape(1, own_rows))
 
 
 def per_device(
@@ -184,40 +220,14 @@
         held_shards[:, None] * slot_count + jnp.arange(slot_count, dtype=jnp.int32)[None, :]
     ).reshape(total_slots)
 
-    all_attended, all_logs, all_deltas = forward_all(
+    all_attended, _, _, query_grad, key_grad, value_grad = attention_all(
         all_queries, all_keys, all_values, all_grads,
-        jnp.where(all_live, slot_ids, total_slots), held_shards,
-    )
-    all_logs = all_logs.reshape(total_slots)
-    all_deltas = all_deltas.reshape(total_slots)
+        jnp.where(all_live, slot_ids, total_slots), held_shards, slot_count,
+    )
     attended = jnp.where(live_mask[:, None], all_attended[:slot_count], jnp.bfloat16(0.0))
-    own_logs = all_logs[:slot_count]
-    own_deltas = all_deltas[:slot_count]
-
-    allowed = (slot_ids[None, :] <= own_ids[:, None]) & all_live[None, :]
-    scores = jnp.dot(queries, all_keys.T, preferred_element_type=jnp.float32) * score_scale
-    scores = jnp.where(allowed, scores, masked_score)
-    probs_full = jnp.exp(scores - own_logs[:, None])
-    grad_probs = jnp.dot(grad_rows, all_values.T, preferred_element_type=jnp.float32)
-    grad_scores = (probs_full * (grad_probs - own_deltas[:, None])).astype(jnp.bfloat16)
-    query_grad_rows = (
-        jnp.dot(grad_scores, all_keys, preferred_element_type=jnp.float32) * score_scale
-    ).astype(jnp.bfloat16)
-
-    allowed = (own_ids[None, :] <= slot_ids[:, None]) & live_mask[None, :]
-    scores = jnp.dot(all_queries, key_rows.T, preferred_element_type=jnp.float32) * score_scale
-    scores = jnp.where(allowed, scores, masked_score)
-    probs_full = jnp.exp(scores - all_logs[:, None])
-    contract_rows = (((0,), (0,)), ((), ()))
-    value_grad_rows = lax.dot_general(
-        probs_full.astype(jnp.bfloat16), all_grads, contract_rows, preferred_element_type=jnp.float32
-    ).astype(jnp.bfloat16)
-    grad_probs = jnp.dot(all_grads, value_rows.T, preferred_element_type=jnp.float32)
-    grad_scores = (probs_full * (grad_probs - all_deltas[:, None])).astype(jnp.bfloat16)
-    key_grad_rows = (
-        lax.dot_general(grad_scores, all_queries, contract_rows, preferred_element_type=jnp.float32)
-        * score_scale
-    ).astype(jnp.bfloat16)
+    query_grad_rows = (query_grad * score_scale).astype(jnp.bfloat16)
+    key_grad_rows = (key_grad * score_scale).astype(jnp.bfloat16)
+    value_grad_rows = value_grad.astype(jnp.bfloat16)
 
     contract = (((1,), (1,)), ((), ()))
     partial_normed = lax.dot_general(

time: 153 us -> 145 us (0.948)
  matrix products: 15.7 us -> 7.35 us
  Pallas kernels: 12.6 us -> 17.7 us
  other arithmetic: 9.53 us -> 6.96 us
    dot_general x4 -> x0, matrix products: 6.66 us -> none  [the longest x1 2.24 us: per_device(): jnp.dot(queries, all_keys.T, preferred_element_type=jnp.float32)]
    pallas_call x1, Pallas kernels: 12.6 us -> 17.7 us  [attention_all(): pl.pallas_call(forward_kernel, grid_spec=grid_spec, out_shape=[jax.ShapeD...]
    pallas_call x2 -> x0, other arithmetic: 3.19 us -> none  [forward_all(): pl.pallas_call(forward_kernel, grid_spec=grid_spec, out_shape=[jax.ShapeD...]
where the time goes in v9:
time: 145 us; the launch traced here: 144 us
  waiting for transfers between devices  54.6 us (38%)
  starting transfers between devices  49 us (34%)
  Pallas kernels  17.7 us (12%)
  matrix products  7.35 us (5%)
  local copies, waits for them, and re-layouts  7.12 us (5%)
  other arithmetic  6.96 us (5%)
  between operations  1.7 us (1%)
    ppermute x3, waiting for transfers between devices, gather_blocks(): other = lax.ppermute(held, axis, [(i, i ^ step) for i in range(devices)])  25.6 us
    ppermute x3, starting transfers between devices, summed_over(): got = lax.ppermute(sent, axis, [(i, i ^ step) for i in range(devices)])  23.7 us
    pallas_call x1, Pallas kernels, attention_all(): pl.pallas_call(forward_kernel, grid_spec=grid_spec, out_shape=[jax.ShapeD...  17.7 us
    ppermute x4, waiting for transfers between devices, shifted(): lax.ppermute(array, axis, [(i, (i + by) % devices) for i in range(devices)])  15.4 us
    ppermute x4, starting transfers between devices, shifted(): lax.ppermute(array, axis, [(i, (i + by) % devices) for i in range(devices)])  11.7 us
    ppermute x3, waiting for transfers between devices, summed_over(): got = lax.ppermute(sent, axis, [(i, i ^ step) for i in range(devices)])  10.1 us
    ppermute x3, starting transfers between devices, gather_blocks(): other = lax.ppermute(held, axis, [(i, i ^ step) for i in range(devices)])  7.05 us
    ppermute x2, starting transfers between devices, passed_along(): return lax.ppermute(array, axis, pairs)  6.6 us
  transfers between devices with their start and end apart: 12, of which 10 were waited for; matrix products, arithmetic and copies ran while one was open for 3% of the time, Pallas kernels for 0%

profile of v9, /device:TPU:30, one launch (start us, length us, event | category | flops | bytes accessed | tf_op | source)
XLA Modules:
  0.0 144.5 jit_solution(5977943588817169221)
XLA Ops:
  0.6 0.0 copy-start
  0.6 0.9 slice.133
  1.5 4.7 %collective-permute-start = (bf16[3,1024]{1,0:T(4,128)(2,1)S(1)}, bf16[3,1024]{1,0:T(4,128)(2,1)S(1)}, u32[]{:S(2)}, u32[]{:S(2)}) collective-permute-start(bf16[3,1024]{1,0:T(4,128)(2,1)S(1)} %slice.133), channel_id=1, source_target_pairs={{0,16},{16,32},{32,48},{48,64},{64,80},{80,96},{96,112},{112,128},... | collective-permute-start | bytes 18440 | tf_op jit(solution)/shard_map/ppermute | solution.py:23
  6.2 0.7 iota_subtract_fusion
  7.0 0.1 add.182
  7.0 0.1 add.179
  7.1 0.9 fusion.36
  8.7 0.0 collective-permute-done
  8.7 1.5 %pad_maximum_fusion = bf16[515,1024]{1,0:T(8,128)(2,1)S(1)} fusion(bf16[512,1024]{1,0:T(8,128)(2,1)} %param.10, bf16[3,1024]{1,0:T(4,128)(2,1)S(1)} %collective-permute-done), kind=kLoop, calls=%fused_computation.12 | loop fusion | flops 2109440 | bytes 2109440 | tf_op jit(solution)/shard_map/concatenate | solution.py:186
  10.2 2.0 %gather_fusion = bf16[256,1024]{1,0:T(8,128)(2,1)} fusion(bf16[515,1024]{1,0:T(8,128)(2,1)S(1)} %pad_maximum_fusion, s32[1024]{0:T(1024)S(1)} %pad_clamp_fusion), kind=kCustom, calls=%fused_computation | custom fusion | bytes 1049600 | tf_op jit(solution)/shard_map/jit(_take)/gather | solution.py:188
  12.2 1.2 select_convert_fusion
  13.4 0.0 copy-start.3
  13.4 0.0 copy-start.6
  13.5 0.6 multiply_reduce_fusion.1
  14.1 0.0 copy-done.5
  14.1 0.1 multiply_convert_fusion
  14.2 0.0 copy-done.2
  14.2 0.2 fusion.3
  14.4 0.2 fusion.2
  14.6 0.2 fusion.1
  14.8 0.1 constant_dynamic-update-slice_fusion.1
  14.9 1.9 %collective-permute-start.1 = (bf16[1,272,128]{2,1,0:T(8,128)(2,1)S(1)}, bf16[1,272,128]{2,1,0:T(8,128)(2,1)S(1)}, u32[]{:S(2)}, u32[]{:S(2)}) collective-permute-start(bf16[1,272,128]{2,1,0:T(8,128)(2,1)S(1)} %bitcast.29), channel_id=1, source_target_pairs={{0,16},{16,0},{32,48},{48,32},{64,80},{80,64},{96,112},{112,96},{1... | collective-permute-start | bytes 208904 | tf_op jit(solution)/shard_map/ppermute | solution.py:36
  16.8 4.3 %collective-permute-done.1 = bf16[1,272,128]{2,1,0:T(8,128)(2,1)S(1)} collective-permute-done((bf16[1,272,128]{2,1,0:T(8,128)(2,1)S(1)}, bf16[1,272,128]{2,1,0:T(8,128)(2,1)S(1)}, u32[]{:S(2)}, u32[]{:S(2)}) %collective-permute-start.1) | collective-permute-done | bytes 69664 | tf_op jit(solution)/shard_map/ppermute | solution.py:36
  21.1 1.9 %collective-permute-start.2 = (bf16[2,272,128]{2,1,0:T(8,128)(2,1)S(1)}, bf16[2,272,128]{2,1,0:T(8,128)(2,1)S(1)}, u32[]{:S(2)}, u32[]{:S(2)}) collective-permute-start(bf16[2,272,128]{2,1,0:T(8,128)(2,1)S(1)} %pad_maximum_fusion.8), channel_id=1, source_target_pairs={{0,32},{16,48},{32,0},{48,16},{64,96},{80,112},{96,64},{112,80},{1... | collective-permute-start | bytes 417800 | tf_op jit(solution)/shard_map/ppermute | solution.py:36
  23.0 7.5 %collective-permute-done.2 = bf16[2,272,128]{2,1,0:T(8,128)(2,1)S(1)} collective-permute-done((bf16[2,272,128]{2,1,0:T(8,128)(2,1)S(1)}, bf16[2,272,128]{2,1,0:T(8,128)(2,1)S(1)}, u32[]{:S(2)}, u32[]{:S(2)}) %collective-permute-start.2) | collective-permute-done | bytes 139296 | tf_op jit(solution)/shard_map/ppermute | solution.py:36
  30.6 0.7 pad_maximum_fusion.7
  31.3 3.2 %collective-permute-start.3 = (bf16[4,272,128]{2,1,0:T(8,128)(2,1)}, bf16[4,272,128]{2,1,0:T(8,128)(2,1)S(1)}, u32[]{:S(2)}, u32[]{:S(2)}) collective-permute-start(bf16[4,272,128]{2,1,0:T(8,128)(2,1)} %pad_maximum_fusion.7), channel_id=1, source_target_pairs={{0,64},{16,80},{32,96},{48,112},{64,0},{80,16},{96,32},{112,48},{1... | collective-permute-start | bytes 835592 | tf_op jit(solution)/shard_map/ppermute | solution.py:36
  34.6 0.1 and_select_fusion
  34.6 0.1 concatenate.34.shards_ref
  34.7 13.8 %collective-permute-done.3 = bf16[4,272,128]{2,1,0:T(8,128)(2,1)S(1)} collective-permute-done((bf16[4,272,128]{2,1,0:T(8,128)(2,1)}, bf16[4,272,128]{2,1,0:T(8,128)(2,1)S(1)}, u32[]{:S(2)}, u32[]{:S(2)}) %collective-permute-start.3) | collective-permute-done | bytes 278560 | tf_op jit(solution)/shard_map/ppermute | solution.py:36
  48.5 0.1 pad_maximum_fusion.6
  48.6 2.4 %collective-permute-start.4 = (bf16[8,272,128]{2,1,0:T(8,128)(2,1)S(1)}, bf16[8,272,128]{2,1,0:T(8,128)(2,1)S(1)}, u32[]{:S(2)}, u32[]{:S(2)}) collective-permute-start(bf16[8,272,128]{2,1,0:T(8,128)(2,1)S(1)} %pad_maximum_fusion.6), channel_id=1, source_target_pairs={{0,128},{16,144},{32,160},{48,176},{64,192},{80,208},{96,224},{112... | collective-permute-start | bytes 1671176 | tf_op jit(solution)/shard_map/ppermute | solution.py:45
  51.0 3.5 %collective-permute-start.5 = (bf16[8,272,128]{2,1,0:T(8,128)(2,1)S(1)}, bf16[8,272,128]{2,1,0:T(8,128)(2,1)S(1)}, u32[]{:S(2)}, u32[]{:S(2)}) collective-permute-start(bf16[8,272,128]{2,1,0:T(8,128)(2,1)S(1)} %pad_maximum_fusion.6), channel_id=1, source_target_pairs={{0,384},{16,400},{32,416},{48,432},{64,448},{80,464},{96,480},{112... | collective-permute-start | bytes 1671176 | tf_op jit(solution)/shard_map/ppermute | solution.py:45
  54.5 8.2 %collective-permute-done.4 = bf16[8,272,128]{2,1,0:T(8,128)(2,1)S(1)} collective-permute-done((bf16[8,272,128]{2,1,0:T(8,128)(2,1)S(1)}, bf16[8,272,128]{2,1,0:T(8,128)(2,1)S(1)}, u32[]{:S(2)}, u32[]{:S(2)}) %collective-permute-start.4) | collective-permute-done | bytes 557088 | tf_op jit(solution)/shard_map/ppermute | solution.py:45
  62.8 3.6 %collective-permute-start.6 = (bf16[4,272,128]{2,1,0:T(8,128)(2,1)S(1)}, bf16[4,272,128]{2,1,0:T(8,128)(2,1)S(1)}, u32[]{:S(2)}, u32[]{:S(2)}) collective-permute-start(bf16[4,272,128]{2,1,0:T(8,128)(2,1)S(1)} %slice.96), channel_id=1, source_target_pairs={{0,128},{16,144},{32,160},{48,176},{64,192},{80,208},{96,224},{112... | collective-permute-start | bytes 835592 | tf_op jit(solution)/shard_map/ppermute | solution.py:45
  66.4 0.0 collective-permute-done.5
  66.4 2.2 %collective-permute-start.7 = (bf16[4,272,128]{2,1,0:T(8,128)(2,1)S(1)}, bf16[4,272,128]{2,1,0:T(8,128)(2,1)S(1)}, u32[]{:S(2)}, u32[]{:S(2)}) collective-permute-start(bf16[4,272,128]{2,1,0:T(8,128)(2,1)S(1)} %slice.97), channel_id=1, source_target_pairs={{0,384},{16,400},{32,416},{48,432},{64,448},{80,464},{96,480},{112... | collective-permute-start | bytes 835592 | tf_op jit(solution)/shard_map/ppermute | solution.py:45
  68.7 0.1 constant_dynamic-update-slice_fusion.5
  68.8 0.1 constant_dynamic-update-slice_fusion.4
  68.9 2.3 %collective-permute-done.6 = bf16[4,272,128]{2,1,0:T(8,128)(2,1)S(1)} collective-permute-done((bf16[4,272,128]{2,1,0:T(8,128)(2,1)S(1)}, bf16[4,272,128]{2,1,0:T(8,128)(2,1)S(1)}, u32[]{:S(2)}, u32[]{:S(2)}) %collective-permute-start.6) | collective-permute-done | bytes 278560 | tf_op jit(solution)/shard_map/ppermute | solution.py:45
  71.2 4.9 %collective-permute-done.7 = bf16[4,272,128]{2,1,0:T(8,128)(2,1)S(1)} collective-permute-done((bf16[4,272,128]{2,1,0:T(8,128)(2,1)S(1)}, bf16[4,272,128]{2,1,0:T(8,128)(2,1)S(1)}, u32[]{:S(2)}, u32[]{:S(2)}) %collective-permute-start.7) | collective-permute-done | bytes 278560 | tf_op jit(solution)/shard_map/ppermute | solution.py:45
  76.1 1.4 fusion.35
  77.6 0.7 fusion.20
  78.2 0.1 add_select_fusion
  78.3 0.7 select_n.81.key_code_ref
  79.0 0.6 slice.103.own_code_ref
  79.6 17.7 %shard_map.113 = (bf16[2048,128]{1,0:T(8,128)(2,1)}, f32[2048,1]{1,0:T(8,128)}, f32[2048,1]{1,0:T(8,128)}, f32[64,128]{1,0:T(8,128)}, f32[64,128]{1,0:T(8,128)}, /*index=5*/f32[64,128]{1,0:T(8,128)}) custom-call(s32[32]{0:T(128)} %copy-done.7, bf16[2048,128]{1,0:T(8,128)(2,1)} %bitcast.28, bf16[2048,128]{1,0:T(8,128)(2,1)} %bitcast.27, ...), custom_call_target="tpu_custom_call" | custom-call | tf_op jit(solution)/shard_map/pallas_call | solution.py:152
  97.2 1.0 fusion.19
  98.2 1.0 convolution_add_fusion.1
  99.2 1.0 fusion
  100.1 4.3 %collective-permute-start.8 = (bf16[64,1024]{1,0:T(8,128)(2,1)S(1)}, bf16[64,1024]{1,0:T(8,128)(2,1)S(1)}, u32[]{:S(2)}, u32[]{:S(2)}) collective-permute-start(bf16[64,1024]{1,0:T(8,128)(2,1)S(1)} %fusion), channel_id=1, source_target_pairs={{0,2},{2,0},{4,6},{6,4},{8,10},{10,8},{12,14},{14,12},{1,3},{3,1},... | collective-permute-start | bytes 393224 | tf_op jit(solution)/shard_map/ppermute | solution.py:73
  104.4 2.9 %collective-permute-done.8 = bf16[64,1024]{1,0:T(8,128)(2,1)S(1)} collective-permute-done((bf16[64,1024]{1,0:T(8,128)(2,1)S(1)}, bf16[64,1024]{1,0:T(8,128)(2,1)S(1)}, u32[]{:S(2)}, u32[]{:S(2)}) %collective-permute-start.8) | collective-permute-done | bytes 131104 | tf_op jit(solution)/shard_map/ppermute | solution.py:73
  107.4 7.1 %collective-permute-start.9 = (bf16[64,1024]{1,0:T(8,128)(2,1)S(1)}, bf16[64,1024]{1,0:T(8,128)(2,1)S(1)}, u32[]{:S(2)}, u32[]{:S(2)}) collective-permute-start(bf16[64,1024]{1,0:T(8,128)(2,1)S(1)} %add_convert_fusion.2), channel_id=1, source_target_pairs={{0,4},{2,6},{4,0},{6,2},{8,12},{10,14},{12,8},{14,10},{1,5},{3,7},... | collective-permute-start | bytes 393224 | tf_op jit(solution)/shard_map/ppermute | solution.py:73
  114.5 4.3 %collective-permute-done.9 = bf16[64,1024]{1,0:T(8,128)(2,1)S(1)} collective-permute-done((bf16[64,1024]{1,0:T(8,128)(2,1)S(1)}, bf16[64,1024]{1,0:T(8,128)(2,1)S(1)}, u32[]{:S(2)}, u32[]{:S(2)}) %collective-permute-start.9) | collective-permute-done | bytes 131104 | tf_op jit(solution)/shard_map/ppermute | solution.py:73
  118.9 12.3 %collective-permute-start.10 = (bf16[64,1024]{1,0:T(8,128)(2,1)S(1)}, bf16[64,1024]{1,0:T(8,128)(2,1)S(1)}, u32[]{:S(2)}, u32[]{:S(2)}) collective-permute-start(bf16[64,1024]{1,0:T(8,128)(2,1)S(1)} %add_convert_fusion.1), channel_id=1, source_target_pairs={{0,8},{2,10},{4,12},{6,14},{8,0},{10,2},{12,4},{14,6},{1,9},{3,11}... | collective-permute-start | bytes 393224 | tf_op jit(solution)/shard_map/ppermute | solution.py:73
  131.2 0.1 sub.31
  131.3 2.8 %collective-permute-done.10 = bf16[64,1024]{1,0:T(8,128)(2,1)S(1)} collective-permute-done((bf16[64,1024]{1,0:T(8,128)(2,1)S(1)}, bf16[64,1024]{1,0:T(8,128)(2,1)S(1)}, u32[]{:S(2)}, u32[]{:S(2)}) %collective-permute-start.10) | collective-permute-done | bytes 131104 | tf_op jit(solution)/shard_map/ppermute | solution.py:73
  134.2 0.2 multiply_reduce_fusion
  134.3 0.8 multiply_add_fusion
  135.1 0.5 fusion.4
  135.6 1.9 %collective-permute-start.11 = (f32[3,1024]{1,0:T(4,128)S(1)}, f32[3,1024]{1,0:T(4,128)S(1)}, u32[]{:S(2)}, u32[]{:S(2)}) collective-permute-start(f32[3,1024]{1,0:T(4,128)S(1)} %fusion.4), channel_id=1, source_target_pairs={{16,0},{32,16},{48,32},{64,48},{80,64},{96,80},{112,96},{128,112},... | collective-permute-start | bytes 36872 | tf_op jit(solution)/shard_map/ppermute | solution.py:23
  137.5 1.4 slice_select_fusion
  138.9 3.5 %collective-permute-done.11 = f32[3,1024]{1,0:T(4,128)S(1)} collective-permute-done((f32[3,1024]{1,0:T(4,128)S(1)}, f32[3,1024]{1,0:T(4,128)S(1)}, u32[]{:S(2)}, u32[]{:S(2)}) %collective-permute-start.11) | collective-permute-done | bytes 12320 | tf_op jit(solution)/shard_map/ppermute | solution.py:23
  142.4 2.0 %add_convert_fusion = bf16[512,1024]{1,0:T(8,128)(2,1)} fusion(f32[3,1024]{1,0:T(4,128)S(1)} %collective-permute-done.11, f32[64,1024]{1,0:T(8,128)S(1)} %get-tuple-element.15, f32[64,1024]{1,0:T(8,128)S(1)} %get-tuple-element.16, f32[64,1024]{1,0:T(8,128)S(1)} %get-tuple-element.17, f32[64,1024]{1,0:T(8,128)S(1)} %get-tuple-element.14, s32[256]{0:T(256)S(1)} %sub.31), kind=kOutput, calls=%fused_computation.1 | convolution fusion | flops 1612578816 | bytes 2110464 | tf_op jit(solution)/shard_map/dot_general | solution.py:270
  (34 shorter events, 0.4 us)
Async XLA Ops:
  0.6 12.8 %copy-start = (bf16[1024,1024]{1,0:T(8,128)(2,1)S(1)}, bf16[1024,1024]{1,0:T(8,128)(2,1)}, u32[]{:S(2)}) copy-start(bf16[1024,1024]{1,0:T(8,128)(2,1)} %param.12) | copy-start | bytes 6291460
  1.5 7.2 %collective-permute-start = (bf16[3,1024]{1,0:T(4,128)(2,1)S(1)}, bf16[3,1024]{1,0:T(4,128)(2,1)S(1)}, u32[]{:S(2)}, u32[]{:S(2)}) collective-permute-start(bf16[3,1024]{1,0:T(4,128)(2,1)S(1)} %slice.133), channel_id=1, source_target_pairs={{0,16},{16,32},{32,48},{48,64},{64,80},{80,96},{96,112},{112,128},... | collective-permute-start | bytes 18440 | tf_op jit(solution)/shard_map/ppermute | solution.py:23
  12.2 1.9 %copy-start.5 = (f32[1024]{0:T(1024)S(1)}, f32[1024]{0:T(1024)}, u32[]{:S(2)}) copy-start(f32[1024]{0:T(1024)} %param.13) | copy-start | bytes 12292
  12.2 2.0 %copy-start.2 = (bf16[1024,128]{1,0:T(8,128)(2,1)S(1)}, bf16[1024,128]{1,0:T(8,128)(2,1)}, u32[]{:S(2)}) copy-start(bf16[1024,128]{1,0:T(8,128)(2,1)} %param.14) | copy-start | bytes 786436
  12.2 2.2 %copy-start.1 = (bf16[1024,128]{1,0:T(8,128)(2,1)S(1)}, bf16[1024,128]{1,0:T(8,128)(2,1)}, u32[]{:S(2)}) copy-start(bf16[1024,128]{1,0:T(8,128)(2,1)} %param.15) | copy-start | bytes 786436
  13.4 1.1 copy-start.3
  13.4 1.3 copy-start.6
  14.9 6.2 %collective-permute-start.1 = (bf16[1,272,128]{2,1,0:T(8,128)(2,1)S(1)}, bf16[1,272,128]{2,1,0:T(8,128)(2,1)S(1)}, u32[]{:S(2)}, u32[]{:S(2)}) collective-permute-start(bf16[1,272,128]{2,1,0:T(8,128)(2,1)S(1)} %bitcast.29), channel_id=1, source_target_pairs={{0,16},{16,0},{32,48},{48,32},{64,80},{80,64},{96,112},{112,96},{1... | collective-permute-start | bytes 208904 | tf_op jit(solution)/shard_map/ppermute | solution.py:36
  21.1 9.5 %collective-permute-start.2 = (bf16[2,272,128]{2,1,0:T(8,128)(2,1)S(1)}, bf16[2,272,128]{2,1,0:T(8,128)(2,1)S(1)}, u32[]{:S(2)}, u32[]{:S(2)}) collective-permute-start(bf16[2,272,128]{2,1,0:T(8,128)(2,1)S(1)} %pad_maximum_fusion.8), channel_id=1, source_target_pairs={{0,32},{16,48},{32,0},{48,16},{64,96},{80,112},{96,64},{112,80},{1... | collective-permute-start | bytes 417800 | tf_op jit(solution)/shard_map/ppermute | solution.py:36
  31.3 17.2 %collective-permute-start.3 = (bf16[4,272,128]{2,1,0:T(8,128)(2,1)}, bf16[4,272,128]{2,1,0:T(8,128)(2,1)S(1)}, u32[]{:S(2)}, u32[]{:S(2)}) collective-permute-start(bf16[4,272,128]{2,1,0:T(8,128)(2,1)} %pad_maximum_fusion.7), channel_id=1, source_target_pairs={{0,64},{16,80},{32,96},{48,112},{64,0},{80,16},{96,32},{112,48},{1... | collective-permute-start | bytes 835592 | tf_op jit(solution)/shard_map/ppermute | solution.py:36
  34.7 34.1 %copy-start.7 = (s32[32]{0:T(128)}, s32[32]{0:T(128)S(1)}, u32[]{:S(2)}) copy-start(s32[32]{0:T(128)S(1)} %concatenate.34.shards_ref) | copy-start | bytes 388
  48.6 14.2 %collective-permute-start.4 = (bf16[8,272,128]{2,1,0:T(8,128)(2,1)S(1)}, bf16[8,272,128]{2,1,0:T(8,128)(2,1)S(1)}, u32[]{:S(2)}, u32[]{:S(2)}) collective-permute-start(bf16[8,272,128]{2,1,0:T(8,128)(2,1)S(1)} %pad_maximum_fusion.6), channel_id=1, source_target_pairs={{0,128},{16,144},{32,160},{48,176},{64,192},{80,208},{96,224},{112... | collective-permute-start | bytes 1671176 | tf_op jit(solution)/shard_map/ppermute | solution.py:45
  51.0 15.4 %collective-permute-start.5 = (bf16[8,272,128]{2,1,0:T(8,128)(2,1)S(1)}, bf16[8,272,128]{2,1,0:T(8,128)(2,1)S(1)}, u32[]{:S(2)}, u32[]{:S(2)}) collective-permute-start(bf16[8,272,128]{2,1,0:T(8,128)(2,1)S(1)} %pad_maximum_fusion.6), channel_id=1, source_target_pairs={{0,384},{16,400},{32,416},{48,432},{64,448},{80,464},{96,480},{112... | collective-permute-start | bytes 1671176 | tf_op jit(solution)/shard_map/ppermute | solution.py:45
  62.8 8.4 %collective-permute-start.6 = (bf16[4,272,128]{2,1,0:T(8,128)(2,1)S(1)}, bf16[4,272,128]{2,1,0:T(8,128)(2,1)S(1)}, u32[]{:S(2)}, u32[]{:S(2)}) collective-permute-start(bf16[4,272,128]{2,1,0:T(8,128)(2,1)S(1)} %slice.96), channel_id=1, source_target_pairs={{0,128},{16,144},{32,160},{48,176},{64,192},{80,208},{96,224},{112... | collective-permute-start | bytes 835592 | tf_op jit(solution)/shard_map/ppermute | solution.py:45
  66.4 9.7 %collective-permute-start.7 = (bf16[4,272,128]{2,1,0:T(8,128)(2,1)S(1)}, bf16[4,272,128]{2,1,0:T(8,128)(2,1)S(1)}, u32[]{:S(2)}, u32[]{:S(2)}) collective-permute-start(bf16[4,272,128]{2,1,0:T(8,128)(2,1)S(1)} %slice.97), channel_id=1, source_target_pairs={{0,384},{16,400},{32,416},{48,432},{64,448},{80,464},{96,480},{112... | collective-permute-start | bytes 835592 | tf_op jit(solution)/shard_map/ppermute | solution.py:45
  77.6 21.6 %copy-start.4 = (bf16[1024,128]{1,0:T(8,128)(2,1)S(1)}, bf16[1024,128]{1,0:T(8,128)(2,1)}, u32[]{:S(2)}) copy-start(bf16[1024,128]{1,0:T(8,128)(2,1)} %param.16) | copy-start | bytes 786436
  100.1 7.2 %collective-permute-start.8 = (bf16[64,1024]{1,0:T(8,128)(2,1)S(1)}, bf16[64,1024]{1,0:T(8,128)(2,1)S(1)}, u32[]{:S(2)}, u32[]{:S(2)}) collective-permute-start(bf16[64,1024]{1,0:T(8,128)(2,1)S(1)} %fusion), channel_id=1, source_target_pairs={{0,2},{2,0},{4,6},{6,4},{8,10},{10,8},{12,14},{14,12},{1,3},{3,1},... | collective-permute-start | bytes 393224 | tf_op jit(solution)/shard_map/ppermute | solution.py:73
  107.4 11.5 %collective-permute-start.9 = (bf16[64,1024]{1,0:T(8,128)(2,1)S(1)}, bf16[64,1024]{1,0:T(8,128)(2,1)S(1)}, u32[]{:S(2)}, u32[]{:S(2)}) collective-permute-start(bf16[64,1024]{1,0:T(8,128)(2,1)S(1)} %add_convert_fusion.2), channel_id=1, source_target_pairs={{0,4},{2,6},{4,0},{6,2},{8,12},{10,14},{12,8},{14,10},{1,5},{3,7},... | collective-permute-start | bytes 393224 | tf_op jit(solution)/shard_map/ppermute | solution.py:73
  118.9 15.3 %collective-permute-start.10 = (bf16[64,1024]{1,0:T(8,128)(2,1)S(1)}, bf16[64,1024]{1,0:T(8,128)(2,1)S(1)}, u32[]{:S(2)}, u32[]{:S(2)}) collective-permute-start(bf16[64,1024]{1,0:T(8,128)(2,1)S(1)} %add_convert_fusion.1), channel_id=1, source_target_pairs={{0,8},{2,10},{4,12},{6,14},{8,0},{10,2},{12,4},{14,6},{1,9},{3,11}... | collective-permute-start | bytes 393224 | tf_op jit(solution)/shard_map/ppermute | solution.py:73
  135.6 6.8 %collective-permute-start.11 = (f32[3,1024]{1,0:T(4,128)S(1)}, f32[3,1024]{1,0:T(4,128)S(1)}, u32[]{:S(2)}, u32[]{:S(2)}) collective-permute-start(f32[3,1024]{1,0:T(4,128)S(1)} %fusion.4), channel_id=1, source_target_pairs={{16,0},{32,16},{48,32},{64,48},{80,64},{96,80},{112,96},{128,112},... | collective-permute-start | bytes 36872 | tf_op jit(solution)/shard_map/ppermute | solution.py:23

commit v10 on v9

--- a/solution.py
+++ b/solution.py
@@ -10,8 +10,8 @@
 D = 1024
 HD = 128
 KCONV = 4
-QBLOCK = 256
-BLOCKS_PER_STEP = 4
+QBLOCK = 512
+BLOCKS_PER_STEP = 8
 
 
 masked_score = -1e30

time: 145 us -> 146 us (level)
  no operation moved by 1% of the time
where the time goes in v10:
time: 146 us; the launch traced here: 145 us
  waiting for transfers between devices  54.6 us (37%)
  starting transfers between devices  49 us (34%)
  Pallas kernels  18.5 us (13%)
  matrix products  7.34 us (5%)
  local copies, waits for them, and re-layouts  7.12 us (5%)
  other arithmetic  6.96 us (5%)
  between operations  1.71 us (1%)
    ppermute x3, waiting for transfers between devices, gather_blocks(): other = lax.ppermute(held, axis, [(i, i ^ step) for i in range(devices)])  25.6 us
    ppermute x3, starting transfers between devices, summed_over(): got = lax.ppermute(sent, axis, [(i, i ^ step) for i in range(devices)])  23.7 us
    pallas_call x1, Pallas kernels, attention_all(): pl.pallas_call(forward_kernel, grid_spec=grid_spec, out_shape=[jax.ShapeD...  18.5 us
    ppermute x4, waiting for transfers between devices, shifted(): lax.ppermute(array, axis, [(i, (i + by) % devices) for i in range(devices)])  15.4 us
    ppermute x4, starting transfers between devices, shifted(): lax.ppermute(array, axis, [(i, (i + by) % devices) for i in range(devices)])  11.7 us
    ppermute x3, waiting for transfers between devices, summed_over(): got = lax.ppermute(sent, axis, [(i, i ^ step) for i in range(devices)])  10.1 us
    ppermute x3, starting transfers between devices, gather_blocks(): other = lax.ppermute(held, axis, [(i, i ^ step) for i in range(devices)])  7.05 us
    ppermute x2, starting transfers between devices, passed_along(): return lax.ppermute(array, axis, pairs)  6.6 us
  transfers between devices with their start and end apart: 12, of which 10 were waited for; matrix products, arithmetic and copies ran while one was open for 3% of the time, Pallas kernels for 0%

profile of v10, /device:TPU:30, one launch (start us, length us, event | category | flops | bytes accessed | tf_op | source)
XLA Modules:
  0.0 145.3 jit_solution(6360751182777590797)
XLA Ops:
  0.6 0.0 copy-start
  0.6 0.9 slice.133
  1.5 4.7 %collective-permute-start = (bf16[3,1024]{1,0:T(4,128)(2,1)S(1)}, bf16[3,1024]{1,0:T(4,128)(2,1)S(1)}, u32[]{:S(2)}, u32[]{:S(2)}) collective-permute-start(bf16[3,1024]{1,0:T(4,128)(2,1)S(1)} %slice.133), channel_id=1, source_target_pairs={{0,16},{16,32},{32,48},{48,64},{64,80},{80,96},{96,112},{112,128},... | collective-permute-start | bytes 18440 | tf_op jit(solution)/shard_map/ppermute | solution.py:23
  6.2 0.7 iota_subtract_fusion
  7.0 0.1 add.182
  7.0 0.1 add.179
  7.1 0.9 fusion.36
  8.7 0.0 collective-permute-done
  8.7 1.5 %pad_maximum_fusion = bf16[515,1024]{1,0:T(8,128)(2,1)S(1)} fusion(bf16[512,1024]{1,0:T(8,128)(2,1)} %param.10, bf16[3,1024]{1,0:T(4,128)(2,1)S(1)} %collective-permute-done), kind=kLoop, calls=%fused_computation.12 | loop fusion | flops 2109440 | bytes 2109440 | tf_op jit(solution)/shard_map/concatenate | solution.py:186
  10.2 2.0 %gather_fusion = bf16[256,1024]{1,0:T(8,128)(2,1)} fusion(bf16[515,1024]{1,0:T(8,128)(2,1)S(1)} %pad_maximum_fusion, s32[1024]{0:T(1024)S(1)} %pad_clamp_fusion), kind=kCustom, calls=%fused_computation | custom fusion | bytes 1049600 | tf_op jit(solution)/shard_map/jit(_take)/gather | solution.py:188
  12.2 1.2 select_convert_fusion
  13.4 0.0 copy-start.3
  13.4 0.0 copy-start.6
  13.5 0.6 multiply_reduce_fusion.1
  14.1 0.0 copy-done.5
  14.1 0.1 multiply_convert_fusion
  14.2 0.0 copy-done.2
  14.2 0.2 fusion.3
  14.4 0.2 fusion.2
  14.6 0.2 fusion.1
  14.8 0.1 constant_dynamic-update-slice_fusion.1
  14.9 1.9 %collective-permute-start.1 = (bf16[1,272,128]{2,1,0:T(8,128)(2,1)S(1)}, bf16[1,272,128]{2,1,0:T(8,128)(2,1)S(1)}, u32[]{:S(2)}, u32[]{:S(2)}) collective-permute-start(bf16[1,272,128]{2,1,0:T(8,128)(2,1)S(1)} %bitcast.29), channel_id=1, source_target_pairs={{0,16},{16,0},{32,48},{48,32},{64,80},{80,64},{96,112},{112,96},{1... | collective-permute-start | bytes 208904 | tf_op jit(solution)/shard_map/ppermute | solution.py:36
  16.8 4.3 %collective-permute-done.1 = bf16[1,272,128]{2,1,0:T(8,128)(2,1)S(1)} collective-permute-done((bf16[1,272,128]{2,1,0:T(8,128)(2,1)S(1)}, bf16[1,272,128]{2,1,0:T(8,128)(2,1)S(1)}, u32[]{:S(2)}, u32[]{:S(2)}) %collective-permute-start.1) | collective-permute-done | bytes 69664 | tf_op jit(solution)/shard_map/ppermute | solution.py:36
  21.1 1.9 %collective-permute-start.2 = (bf16[2,272,128]{2,1,0:T(8,128)(2,1)S(1)}, bf16[2,272,128]{2,1,0:T(8,128)(2,1)S(1)}, u32[]{:S(2)}, u32[]{:S(2)}) collective-permute-start(bf16[2,272,128]{2,1,0:T(8,128)(2,1)S(1)} %pad_maximum_fusion.8), channel_id=1, source_target_pairs={{0,32},{16,48},{32,0},{48,16},{64,96},{80,112},{96,64},{112,80},{1... | collective-permute-start | bytes 417800 | tf_op jit(solution)/shard_map/ppermute | solution.py:36
  23.0 7.5 %collective-permute-done.2 = bf16[2,272,128]{2,1,0:T(8,128)(2,1)S(1)} collective-permute-done((bf16[2,272,128]{2,1,0:T(8,128)(2,1)S(1)}, bf16[2,272,128]{2,1,0:T(8,128)(2,1)S(1)}, u32[]{:S(2)}, u32[]{:S(2)}) %collective-permute-start.2) | collective-permute-done | bytes 139296 | tf_op jit(solution)/shard_map/ppermute | solution.py:36
  30.6 0.7 pad_maximum_fusion.7
  31.3 3.2 %collective-permute-start.3 = (bf16[4,272,128]{2,1,0:T(8,128)(2,1)}, bf16[4,272,128]{2,1,0:T(8,128)(2,1)S(1)}, u32[]{:S(2)}, u32[]{:S(2)}) collective-permute-start(bf16[4,272,128]{2,1,0:T(8,128)(2,1)} %pad_maximum_fusion.7), channel_id=1, source_target_pairs={{0,64},{16,80},{32,96},{48,112},{64,0},{80,16},{96,32},{112,48},{1... | collective-permute-start | bytes 835592 | tf_op jit(solution)/shard_map/ppermute | solution.py:36
  34.6 0.1 and_select_fusion
  34.6 0.1 concatenate.34.shards_ref
  34.7 13.8 %collective-permute-done.3 = bf16[4,272,128]{2,1,0:T(8,128)(2,1)S(1)} collective-permute-done((bf16[4,272,128]{2,1,0:T(8,128)(2,1)}, bf16[4,272,128]{2,1,0:T(8,128)(2,1)S(1)}, u32[]{:S(2)}, u32[]{:S(2)}) %collective-permute-start.3) | collective-permute-done | bytes 278560 | tf_op jit(solution)/shard_map/ppermute | solution.py:36
  48.5 0.1 pad_maximum_fusion.6
  48.6 2.4 %collective-permute-start.4 = (bf16[8,272,128]{2,1,0:T(8,128)(2,1)S(1)}, bf16[8,272,128]{2,1,0:T(8,128)(2,1)S(1)}, u32[]{:S(2)}, u32[]{:S(2)}) collective-permute-start(bf16[8,272,128]{2,1,0:T(8,128)(2,1)S(1)} %pad_maximum_fusion.6), channel_id=1, source_target_pairs={{0,128},{16,144},{32,160},{48,176},{64,192},{80,208},{96,224},{112... | collective-permute-start | bytes 1671176 | tf_op jit(solution)/shard_map/ppermute | solution.py:45
  51.0 3.5 %collective-permute-start.5 = (bf16[8,272,128]{2,1,0:T(8,128)(2,1)S(1)}, bf16[8,272,128]{2,1,0:T(8,128)(2,1)S(1)}, u32[]{:S(2)}, u32[]{:S(2)}) collective-permute-start(bf16[8,272,128]{2,1,0:T(8,128)(2,1)S(1)} %pad_maximum_fusion.6), channel_id=1, source_target_pairs={{0,384},{16,400},{32,416},{48,432},{64,448},{80,464},{96,480},{112... | collective-permute-start | bytes 1671176 | tf_op jit(solution)/shard_map/ppermute | solution.py:45
  54.5 8.2 %collective-permute-done.4 = bf16[8,272,128]{2,1,0:T(8,128)(2,1)S(1)} collective-permute-done((bf16[8,272,128]{2,1,0:T(8,128)(2,1)S(1)}, bf16[8,272,128]{2,1,0:T(8,128)(2,1)S(1)}, u32[]{:S(2)}, u32[]{:S(2)}) %collective-permute-start.4) | collective-permute-done | bytes 557088 | tf_op jit(solution)/shard_map/ppermute | solution.py:45
  62.8 3.6 %collective-permute-start.6 = (bf16[4,272,128]{2,1,0:T(8,128)(2,1)S(1)}, bf16[4,272,128]{2,1,0:T(8,128)(2,1)S(1)}, u32[]{:S(2)}, u32[]{:S(2)}) collective-permute-start(bf16[4,272,128]{2,1,0:T(8,128)(2,1)S(1)} %slice.96), channel_id=1, source_target_pairs={{0,128},{16,144},{32,160},{48,176},{64,192},{80,208},{96,224},{112... | collective-permute-start | bytes 835592 | tf_op jit(solution)/shard_map/ppermute | solution.py:45
  66.4 0.0 collective-permute-done.5
  66.4 2.2 %collective-permute-start.7 = (bf16[4,272,128]{2,1,0:T(8,128)(2,1)S(1)}, bf16[4,272,128]{2,1,0:T(8,128)(2,1)S(1)}, u32[]{:S(2)}, u32[]{:S(2)}) collective-permute-start(bf16[4,272,128]{2,1,0:T(8,128)(2,1)S(1)} %slice.97), channel_id=1, source_target_pairs={{0,384},{16,400},{32,416},{48,432},{64,448},{80,464},{96,480},{112... | collective-permute-start | bytes 835592 | tf_op jit(solution)/shard_map/ppermute | solution.py:45
  68.7 0.1 constant_dynamic-update-slice_fusion.5
  68.8 0.1 constant_dynamic-update-slice_fusion.4
  68.9 2.3 %collective-permute-done.6 = bf16[4,272,128]{2,1,0:T(8,128)(2,1)S(1)} collective-permute-done((bf16[4,272,128]{2,1,0:T(8,128)(2,1)S(1)}, bf16[4,272,128]{2,1,0:T(8,128)(2,1)S(1)}, u32[]{:S(2)}, u32[]{:S(2)}) %collective-permute-start.6) | collective-permute-done | bytes 278560 | tf_op jit(solution)/shard_map/ppermute | solution.py:45
  71.2 4.9 %collective-permute-done.7 = bf16[4,272,128]{2,1,0:T(8,128)(2,1)S(1)} collective-permute-done((bf16[4,272,128]{2,1,0:T(8,128)(2,1)S(1)}, bf16[4,272,128]{2,1,0:T(8,128)(2,1)S(1)}, u32[]{:S(2)}, u32[]{:S(2)}) %collective-permute-start.7) | collective-permute-done | bytes 278560 | tf_op jit(solution)/shard_map/ppermute | solution.py:45
  76.1 1.4 fusion.35
  77.6 0.7 fusion.20
  78.2 0.1 add_select_fusion
  78.3 0.7 select_n.81.key_code_ref
  79.0 0.6 slice.103.own_code_ref
  79.6 18.5 %shard_map.113 = (bf16[2048,128]{1,0:T(8,128)(2,1)}, f32[2048,1]{1,0:T(8,128)}, f32[2048,1]{1,0:T(8,128)}, f32[64,128]{1,0:T(8,128)}, f32[64,128]{1,0:T(8,128)}, /*index=5*/f32[64,128]{1,0:T(8,128)}) custom-call(s32[32]{0:T(128)} %copy-done.7, bf16[2048,128]{1,0:T(8,128)(2,1)} %bitcast.28, bf16[2048,128]{1,0:T(8,128)(2,1)} %bitcast.27, ...), custom_call_target="tpu_custom_call" | custom-call | tf_op jit(solution)/shard_map/pallas_call | solution.py:152
  98.0 1.0 fusion.19
  99.0 1.0 convolution_add_fusion.1
  100.0 1.0 fusion
  101.0 4.3 %collective-permute-start.8 = (bf16[64,1024]{1,0:T(8,128)(2,1)S(1)}, bf16[64,1024]{1,0:T(8,128)(2,1)S(1)}, u32[]{:S(2)}, u32[]{:S(2)}) collective-permute-start(bf16[64,1024]{1,0:T(8,128)(2,1)S(1)} %fusion), channel_id=1, source_target_pairs={{0,2},{2,0},{4,6},{6,4},{8,10},{10,8},{12,14},{14,12},{1,3},{3,1},... | collective-permute-start | bytes 393224 | tf_op jit(solution)/shard_map/ppermute | solution.py:73
  105.2 2.9 %collective-permute-done.8 = bf16[64,1024]{1,0:T(8,128)(2,1)S(1)} collective-permute-done((bf16[64,1024]{1,0:T(8,128)(2,1)S(1)}, bf16[64,1024]{1,0:T(8,128)(2,1)S(1)}, u32[]{:S(2)}, u32[]{:S(2)}) %collective-permute-start.8) | collective-permute-done | bytes 131104 | tf_op jit(solution)/shard_map/ppermute | solution.py:73
  108.2 7.1 %collective-permute-start.9 = (bf16[64,1024]{1,0:T(8,128)(2,1)S(1)}, bf16[64,1024]{1,0:T(8,128)(2,1)S(1)}, u32[]{:S(2)}, u32[]{:S(2)}) collective-permute-start(bf16[64,1024]{1,0:T(8,128)(2,1)S(1)} %add_convert_fusion.2), channel_id=1, source_target_pairs={{0,4},{2,6},{4,0},{6,2},{8,12},{10,14},{12,8},{14,10},{1,5},{3,7},... | collective-permute-start | bytes 393224 | tf_op jit(solution)/shard_map/ppermute | solution.py:73
  115.3 4.3 %collective-permute-done.9 = bf16[64,1024]{1,0:T(8,128)(2,1)S(1)} collective-permute-done((bf16[64,1024]{1,0:T(8,128)(2,1)S(1)}, bf16[64,1024]{1,0:T(8,128)(2,1)S(1)}, u32[]{:S(2)}, u32[]{:S(2)}) %collective-permute-start.9) | collective-permute-done | bytes 131104 | tf_op jit(solution)/shard_map/ppermute | solution.py:73
  119.7 12.3 %collective-permute-start.10 = (bf16[64,1024]{1,0:T(8,128)(2,1)S(1)}, bf16[64,1024]{1,0:T(8,128)(2,1)S(1)}, u32[]{:S(2)}, u32[]{:S(2)}) collective-permute-start(bf16[64,1024]{1,0:T(8,128)(2,1)S(1)} %add_convert_fusion.1), channel_id=1, source_target_pairs={{0,8},{2,10},{4,12},{6,14},{8,0},{10,2},{12,4},{14,6},{1,9},{3,11}... | collective-permute-start | bytes 393224 | tf_op jit(solution)/shard_map/ppermute | solution.py:73
  132.0 0.1 sub.31
  132.1 2.8 %collective-permute-done.10 = bf16[64,1024]{1,0:T(8,128)(2,1)S(1)} collective-permute-done((bf16[64,1024]{1,0:T(8,128)(2,1)S(1)}, bf16[64,1024]{1,0:T(8,128)(2,1)S(1)}, u32[]{:S(2)}, u32[]{:S(2)}) %collective-permute-start.10) | collective-permute-done | bytes 131104 | tf_op jit(solution)/shard_map/ppermute | solution.py:73
  135.0 0.2 multiply_reduce_fusion
  135.1 0.8 multiply_add_fusion
  136.0 0.5 fusion.4
  136.4 1.9 %collective-permute-start.11 = (f32[3,1024]{1,0:T(4,128)S(1)}, f32[3,1024]{1,0:T(4,128)S(1)}, u32[]{:S(2)}, u32[]{:S(2)}) collective-permute-start(f32[3,1024]{1,0:T(4,128)S(1)} %fusion.4), channel_id=1, source_target_pairs={{16,0},{32,16},{48,32},{64,48},{80,64},{96,80},{112,96},{128,112},... | collective-permute-start | bytes 36872 | tf_op jit(solution)/shard_map/ppermute | solution.py:23
  138.3 1.4 slice_select_fusion
  139.7 3.5 %collective-permute-done.11 = f32[3,1024]{1,0:T(4,128)S(1)} collective-permute-done((f32[3,1024]{1,0:T(4,128)S(1)}, f32[3,1024]{1,0:T(4,128)S(1)}, u32[]{:S(2)}, u32[]{:S(2)}) %collective-permute-start.11) | collective-permute-done | bytes 12320 | tf_op jit(solution)/shard_map/ppermute | solution.py:23
  143.3 2.0 %add_convert_fusion = bf16[512,1024]{1,0:T(8,128)(2,1)} fusion(f32[3,1024]{1,0:T(4,128)S(1)} %collective-permute-done.11, f32[64,1024]{1,0:T(8,128)S(1)} %get-tuple-element.15, f32[64,1024]{1,0:T(8,128)S(1)} %get-tuple-element.16, f32[64,1024]{1,0:T(8,128)S(1)} %get-tuple-element.17, f32[64,1024]{1,0:T(8,128)S(1)} %get-tuple-element.14, s32[256]{0:T(256)S(1)} %sub.31), kind=kOutput, calls=%fused_computation.1 | convolution fusion | flops 1612578816 | bytes 2110464 | tf_op jit(solution)/shard_map/dot_general | solution.py:270
  (34 shorter events, 0.4 us)
Async XLA Ops:
  0.6 12.8 %copy-start = (bf16[1024,1024]{1,0:T(8,128)(2,1)S(1)}, bf16[1024,1024]{1,0:T(8,128)(2,1)}, u32[]{:S(2)}) copy-start(bf16[1024,1024]{1,0:T(8,128)(2,1)} %param.12) | copy-start | bytes 6291460
  1.5 7.2 %collective-permute-start = (bf16[3,1024]{1,0:T(4,128)(2,1)S(1)}, bf16[3,1024]{1,0:T(4,128)(2,1)S(1)}, u32[]{:S(2)}, u32[]{:S(2)}) collective-permute-start(bf16[3,1024]{1,0:T(4,128)(2,1)S(1)} %slice.133), channel_id=1, source_target_pairs={{0,16},{16,32},{32,48},{48,64},{64,80},{80,96},{96,112},{112,128},... | collective-permute-start | bytes 18440 | tf_op jit(solution)/shard_map/ppermute | solution.py:23
  12.2 1.9 %copy-start.5 = (f32[1024]{0:T(1024)S(1)}, f32[1024]{0:T(1024)}, u32[]{:S(2)}) copy-start(f32[1024]{0:T(1024)} %param.13) | copy-start | bytes 12292
  12.2 2.0 %copy-start.2 = (bf16[1024,128]{1,0:T(8,128)(2,1)S(1)}, bf16[1024,128]{1,0:T(8,128)(2,1)}, u32[]{:S(2)}) copy-start(bf16[1024,128]{1,0:T(8,128)(2,1)} %param.14) | copy-start | bytes 786436
  12.2 2.2 %copy-start.1 = (bf16[1024,128]{1,0:T(8,128)(2,1)S(1)}, bf16[1024,128]{1,0:T(8,128)(2,1)}, u32[]{:S(2)}) copy-start(bf16[1024,128]{1,0:T(8,128)(2,1)} %param.15) | copy-start | bytes 786436
  13.4 1.1 copy-start.3
  13.4 1.3 copy-start.6
  14.9 6.2 %collective-permute-start.1 = (bf16[1,272,128]{2,1,0:T(8,128)(2,1)S(1)}, bf16[1,272,128]{2,1,0:T(8,128)(2,1)S(1)}, u32[]{:S(2)}, u32[]{:S(2)}) collective-permute-start(bf16[1,272,128]{2,1,0:T(8,128)(2,1)S(1)} %bitcast.29), channel_id=1, source_target_pairs={{0,16},{16,0},{32,48},{48,32},{64,80},{80,64},{96,112},{112,96},{1... | collective-permute-start | bytes 208904 | tf_op jit(solution)/shard_map/ppermute | solution.py:36
  21.1 9.5 %collective-permute-start.2 = (bf16[2,272,128]{2,1,0:T(8,128)(2,1)S(1)}, bf16[2,272,128]{2,1,0:T(8,128)(2,1)S(1)}, u32[]{:S(2)}, u32[]{:S(2)}) collective-permute-start(bf16[2,272,128]{2,1,0:T(8,128)(2,1)S(1)} %pad_maximum_fusion.8), channel_id=1, source_target_pairs={{0,32},{16,48},{32,0},{48,16},{64,96},{80,112},{96,64},{112,80},{1... | collective-permute-start | bytes 417800 | tf_op jit(solution)/shard_map/ppermute | solution.py:36
  31.3 17.2 %collective-permute-start.3 = (bf16[4,272,128]{2,1,0:T(8,128)(2,1)}, bf16[4,272,128]{2,1,0:T(8,128)(2,1)S(1)}, u32[]{:S(2)}, u32[]{:S(2)}) collective-permute-start(bf16[4,272,128]{2,1,0:T(8,128)(2,1)} %pad_maximum_fusion.7), channel_id=1, source_target_pairs={{0,64},{16,80},{32,96},{48,112},{64,0},{80,16},{96,32},{112,48},{1... | collective-permute-start | bytes 835592 | tf_op jit(solution)/shard_map/ppermute | solution.py:36
  34.7 34.1 %copy-start.7 = (s32[32]{0:T(128)}, s32[32]{0:T(128)S(1)}, u32[]{:S(2)}) copy-start(s32[32]{0:T(128)S(1)} %concatenate.34.shards_ref) | copy-start | bytes 388
  48.6 14.2 %collective-permute-start.4 = (bf16[8,272,128]{2,1,0:T(8,128)(2,1)S(1)}, bf16[8,272,128]{2,1,0:T(8,128)(2,1)S(1)}, u32[]{:S(2)}, u32[]{:S(2)}) collective-permute-start(bf16[8,272,128]{2,1,0:T(8,128)(2,1)S(1)} %pad_maximum_fusion.6), channel_id=1, source_target_pairs={{0,128},{16,144},{32,160},{48,176},{64,192},{80,208},{96,224},{112... | collective-permute-start | bytes 1671176 | tf_op jit(solution)/shard_map/ppermute | solution.py:45
  51.0 15.4 %collective-permute-start.5 = (bf16[8,272,128]{2,1,0:T(8,128)(2,1)S(1)}, bf16[8,272,128]{2,1,0:T(8,128)(2,1)S(1)}, u32[]{:S(2)}, u32[]{:S(2)}) collective-permute-start(bf16[8,272,128]{2,1,0:T(8,128)(2,1)S(1)} %pad_maximum_fusion.6), channel_id=1, source_target_pairs={{0,384},{16,400},{32,416},{48,432},{64,448},{80,464},{96,480},{112... | collective-permute-start | bytes 1671176 | tf_op jit(solution)/shard_map/ppermute | solution.py:45
  62.8 8.4 %collective-permute-start.6 = (bf16[4,272,128]{2,1,0:T(8,128)(2,1)S(1)}, bf16[4,272,128]{2,1,0:T(8,128)(2,1)S(1)}, u32[]{:S(2)}, u32[]{:S(2)}) collective-permute-start(bf16[4,272,128]{2,1,0:T(8,128)(2,1)S(1)} %slice.96), channel_id=1, source_target_pairs={{0,128},{16,144},{32,160},{48,176},{64,192},{80,208},{96,224},{112... | collective-permute-start | bytes 835592 | tf_op jit(solution)/shard_map/ppermute | solution.py:45
  66.4 9.7 %collective-permute-start.7 = (bf16[4,272,128]{2,1,0:T(8,128)(2,1)S(1)}, bf16[4,272,128]{2,1,0:T(8,128)(2,1)S(1)}, u32[]{:S(2)}, u32[]{:S(2)}) collective-permute-start(bf16[4,272,128]{2,1,0:T(8,128)(2,1)S(1)} %slice.97), channel_id=1, source_target_pairs={{0,384},{16,400},{32,416},{48,432},{64,448},{80,464},{96,480},{112... | collective-permute-start | bytes 835592 | tf_op jit(solution)/shard_map/ppermute | solution.py:45
  77.6 22.4 %copy-start.4 = (bf16[1024,128]{1,0:T(8,128)(2,1)S(1)}, bf16[1024,128]{1,0:T(8,128)(2,1)}, u32[]{:S(2)}) copy-start(bf16[1024,128]{1,0:T(8,128)(2,1)} %param.16) | copy-start | bytes 786436
  101.0 7.2 %collective-permute-start.8 = (bf16[64,1024]{1,0:T(8,128)(2,1)S(1)}, bf16[64,1024]{1,0:T(8,128)(2,1)S(1)}, u32[]{:S(2)}, u32[]{:S(2)}) collective-permute-start(bf16[64,1024]{1,0:T(8,128)(2,1)S(1)} %fusion), channel_id=1, source_target_pairs={{0,2},{2,0},{4,6},{6,4},{8,10},{10,8},{12,14},{14,12},{1,3},{3,1},... | collective-permute-start | bytes 393224 | tf_op jit(solution)/shard_map/ppermute | solution.py:73
  108.2 11.5 %collective-permute-start.9 = (bf16[64,1024]{1,0:T(8,128)(2,1)S(1)}, bf16[64,1024]{1,0:T(8,128)(2,1)S(1)}, u32[]{:S(2)}, u32[]{:S(2)}) collective-permute-start(bf16[64,1024]{1,0:T(8,128)(2,1)S(1)} %add_convert_fusion.2), channel_id=1, source_target_pairs={{0,4},{2,6},{4,0},{6,2},{8,12},{10,14},{12,8},{14,10},{1,5},{3,7},... | collective-permute-start | bytes 393224 | tf_op jit(solution)/shard_map/ppermute | solution.py:73
  119.7 15.3 %collective-permute-start.10 = (bf16[64,1024]{1,0:T(8,128)(2,1)S(1)}, bf16[64,1024]{1,0:T(8,128)(2,1)S(1)}, u32[]{:S(2)}, u32[]{:S(2)}) collective-permute-start(bf16[64,1024]{1,0:T(8,128)(2,1)S(1)} %add_convert_fusion.1), channel_id=1, source_target_pairs={{0,8},{2,10},{4,12},{6,14},{8,0},{10,2},{12,4},{14,6},{1,9},{3,11}... | collective-permute-start | bytes 393224 | tf_op jit(solution)/shard_map/ppermute | solution.py:73
  136.4 6.8 %collective-permute-start.11 = (f32[3,1024]{1,0:T(4,128)S(1)}, f32[3,1024]{1,0:T(4,128)S(1)}, u32[]{:S(2)}, u32[]{:S(2)}) collective-permute-start(f32[3,1024]{1,0:T(4,128)S(1)} %fusion.4), channel_id=1, source_target_pairs={{16,0},{32,16},{48,32},{64,48},{80,64},{96,80},{112,96},{128,112},... | collective-permute-start | bytes 36872 | tf_op jit(solution)/shard_map/ppermute | solution.py:23

commit v11 on v9

--- a/solution.py
+++ b/solution.py
@@ -231,13 +231,10 @@
 
     contract = (((1,), (1,)), ((), ()))
     partial_normed = lax.dot_general(
-        query_grad_rows, query_weight, contract, preferred_element_type=jnp.float32
-    )
-    partial_normed = partial_normed + lax.dot_general(
-        key_grad_rows, key_weight, contract, preferred_element_type=jnp.float32
-    )
-    partial_normed = partial_normed + lax.dot_general(
-        value_grad_rows, value_weight, contract, preferred_element_type=jnp.float32
+        jnp.concatenate([query_grad_rows, key_grad_rows, value_grad_rows], axis=1),
+        jnp.concatenate([query_weight, key_weight, value_weight], axis=1),
+        contract,
+        preferred_element_type=jnp.float32,
     )
     grad_normed = summed_over(partial_normed, "head")
     scaled_grad = norm_gain * grad_normed
@@ -267,7 +264,7 @@
     row_pick = (
         jnp.arange(row_count, dtype=jnp.int32)[:, None] == target_rows[None, :]
     ).astype(jnp.float32)
-    local_grad = jnp.dot(row_pick, contributions, precision=exact)
+    local_grad = lax.optimization_barrier(jnp.dot(row_pick, contributions, precision=exact))
     tail = jnp.concatenate(
         [jnp.zeros((row_count - (KCONV - 1), D), jnp.float32), after_rim], axis=0
     )

time: 145 us -> 143 us (0.986)
  matrix products: 7.35 us -> 3.87 us
  other arithmetic: 6.96 us -> 9.67 us
    dot_general x4 -> x2, matrix products: 4.94 us -> 1.46 us  [the longest x1 1.09 us: per_device(): jnp.dot(row_pick, contributions, precision=exact)]
    convert_element_type x0 -> x4, other arithmetic: none -> 3.41 us  [the longest x1 1.13 us: per_device(): grad_bytes = (local_grad + tail).astype(jnp.bfloat16)]
where the time goes in v11:
time: 143 us; the launch traced here: 142 us
  waiting for transfers between devices  53.3 us (37%)
  starting transfers between devices  49.1 us (34%)
  Pallas kernels  17.6 us (12%)
  other arithmetic  9.67 us (7%)
  local copies, waits for them, and re-layouts  7.16 us (5%)
  matrix products  3.87 us (3%)
  between operations  1.71 us (1%)
    ppermute x3, waiting for transfers between devices, gather_blocks(): other = lax.ppermute(held, axis, [(i, i ^ step) for i in range(devices)])  25.4 us
    ppermute x3, starting transfers between devices, summed_over(): got = lax.ppermute(sent, axis, [(i, i ^ step) for i in range(devices)])  23.7 us
    pallas_call x1, Pallas kernels, attention_all(): pl.pallas_call(forward_kernel, grid_spec=grid_spec, out_shape=[jax.ShapeD...  17.6 us
    ppermute x4, waiting for transfers between devices, shifted(): lax.ppermute(array, axis, [(i, (i + by) % devices) for i in range(devices)])  15.4 us
    ppermute x4, starting transfers between devices, shifted(): lax.ppermute(array, axis, [(i, (i + by) % devices) for i in range(devices)])  11.7 us
    ppermute x3, waiting for transfers between devices, summed_over(): got = lax.ppermute(sent, axis, [(i, i ^ step) for i in range(devices)])  8.71 us
    ppermute x3, starting transfers between devices, gather_blocks(): other = lax.ppermute(held, axis, [(i, i ^ step) for i in range(devices)])  7.07 us
    ppermute x2, starting transfers between devices, passed_along(): return lax.ppermute(array, axis, pairs)  6.6 us
  transfers between devices with their start and end apart: 12, of which 10 were waited for; matrix products, arithmetic and copies ran while one was open for 3% of the time, Pallas kernels for 0%

profile of v11, /device:TPU:30, one launch (start us, length us, event | category | flops | bytes accessed | tf_op | source)
XLA Modules:
  0.0 142.4 jit_solution(2600205218374042973)
XLA Ops:
  0.6 0.0 copy-start
  0.6 0.9 slice.133
  1.5 4.7 %collective-permute-start = (bf16[3,1024]{1,0:T(4,128)(2,1)S(1)}, bf16[3,1024]{1,0:T(4,128)(2,1)S(1)}, u32[]{:S(2)}, u32[]{:S(2)}) collective-permute-start(bf16[3,1024]{1,0:T(4,128)(2,1)S(1)} %slice.133), channel_id=1, source_target_pairs={{0,16},{16,32},{32,48},{48,64},{64,80},{80,96},{96,112},{112,128},... | collective-permute-start | bytes 18440 | tf_op jit(solution)/shard_map/ppermute | solution.py:23
  6.2 0.7 iota_subtract_fusion
  7.0 0.1 add.176
  7.0 0.1 add.173
  7.1 0.9 fusion.40
  8.7 0.0 collective-permute-done
  8.7 1.5 %pad_maximum_fusion = bf16[515,1024]{1,0:T(8,128)(2,1)S(1)} fusion(bf16[512,1024]{1,0:T(8,128)(2,1)} %param.10, bf16[3,1024]{1,0:T(4,128)(2,1)S(1)} %collective-permute-done), kind=kLoop, calls=%fused_computation.10 | loop fusion | flops 2109440 | bytes 2109440 | tf_op jit(solution)/shard_map/concatenate | solution.py:186
  10.2 2.0 %gather_fusion = bf16[256,1024]{1,0:T(8,128)(2,1)} fusion(bf16[515,1024]{1,0:T(8,128)(2,1)S(1)} %pad_maximum_fusion, s32[1024]{0:T(1024)S(1)} %pad_clamp_fusion), kind=kCustom, calls=%fused_computation | custom fusion | bytes 1049600 | tf_op jit(solution)/shard_map/jit(_take)/gather | solution.py:188
  12.2 1.2 select_convert_fusion
  13.4 0.0 copy-start.4
  13.4 0.0 copy-start.7
  13.5 0.6 multiply_reduce_fusion.1
  14.1 0.1 multiply_convert_fusion
  14.2 0.2 fusion.2
  14.4 0.2 fusion.1
  14.6 0.2 fusion
  14.8 0.1 constant_dynamic-update-slice_fusion.1
  14.9 1.9 %collective-permute-start.1 = (bf16[1,272,128]{2,1,0:T(8,128)(2,1)S(1)}, bf16[1,272,128]{2,1,0:T(8,128)(2,1)S(1)}, u32[]{:S(2)}, u32[]{:S(2)}) collective-permute-start(bf16[1,272,128]{2,1,0:T(8,128)(2,1)S(1)} %bitcast.26), channel_id=1, source_target_pairs={{0,16},{16,0},{32,48},{48,32},{64,80},{80,64},{96,112},{112,96},{1... | collective-permute-start | bytes 208904 | tf_op jit(solution)/shard_map/ppermute | solution.py:36
  16.8 4.3 %collective-permute-done.1 = bf16[1,272,128]{2,1,0:T(8,128)(2,1)S(1)} collective-permute-done((bf16[1,272,128]{2,1,0:T(8,128)(2,1)S(1)}, bf16[1,272,128]{2,1,0:T(8,128)(2,1)S(1)}, u32[]{:S(2)}, u32[]{:S(2)}) %collective-permute-start.1) | collective-permute-done | bytes 69664 | tf_op jit(solution)/shard_map/ppermute | solution.py:36
  21.1 1.9 %collective-permute-start.2 = (bf16[2,272,128]{2,1,0:T(8,128)(2,1)S(1)}, bf16[2,272,128]{2,1,0:T(8,128)(2,1)S(1)}, u32[]{:S(2)}, u32[]{:S(2)}) collective-permute-start(bf16[2,272,128]{2,1,0:T(8,128)(2,1)S(1)} %pad_maximum_fusion.6), channel_id=1, source_target_pairs={{0,32},{16,48},{32,0},{48,16},{64,96},{80,112},{96,64},{112,80},{1... | collective-permute-start | bytes 417800 | tf_op jit(solution)/shard_map/ppermute | solution.py:36
  23.0 7.5 %collective-permute-done.2 = bf16[2,272,128]{2,1,0:T(8,128)(2,1)S(1)} collective-permute-done((bf16[2,272,128]{2,1,0:T(8,128)(2,1)S(1)}, bf16[2,272,128]{2,1,0:T(8,128)(2,1)S(1)}, u32[]{:S(2)}, u32[]{:S(2)}) %collective-permute-start.2) | collective-permute-done | bytes 139296 | tf_op jit(solution)/shard_map/ppermute | solution.py:36
  30.6 3.2 %collective-permute-start.3 = (bf16[4,272,128]{2,1,0:T(8,128)(2,1)S(1)}, bf16[4,272,128]{2,1,0:T(8,128)(2,1)S(1)}, u32[]{:S(2)}, u32[]{:S(2)}) collective-permute-start(bf16[4,272,128]{2,1,0:T(8,128)(2,1)S(1)} %pad_maximum_fusion.5), channel_id=1, source_target_pairs={{0,64},{16,80},{32,96},{48,112},{64,0},{80,16},{96,32},{112,48},{1... | collective-permute-start | bytes 835592 | tf_op jit(solution)/shard_map/ppermute | solution.py:36
  33.9 0.1 and_select_fusion
  33.9 0.1 concatenate.40.shards_ref
  34.0 13.6 %collective-permute-done.3 = bf16[4,272,128]{2,1,0:T(8,128)(2,1)S(1)} collective-permute-done((bf16[4,272,128]{2,1,0:T(8,128)(2,1)S(1)}, bf16[4,272,128]{2,1,0:T(8,128)(2,1)S(1)}, u32[]{:S(2)}, u32[]{:S(2)}) %collective-permute-start.3) | collective-permute-done | bytes 278560 | tf_op jit(solution)/shard_map/ppermute | solution.py:36
  47.6 0.1 pad_maximum_fusion.4
  47.6 2.4 %collective-permute-start.4 = (bf16[8,272,128]{2,1,0:T(8,128)(2,1)S(1)}, bf16[8,272,128]{2,1,0:T(8,128)(2,1)S(1)}, u32[]{:S(2)}, u32[]{:S(2)}) collective-permute-start(bf16[8,272,128]{2,1,0:T(8,128)(2,1)S(1)} %pad_maximum_fusion.4), channel_id=1, source_target_pairs={{0,128},{16,144},{32,160},{48,176},{64,192},{80,208},{96,224},{112... | collective-permute-start | bytes 1671176 | tf_op jit(solution)/shard_map/ppermute | solution.py:45
  50.0 3.5 %collective-permute-start.5 = (bf16[8,272,128]{2,1,0:T(8,128)(2,1)S(1)}, bf16[8,272,128]{2,1,0:T(8,128)(2,1)S(1)}, u32[]{:S(2)}, u32[]{:S(2)}) collective-permute-start(bf16[8,272,128]{2,1,0:T(8,128)(2,1)S(1)} %pad_maximum_fusion.4), channel_id=1, source_target_pairs={{0,384},{16,400},{32,416},{48,432},{64,448},{80,464},{96,480},{112... | collective-permute-start | bytes 1671176 | tf_op jit(solution)/shard_map/ppermute | solution.py:45
  53.6 8.2 %collective-permute-done.4 = bf16[8,272,128]{2,1,0:T(8,128)(2,1)S(1)} collective-permute-done((bf16[8,272,128]{2,1,0:T(8,128)(2,1)S(1)}, bf16[8,272,128]{2,1,0:T(8,128)(2,1)S(1)}, u32[]{:S(2)}, u32[]{:S(2)}) %collective-permute-start.4) | collective-permute-done | bytes 557088 | tf_op jit(solution)/shard_map/ppermute | solution.py:45
  61.8 3.6 %collective-permute-start.6 = (bf16[4,272,128]{2,1,0:T(8,128)(2,1)S(1)}, bf16[4,272,128]{2,1,0:T(8,128)(2,1)S(1)}, u32[]{:S(2)}, u32[]{:S(2)}) collective-permute-start(bf16[4,272,128]{2,1,0:T(8,128)(2,1)S(1)} %slice.96), channel_id=1, source_target_pairs={{0,128},{16,144},{32,160},{48,176},{64,192},{80,208},{96,224},{112... | collective-permute-start | bytes 835592 | tf_op jit(solution)/shard_map/ppermute | solution.py:45
  65.5 2.2 %collective-permute-start.7 = (bf16[4,272,128]{2,1,0:T(8,128)(2,1)S(1)}, bf16[4,272,128]{2,1,0:T(8,128)(2,1)S(1)}, u32[]{:S(2)}, u32[]{:S(2)}) collective-permute-start(bf16[4,272,128]{2,1,0:T(8,128)(2,1)S(1)} %slice.97), channel_id=1, source_target_pairs={{0,384},{16,400},{32,416},{48,432},{64,448},{80,464},{96,480},{112... | collective-permute-start | bytes 835592 | tf_op jit(solution)/shard_map/ppermute | solution.py:45
  67.8 0.1 constant_dynamic-update-slice_fusion.5
  67.9 0.1 constant_dynamic-update-slice_fusion.4
  67.9 2.3 %collective-permute-done.6 = bf16[4,272,128]{2,1,0:T(8,128)(2,1)S(1)} collective-permute-done((bf16[4,272,128]{2,1,0:T(8,128)(2,1)S(1)}, bf16[4,272,128]{2,1,0:T(8,128)(2,1)S(1)}, u32[]{:S(2)}, u32[]{:S(2)}) %collective-permute-start.6) | collective-permute-done | bytes 278560 | tf_op jit(solution)/shard_map/ppermute | solution.py:45
  70.3 4.9 %collective-permute-done.7 = bf16[4,272,128]{2,1,0:T(8,128)(2,1)S(1)} collective-permute-done((bf16[4,272,128]{2,1,0:T(8,128)(2,1)S(1)}, bf16[4,272,128]{2,1,0:T(8,128)(2,1)S(1)}, u32[]{:S(2)}, u32[]{:S(2)}) %collective-permute-start.7) | collective-permute-done | bytes 278560 | tf_op jit(solution)/shard_map/ppermute | solution.py:45
  75.2 0.0 copy-start.3
  75.2 0.0 copy-start.5
  75.2 1.4 %fusion.39 = (bf16[32,64,128]{2,1,0:T(8,128)(2,1)}, bf16[32,64,128]{2,1,0:T(8,128)(2,1)}, bf16[32,64,128]{2,1,0:T(8,128)(2,1)}, bf16[32,64,128]{2,1,0:T(8,128)(2,1)}) fusion(bf16[32,272,128]{2,1,0:T(8,128)(2,1)S(1)} %constant_dynamic-update-slice_fusion.2), kind=kLoop, calls=%fused_computation.109 | loop fusion | bytes 4194304 | tf_op jit(solution)/shard_map/slice | solution.py:212
  76.7 0.7 fusion.28
  77.3 0.1 add_select_fusion
  77.4 0.7 select_n.81.key_code_ref
  78.1 0.6 slice.103.own_code_ref
  78.7 17.6 %shard_map.113 = (bf16[2048,128]{1,0:T(8,128)(2,1)}, f32[2048,1]{1,0:T(8,128)}, f32[2048,1]{1,0:T(8,128)}, f32[64,128]{1,0:T(8,128)}, f32[64,128]{1,0:T(8,128)}, /*index=5*/f32[64,128]{1,0:T(8,128)}) custom-call(s32[32]{0:T(128)} %copy-done.8, bf16[2048,128]{1,0:T(8,128)(2,1)} %bitcast.25, bf16[2048,128]{1,0:T(8,128)(2,1)} %bitcast.24, ...), custom_call_target="tpu_custom_call" | custom-call | tf_op jit(solution)/shard_map/pallas_call | solution.py:152
  96.3 0.8 convert_element_type.94
  97.1 0.8 multiply_convert_fusion.1
  97.9 0.8 multiply_convert_fusion.2
  98.6 0.4 convolution_convert_fusion
  99.0 4.3 %collective-permute-start.8 = (bf16[64,1024]{1,0:T(8,128)(2,1)S(1)}, bf16[64,1024]{1,0:T(8,128)(2,1)S(1)}, u32[]{:S(2)}, u32[]{:S(2)}) collective-permute-start(bf16[64,1024]{1,0:T(8,128)(2,1)S(1)} %convolution_convert_fusion), channel_id=1, source_target_pairs={{0,2},{2,0},{4,6},{6,4},{8,10},{10,8},{12,14},{14,12},{1,3},{3,1},... | collective-permute-start | bytes 393224 | tf_op jit(solution)/shard_map/ppermute | solution.py:73
  103.3 2.9 %collective-permute-done.8 = bf16[64,1024]{1,0:T(8,128)(2,1)S(1)} collective-permute-done((bf16[64,1024]{1,0:T(8,128)(2,1)S(1)}, bf16[64,1024]{1,0:T(8,128)(2,1)S(1)}, u32[]{:S(2)}, u32[]{:S(2)}) %collective-permute-start.8) | collective-permute-done | bytes 131104 | tf_op jit(solution)/shard_map/ppermute | solution.py:73
  106.3 7.1 %collective-permute-start.9 = (bf16[64,1024]{1,0:T(8,128)(2,1)S(1)}, bf16[64,1024]{1,0:T(8,128)(2,1)S(1)}, u32[]{:S(2)}, u32[]{:S(2)}) collective-permute-start(bf16[64,1024]{1,0:T(8,128)(2,1)S(1)} %add_convert_fusion.2), channel_id=1, source_target_pairs={{0,4},{2,6},{4,0},{6,2},{8,12},{10,14},{12,8},{14,10},{1,5},{3,7},... | collective-permute-start | bytes 393224 | tf_op jit(solution)/shard_map/ppermute | solution.py:73
  113.4 0.1 sub.31
  113.5 4.2 %collective-permute-done.9 = bf16[64,1024]{1,0:T(8,128)(2,1)S(1)} collective-permute-done((bf16[64,1024]{1,0:T(8,128)(2,1)S(1)}, bf16[64,1024]{1,0:T(8,128)(2,1)S(1)}, u32[]{:S(2)}, u32[]{:S(2)}) %collective-permute-start.9) | collective-permute-done | bytes 131104 | tf_op jit(solution)/shard_map/ppermute | solution.py:73
  117.8 12.3 %collective-permute-start.10 = (bf16[64,1024]{1,0:T(8,128)(2,1)S(1)}, bf16[64,1024]{1,0:T(8,128)(2,1)S(1)}, u32[]{:S(2)}, u32[]{:S(2)}) collective-permute-start(bf16[64,1024]{1,0:T(8,128)(2,1)S(1)} %add_convert_fusion.1), channel_id=1, source_target_pairs={{0,8},{2,10},{4,12},{6,14},{8,0},{10,2},{12,4},{14,6},{1,9},{3,11}... | collective-permute-start | bytes 393224 | tf_op jit(solution)/shard_map/ppermute | solution.py:73
  130.1 1.4 slice_select_fusion
  131.5 1.5 %collective-permute-done.10 = bf16[64,1024]{1,0:T(8,128)(2,1)S(1)} collective-permute-done((bf16[64,1024]{1,0:T(8,128)(2,1)S(1)}, bf16[64,1024]{1,0:T(8,128)(2,1)S(1)}, u32[]{:S(2)}, u32[]{:S(2)}) %collective-permute-start.10) | collective-permute-done | bytes 131104 | tf_op jit(solution)/shard_map/ppermute | solution.py:73
  133.0 0.2 multiply_reduce_fusion
  133.2 0.8 multiply_add_fusion
  134.0 0.5 fusion.8
  134.5 1.9 %collective-permute-start.11 = (f32[3,1024]{1,0:T(4,128)S(1)}, f32[3,1024]{1,0:T(4,128)S(1)}, u32[]{:S(2)}, u32[]{:S(2)}) collective-permute-start(f32[3,1024]{1,0:T(4,128)S(1)} %fusion.8), channel_id=1, source_target_pairs={{16,0},{32,16},{48,32},{64,48},{80,64},{96,80},{112,96},{128,112},... | collective-permute-start | bytes 36872 | tf_op jit(solution)/shard_map/ppermute | solution.py:23
  136.4 1.1 fusion.9
  137.5 3.8 %collective-permute-done.11 = f32[3,1024]{1,0:T(4,128)S(1)} collective-permute-done((f32[3,1024]{1,0:T(4,128)S(1)}, f32[3,1024]{1,0:T(4,128)S(1)}, u32[]{:S(2)}, u32[]{:S(2)}) %collective-permute-start.11) | collective-permute-done | bytes 12320 | tf_op jit(solution)/shard_map/ppermute | solution.py:23
  141.3 1.1 add_convert_fusion
  (38 shorter events, 0.4 us)
Async XLA Ops:
  0.6 12.8 %copy-start = (bf16[1024,1024]{1,0:T(8,128)(2,1)S(1)}, bf16[1024,1024]{1,0:T(8,128)(2,1)}, u32[]{:S(2)}) copy-start(bf16[1024,1024]{1,0:T(8,128)(2,1)} %param.12) | copy-start | bytes 6291460
  1.5 7.2 %collective-permute-start = (bf16[3,1024]{1,0:T(4,128)(2,1)S(1)}, bf16[3,1024]{1,0:T(4,128)(2,1)S(1)}, u32[]{:S(2)}, u32[]{:S(2)}) collective-permute-start(bf16[3,1024]{1,0:T(4,128)(2,1)S(1)} %slice.133), channel_id=1, source_target_pairs={{0,16},{16,32},{32,48},{48,64},{64,80},{80,96},{96,112},{112,128},... | collective-permute-start | bytes 18440 | tf_op jit(solution)/shard_map/ppermute | solution.py:23
  12.2 1.9 %copy-start.6 = (f32[1024]{0:T(1024)S(1)}, f32[1024]{0:T(1024)}, u32[]{:S(2)}) copy-start(f32[1024]{0:T(1024)} %param.13) | copy-start | bytes 12292
  12.2 2.0 %copy-start.1 = (bf16[1024,128]{1,0:T(8,128)(2,1)S(1)}, bf16[1024,128]{1,0:T(8,128)(2,1)}, u32[]{:S(2)}) copy-start(bf16[1024,128]{1,0:T(8,128)(2,1)} %param.14) | copy-start | bytes 786436
  12.2 2.2 %copy-start.2 = (bf16[1024,128]{1,0:T(8,128)(2,1)S(1)}, bf16[1024,128]{1,0:T(8,128)(2,1)}, u32[]{:S(2)}) copy-start(bf16[1024,128]{1,0:T(8,128)(2,1)} %param.15) | copy-start | bytes 786436
  13.4 1.1 copy-start.4
  13.4 1.3 copy-start.7
  14.9 6.2 %collective-permute-start.1 = (bf16[1,272,128]{2,1,0:T(8,128)(2,1)S(1)}, bf16[1,272,128]{2,1,0:T(8,128)(2,1)S(1)}, u32[]{:S(2)}, u32[]{:S(2)}) collective-permute-start(bf16[1,272,128]{2,1,0:T(8,128)(2,1)S(1)} %bitcast.26), channel_id=1, source_target_pairs={{0,16},{16,0},{32,48},{48,32},{64,80},{80,64},{96,112},{112,96},{1... | collective-permute-start | bytes 208904 | tf_op jit(solution)/shard_map/ppermute | solution.py:36
  21.1 9.5 %collective-permute-start.2 = (bf16[2,272,128]{2,1,0:T(8,128)(2,1)S(1)}, bf16[2,272,128]{2,1,0:T(8,128)(2,1)S(1)}, u32[]{:S(2)}, u32[]{:S(2)}) collective-permute-start(bf16[2,272,128]{2,1,0:T(8,128)(2,1)S(1)} %pad_maximum_fusion.6), channel_id=1, source_target_pairs={{0,32},{16,48},{32,0},{48,16},{64,96},{80,112},{96,64},{112,80},{1... | collective-permute-start | bytes 417800 | tf_op jit(solution)/shard_map/ppermute | solution.py:36
  30.6 17.0 %collective-permute-start.3 = (bf16[4,272,128]{2,1,0:T(8,128)(2,1)S(1)}, bf16[4,272,128]{2,1,0:T(8,128)(2,1)S(1)}, u32[]{:S(2)}, u32[]{:S(2)}) collective-permute-start(bf16[4,272,128]{2,1,0:T(8,128)(2,1)S(1)} %pad_maximum_fusion.5), channel_id=1, source_target_pairs={{0,64},{16,80},{32,96},{48,112},{64,0},{80,16},{96,32},{112,48},{1... | collective-permute-start | bytes 835592 | tf_op jit(solution)/shard_map/ppermute | solution.py:36
  34.0 33.8 %copy-start.8 = (s32[32]{0:T(128)}, s32[32]{0:T(128)S(1)}, u32[]{:S(2)}) copy-start(s32[32]{0:T(128)S(1)} %concatenate.40.shards_ref) | copy-start | bytes 388
  47.6 14.2 %collective-permute-start.4 = (bf16[8,272,128]{2,1,0:T(8,128)(2,1)S(1)}, bf16[8,272,128]{2,1,0:T(8,128)(2,1)S(1)}, u32[]{:S(2)}, u32[]{:S(2)}) collective-permute-start(bf16[8,272,128]{2,1,0:T(8,128)(2,1)S(1)} %pad_maximum_fusion.4), channel_id=1, source_target_pairs={{0,128},{16,144},{32,160},{48,176},{64,192},{80,208},{96,224},{112... | collective-permute-start | bytes 1671176 | tf_op jit(solution)/shard_map/ppermute | solution.py:45
  50.0 15.4 %collective-permute-start.5 = (bf16[8,272,128]{2,1,0:T(8,128)(2,1)S(1)}, bf16[8,272,128]{2,1,0:T(8,128)(2,1)S(1)}, u32[]{:S(2)}, u32[]{:S(2)}) collective-permute-start(bf16[8,272,128]{2,1,0:T(8,128)(2,1)S(1)} %pad_maximum_fusion.4), channel_id=1, source_target_pairs={{0,384},{16,400},{32,416},{48,432},{64,448},{80,464},{96,480},{112... | collective-permute-start | bytes 1671176 | tf_op jit(solution)/shard_map/ppermute | solution.py:45
  61.8 8.4 %collective-permute-start.6 = (bf16[4,272,128]{2,1,0:T(8,128)(2,1)S(1)}, bf16[4,272,128]{2,1,0:T(8,128)(2,1)S(1)}, u32[]{:S(2)}, u32[]{:S(2)}) collective-permute-start(bf16[4,272,128]{2,1,0:T(8,128)(2,1)S(1)} %slice.96), channel_id=1, source_target_pairs={{0,128},{16,144},{32,160},{48,176},{64,192},{80,208},{96,224},{112... | collective-permute-start | bytes 835592 | tf_op jit(solution)/shard_map/ppermute | solution.py:45
  65.5 9.7 %collective-permute-start.7 = (bf16[4,272,128]{2,1,0:T(8,128)(2,1)S(1)}, bf16[4,272,128]{2,1,0:T(8,128)(2,1)S(1)}, u32[]{:S(2)}, u32[]{:S(2)}) collective-permute-start(bf16[4,272,128]{2,1,0:T(8,128)(2,1)S(1)} %slice.97), channel_id=1, source_target_pairs={{0,384},{16,400},{32,416},{48,432},{64,448},{80,464},{96,480},{112... | collective-permute-start | bytes 835592 | tf_op jit(solution)/shard_map/ppermute | solution.py:45
  75.2 23.4 %copy-start.3 = (bf16[1024,128]{1,0:T(8,128)(2,1)S(1)}, bf16[1024,128]{1,0:T(8,128)(2,1)}, u32[]{:S(2)}) copy-start(bf16[1024,128]{1,0:T(8,128)(2,1)} %param.15) | copy-start | bytes 786436
  75.2 23.4 %copy-start.5 = (bf16[1024,128]{1,0:T(8,128)(2,1)S(1)}, bf16[1024,128]{1,0:T(8,128)(2,1)}, u32[]{:S(2)}) copy-start(bf16[1024,128]{1,0:T(8,128)(2,1)} %param.16) | copy-start | bytes 786436
  99.0 7.2 %collective-permute-start.8 = (bf16[64,1024]{1,0:T(8,128)(2,1)S(1)}, bf16[64,1024]{1,0:T(8,128)(2,1)S(1)}, u32[]{:S(2)}, u32[]{:S(2)}) collective-permute-start(bf16[64,1024]{1,0:T(8,128)(2,1)S(1)} %convolution_convert_fusion), channel_id=1, source_target_pairs={{0,2},{2,0},{4,6},{6,4},{8,10},{10,8},{12,14},{14,12},{1,3},{3,1},... | collective-permute-start | bytes 393224 | tf_op jit(solution)/shard_map/ppermute | solution.py:73
  106.3 11.5 %collective-permute-start.9 = (bf16[64,1024]{1,0:T(8,128)(2,1)S(1)}, bf16[64,1024]{1,0:T(8,128)(2,1)S(1)}, u32[]{:S(2)}, u32[]{:S(2)}) collective-permute-start(bf16[64,1024]{1,0:T(8,128)(2,1)S(1)} %add_convert_fusion.2), channel_id=1, source_target_pairs={{0,4},{2,6},{4,0},{6,2},{8,12},{10,14},{12,8},{14,10},{1,5},{3,7},... | collective-permute-start | bytes 393224 | tf_op jit(solution)/shard_map/ppermute | solution.py:73
  117.8 15.3 %collective-permute-start.10 = (bf16[64,1024]{1,0:T(8,128)(2,1)S(1)}, bf16[64,1024]{1,0:T(8,128)(2,1)S(1)}, u32[]{:S(2)}, u32[]{:S(2)}) collective-permute-start(bf16[64,1024]{1,0:T(8,128)(2,1)S(1)} %add_convert_fusion.1), channel_id=1, source_target_pairs={{0,8},{2,10},{4,12},{6,14},{8,0},{10,2},{12,4},{14,6},{1,9},{3,11}... | collective-permute-start | bytes 393224 | tf_op jit(solution)/shard_map/ppermute | solution.py:73
  134.5 6.8 %collective-permute-start.11 = (f32[3,1024]{1,0:T(4,128)S(1)}, f32[3,1024]{1,0:T(4,128)S(1)}, u32[]{:S(2)}, u32[]{:S(2)}) collective-permute-start(f32[3,1024]{1,0:T(4,128)S(1)} %fusion.8), channel_id=1, source_target_pairs={{16,0},{32,16},{48,32},{64,48},{80,64},{96,80},{112,96},{128,112},... | collective-permute-start | bytes 36872 | tf_op jit(solution)/shard_map/ppermute | solution.py:23

commit v12 on v11

--- a/solution.py
+++ b/solution.py
@@ -27,41 +27,50 @@
     return passed_along(rim_rows, "seq", offset_by)
 
 
-def gather_blocks(block, axis, inner):
+def ring_neighbour(index, by, ring, stride):
+    place = (index // stride) % ring
+    return index + ((place + by) % ring - place) * stride
+
+
+def ring_phase(held, sources, axis, ring, stride):
+    devices = lax.axis_size(axis)
+
+    def shifted(array, by):
+        pairs = [(i, ring_neighbour(i, by, ring, stride)) for i in range(devices)]
+        return lax.ppermute(array, axis, pairs)
+
+    half = held.shape[0] // 2
+    from_below = shifted(held, 1)
+    from_above = shifted(held, -1)
+    parts = [held, from_below, from_above, shifted(from_below[:half], 1), shifted(from_above[half:], -1)]
+    origins = [
+        sources,
+        ring_neighbour(sources, -1, ring, stride),
+        ring_neighbour(sources, 1, ring, stride),
+        ring_neighbour(sources[:half], -2, ring, stride),
+        ring_neighbour(sources[half:], 2, ring, stride),
+    ]
+    return jnp.concatenate(parts, axis=0), jnp.concatenate(origins)
+
+
+def gather_blocks(block, axis):
     devices = lax.axis_size(axis)
     me = lax.axis_index(axis)
     held = block[None]
+    sources = me[None]
+    if devices == 32:
+        other = lax.ppermute(held, axis, [(i, i ^ 1) for i in range(devices)])
+        held = jnp.concatenate([held, other], axis=0)
+        sources = jnp.concatenate([sources, sources ^ 1])
+        held, sources = ring_phase(held, sources, axis, 4, 2)
+        return ring_phase(held, sources, axis, 4, 8)
     step = 1
-    while step < inner:
+    while step < devices:
         other = lax.ppermute(held, axis, [(i, i ^ step) for i in range(devices)])
         held = jnp.concatenate([held, other], axis=0)
+        sources = jnp.concatenate([sources, sources ^ step])
         step *= 2
-    sources = jnp.arange(inner, dtype=jnp.int32) ^ me
-    outer = devices // inner
-    if outer == 1:
-        return held, sources
-
-    def shifted(array, by):
-        return lax.ppermute(array, axis, [(i, (i + by) % devices) for i in range(devices)])
-
-    parts = [held]
-    origins = [sources]
-    from_below = shifted(held, inner)
-    from_above = shifted(held, -inner) if outer > 2 else None
-    parts.append(from_below)
-    origins.append((sources - inner) % devices)
-    if outer > 2:
-        parts.append(from_above)
-        origins.append((sources + inner) % devices)
-    if outer == 4:
-        half = inner // 2
-        parts.append(shifted(from_below[:half], inner))
-        origins.append((sources[:half] - 2 * inner) % devices)
-        parts.append(shifted(from_above[half:], -inner))
-        origins.append((sources[half:] + 2 * inner) % devices)
-    else:
-        assert outer <= 3
-    return jnp.concatenate(parts, axis=0), jnp.concatenate(origins)
+    return held, sources
 
 
 def summed_over(partial, axis):
@@ -205,7 +214,7 @@
 
     count_rows = jnp.broadcast_to(span_counts[0].astype(jnp.bfloat16), (16, head_width))
     packed = jnp.concatenate([queries, key_rows, value_rows, grad_rows, count_rows], axis=0)
-    gathered, held_shards = gather_blocks(packed, "seq", 8 if shards == 32 else shards)
+    gathered, held_shards = gather_blocks(packed, "seq")
     total_slots = shards * slot_count
 
     def piece(k):

time: 143 us -> 142 us (level)
  waiting for transfers between devices: 53.3 us -> 34.4 us
  local copies, waits for them, and re-layouts: 7.16 us -> 15.7 us
  starting transfers between devices: 49.1 us -> 57.4 us
    ppermute x7 -> x9, waiting for transfers between devices: 40.8 us -> 21.9 us  [the longest x8 17.8 us: shifted(): return lax.ppermute(array, axis, pairs)]
    ppermute x7 -> x9, starting transfers between devices: 18.8 us -> 27.1 us  [the longest x8 25.1 us: shifted(): return lax.ppermute(array, axis, pairs)]
    unnamed x25 -> x28, local copies, waits for them, and re-layouts: 0.32 us -> 5.94 us
    slice x1, local copies, waits for them, and re-layouts: 1.42 us -> 2.95 us  [piece(): gathered[:, k * slot_count:(k + 1) * slot_count]]
    concatenate x2 -> x4, local copies, waits for them, and re-layouts: 0.12 us -> 1.55 us  [ring_phase(): return (jnp.concatenate(parts, axis=0), jnp.concatenate(origins))]
  transfers between devices with their start and end apart: 12 -> 14, of which waited for: 10 -> 10; matrix products, arithmetic and copies ran while one was open for 3% -> 8% of each run, Pallas kernels for 0% -> 0%
where the time goes in v12:
time: 142 us; the launch traced here: 141 us
  starting transfers between devices  57.4 us (40%)
  waiting for transfers between devices  34.4 us (24%)
  Pallas kernels  17.6 us (12%)
  local copies, waits for them, and re-layouts  15.7 us (11%)
  other arithmetic  10.6 us (7%)
  matrix products  3.88 us (3%)
  between operations  1.72 us (1%)
    ppermute x8, starting transfers between devices, shifted(): return lax.ppermute(array, axis, pairs)  25.1 us
    ppermute x3, starting transfers between devices, summed_over(): got = lax.ppermute(sent, axis, [(i, i ^ step) for i in range(devices)])  23.7 us
    ppermute x8, waiting for transfers between devices, shifted(): return lax.ppermute(array, axis, pairs)  17.8 us
    pallas_call x1, Pallas kernels, attention_all(): pl.pallas_call(forward_kernel, grid_spec=grid_spec, out_shape=[jax.ShapeD...  17.6 us
    ppermute x3, waiting for transfers between devices, summed_over(): got = lax.ppermute(sent, axis, [(i, i ^ step) for i in range(devices)])  8.71 us
    ppermute x2, starting transfers between devices, passed_along(): return lax.ppermute(array, axis, pairs)  6.6 us
    unnamed x28, local copies, waits for them, and re-layouts  5.94 us
    ppermute x1, waiting for transfers between devices, gather_blocks(): other = lax.ppermute(held, axis, [(i, i ^ 1) for i in range(devices)])  4.08 us
  transfers between devices with their start and end apart: 14, of which 10 were waited for; matrix products, arithmetic and copies ran while one was open for 8% of the time, Pallas kernels for 0%

profile of v12, /device:TPU:30, one launch (start us, length us, event | category | flops | bytes accessed | tf_op | source)
XLA Modules:
  0.0 141.4 jit_solution(10649133727240210549)
XLA Ops:
  0.6 0.9 slice.137
  1.5 4.7 %collective-permute-start = (bf16[3,1024]{1,0:T(4,128)(2,1)S(1)}, bf16[3,1024]{1,0:T(4,128)(2,1)S(1)}, u32[]{:S(2)}, u32[]{:S(2)}) collective-permute-start(bf16[3,1024]{1,0:T(4,128)(2,1)S(1)} %slice.137), channel_id=1, source_target_pairs={{0,16},{16,32},{32,48},{48,64},{64,80},{80,96},{96,112},{112,128},... | collective-permute-start | bytes 18440 | tf_op jit(solution)/shard_map/ppermute | solution.py:23
  6.2 0.7 iota_subtract_fusion
  7.0 0.1 add.346
  7.1 0.9 fusion.52
  8.7 0.1 multiply_add_fusion.6
  8.8 1.5 %pad_maximum_fusion = bf16[515,1024]{1,0:T(8,128)(2,1)S(1)} fusion(bf16[512,1024]{1,0:T(8,128)(2,1)} %param.10, bf16[3,1024]{1,0:T(4,128)(2,1)S(1)} %collective-permute-done), kind=kLoop, calls=%fused_computation.10 | loop fusion | flops 2109440 | bytes 2109440 | tf_op jit(solution)/shard_map/concatenate | solution.py:195
  10.3 2.0 %gather_fusion = bf16[256,1024]{1,0:T(8,128)(2,1)} fusion(bf16[515,1024]{1,0:T(8,128)(2,1)S(1)} %pad_maximum_fusion, s32[1024]{0:T(1024)S(1)} %pad_clamp_fusion), kind=kCustom, calls=%fused_computation | custom fusion | bytes 1049600 | tf_op jit(solution)/shard_map/jit(_take)/gather | solution.py:197
  12.3 1.2 select_convert_fusion
  13.6 0.6 multiply_reduce_fusion.1
  14.2 0.1 multiply_convert_fusion
  14.3 0.2 fusion.2
  14.5 0.2 fusion.1
  14.7 0.2 fusion
  14.9 0.1 constant_dynamic-update-slice_fusion.1
  15.0 1.9 %collective-permute-start.1 = (bf16[1,272,128]{2,1,0:T(8,128)(2,1)S(1)}, bf16[1,272,128]{2,1,0:T(8,128)(2,1)S(1)}, u32[]{:S(2)}, u32[]{:S(2)}) collective-permute-start(bf16[1,272,128]{2,1,0:T(8,128)(2,1)S(1)} %bitcast.28), channel_id=1, source_target_pairs={{0,16},{16,0},{32,48},{48,32},{64,80},{80,64},{96,112},{112,96},{1... | collective-permute-start | bytes 208904 | tf_op jit(solution)/shard_map/ppermute | solution.py:62
  17.1 4.1 %collective-permute-done.1 = bf16[1,272,128]{2,1,0:T(8,128)(2,1)S(1)} collective-permute-done((bf16[1,272,128]{2,1,0:T(8,128)(2,1)S(1)}, bf16[1,272,128]{2,1,0:T(8,128)(2,1)S(1)}, u32[]{:S(2)}, u32[]{:S(2)}) %collective-permute-start.1) | collective-permute-done | bytes 69664 | tf_op jit(solution)/shard_map/ppermute | solution.py:62
  21.2 3.6 %collective-permute-start.2 = (bf16[2,272,128]{2,1,0:T(8,128)(2,1)S(1)}, bf16[2,272,128]{2,1,0:T(8,128)(2,1)S(1)}, u32[]{:S(2)}, u32[]{:S(2)}) collective-permute-start(bf16[2,272,128]{2,1,0:T(8,128)(2,1)S(1)} %pad_maximum_fusion.4), channel_id=1, source_target_pairs={{0,32},{16,48},{32,64},{48,80},{64,96},{80,112},{96,0},{112,16},{1... | collective-permute-start | bytes 417800 | tf_op jit(solution)/shard_map/ppermute | solution.py:40
  24.8 3.2 %collective-permute-start.3 = (bf16[2,272,128]{2,1,0:T(8,128)(2,1)S(1)}, bf16[2,272,128]{2,1,0:T(8,128)(2,1)S(1)}, u32[]{:S(2)}, u32[]{:S(2)}) collective-permute-start(bf16[2,272,128]{2,1,0:T(8,128)(2,1)S(1)} %pad_maximum_fusion.4), channel_id=1, source_target_pairs={{0,96},{16,112},{32,0},{48,16},{64,32},{80,48},{96,64},{112,80},{1... | collective-permute-start | bytes 417800 | tf_op jit(solution)/shard_map/ppermute | solution.py:40
  27.9 0.7 constant_dynamic-update-slice_fusion.7
  28.6 0.7 constant_dynamic-update-slice_fusion.6
  29.3 1.7 %collective-permute-done.2 = bf16[2,272,128]{2,1,0:T(8,128)(2,1)S(1)} collective-permute-done((bf16[2,272,128]{2,1,0:T(8,128)(2,1)S(1)}, bf16[2,272,128]{2,1,0:T(8,128)(2,1)S(1)}, u32[]{:S(2)}, u32[]{:S(2)}) %collective-permute-start.2) | collective-permute-done | bytes 139296 | tf_op jit(solution)/shard_map/ppermute | solution.py:40
  31.0 3.9 %collective-permute-start.4 = (bf16[1,272,128]{2,1,0:T(8,128)(2,1)S(1)}, bf16[1,272,128]{2,1,0:T(8,128)(2,1)S(1)}, u32[]{:S(2)}, u32[]{:S(2)}) collective-permute-start(bf16[1,272,128]{2,1,0:T(8,128)(2,1)S(1)} %slice.100), channel_id=1, source_target_pairs={{0,32},{16,48},{32,64},{48,80},{64,96},{80,112},{96,0},{112,16},{1... | collective-permute-start | bytes 208904 | tf_op jit(solution)/shard_map/ppermute | solution.py:40
  34.9 2.8 %collective-permute-start.5 = (bf16[1,272,128]{2,1,0:T(8,128)(2,1)S(1)}, bf16[1,272,128]{2,1,0:T(8,128)(2,1)S(1)}, u32[]{:S(2)}, u32[]{:S(2)}) collective-permute-start(bf16[1,272,128]{2,1,0:T(8,128)(2,1)S(1)} %slice.101), channel_id=1, source_target_pairs={{0,96},{16,112},{32,0},{48,16},{64,32},{80,48},{96,64},{112,80},{1... | collective-permute-start | bytes 208904 | tf_op jit(solution)/shard_map/ppermute | solution.py:40
  37.7 0.7 constant_dynamic-update-slice_fusion.5
  38.5 0.7 constant_dynamic-update-slice_fusion.4
  39.2 0.7 constant_dynamic-update-slice_fusion.3
  39.9 3.3 %collective-permute-done.5 = bf16[1,272,128]{2,1,0:T(8,128)(2,1)S(1)} collective-permute-done((bf16[1,272,128]{2,1,0:T(8,128)(2,1)S(1)}, bf16[1,272,128]{2,1,0:T(8,128)(2,1)S(1)}, u32[]{:S(2)}, u32[]{:S(2)}) %collective-permute-start.5) | collective-permute-done | bytes 69664 | tf_op jit(solution)/shard_map/ppermute | solution.py:40
  43.2 0.7 constant_dynamic-update-slice_fusion.2
  43.9 3.2 %collective-permute-start.6 = (bf16[8,272,128]{2,1,0:T(8,128)(2,1)}, bf16[8,272,128]{2,1,0:T(8,128)(2,1)S(1)}, u32[]{:S(2)}, u32[]{:S(2)}) collective-permute-start(bf16[8,272,128]{2,1,0:T(8,128)(2,1)} %get-tuple-element.26), channel_id=1, source_target_pairs={{0,128},{16,144},{32,160},{48,176},{64,192},{80,208},{96,224},{112... | collective-permute-start | bytes 1671176 | tf_op jit(solution)/shard_map/ppermute | solution.py:40
  47.1 2.6 %collective-permute-start.7 = (bf16[8,272,128]{2,1,0:T(8,128)(2,1)}, bf16[8,272,128]{2,1,0:T(8,128)(2,1)S(1)}, u32[]{:S(2)}, u32[]{:S(2)}) collective-permute-start(bf16[8,272,128]{2,1,0:T(8,128)(2,1)} %get-tuple-element.26), channel_id=1, source_target_pairs={{0,384},{16,400},{32,416},{48,432},{64,448},{80,464},{96,480},{112... | collective-permute-start | bytes 1671176 | tf_op jit(solution)/shard_map/ppermute | solution.py:40
  49.7 0.1 multiply_add_fusion.2
  50.0 8.0 %collective-permute-done.6 = bf16[8,272,128]{2,1,0:T(8,128)(2,1)S(1)} collective-permute-done((bf16[8,272,128]{2,1,0:T(8,128)(2,1)}, bf16[8,272,128]{2,1,0:T(8,128)(2,1)S(1)}, u32[]{:S(2)}, u32[]{:S(2)}) %collective-permute-start.6) | collective-permute-done | bytes 557088 | tf_op jit(solution)/shard_map/ppermute | solution.py:40
  58.0 3.4 %collective-permute-start.8 = (bf16[4,272,128]{2,1,0:T(8,128)(2,1)S(1)}, bf16[4,272,128]{2,1,0:T(8,128)(2,1)S(1)}, u32[]{:S(2)}, u32[]{:S(2)}) collective-permute-start(bf16[4,272,128]{2,1,0:T(8,128)(2,1)S(1)} %slice.102), channel_id=1, source_target_pairs={{0,128},{16,144},{32,160},{48,176},{64,192},{80,208},{96,224},{112... | collective-permute-start | bytes 835592 | tf_op jit(solution)/shard_map/ppermute | solution.py:40
  61.5 2.4 %collective-permute-start.9 = (bf16[4,272,128]{2,1,0:T(8,128)(2,1)S(1)}, bf16[4,272,128]{2,1,0:T(8,128)(2,1)S(1)}, u32[]{:S(2)}, u32[]{:S(2)}) collective-permute-start(bf16[4,272,128]{2,1,0:T(8,128)(2,1)S(1)} %slice.103), channel_id=1, source_target_pairs={{0,384},{16,400},{32,416},{48,432},{64,448},{80,464},{96,480},{112... | collective-permute-start | bytes 835592 | tf_op jit(solution)/shard_map/ppermute | solution.py:40
  63.9 0.9 constant_dynamic-update-slice_fusion.11
  64.8 0.8 constant_dynamic-update-slice_fusion.10
  65.6 0.8 collective-permute-done.8
  66.4 0.7 constant_dynamic-update-slice_fusion.9
  67.2 4.0 %collective-permute-done.9 = bf16[4,272,128]{2,1,0:T(8,128)(2,1)S(1)} collective-permute-done((bf16[4,272,128]{2,1,0:T(8,128)(2,1)S(1)}, bf16[4,272,128]{2,1,0:T(8,128)(2,1)S(1)}, u32[]{:S(2)}, u32[]{:S(2)}) %collective-permute-start.9) | collective-permute-done | bytes 278560 | tf_op jit(solution)/shard_map/ppermute | solution.py:40
  71.1 0.7 constant_dynamic-update-slice_fusion.8
  71.9 2.9 %fusion.51 = (bf16[32,64,128]{2,1,0:T(8,128)(2,1)}, bf16[32,64,128]{2,1,0:T(8,128)(2,1)}, bf16[32,64,128]{2,1,0:T(8,128)(2,1)}, bf16[32,64,128]{2,1,0:T(8,128)(2,1)}) fusion(bf16[32,272,128]{2,1,0:T(8,128)(2,1)} %constant_dynamic-update-slice_fusion.8), kind=kLoop, calls=%fused_computation.169 | loop fusion | bytes 4194304 | tf_op jit(solution)/shard_map/slice | solution.py:221
  74.8 1.5 %fusion.28 = s32[32]{0:T(128)S(1)} fusion(bf16[32,272,128]{2,1,0:T(8,128)(2,1)} %constant_dynamic-update-slice_fusion.8), kind=kLoop, calls=%fused_computation.74 | loop fusion | flops 32 | bytes 192 | tf_op jit(solution)/shard_map/convert_element_type | solution.py:224
  76.4 0.7 select_n.205.key_code_ref
  77.1 0.5 slice.109.own_code_ref
  77.6 17.6 %shard_map.113 = (bf16[2048,128]{1,0:T(8,128)(2,1)}, f32[2048,1]{1,0:T(8,128)}, f32[2048,1]{1,0:T(8,128)}, f32[64,128]{1,0:T(8,128)}, f32[64,128]{1,0:T(8,128)}, /*index=5*/f32[64,128]{1,0:T(8,128)}) custom-call(s32[32]{0:T(128)} %copy-done.9, bf16[2048,128]{1,0:T(8,128)(2,1)} %bitcast.27, bf16[2048,128]{1,0:T(8,128)(2,1)} %bitcast.26, ...), custom_call_target="tpu_custom_call" | custom-call | tf_op jit(solution)/shard_map/pallas_call | solution.py:161
  95.2 0.8 convert_element_type.94
  96.0 0.8 multiply_convert_fusion.1
  96.8 0.8 multiply_convert_fusion.2
  97.5 0.4 convolution_convert_fusion
  97.9 4.2 %collective-permute-start.10 = (bf16[64,1024]{1,0:T(8,128)(2,1)S(1)}, bf16[64,1024]{1,0:T(8,128)(2,1)S(1)}, u32[]{:S(2)}, u32[]{:S(2)}) collective-permute-start(bf16[64,1024]{1,0:T(8,128)(2,1)S(1)} %convolution_convert_fusion), channel_id=1, source_target_pairs={{0,2},{2,0},{4,6},{6,4},{8,10},{10,8},{12,14},{14,12},{1,3},{3,1},... | collective-permute-start | bytes 393224 | tf_op jit(solution)/shard_map/ppermute | solution.py:82
  102.2 2.9 %collective-permute-done.10 = bf16[64,1024]{1,0:T(8,128)(2,1)S(1)} collective-permute-done((bf16[64,1024]{1,0:T(8,128)(2,1)S(1)}, bf16[64,1024]{1,0:T(8,128)(2,1)S(1)}, u32[]{:S(2)}, u32[]{:S(2)}) %collective-permute-start.10) | collective-permute-done | bytes 131104 | tf_op jit(solution)/shard_map/ppermute | solution.py:82
  105.1 7.3 %collective-permute-start.11 = (bf16[64,1024]{1,0:T(8,128)(2,1)S(1)}, bf16[64,1024]{1,0:T(8,128)(2,1)S(1)}, u32[]{:S(2)}, u32[]{:S(2)}) collective-permute-start(bf16[64,1024]{1,0:T(8,128)(2,1)S(1)} %add_convert_fusion.2), channel_id=1, source_target_pairs={{0,4},{2,6},{4,0},{6,2},{8,12},{10,14},{12,8},{14,10},{1,5},{3,7},... | collective-permute-start | bytes 393224 | tf_op jit(solution)/shard_map/ppermute | solution.py:82
  112.5 4.2 %collective-permute-done.11 = bf16[64,1024]{1,0:T(8,128)(2,1)S(1)} collective-permute-done((bf16[64,1024]{1,0:T(8,128)(2,1)S(1)}, bf16[64,1024]{1,0:T(8,128)(2,1)S(1)}, u32[]{:S(2)}, u32[]{:S(2)}) %collective-permute-start.11) | collective-permute-done | bytes 131104 | tf_op jit(solution)/shard_map/ppermute | solution.py:82
  116.8 12.2 %collective-permute-start.12 = (bf16[64,1024]{1,0:T(8,128)(2,1)S(1)}, bf16[64,1024]{1,0:T(8,128)(2,1)S(1)}, u32[]{:S(2)}, u32[]{:S(2)}) collective-permute-start(bf16[64,1024]{1,0:T(8,128)(2,1)S(1)} %add_convert_fusion.1), channel_id=1, source_target_pairs={{0,8},{2,10},{4,12},{6,14},{8,0},{10,2},{12,4},{14,6},{1,9},{3,11}... | collective-permute-start | bytes 393224 | tf_op jit(solution)/shard_map/ppermute | solution.py:82
  129.0 1.4 slice_select_fusion
  130.4 1.5 %collective-permute-done.12 = bf16[64,1024]{1,0:T(8,128)(2,1)S(1)} collective-permute-done((bf16[64,1024]{1,0:T(8,128)(2,1)S(1)}, bf16[64,1024]{1,0:T(8,128)(2,1)S(1)}, u32[]{:S(2)}, u32[]{:S(2)}) %collective-permute-start.12) | collective-permute-done | bytes 131104 | tf_op jit(solution)/shard_map/ppermute | solution.py:82
  131.9 0.2 multiply_reduce_fusion
  132.1 0.8 multiply_add_fusion
  132.9 0.5 fusion.8
  133.4 1.9 %collective-permute-start.13 = (f32[3,1024]{1,0:T(4,128)S(1)}, f32[3,1024]{1,0:T(4,128)S(1)}, u32[]{:S(2)}, u32[]{:S(2)}) collective-permute-start(f32[3,1024]{1,0:T(4,128)S(1)} %fusion.8), channel_id=1, source_target_pairs={{16,0},{32,16},{48,32},{64,48},{80,64},{96,80},{112,96},{128,112},... | collective-permute-start | bytes 36872 | tf_op jit(solution)/shard_map/ppermute | solution.py:23
  135.3 1.1 fusion.9
  136.4 3.8 %collective-permute-done.13 = f32[3,1024]{1,0:T(4,128)S(1)} collective-permute-done((f32[3,1024]{1,0:T(4,128)S(1)}, f32[3,1024]{1,0:T(4,128)S(1)}, u32[]{:S(2)}, u32[]{:S(2)}) %collective-permute-start.13) | collective-permute-done | bytes 12320 | tf_op jit(solution)/shard_map/ppermute | solution.py:23
  140.2 1.1 add_convert_fusion
  (49 shorter events, 0.8 us)
Async XLA Ops:
  0.6 12.9 %copy-start = (bf16[1024,1024]{1,0:T(8,128)(2,1)S(1)}, bf16[1024,1024]{1,0:T(8,128)(2,1)}, u32[]{:S(2)}) copy-start(bf16[1024,1024]{1,0:T(8,128)(2,1)} %param.12) | copy-start | bytes 6291460
  1.5 7.3 %collective-permute-start = (bf16[3,1024]{1,0:T(4,128)(2,1)S(1)}, bf16[3,1024]{1,0:T(4,128)(2,1)S(1)}, u32[]{:S(2)}, u32[]{:S(2)}) collective-permute-start(bf16[3,1024]{1,0:T(4,128)(2,1)S(1)} %slice.137), channel_id=1, source_target_pairs={{0,16},{16,32},{32,48},{48,64},{64,80},{80,96},{96,112},{112,128},... | collective-permute-start | bytes 18440 | tf_op jit(solution)/shard_map/ppermute | solution.py:23
  12.3 1.9 %copy-start.7 = (f32[1024]{0:T(1024)S(1)}, f32[1024]{0:T(1024)}, u32[]{:S(2)}) copy-start(f32[1024]{0:T(1024)} %param.13) | copy-start | bytes 12292
  12.3 2.0 %copy-start.1 = (bf16[1024,128]{1,0:T(8,128)(2,1)S(1)}, bf16[1024,128]{1,0:T(8,128)(2,1)}, u32[]{:S(2)}) copy-start(bf16[1024,128]{1,0:T(8,128)(2,1)} %param.14) | copy-start | bytes 786436
  12.3 2.2 %copy-start.3 = (bf16[1024,128]{1,0:T(8,128)(2,1)S(1)}, bf16[1024,128]{1,0:T(8,128)(2,1)}, u32[]{:S(2)}) copy-start(bf16[1024,128]{1,0:T(8,128)(2,1)} %param.15) | copy-start | bytes 786436
  13.5 1.1 copy-start.5
  13.5 1.3 copy-start.8
  15.0 6.2 %collective-permute-start.1 = (bf16[1,272,128]{2,1,0:T(8,128)(2,1)S(1)}, bf16[1,272,128]{2,1,0:T(8,128)(2,1)S(1)}, u32[]{:S(2)}, u32[]{:S(2)}) collective-permute-start(bf16[1,272,128]{2,1,0:T(8,128)(2,1)S(1)} %bitcast.28), channel_id=1, source_target_pairs={{0,16},{16,0},{32,48},{48,32},{64,80},{80,64},{96,112},{112,96},{1... | collective-permute-start | bytes 208904 | tf_op jit(solution)/shard_map/ppermute | solution.py:62
  21.2 9.8 %collective-permute-start.2 = (bf16[2,272,128]{2,1,0:T(8,128)(2,1)S(1)}, bf16[2,272,128]{2,1,0:T(8,128)(2,1)S(1)}, u32[]{:S(2)}, u32[]{:S(2)}) collective-permute-start(bf16[2,272,128]{2,1,0:T(8,128)(2,1)S(1)} %pad_maximum_fusion.4), channel_id=1, source_target_pairs={{0,32},{16,48},{32,64},{48,80},{64,96},{80,112},{96,0},{112,16},{1... | collective-permute-start | bytes 417800 | tf_op jit(solution)/shard_map/ppermute | solution.py:40
  24.8 10.1 %collective-permute-start.3 = (bf16[2,272,128]{2,1,0:T(8,128)(2,1)S(1)}, bf16[2,272,128]{2,1,0:T(8,128)(2,1)S(1)}, u32[]{:S(2)}, u32[]{:S(2)}) collective-permute-start(bf16[2,272,128]{2,1,0:T(8,128)(2,1)S(1)} %pad_maximum_fusion.4), channel_id=1, source_target_pairs={{0,96},{16,112},{32,0},{48,16},{64,32},{80,48},{96,64},{112,80},{1... | collective-permute-start | bytes 417800 | tf_op jit(solution)/shard_map/ppermute | solution.py:40
  31.0 8.3 %collective-permute-start.4 = (bf16[1,272,128]{2,1,0:T(8,128)(2,1)S(1)}, bf16[1,272,128]{2,1,0:T(8,128)(2,1)S(1)}, u32[]{:S(2)}, u32[]{:S(2)}) collective-permute-start(bf16[1,272,128]{2,1,0:T(8,128)(2,1)S(1)} %slice.100), channel_id=1, source_target_pairs={{0,32},{16,48},{32,64},{48,80},{64,96},{80,112},{96,0},{112,16},{1... | collective-permute-start | bytes 208904 | tf_op jit(solution)/shard_map/ppermute | solution.py:40
  34.9 8.3 %collective-permute-start.5 = (bf16[1,272,128]{2,1,0:T(8,128)(2,1)S(1)}, bf16[1,272,128]{2,1,0:T(8,128)(2,1)S(1)}, u32[]{:S(2)}, u32[]{:S(2)}) collective-permute-start(bf16[1,272,128]{2,1,0:T(8,128)(2,1)S(1)} %slice.101), channel_id=1, source_target_pairs={{0,96},{16,112},{32,0},{48,16},{64,32},{80,48},{96,64},{112,80},{1... | collective-permute-start | bytes 208904 | tf_op jit(solution)/shard_map/ppermute | solution.py:40
  43.9 14.1 %collective-permute-start.6 = (bf16[8,272,128]{2,1,0:T(8,128)(2,1)}, bf16[8,272,128]{2,1,0:T(8,128)(2,1)S(1)}, u32[]{:S(2)}, u32[]{:S(2)}) collective-permute-start(bf16[8,272,128]{2,1,0:T(8,128)(2,1)} %get-tuple-element.26), channel_id=1, source_target_pairs={{0,128},{16,144},{32,160},{48,176},{64,192},{80,208},{96,224},{112... | collective-permute-start | bytes 1671176 | tf_op jit(solution)/shard_map/ppermute | solution.py:40
  47.1 14.3 %collective-permute-start.7 = (bf16[8,272,128]{2,1,0:T(8,128)(2,1)}, bf16[8,272,128]{2,1,0:T(8,128)(2,1)S(1)}, u32[]{:S(2)}, u32[]{:S(2)}) collective-permute-start(bf16[8,272,128]{2,1,0:T(8,128)(2,1)} %get-tuple-element.26), channel_id=1, source_target_pairs={{0,384},{16,400},{32,416},{48,432},{64,448},{80,464},{96,480},{112... | collective-permute-start | bytes 1671176 | tf_op jit(solution)/shard_map/ppermute | solution.py:40
  49.9 21.9 %copy-start.9 = (s32[32]{0:T(128)}, s32[32]{0:T(128)S(1)}, u32[]{:S(2)}) copy-start(s32[32]{0:T(128)S(1)} %concatenate.66.shards_ref) | copy-start | bytes 388
  58.0 8.4 %collective-permute-start.8 = (bf16[4,272,128]{2,1,0:T(8,128)(2,1)S(1)}, bf16[4,272,128]{2,1,0:T(8,128)(2,1)S(1)}, u32[]{:S(2)}, u32[]{:S(2)}) collective-permute-start(bf16[4,272,128]{2,1,0:T(8,128)(2,1)S(1)} %slice.102), channel_id=1, source_target_pairs={{0,128},{16,144},{32,160},{48,176},{64,192},{80,208},{96,224},{112... | collective-permute-start | bytes 835592 | tf_op jit(solution)/shard_map/ppermute | solution.py:40
  61.5 9.7 %collective-permute-start.9 = (bf16[4,272,128]{2,1,0:T(8,128)(2,1)S(1)}, bf16[4,272,128]{2,1,0:T(8,128)(2,1)S(1)}, u32[]{:S(2)}, u32[]{:S(2)}) collective-permute-start(bf16[4,272,128]{2,1,0:T(8,128)(2,1)S(1)} %slice.103), channel_id=1, source_target_pairs={{0,384},{16,400},{32,416},{48,432},{64,448},{80,464},{96,480},{112... | collective-permute-start | bytes 835592 | tf_op jit(solution)/shard_map/ppermute | solution.py:40
  71.8 25.7 %copy-start.2 = (bf16[1024,128]{1,0:T(8,128)(2,1)S(1)}, bf16[1024,128]{1,0:T(8,128)(2,1)}, u32[]{:S(2)}) copy-start(bf16[1024,128]{1,0:T(8,128)(2,1)} %param.14) | copy-start | bytes 786436
  71.8 25.7 %copy-start.4 = (bf16[1024,128]{1,0:T(8,128)(2,1)S(1)}, bf16[1024,128]{1,0:T(8,128)(2,1)}, u32[]{:S(2)}) copy-start(bf16[1024,128]{1,0:T(8,128)(2,1)} %param.15) | copy-start | bytes 786436
  71.8 25.7 %copy-start.6 = (bf16[1024,128]{1,0:T(8,128)(2,1)S(1)}, bf16[1024,128]{1,0:T(8,128)(2,1)}, u32[]{:S(2)}) copy-start(bf16[1024,128]{1,0:T(8,128)(2,1)} %param.16) | copy-start | bytes 786436
  97.9 7.2 %collective-permute-start.10 = (bf16[64,1024]{1,0:T(8,128)(2,1)S(1)}, bf16[64,1024]{1,0:T(8,128)(2,1)S(1)}, u32[]{:S(2)}, u32[]{:S(2)}) collective-permute-start(bf16[64,1024]{1,0:T(8,128)(2,1)S(1)} %convolution_convert_fusion), channel_id=1, source_target_pairs={{0,2},{2,0},{4,6},{6,4},{8,10},{10,8},{12,14},{14,12},{1,3},{3,1},... | collective-permute-start | bytes 393224 | tf_op jit(solution)/shard_map/ppermute | solution.py:82
  105.1 11.6 %collective-permute-start.11 = (bf16[64,1024]{1,0:T(8,128)(2,1)S(1)}, bf16[64,1024]{1,0:T(8,128)(2,1)S(1)}, u32[]{:S(2)}, u32[]{:S(2)}) collective-permute-start(bf16[64,1024]{1,0:T(8,128)(2,1)S(1)} %add_convert_fusion.2), channel_id=1, source_target_pairs={{0,4},{2,6},{4,0},{6,2},{8,12},{10,14},{12,8},{14,10},{1,5},{3,7},... | collective-permute-start | bytes 393224 | tf_op jit(solution)/shard_map/ppermute | solution.py:82
  116.8 15.1 %collective-permute-start.12 = (bf16[64,1024]{1,0:T(8,128)(2,1)S(1)}, bf16[64,1024]{1,0:T(8,128)(2,1)S(1)}, u32[]{:S(2)}, u32[]{:S(2)}) collective-permute-start(bf16[64,1024]{1,0:T(8,128)(2,1)S(1)} %add_convert_fusion.1), channel_id=1, source_target_pairs={{0,8},{2,10},{4,12},{6,14},{8,0},{10,2},{12,4},{14,6},{1,9},{3,11}... | collective-permute-start | bytes 393224 | tf_op jit(solution)/shard_map/ppermute | solution.py:82
  133.4 6.8 %collective-permute-start.13 = (f32[3,1024]{1,0:T(4,128)S(1)}, f32[3,1024]{1,0:T(4,128)S(1)}, u32[]{:S(2)}, u32[]{:S(2)}) collective-permute-start(f32[3,1024]{1,0:T(4,128)S(1)} %fusion.8), channel_id=1, source_target_pairs={{16,0},{32,16},{48,32},{64,48},{80,64},{96,80},{112,96},{128,112},... | collective-permute-start | bytes 36872 | tf_op jit(solution)/shard_map/ppermute | solution.py:23

commit v13 on v12

--- a/solution.py
+++ b/solution.py
@@ -77,11 +77,21 @@
     devices = lax.axis_size(axis)
     total = partial
     step = 1
-    while step < devices:
+    last = devices // 2 if devices == 8 else devices
+    while step < last:
         sent = total.astype(jnp.bfloat16)
         got = lax.ppermute(sent, axis, [(i, i ^ step) for i in range(devices)])
         total = sent.astype(jnp.float32) + got.astype(jnp.float32)
         step *= 2
+    if devices == 8:
+        nearest = {0: 7, 1: 7, 2: 4, 3: 4, 4: 3, 5: 3, 6: 0, 7: 0}
+        sent = total.astype(jnp.bfloat16)
+        near = [(src, dst) for dst, src in nearest.items() if min((dst - src) % 8, (src - dst) % 8) == 1]
+        far = [(src, dst) for dst, src in nearest.items() if min((dst - src) % 8, (src - dst) % 8) == 2]
+        got = lax.ppermute(sent, axis, near).astype(jnp.float32) + lax.ppermute(
+            sent, axis, far
+        ).astype(jnp.float32)
+        total = sent.astype(jnp.float32) + got
     return total
 
 

time: 142 us -> 140 us (0.986)
    ppermute x3 -> x2, starting transfers between devices: 23.7 us -> 11.5 us  [summed_over(): got = lax.ppermute(sent, axis, [(i, i ^ step) for i in range(devices)])]
    ppermute x0 -> x2, starting transfers between devices: none -> 10.3 us  [the longest x1 8.98 us: summed_over(): lax.ppermute(sent, axis, near).astype(jnp.float32)]
    ppermute x3 -> x2, waiting for transfers between devices: 8.71 us -> 7.18 us  [summed_over(): got = lax.ppermute(sent, axis, [(i, i ^ step) for i in range(devices)])]
  transfers between devices with their start and end apart: 14 -> 15, of which waited for: 10 -> 11; matrix products, arithmetic and copies ran while one was open for 8% -> 8% of each run, Pallas kernels for 0% -> 0%
where the time goes in v13:
time: 140 us; the launch traced here: 139 us
  starting transfers between devices  56.6 us (40%)
  waiting for transfers between devices  33 us (24%)
  Pallas kernels  17.7 us (13%)
  local copies, waits for them, and re-layouts  15.7 us (11%)
  other arithmetic  10.7 us (8%)
  matrix products  3.86 us (3%)
  between operations  1.73 us (1%)
    ppermute x8, starting transfers between devices, shifted(): return lax.ppermute(array, axis, pairs)  25.1 us
    ppermute x8, waiting for transfers between devices, shifted(): return lax.ppermute(array, axis, pairs)  17.8 us
    pallas_call x1, Pallas kernels, attention_all(): pl.pallas_call(forward_kernel, grid_spec=grid_spec, out_shape=[jax.ShapeD...  17.7 us
    ppermute x2, starting transfers between devices, summed_over(): got = lax.ppermute(sent, axis, [(i, i ^ step) for i in range(devices)])  11.5 us
    ppermute x1, starting transfers between devices, summed_over(): lax.ppermute(sent, axis, near).astype(jnp.float32)  8.98 us
    ppermute x2, starting transfers between devices, passed_along(): return lax.ppermute(array, axis, pairs)  7.67 us
    ppermute x2, waiting for transfers between devices, summed_over(): got = lax.ppermute(sent, axis, [(i, i ^ step) for i in range(devices)])  7.18 us
    unnamed x28, local copies, waits for them, and re-layouts  5.94 us
  transfers between devices with their start and end apart: 15, of which 11 were waited for; matrix products, arithmetic and copies ran while one was open for 8% of the time, Pallas kernels for 0%

profile of v13, /device:TPU:30, one launch (start us, length us, event | category | flops | bytes accessed | tf_op | source)
XLA Modules:
  0.0 139.2 jit_solution(6231314147039624708)
XLA Ops:
  0.6 0.9 slice.137
  1.5 4.7 %collective-permute-start = (bf16[3,1024]{1,0:T(4,128)(2,1)S(1)}, bf16[3,1024]{1,0:T(4,128)(2,1)S(1)}, u32[]{:S(2)}, u32[]{:S(2)}) collective-permute-start(bf16[3,1024]{1,0:T(4,128)(2,1)S(1)} %slice.137), channel_id=1, source_target_pairs={{0,16},{16,32},{32,48},{48,64},{64,80},{80,96},{96,112},{112,128},... | collective-permute-start | bytes 18440 | tf_op jit(solution)/shard_map/ppermute | solution.py:23
  6.2 0.7 iota_subtract_fusion
  7.1 0.9 fusion.52
  8.7 0.1 multiply_add_fusion.6
  8.8 1.5 %pad_maximum_fusion = bf16[515,1024]{1,0:T(8,128)(2,1)S(1)} fusion(bf16[512,1024]{1,0:T(8,128)(2,1)} %param.10, bf16[3,1024]{1,0:T(4,128)(2,1)S(1)} %collective-permute-done), kind=kLoop, calls=%fused_computation.10 | loop fusion | flops 2109440 | bytes 2109440 | tf_op jit(solution)/shard_map/concatenate | solution.py:205
  10.3 2.0 %gather_fusion = bf16[256,1024]{1,0:T(8,128)(2,1)} fusion(bf16[515,1024]{1,0:T(8,128)(2,1)S(1)} %pad_maximum_fusion, s32[1024]{0:T(1024)S(1)} %pad_clamp_fusion), kind=kCustom, calls=%fused_computation | custom fusion | bytes 1049600 | tf_op jit(solution)/shard_map/jit(_take)/gather | solution.py:207
  12.3 1.2 select_convert_fusion
  13.6 0.6 multiply_reduce_fusion.1
  14.2 0.1 multiply_convert_fusion
  14.3 0.2 fusion.2
  14.5 0.2 fusion.1
  14.7 0.2 fusion
  15.0 1.9 %collective-permute-start.1 = (bf16[1,272,128]{2,1,0:T(8,128)(2,1)S(1)}, bf16[1,272,128]{2,1,0:T(8,128)(2,1)S(1)}, u32[]{:S(2)}, u32[]{:S(2)}) collective-permute-start(bf16[1,272,128]{2,1,0:T(8,128)(2,1)S(1)} %bitcast.28), channel_id=1, source_target_pairs={{0,16},{16,0},{32,48},{48,32},{64,80},{80,64},{96,112},{112,96},{1... | collective-permute-start | bytes 208904 | tf_op jit(solution)/shard_map/ppermute | solution.py:62
  17.1 4.1 %collective-permute-done.1 = bf16[1,272,128]{2,1,0:T(8,128)(2,1)S(1)} collective-permute-done((bf16[1,272,128]{2,1,0:T(8,128)(2,1)S(1)}, bf16[1,272,128]{2,1,0:T(8,128)(2,1)S(1)}, u32[]{:S(2)}, u32[]{:S(2)}) %collective-permute-start.1) | collective-permute-done | bytes 69664 | tf_op jit(solution)/shard_map/ppermute | solution.py:62
  21.2 3.6 %collective-permute-start.2 = (bf16[2,272,128]{2,1,0:T(8,128)(2,1)S(1)}, bf16[2,272,128]{2,1,0:T(8,128)(2,1)S(1)}, u32[]{:S(2)}, u32[]{:S(2)}) collective-permute-start(bf16[2,272,128]{2,1,0:T(8,128)(2,1)S(1)} %pad_maximum_fusion.4), channel_id=1, source_target_pairs={{0,32},{16,48},{32,64},{48,80},{64,96},{80,112},{96,0},{112,16},{1... | collective-permute-start | bytes 417800 | tf_op jit(solution)/shard_map/ppermute | solution.py:40
  24.8 3.2 %collective-permute-start.3 = (bf16[2,272,128]{2,1,0:T(8,128)(2,1)S(1)}, bf16[2,272,128]{2,1,0:T(8,128)(2,1)S(1)}, u32[]{:S(2)}, u32[]{:S(2)}) collective-permute-start(bf16[2,272,128]{2,1,0:T(8,128)(2,1)S(1)} %pad_maximum_fusion.4), channel_id=1, source_target_pairs={{0,96},{16,112},{32,0},{48,16},{64,32},{80,48},{96,64},{112,80},{1... | collective-permute-start | bytes 417800 | tf_op jit(solution)/shard_map/ppermute | solution.py:40
  27.9 0.7 constant_dynamic-update-slice_fusion.7
  28.6 0.7 constant_dynamic-update-slice_fusion.6
  29.3 1.7 %collective-permute-done.2 = bf16[2,272,128]{2,1,0:T(8,128)(2,1)S(1)} collective-permute-done((bf16[2,272,128]{2,1,0:T(8,128)(2,1)S(1)}, bf16[2,272,128]{2,1,0:T(8,128)(2,1)S(1)}, u32[]{:S(2)}, u32[]{:S(2)}) %collective-permute-start.2) | collective-permute-done | bytes 139296 | tf_op jit(solution)/shard_map/ppermute | solution.py:40
  31.0 3.9 %collective-permute-start.4 = (bf16[1,272,128]{2,1,0:T(8,128)(2,1)S(1)}, bf16[1,272,128]{2,1,0:T(8,128)(2,1)S(1)}, u32[]{:S(2)}, u32[]{:S(2)}) collective-permute-start(bf16[1,272,128]{2,1,0:T(8,128)(2,1)S(1)} %slice.100), channel_id=1, source_target_pairs={{0,32},{16,48},{32,64},{48,80},{64,96},{80,112},{96,0},{112,16},{1... | collective-permute-start | bytes 208904 | tf_op jit(solution)/shard_map/ppermute | solution.py:40
  34.9 2.8 %collective-permute-start.5 = (bf16[1,272,128]{2,1,0:T(8,128)(2,1)S(1)}, bf16[1,272,128]{2,1,0:T(8,128)(2,1)S(1)}, u32[]{:S(2)}, u32[]{:S(2)}) collective-permute-start(bf16[1,272,128]{2,1,0:T(8,128)(2,1)S(1)} %slice.101), channel_id=1, source_target_pairs={{0,96},{16,112},{32,0},{48,16},{64,32},{80,48},{96,64},{112,80},{1... | collective-permute-start | bytes 208904 | tf_op jit(solution)/shard_map/ppermute | solution.py:40
  37.7 0.7 constant_dynamic-update-slice_fusion.5
  38.5 0.7 constant_dynamic-update-slice_fusion.4
  39.2 0.7 constant_dynamic-update-slice_fusion.3
  39.9 3.3 %collective-permute-done.5 = bf16[1,272,128]{2,1,0:T(8,128)(2,1)S(1)} collective-permute-done((bf16[1,272,128]{2,1,0:T(8,128)(2,1)S(1)}, bf16[1,272,128]{2,1,0:T(8,128)(2,1)S(1)}, u32[]{:S(2)}, u32[]{:S(2)}) %collective-permute-start.5) | collective-permute-done | bytes 69664 | tf_op jit(solution)/shard_map/ppermute | solution.py:40
  43.2 0.7 constant_dynamic-update-slice_fusion.2
  43.9 3.2 %collective-permute-start.6 = (bf16[8,272,128]{2,1,0:T(8,128)(2,1)}, bf16[8,272,128]{2,1,0:T(8,128)(2,1)S(1)}, u32[]{:S(2)}, u32[]{:S(2)}) collective-permute-start(bf16[8,272,128]{2,1,0:T(8,128)(2,1)} %get-tuple-element.26), channel_id=1, source_target_pairs={{0,128},{16,144},{32,160},{48,176},{64,192},{80,208},{96,224},{112... | collective-permute-start | bytes 1671176 | tf_op jit(solution)/shard_map/ppermute | solution.py:40
  47.1 2.6 %collective-permute-start.7 = (bf16[8,272,128]{2,1,0:T(8,128)(2,1)}, bf16[8,272,128]{2,1,0:T(8,128)(2,1)S(1)}, u32[]{:S(2)}, u32[]{:S(2)}) collective-permute-start(bf16[8,272,128]{2,1,0:T(8,128)(2,1)} %get-tuple-element.26), channel_id=1, source_target_pairs={{0,384},{16,400},{32,416},{48,432},{64,448},{80,464},{96,480},{112... | collective-permute-start | bytes 1671176 | tf_op jit(solution)/shard_map/ppermute | solution.py:40
  49.7 0.1 multiply_add_fusion.2
  50.0 8.0 %collective-permute-done.6 = bf16[8,272,128]{2,1,0:T(8,128)(2,1)S(1)} collective-permute-done((bf16[8,272,128]{2,1,0:T(8,128)(2,1)}, bf16[8,272,128]{2,1,0:T(8,128)(2,1)S(1)}, u32[]{:S(2)}, u32[]{:S(2)}) %collective-permute-start.6) | collective-permute-done | bytes 557088 | tf_op jit(solution)/shard_map/ppermute | solution.py:40
  58.0 3.4 %collective-permute-start.8 = (bf16[4,272,128]{2,1,0:T(8,128)(2,1)S(1)}, bf16[4,272,128]{2,1,0:T(8,128)(2,1)S(1)}, u32[]{:S(2)}, u32[]{:S(2)}) collective-permute-start(bf16[4,272,128]{2,1,0:T(8,128)(2,1)S(1)} %slice.102), channel_id=1, source_target_pairs={{0,128},{16,144},{32,160},{48,176},{64,192},{80,208},{96,224},{112... | collective-permute-start | bytes 835592 | tf_op jit(solution)/shard_map/ppermute | solution.py:40
  61.5 2.4 %collective-permute-start.9 = (bf16[4,272,128]{2,1,0:T(8,128)(2,1)S(1)}, bf16[4,272,128]{2,1,0:T(8,128)(2,1)S(1)}, u32[]{:S(2)}, u32[]{:S(2)}) collective-permute-start(bf16[4,272,128]{2,1,0:T(8,128)(2,1)S(1)} %slice.103), channel_id=1, source_target_pairs={{0,384},{16,400},{32,416},{48,432},{64,448},{80,464},{96,480},{112... | collective-permute-start | bytes 835592 | tf_op jit(solution)/shard_map/ppermute | solution.py:40
  63.9 0.9 constant_dynamic-update-slice_fusion.11
  64.8 0.8 constant_dynamic-update-slice_fusion.10
  65.6 0.8 collective-permute-done.8
  66.4 0.7 constant_dynamic-update-slice_fusion.9
  67.1 4.0 %collective-permute-done.9 = bf16[4,272,128]{2,1,0:T(8,128)(2,1)S(1)} collective-permute-done((bf16[4,272,128]{2,1,0:T(8,128)(2,1)S(1)}, bf16[4,272,128]{2,1,0:T(8,128)(2,1)S(1)}, u32[]{:S(2)}, u32[]{:S(2)}) %collective-permute-start.9) | collective-permute-done | bytes 278560 | tf_op jit(solution)/shard_map/ppermute | solution.py:40
  71.1 0.7 constant_dynamic-update-slice_fusion.8
  71.8 3.0 %fusion.51 = (bf16[32,64,128]{2,1,0:T(8,128)(2,1)}, bf16[32,64,128]{2,1,0:T(8,128)(2,1)}, bf16[32,64,128]{2,1,0:T(8,128)(2,1)}, bf16[32,64,128]{2,1,0:T(8,128)(2,1)}) fusion(bf16[32,272,128]{2,1,0:T(8,128)(2,1)} %constant_dynamic-update-slice_fusion.8), kind=kLoop, calls=%fused_computation.169 | loop fusion | bytes 4194304 | tf_op jit(solution)/shard_map/slice | solution.py:231
  74.8 1.5 %fusion.28 = s32[32]{0:T(128)S(1)} fusion(bf16[32,272,128]{2,1,0:T(8,128)(2,1)} %constant_dynamic-update-slice_fusion.8), kind=kLoop, calls=%fused_computation.74 | loop fusion | flops 32 | bytes 192 | tf_op jit(solution)/shard_map/convert_element_type | solution.py:234
  76.4 0.7 select_n.205.key_code_ref
  77.1 0.6 slice.109.own_code_ref
  77.7 17.7 %shard_map.113 = (bf16[2048,128]{1,0:T(8,128)(2,1)}, f32[2048,1]{1,0:T(8,128)}, f32[2048,1]{1,0:T(8,128)}, f32[64,128]{1,0:T(8,128)}, f32[64,128]{1,0:T(8,128)}, /*index=5*/f32[64,128]{1,0:T(8,128)}) custom-call(s32[32]{0:T(128)} %copy-done.9, bf16[2048,128]{1,0:T(8,128)(2,1)} %bitcast.27, bf16[2048,128]{1,0:T(8,128)(2,1)} %bitcast.26, ...), custom_call_target="tpu_custom_call" | custom-call | tf_op jit(solution)/shard_map/pallas_call | solution.py:171
  95.3 0.8 convert_element_type.97
  96.1 0.8 multiply_convert_fusion.1
  96.8 0.8 multiply_convert_fusion.2
  97.6 0.4 convolution_convert_fusion
  98.0 4.3 %collective-permute-start.10 = (bf16[64,1024]{1,0:T(8,128)(2,1)S(1)}, bf16[64,1024]{1,0:T(8,128)(2,1)S(1)}, u32[]{:S(2)}, u32[]{:S(2)}) collective-permute-start(bf16[64,1024]{1,0:T(8,128)(2,1)S(1)} %convolution_convert_fusion), channel_id=1, source_target_pairs={{0,2},{2,0},{4,6},{6,4},{8,10},{10,8},{12,14},{14,12},{1,3},{3,1},... | collective-permute-start | bytes 393224 | tf_op jit(solution)/shard_map/ppermute | solution.py:83
  102.3 2.9 %collective-permute-done.10 = bf16[64,1024]{1,0:T(8,128)(2,1)S(1)} collective-permute-done((bf16[64,1024]{1,0:T(8,128)(2,1)S(1)}, bf16[64,1024]{1,0:T(8,128)(2,1)S(1)}, u32[]{:S(2)}, u32[]{:S(2)}) %collective-permute-start.10) | collective-permute-done | bytes 131104 | tf_op jit(solution)/shard_map/ppermute | solution.py:83
  105.2 7.3 %collective-permute-start.11 = (bf16[64,1024]{1,0:T(8,128)(2,1)S(1)}, bf16[64,1024]{1,0:T(8,128)(2,1)S(1)}, u32[]{:S(2)}, u32[]{:S(2)}) collective-permute-start(bf16[64,1024]{1,0:T(8,128)(2,1)S(1)} %add_convert_fusion.2), channel_id=1, source_target_pairs={{0,4},{2,6},{4,0},{6,2},{8,12},{10,14},{12,8},{14,10},{1,5},{3,7},... | collective-permute-start | bytes 393224 | tf_op jit(solution)/shard_map/ppermute | solution.py:83
  112.6 4.2 %collective-permute-done.11 = bf16[64,1024]{1,0:T(8,128)(2,1)S(1)} collective-permute-done((bf16[64,1024]{1,0:T(8,128)(2,1)S(1)}, bf16[64,1024]{1,0:T(8,128)(2,1)S(1)}, u32[]{:S(2)}, u32[]{:S(2)}) %collective-permute-start.11) | collective-permute-done | bytes 131104 | tf_op jit(solution)/shard_map/ppermute | solution.py:83
  116.9 9.0 %collective-permute-start.12 = (bf16[64,1024]{1,0:T(8,128)(2,1)S(1)}, bf16[64,1024]{1,0:T(8,128)(2,1)S(1)}, u32[]{:S(2)}, u32[]{:S(2)}) collective-permute-start(bf16[64,1024]{1,0:T(8,128)(2,1)S(1)} %add_convert_fusion.1), channel_id=1, source_target_pairs={{14,0},{8,6},{6,8},{0,14},{15,1},{9,7},{7,9},{1,15},{30,16},{24,22... | collective-permute-start | bytes 393224 | tf_op jit(solution)/shard_map/ppermute | solution.py:91
  125.9 1.3 collective-permute-start.13
  127.2 1.4 %slice_select_fusion = bf16[64,128]{1,0:T(8,128)(2,1)} fusion(bf16[2048,128]{1,0:T(8,128)(2,1)} %get-tuple-element.6, pred[64]{0:T(512)(128)(4,1)S(1)} %iota_compare_fusion.3), kind=kLoop, calls=%fused_computation.75 | loop fusion | flops 8192 | bytes 32832 | tf_op jit(solution)/shard_map/jit(_where)/select_n | solution.py:246
  128.6 0.2 collective-permute-done.12
  128.8 0.9 collective-permute-done.13
  129.8 0.2 multiply_reduce_fusion
  129.9 0.8 multiply_add_fusion
  130.8 0.5 fusion.8
  131.2 3.0 %collective-permute-start.14 = (f32[3,1024]{1,0:T(4,128)S(1)}, f32[3,1024]{1,0:T(4,128)S(1)}, u32[]{:S(2)}, u32[]{:S(2)}) collective-permute-start(f32[3,1024]{1,0:T(4,128)S(1)} %fusion.8), channel_id=1, source_target_pairs={{16,0},{32,16},{48,32},{64,48},{80,64},{96,80},{112,96},{128,112},... | collective-permute-start | bytes 36872 | tf_op jit(solution)/shard_map/ppermute | solution.py:23
  134.2 1.1 fusion.9
  135.3 2.7 %collective-permute-done.14 = f32[3,1024]{1,0:T(4,128)S(1)} collective-permute-done((f32[3,1024]{1,0:T(4,128)S(1)}, f32[3,1024]{1,0:T(4,128)S(1)}, u32[]{:S(2)}, u32[]{:S(2)}) %collective-permute-start.14) | collective-permute-done | bytes 12320 | tf_op jit(solution)/shard_map/ppermute | solution.py:23
  138.1 1.1 add_convert_fusion
  (51 shorter events, 0.9 us)
Async XLA Ops:
  0.6 12.9 %copy-start = (bf16[1024,1024]{1,0:T(8,128)(2,1)S(1)}, bf16[1024,1024]{1,0:T(8,128)(2,1)}, u32[]{:S(2)}) copy-start(bf16[1024,1024]{1,0:T(8,128)(2,1)} %param.12) | copy-start | bytes 6291460
  1.5 7.3 %collective-permute-start = (bf16[3,1024]{1,0:T(4,128)(2,1)S(1)}, bf16[3,1024]{1,0:T(4,128)(2,1)S(1)}, u32[]{:S(2)}, u32[]{:S(2)}) collective-permute-start(bf16[3,1024]{1,0:T(4,128)(2,1)S(1)} %slice.137), channel_id=1, source_target_pairs={{0,16},{16,32},{32,48},{48,64},{64,80},{80,96},{96,112},{112,128},... | collective-permute-start | bytes 18440 | tf_op jit(solution)/shard_map/ppermute | solution.py:23
  12.3 1.9 %copy-start.7 = (f32[1024]{0:T(1024)S(1)}, f32[1024]{0:T(1024)}, u32[]{:S(2)}) copy-start(f32[1024]{0:T(1024)} %param.13) | copy-start | bytes 12292
  12.3 2.0 %copy-start.1 = (bf16[1024,128]{1,0:T(8,128)(2,1)S(1)}, bf16[1024,128]{1,0:T(8,128)(2,1)}, u32[]{:S(2)}) copy-start(bf16[1024,128]{1,0:T(8,128)(2,1)} %param.14) | copy-start | bytes 786436
  12.3 2.2 %copy-start.3 = (bf16[1024,128]{1,0:T(8,128)(2,1)S(1)}, bf16[1024,128]{1,0:T(8,128)(2,1)}, u32[]{:S(2)}) copy-start(bf16[1024,128]{1,0:T(8,128)(2,1)} %param.15) | copy-start | bytes 786436
  13.5 1.1 copy-start.5
  13.5 1.3 copy-start.8
  15.0 6.2 %collective-permute-start.1 = (bf16[1,272,128]{2,1,0:T(8,128)(2,1)S(1)}, bf16[1,272,128]{2,1,0:T(8,128)(2,1)S(1)}, u32[]{:S(2)}, u32[]{:S(2)}) collective-permute-start(bf16[1,272,128]{2,1,0:T(8,128)(2,1)S(1)} %bitcast.28), channel_id=1, source_target_pairs={{0,16},{16,0},{32,48},{48,32},{64,80},{80,64},{96,112},{112,96},{1... | collective-permute-start | bytes 208904 | tf_op jit(solution)/shard_map/ppermute | solution.py:62
  21.2 9.8 %collective-permute-start.2 = (bf16[2,272,128]{2,1,0:T(8,128)(2,1)S(1)}, bf16[2,272,128]{2,1,0:T(8,128)(2,1)S(1)}, u32[]{:S(2)}, u32[]{:S(2)}) collective-permute-start(bf16[2,272,128]{2,1,0:T(8,128)(2,1)S(1)} %pad_maximum_fusion.4), channel_id=1, source_target_pairs={{0,32},{16,48},{32,64},{48,80},{64,96},{80,112},{96,0},{112,16},{1... | collective-permute-start | bytes 417800 | tf_op jit(solution)/shard_map/ppermute | solution.py:40
  24.8 10.1 %collective-permute-start.3 = (bf16[2,272,128]{2,1,0:T(8,128)(2,1)S(1)}, bf16[2,272,128]{2,1,0:T(8,128)(2,1)S(1)}, u32[]{:S(2)}, u32[]{:S(2)}) collective-permute-start(bf16[2,272,128]{2,1,0:T(8,128)(2,1)S(1)} %pad_maximum_fusion.4), channel_id=1, source_target_pairs={{0,96},{16,112},{32,0},{48,16},{64,32},{80,48},{96,64},{112,80},{1... | collective-permute-start | bytes 417800 | tf_op jit(solution)/shard_map/ppermute | solution.py:40
  31.0 8.2 %collective-permute-start.4 = (bf16[1,272,128]{2,1,0:T(8,128)(2,1)S(1)}, bf16[1,272,128]{2,1,0:T(8,128)(2,1)S(1)}, u32[]{:S(2)}, u32[]{:S(2)}) collective-permute-start(bf16[1,272,128]{2,1,0:T(8,128)(2,1)S(1)} %slice.100), channel_id=1, source_target_pairs={{0,32},{16,48},{32,64},{48,80},{64,96},{80,112},{96,0},{112,16},{1... | collective-permute-start | bytes 208904 | tf_op jit(solution)/shard_map/ppermute | solution.py:40
  34.9 8.3 %collective-permute-start.5 = (bf16[1,272,128]{2,1,0:T(8,128)(2,1)S(1)}, bf16[1,272,128]{2,1,0:T(8,128)(2,1)S(1)}, u32[]{:S(2)}, u32[]{:S(2)}) collective-permute-start(bf16[1,272,128]{2,1,0:T(8,128)(2,1)S(1)} %slice.101), channel_id=1, source_target_pairs={{0,96},{16,112},{32,0},{48,16},{64,32},{80,48},{96,64},{112,80},{1... | collective-permute-start | bytes 208904 | tf_op jit(solution)/shard_map/ppermute | solution.py:40
  43.9 14.1 %collective-permute-start.6 = (bf16[8,272,128]{2,1,0:T(8,128)(2,1)}, bf16[8,272,128]{2,1,0:T(8,128)(2,1)S(1)}, u32[]{:S(2)}, u32[]{:S(2)}) collective-permute-start(bf16[8,272,128]{2,1,0:T(8,128)(2,1)} %get-tuple-element.26), channel_id=1, source_target_pairs={{0,128},{16,144},{32,160},{48,176},{64,192},{80,208},{96,224},{112... | collective-permute-start | bytes 1671176 | tf_op jit(solution)/shard_map/ppermute | solution.py:40
  47.1 14.3 %collective-permute-start.7 = (bf16[8,272,128]{2,1,0:T(8,128)(2,1)}, bf16[8,272,128]{2,1,0:T(8,128)(2,1)S(1)}, u32[]{:S(2)}, u32[]{:S(2)}) collective-permute-start(bf16[8,272,128]{2,1,0:T(8,128)(2,1)} %get-tuple-element.26), channel_id=1, source_target_pairs={{0,384},{16,400},{32,416},{48,432},{64,448},{80,464},{96,480},{112... | collective-permute-start | bytes 1671176 | tf_op jit(solution)/shard_map/ppermute | solution.py:40
  49.9 21.9 %copy-start.9 = (s32[32]{0:T(128)}, s32[32]{0:T(128)S(1)}, u32[]{:S(2)}) copy-start(s32[32]{0:T(128)S(1)} %concatenate.66.shards_ref) | copy-start | bytes 388
  58.0 8.4 %collective-permute-start.8 = (bf16[4,272,128]{2,1,0:T(8,128)(2,1)S(1)}, bf16[4,272,128]{2,1,0:T(8,128)(2,1)S(1)}, u32[]{:S(2)}, u32[]{:S(2)}) collective-permute-start(bf16[4,272,128]{2,1,0:T(8,128)(2,1)S(1)} %slice.102), channel_id=1, source_target_pairs={{0,128},{16,144},{32,160},{48,176},{64,192},{80,208},{96,224},{112... | collective-permute-start | bytes 835592 | tf_op jit(solution)/shard_map/ppermute | solution.py:40
  61.5 9.7 %collective-permute-start.9 = (bf16[4,272,128]{2,1,0:T(8,128)(2,1)S(1)}, bf16[4,272,128]{2,1,0:T(8,128)(2,1)S(1)}, u32[]{:S(2)}, u32[]{:S(2)}) collective-permute-start(bf16[4,272,128]{2,1,0:T(8,128)(2,1)S(1)} %slice.103), channel_id=1, source_target_pairs={{0,384},{16,400},{32,416},{48,432},{64,448},{80,464},{96,480},{112... | collective-permute-start | bytes 835592 | tf_op jit(solution)/shard_map/ppermute | solution.py:40
  71.8 25.8 %copy-start.2 = (bf16[1024,128]{1,0:T(8,128)(2,1)S(1)}, bf16[1024,128]{1,0:T(8,128)(2,1)}, u32[]{:S(2)}) copy-start(bf16[1024,128]{1,0:T(8,128)(2,1)} %param.14) | copy-start | bytes 786436
  71.8 25.8 %copy-start.4 = (bf16[1024,128]{1,0:T(8,128)(2,1)S(1)}, bf16[1024,128]{1,0:T(8,128)(2,1)}, u32[]{:S(2)}) copy-start(bf16[1024,128]{1,0:T(8,128)(2,1)} %param.15) | copy-start | bytes 786436
  71.8 25.8 %copy-start.6 = (bf16[1024,128]{1,0:T(8,128)(2,1)S(1)}, bf16[1024,128]{1,0:T(8,128)(2,1)}, u32[]{:S(2)}) copy-start(bf16[1024,128]{1,0:T(8,128)(2,1)} %param.16) | copy-start | bytes 786436
  98.0 7.2 %collective-permute-start.10 = (bf16[64,1024]{1,0:T(8,128)(2,1)S(1)}, bf16[64,1024]{1,0:T(8,128)(2,1)S(1)}, u32[]{:S(2)}, u32[]{:S(2)}) collective-permute-start(bf16[64,1024]{1,0:T(8,128)(2,1)S(1)} %convolution_convert_fusion), channel_id=1, source_target_pairs={{0,2},{2,0},{4,6},{6,4},{8,10},{10,8},{12,14},{14,12},{1,3},{3,1},... | collective-permute-start | bytes 393224 | tf_op jit(solution)/shard_map/ppermute | solution.py:83
  105.2 11.6 %collective-permute-start.11 = (bf16[64,1024]{1,0:T(8,128)(2,1)S(1)}, bf16[64,1024]{1,0:T(8,128)(2,1)S(1)}, u32[]{:S(2)}, u32[]{:S(2)}) collective-permute-start(bf16[64,1024]{1,0:T(8,128)(2,1)S(1)} %add_convert_fusion.2), channel_id=1, source_target_pairs={{0,4},{2,6},{4,0},{6,2},{8,12},{10,14},{12,8},{14,10},{1,5},{3,7},... | collective-permute-start | bytes 393224 | tf_op jit(solution)/shard_map/ppermute | solution.py:83
  116.9 11.9 %collective-permute-start.12 = (bf16[64,1024]{1,0:T(8,128)(2,1)S(1)}, bf16[64,1024]{1,0:T(8,128)(2,1)S(1)}, u32[]{:S(2)}, u32[]{:S(2)}) collective-permute-start(bf16[64,1024]{1,0:T(8,128)(2,1)S(1)} %add_convert_fusion.1), channel_id=1, source_target_pairs={{14,0},{8,6},{6,8},{0,14},{15,1},{9,7},{7,9},{1,15},{30,16},{24,22... | collective-permute-start | bytes 393224 | tf_op jit(solution)/shard_map/ppermute | solution.py:91
  125.9 3.9 %collective-permute-start.13 = (bf16[64,1024]{1,0:T(8,128)(2,1)S(1)}, bf16[64,1024]{1,0:T(8,128)(2,1)S(1)}, u32[]{:S(2)}, u32[]{:S(2)}) collective-permute-start(bf16[64,1024]{1,0:T(8,128)(2,1)S(1)} %add_convert_fusion.1), channel_id=1, source_target_pairs={{14,2},{8,4},{6,10},{0,12},{15,3},{9,5},{7,11},{1,13},{30,18},{24,... | collective-permute-start | bytes 393224 | tf_op jit(solution)/shard_map/ppermute | solution.py:91
  131.2 6.8 %collective-permute-start.14 = (f32[3,1024]{1,0:T(4,128)S(1)}, f32[3,1024]{1,0:T(4,128)S(1)}, u32[]{:S(2)}, u32[]{:S(2)}) collective-permute-start(f32[3,1024]{1,0:T(4,128)S(1)} %fusion.8), channel_id=1, source_target_pairs={{16,0},{32,16},{48,32},{64,48},{80,64},{96,80},{112,96},{128,112},... | collective-permute-start | bytes 36872 | tf_op jit(solution)/shard_map/ppermute | solution.py:23

commit v14 on v13

--- a/solution.py
+++ b/solution.py
@@ -97,10 +97,11 @@
 
 def forward_kernel(
     shards_ref, q_ref, k_ref, v_ref, g_ref, key_code_ref, own_code_ref,
-    att_ref, log_ref, delta_ref, gq_ref, gk_ref, gv_ref,
+    att_ref, gq_ref, gk_ref, gv_ref,
 ):
-    rows = q_ref.shape[0]
-    block_rows = rows // BLOCKS_PER_STEP
+    block_rows = q_ref.shape[1]
+    rows = q_ref.shape[0] * block_rows
+    width = q_ref.shape[2]
     step = pl.program_id(0)
     first = step * BLOCKS_PER_STEP
     row = lax.broadcasted_iota(jnp.int32, (rows, 1), 0)
@@ -110,22 +111,21 @@
     scale = 1.0 / math.sqrt(HD)
     by_rows = (((1,), (1,)), ((), ()))
     by_cols = (((0,), (0,)), ((), ()))
-    queries = q_ref[...]
-    grads = g_ref[...]
-    scores = lax.dot_general(queries, k_ref[...], by_rows, preferred_element_type=jnp.float32) * scale
+    queries = q_ref[...].reshape(rows, width)
+    grads = g_ref[...].reshape(rows, width)
+    keys = k_ref[...].reshape(-1, width)
+    values = v_ref[...].reshape(-1, width)
+    scores = lax.dot_general(queries, keys, by_rows, preferred_element_type=jnp.float32) * scale
     scores = jnp.where(key_code_ref[...] <= q_ids, scores, masked_score)
     row_max = jnp.max(scores, axis=1, keepdims=True)
     softmax_part = jnp.exp(scores - row_max)
     row_sum = jnp.sum(softmax_part, axis=1, keepdims=True)
     product = jnp.dot(
-        softmax_part.astype(jnp.bfloat16), v_ref[...], preferred_element_type=jnp.float32
+        softmax_part.astype(jnp.bfloat16), values, preferred_element_type=jnp.float32
     )
     attention = (product / row_sum).astype(jnp.bfloat16)
     log_total = row_max + jnp.log(row_sum)
     delta = jnp.sum(grads.astype(jnp.float32) * attention.astype(jnp.float32), axis=1, keepdims=True)
-    att_ref[...] = attention
-    log_ref[...] = log_total
-    delta_ref[...] = delta
 
     own = block_rows
 
@@ -133,52 +133,53 @@
     def _():
         probs = jnp.exp(scores[:own] - log_total[:own])
         grad_probs = lax.dot_general(
-            grads[:own], v_ref[...], by_rows, preferred_element_type=jnp.float32
+            grads[:own], values, by_rows, preferred_element_type=jnp.float32
         )
         grad_scores = (probs * (grad_probs - delta[:own])).astype(jnp.bfloat16)
-        gq_ref[...] = jnp.dot(grad_scores, k_ref[...], preferred_element_type=jnp.float32)
+        gq_ref[...] = jnp.dot(grad_scores, keys, preferred_element_type=jnp.float32)
+        att_ref[...] = attention[:own]
         gk_ref[...] = jnp.zeros_like(gk_ref)
         gv_ref[...] = jnp.zeros_like(gv_ref)
 
     own_scores = lax.dot_general(
-        queries, k_ref[:own], by_rows, preferred_element_type=jnp.float32
+        queries, k_ref[0], by_rows, preferred_element_type=jnp.float32
     ) * scale
     own_scores = jnp.where(own_code_ref[...] <= q_ids, own_scores, masked_score)
     probs = jnp.exp(own_scores - log_total)
     gv_ref[...] += lax.dot_general(
         probs.astype(jnp.bfloat16), grads, by_cols, preferred_element_type=jnp.float32
     )
-    grad_probs = lax.dot_general(grads, v_ref[:own], by_rows, preferred_element_type=jnp.float32)
+    grad_probs = lax.dot_general(grads, v_ref[0], by_rows, preferred_element_type=jnp.float32)
     grad_scores = (probs * (grad_probs - delta)).astype(jnp.bfloat16)
     gk_ref[...] += lax.dot_general(grad_scores, queries, by_cols, preferred_element_type=jnp.float32)
 
 
-def attention_all(queries, keys, values, grads, key_code, held_shards, own_rows):
-    slots, width = queries.shape
-    row_spec = pl.BlockSpec((QBLOCK, width), lambda i, shards: (i, 0))
-    full_spec = pl.BlockSpec((slots, width), lambda i, shards: (0, 0))
-    col_spec = pl.BlockSpec((QBLOCK, 1), lambda i, shards: (i, 0))
-    own_spec = pl.BlockSpec((own_rows, width), lambda i, shards: (0, 0))
+def attention_all(gathered, key_code, held_shards):
+    blocks, _, width = gathered.shape
+    block_rows = key_code.shape[0] // blocks
+    slots = blocks * block_rows
+    step_spec = lambda part: pl.BlockSpec(
+        (BLOCKS_PER_STEP, block_rows, width), lambda i, shards: (i, part, 0)
+    )
+    all_spec = lambda part: pl.BlockSpec(
+        (blocks, block_rows, width), lambda i, shards: (0, part, 0)
+    )
+    own_spec = pl.BlockSpec((block_rows, width), lambda i, shards: (0, 0))
     grid_spec = pltpu.PrefetchScalarGridSpec(
         num_scalar_prefetch=1,
-        grid=(slots // QBLOCK,),
-        in_specs=[row_spec, full_spec, full_spec, row_spec,
+        grid=(blocks // BLOCKS_PER_STEP,),
+        in_specs=[step_spec(0), all_spec(1), all_spec(2), step_spec(3),
                   pl.BlockSpec((1, slots), lambda i, shards: (0, 0)),
-                  pl.BlockSpec((1, own_rows), lambda i, shards: (0, 0))],
-        out_specs=[row_spec, col_spec, col_spec, own_spec, own_spec, own_spec],
-    )
-    own_grad = jax.ShapeDtypeStruct((own_rows, width), jnp.float32)
+                  pl.BlockSpec((1, block_rows), lambda i, shards: (0, 0))],
+        out_specs=[own_spec, own_spec, own_spec, own_spec],
+    )
+    own_grad = jax.ShapeDtypeStruct((block_rows, width), jnp.float32)
     return pl.pallas_call(
         forward_kernel,
         grid_spec=grid_spec,
-        out_shape=[
-            jax.ShapeDtypeStruct((slots, width), jnp.bfloat16),
-            jax.ShapeDtypeStruct((slots, 1), jnp.float32),
-            jax.ShapeDtypeStruct((slots, 1), jnp.float32),
-            own_grad, own_grad, own_grad,
-        ],
-    )(held_shards, queries, keys, values, grads, key_code.reshape(1, slots),
-      key_code[:own_rows].reshape(1, own_rows))
+        out_shape=[jax.ShapeDtypeStruct((block_rows, width), jnp.bfloat16), own_grad, own_grad, own_grad],
+    )(held_shards, gathered, gathered, gathered, gathered, key_code.reshape(1, slots),
+      key_code[:block_rows].reshape(1, block_rows))
 
 
 def per_device(
@@ -227,10 +228,6 @@
     gathered, held_shards = gather_blocks(packed, "seq")
     total_slots = shards * slot_count
 
-    def piece(k):
-        return gathered[:, k * slot_count : (k + 1) * slot_count].reshape(total_slots, head_width)
-
-    all_queries, all_keys, all_values, all_grads = piece(0), piece(1), piece(2), piece(3)
     all_counts = gathered[:, 4 * slot_count, 0].astype(jnp.int32)
     all_live = (
         jnp.arange(slot_count, dtype=jnp.int32)[None, :] < all_counts[:, None]
@@ -239,11 +236,10 @@
         held_shards[:, None] * slot_count + jnp.arange(slot_count, dtype=jnp.int32)[None, :]
     ).reshape(total_slots)
 
-    all_attended, _, _, query_grad, key_grad, value_grad = attention_all(
-        all_queries, all_keys, all_values, all_grads,
-        jnp.where(all_live, slot_ids, total_slots), held_shards, slot_count,
-    )
-    attended = jnp.where(live_mask[:, None], all_attended[:slot_count], jnp.bfloat16(0.0))
+    own_attended, query_grad, key_grad, value_grad = attention_all(
+        gathered, jnp.where(all_live, slot_ids, total_slots), held_shards
+    )
+    attended = jnp.where(live_mask[:, None], own_attended, jnp.bfloat16(0.0))
     query_grad_rows = (query_grad * score_scale).astype(jnp.bfloat16)
     key_grad_rows = (key_grad * score_scale).astype(jnp.bfloat16)
     value_grad_rows = value_grad.astype(jnp.bfloat16)

time: 140 us -> 137 us (0.979)
  local copies, waits for them, and re-layouts: 15.7 us -> 12.7 us
    slice x2 -> x1, local copies, waits for them, and re-layouts: 3.54 us -> 0.52 us  [attention_all(): key_code[:block_rows].reshape(1, block_rows)]
    unnamed x28 -> x30, local copies, waits for them, and re-layouts: 5.94 us -> 5.95 us
  transfers between devices with their start and end apart: 15 -> 15, of which waited for: 11 -> 11; matrix products, arithmetic and copies ran while one was open for 8% -> 7% of each run, Pallas kernels for 0% -> 0%
where the time goes in v14:
time: 137 us; the launch traced here: 136 us
  starting transfers between devices  56.6 us (41%)
  waiting for transfers between devices  33.7 us (25%)
  Pallas kernels  17.9 us (13%)
  local copies, waits for them, and re-layouts  12.7 us (9%)
  other arithmetic  9.96 us (7%)
  matrix products  3.86 us (3%)
  between operations  1.73 us (1%)
    ppermute x8, starting transfers between devices, shifted(): return lax.ppermute(array, axis, pairs)  25.1 us
    pallas_call x1, Pallas kernels, attention_all(): pl.pallas_call(forward_kernel, grid_spec=grid_spec, out_shape=[jax.ShapeD...  17.9 us
    ppermute x8, waiting for transfers between devices, shifted(): return lax.ppermute(array, axis, pairs)  17.8 us
    ppermute x2, starting transfers between devices, summed_over(): got = lax.ppermute(sent, axis, [(i, i ^ step) for i in range(devices)])  11.5 us
    ppermute x1, starting transfers between devices, summed_over(): lax.ppermute(sent, axis, near).astype(jnp.float32)  8.97 us
    ppermute x2, starting transfers between devices, passed_along(): return lax.ppermute(array, axis, pairs)  7.67 us
    ppermute x2, waiting for transfers between devices, summed_over(): got = lax.ppermute(sent, axis, [(i, i ^ step) for i in range(devices)])  7.18 us
    unnamed x30, local copies, waits for them, and re-layouts  5.95 us
  transfers between devices with their start and end apart: 15, of which 11 were waited for; matrix products, arithmetic and copies ran while one was open for 7% of the time, Pallas kernels for 0%

profile of v14, /device:TPU:30, one launch (start us, length us, event | category | flops | bytes accessed | tf_op | source)
XLA Modules:
  0.0 136.4 jit_solution(9018557704536493996)
XLA Ops:
  0.6 0.9 slice.112
  1.5 4.7 %collective-permute-start = (bf16[3,1024]{1,0:T(4,128)(2,1)S(1)}, bf16[3,1024]{1,0:T(4,128)(2,1)S(1)}, u32[]{:S(2)}, u32[]{:S(2)}) collective-permute-start(bf16[3,1024]{1,0:T(4,128)(2,1)S(1)} %slice.112), channel_id=1, source_target_pairs={{0,16},{16,32},{32,48},{48,64},{64,80},{80,96},{96,112},{112,128},... | collective-permute-start | bytes 18440 | tf_op jit(solution)/shard_map/ppermute | solution.py:23
  6.2 0.7 iota_subtract_fusion
  7.0 0.1 add.349
  7.1 0.9 fusion.51
  8.7 0.1 multiply_add_fusion.6
  8.8 1.5 %pad_maximum_fusion = bf16[515,1024]{1,0:T(8,128)(2,1)S(1)} fusion(bf16[512,1024]{1,0:T(8,128)(2,1)} %param.10, bf16[3,1024]{1,0:T(4,128)(2,1)S(1)} %collective-permute-done), kind=kLoop, calls=%fused_computation.10 | loop fusion | flops 2109440 | bytes 2109440 | tf_op jit(solution)/shard_map/concatenate | solution.py:206
  10.3 2.0 %gather_fusion = bf16[256,1024]{1,0:T(8,128)(2,1)} fusion(bf16[515,1024]{1,0:T(8,128)(2,1)S(1)} %pad_maximum_fusion, s32[1024]{0:T(1024)S(1)} %pad_clamp_fusion), kind=kCustom, calls=%fused_computation | custom fusion | bytes 1049600 | tf_op jit(solution)/shard_map/jit(_take)/gather | solution.py:208
  12.3 1.2 select_convert_fusion
  13.6 0.6 multiply_reduce_fusion.1
  14.2 0.1 multiply_convert_fusion
  14.3 0.2 fusion.2
  14.5 0.2 fusion.1
  14.7 0.2 fusion
  15.0 1.9 %collective-permute-start.1 = (bf16[1,272,128]{2,1,0:T(8,128)(2,1)S(1)}, bf16[1,272,128]{2,1,0:T(8,128)(2,1)S(1)}, u32[]{:S(2)}, u32[]{:S(2)}) collective-permute-start(bf16[1,272,128]{2,1,0:T(8,128)(2,1)S(1)} %bitcast.20), channel_id=1, source_target_pairs={{0,16},{16,0},{32,48},{48,32},{64,80},{80,64},{96,112},{112,96},{1... | collective-permute-start | bytes 208904 | tf_op jit(solution)/shard_map/ppermute | solution.py:62
  17.1 4.1 %collective-permute-done.1 = bf16[1,272,128]{2,1,0:T(8,128)(2,1)S(1)} collective-permute-done((bf16[1,272,128]{2,1,0:T(8,128)(2,1)S(1)}, bf16[1,272,128]{2,1,0:T(8,128)(2,1)S(1)}, u32[]{:S(2)}, u32[]{:S(2)}) %collective-permute-start.1) | collective-permute-done | bytes 69664 | tf_op jit(solution)/shard_map/ppermute | solution.py:62
  21.2 3.6 %collective-permute-start.2 = (bf16[2,272,128]{2,1,0:T(8,128)(2,1)S(1)}, bf16[2,272,128]{2,1,0:T(8,128)(2,1)S(1)}, u32[]{:S(2)}, u32[]{:S(2)}) collective-permute-start(bf16[2,272,128]{2,1,0:T(8,128)(2,1)S(1)} %pad_maximum_fusion.4), channel_id=1, source_target_pairs={{0,32},{16,48},{32,64},{48,80},{64,96},{80,112},{96,0},{112,16},{1... | collective-permute-start | bytes 417800 | tf_op jit(solution)/shard_map/ppermute | solution.py:40
  24.8 3.2 %collective-permute-start.3 = (bf16[2,272,128]{2,1,0:T(8,128)(2,1)S(1)}, bf16[2,272,128]{2,1,0:T(8,128)(2,1)S(1)}, u32[]{:S(2)}, u32[]{:S(2)}) collective-permute-start(bf16[2,272,128]{2,1,0:T(8,128)(2,1)S(1)} %pad_maximum_fusion.4), channel_id=1, source_target_pairs={{0,96},{16,112},{32,0},{48,16},{64,32},{80,48},{96,64},{112,80},{1... | collective-permute-start | bytes 417800 | tf_op jit(solution)/shard_map/ppermute | solution.py:40
  27.9 0.7 constant_dynamic-update-slice_fusion.7
  28.6 0.7 constant_dynamic-update-slice_fusion.6
  29.3 1.7 %collective-permute-done.2 = bf16[2,272,128]{2,1,0:T(8,128)(2,1)S(1)} collective-permute-done((bf16[2,272,128]{2,1,0:T(8,128)(2,1)S(1)}, bf16[2,272,128]{2,1,0:T(8,128)(2,1)S(1)}, u32[]{:S(2)}, u32[]{:S(2)}) %collective-permute-start.2) | collective-permute-done | bytes 139296 | tf_op jit(solution)/shard_map/ppermute | solution.py:40
  31.0 3.9 %collective-permute-start.4 = (bf16[1,272,128]{2,1,0:T(8,128)(2,1)S(1)}, bf16[1,272,128]{2,1,0:T(8,128)(2,1)S(1)}, u32[]{:S(2)}, u32[]{:S(2)}) collective-permute-start(bf16[1,272,128]{2,1,0:T(8,128)(2,1)S(1)} %slice.80), channel_id=1, source_target_pairs={{0,32},{16,48},{32,64},{48,80},{64,96},{80,112},{96,0},{112,16},{1... | collective-permute-start | bytes 208904 | tf_op jit(solution)/shard_map/ppermute | solution.py:40
  34.9 2.8 %collective-permute-start.5 = (bf16[1,272,128]{2,1,0:T(8,128)(2,1)S(1)}, bf16[1,272,128]{2,1,0:T(8,128)(2,1)S(1)}, u32[]{:S(2)}, u32[]{:S(2)}) collective-permute-start(bf16[1,272,128]{2,1,0:T(8,128)(2,1)S(1)} %slice.81), channel_id=1, source_target_pairs={{0,96},{16,112},{32,0},{48,16},{64,32},{80,48},{96,64},{112,80},{1... | collective-permute-start | bytes 208904 | tf_op jit(solution)/shard_map/ppermute | solution.py:40
  37.7 0.7 constant_dynamic-update-slice_fusion.5
  38.5 0.7 constant_dynamic-update-slice_fusion.4
  39.2 0.7 constant_dynamic-update-slice_fusion.3
  39.9 3.3 %collective-permute-done.5 = bf16[1,272,128]{2,1,0:T(8,128)(2,1)S(1)} collective-permute-done((bf16[1,272,128]{2,1,0:T(8,128)(2,1)S(1)}, bf16[1,272,128]{2,1,0:T(8,128)(2,1)S(1)}, u32[]{:S(2)}, u32[]{:S(2)}) %collective-permute-start.5) | collective-permute-done | bytes 69664 | tf_op jit(solution)/shard_map/ppermute | solution.py:40
  43.2 0.7 constant_dynamic-update-slice_fusion.2
  43.9 3.2 %collective-permute-start.6 = (bf16[8,272,128]{2,1,0:T(8,128)(2,1)}, bf16[8,272,128]{2,1,0:T(8,128)(2,1)S(1)}, u32[]{:S(2)}, u32[]{:S(2)}) collective-permute-start(bf16[8,272,128]{2,1,0:T(8,128)(2,1)} %get-tuple-element.22), channel_id=1, source_target_pairs={{0,128},{16,144},{32,160},{48,176},{64,192},{80,208},{96,224},{112... | collective-permute-start | bytes 1671176 | tf_op jit(solution)/shard_map/ppermute | solution.py:40
  47.1 2.6 %collective-permute-start.7 = (bf16[8,272,128]{2,1,0:T(8,128)(2,1)}, bf16[8,272,128]{2,1,0:T(8,128)(2,1)S(1)}, u32[]{:S(2)}, u32[]{:S(2)}) collective-permute-start(bf16[8,272,128]{2,1,0:T(8,128)(2,1)} %get-tuple-element.22), channel_id=1, source_target_pairs={{0,384},{16,400},{32,416},{48,432},{64,448},{80,464},{96,480},{112... | collective-permute-start | bytes 1671176 | tf_op jit(solution)/shard_map/ppermute | solution.py:40
  49.7 0.1 multiply_add_fusion.2
  50.0 8.0 %collective-permute-done.6 = bf16[8,272,128]{2,1,0:T(8,128)(2,1)S(1)} collective-permute-done((bf16[8,272,128]{2,1,0:T(8,128)(2,1)}, bf16[8,272,128]{2,1,0:T(8,128)(2,1)S(1)}, u32[]{:S(2)}, u32[]{:S(2)}) %collective-permute-start.6) | collective-permute-done | bytes 557088 | tf_op jit(solution)/shard_map/ppermute | solution.py:40
  58.0 3.4 %collective-permute-start.8 = (bf16[4,272,128]{2,1,0:T(8,128)(2,1)S(1)}, bf16[4,272,128]{2,1,0:T(8,128)(2,1)S(1)}, u32[]{:S(2)}, u32[]{:S(2)}) collective-permute-start(bf16[4,272,128]{2,1,0:T(8,128)(2,1)S(1)} %slice.82), channel_id=1, source_target_pairs={{0,128},{16,144},{32,160},{48,176},{64,192},{80,208},{96,224},{112... | collective-permute-start | bytes 835592 | tf_op jit(solution)/shard_map/ppermute | solution.py:40
  61.5 2.4 %collective-permute-start.9 = (bf16[4,272,128]{2,1,0:T(8,128)(2,1)S(1)}, bf16[4,272,128]{2,1,0:T(8,128)(2,1)S(1)}, u32[]{:S(2)}, u32[]{:S(2)}) collective-permute-start(bf16[4,272,128]{2,1,0:T(8,128)(2,1)S(1)} %slice.83), channel_id=1, source_target_pairs={{0,384},{16,400},{32,416},{48,432},{64,448},{80,464},{96,480},{112... | collective-permute-start | bytes 835592 | tf_op jit(solution)/shard_map/ppermute | solution.py:40
  63.9 0.9 constant_dynamic-update-slice_fusion.11
  64.8 0.8 constant_dynamic-update-slice_fusion.10
  65.6 0.8 collective-permute-done.8
  66.4 0.7 constant_dynamic-update-slice_fusion.9
  67.1 4.0 %collective-permute-done.9 = bf16[4,272,128]{2,1,0:T(8,128)(2,1)S(1)} collective-permute-done((bf16[4,272,128]{2,1,0:T(8,128)(2,1)S(1)}, bf16[4,272,128]{2,1,0:T(8,128)(2,1)S(1)}, u32[]{:S(2)}, u32[]{:S(2)}) %collective-permute-start.9) | collective-permute-done | bytes 278560 | tf_op jit(solution)/shard_map/ppermute | solution.py:40
  71.1 0.7 constant_dynamic-update-slice_fusion.8.q_ref.k_ref.v_ref.g_ref
  71.8 1.5 %fusion.28 = s32[32]{0:T(128)S(1)} fusion(bf16[32,272,128]{2,1,0:T(8,128)(2,1)} %constant_dynamic-update-slice_fusion.8.q_ref.k_ref.v_ref.g_ref), kind=kLoop, calls=%fused_computation.74 | loop fusion | flops 32 | bytes 192 | tf_op jit(solution)/shard_map/convert_element_type | solution.py:231
  73.4 0.7 select_n.205.key_code_ref
  74.1 0.5 slice.85.own_code_ref
  74.6 17.9 %shard_map.113 = (bf16[64,128]{1,0:T(8,128)(2,1)}, f32[64,128]{1,0:T(8,128)}, f32[64,128]{1,0:T(8,128)}, f32[64,128]{1,0:T(8,128)}) custom-call(s32[32]{0:T(128)} %copy-done.10, bf16[32,272,128]{2,1,0:T(8,128)(2,1)} %constant_dynamic-update-slice_fusion.8.q_ref.k_ref.v_ref.g_ref, ...), custom_call_target="tpu_custom_call" | custom-call | tf_op jit(solution)/shard_map/pallas_call | solution.py:177
  92.6 0.8 convert_element_type.97
  93.3 0.8 multiply_convert_fusion.1
  94.1 0.8 multiply_convert_fusion.2
  94.9 0.4 convolution_convert_fusion
  95.3 4.3 %collective-permute-start.10 = (bf16[64,1024]{1,0:T(8,128)(2,1)S(1)}, bf16[64,1024]{1,0:T(8,128)(2,1)S(1)}, u32[]{:S(2)}, u32[]{:S(2)}) collective-permute-start(bf16[64,1024]{1,0:T(8,128)(2,1)S(1)} %convolution_convert_fusion), channel_id=1, source_target_pairs={{0,2},{2,0},{4,6},{6,4},{8,10},{10,8},{12,14},{14,12},{1,3},{3,1},... | collective-permute-start | bytes 393224 | tf_op jit(solution)/shard_map/ppermute | solution.py:83
  99.5 2.9 %collective-permute-done.10 = bf16[64,1024]{1,0:T(8,128)(2,1)S(1)} collective-permute-done((bf16[64,1024]{1,0:T(8,128)(2,1)S(1)}, bf16[64,1024]{1,0:T(8,128)(2,1)S(1)}, u32[]{:S(2)}, u32[]{:S(2)}) %collective-permute-start.10) | collective-permute-done | bytes 131104 | tf_op jit(solution)/shard_map/ppermute | solution.py:83
  102.5 7.3 %collective-permute-start.11 = (bf16[64,1024]{1,0:T(8,128)(2,1)S(1)}, bf16[64,1024]{1,0:T(8,128)(2,1)S(1)}, u32[]{:S(2)}, u32[]{:S(2)}) collective-permute-start(bf16[64,1024]{1,0:T(8,128)(2,1)S(1)} %add_convert_fusion.2), channel_id=1, source_target_pairs={{0,4},{2,6},{4,0},{6,2},{8,12},{10,14},{12,8},{14,10},{1,5},{3,7},... | collective-permute-start | bytes 393224 | tf_op jit(solution)/shard_map/ppermute | solution.py:83
  109.9 4.2 %collective-permute-done.11 = bf16[64,1024]{1,0:T(8,128)(2,1)S(1)} collective-permute-done((bf16[64,1024]{1,0:T(8,128)(2,1)S(1)}, bf16[64,1024]{1,0:T(8,128)(2,1)S(1)}, u32[]{:S(2)}, u32[]{:S(2)}) %collective-permute-start.11) | collective-permute-done | bytes 131104 | tf_op jit(solution)/shard_map/ppermute | solution.py:83
  114.2 9.0 %collective-permute-start.12 = (bf16[64,1024]{1,0:T(8,128)(2,1)S(1)}, bf16[64,1024]{1,0:T(8,128)(2,1)S(1)}, u32[]{:S(2)}, u32[]{:S(2)}) collective-permute-start(bf16[64,1024]{1,0:T(8,128)(2,1)S(1)} %add_convert_fusion.1), channel_id=1, source_target_pairs={{14,0},{8,6},{6,8},{0,14},{15,1},{9,7},{7,9},{1,15},{30,16},{24,22... | collective-permute-start | bytes 393224 | tf_op jit(solution)/shard_map/ppermute | solution.py:91
  123.1 1.3 collective-permute-start.13
  124.5 0.7 broadcast_select_fusion
  125.1 0.9 collective-permute-done.12
  126.1 0.9 collective-permute-done.13
  127.0 0.2 multiply_reduce_fusion
  127.2 0.8 multiply_add_fusion
  128.0 0.5 fusion.8
  128.5 3.0 %collective-permute-start.14 = (f32[3,1024]{1,0:T(4,128)S(1)}, f32[3,1024]{1,0:T(4,128)S(1)}, u32[]{:S(2)}, u32[]{:S(2)}) collective-permute-start(f32[3,1024]{1,0:T(4,128)S(1)} %fusion.8), channel_id=1, source_target_pairs={{16,0},{32,16},{48,32},{64,48},{80,64},{96,80},{112,96},{128,112},... | collective-permute-start | bytes 36872 | tf_op jit(solution)/shard_map/ppermute | solution.py:23
  131.5 1.1 fusion.9
  132.6 2.7 %collective-permute-done.14 = f32[3,1024]{1,0:T(4,128)S(1)} collective-permute-done((f32[3,1024]{1,0:T(4,128)S(1)}, f32[3,1024]{1,0:T(4,128)S(1)}, u32[]{:S(2)}, u32[]{:S(2)}) %collective-permute-start.14) | collective-permute-done | bytes 12320 | tf_op jit(solution)/shard_map/ppermute | solution.py:23
  135.3 1.1 add_convert_fusion
  (52 shorter events, 0.9 us)
Async XLA Ops:
  0.6 12.9 %copy-start = (bf16[1024,1024]{1,0:T(8,128)(2,1)S(1)}, bf16[1024,1024]{1,0:T(8,128)(2,1)}, u32[]{:S(2)}) copy-start(bf16[1024,1024]{1,0:T(8,128)(2,1)} %param.12) | copy-start | bytes 6291460
  1.5 7.3 %collective-permute-start = (bf16[3,1024]{1,0:T(4,128)(2,1)S(1)}, bf16[3,1024]{1,0:T(4,128)(2,1)S(1)}, u32[]{:S(2)}, u32[]{:S(2)}) collective-permute-start(bf16[3,1024]{1,0:T(4,128)(2,1)S(1)} %slice.112), channel_id=1, source_target_pairs={{0,16},{16,32},{32,48},{48,64},{64,80},{80,96},{96,112},{112,128},... | collective-permute-start | bytes 18440 | tf_op jit(solution)/shard_map/ppermute | solution.py:23
  12.3 1.9 %copy-start.7 = (f32[1024]{0:T(1024)S(1)}, f32[1024]{0:T(1024)}, u32[]{:S(2)}) copy-start(f32[1024]{0:T(1024)} %param.13) | copy-start | bytes 12292
  12.3 2.0 %copy-start.1 = (bf16[1024,128]{1,0:T(8,128)(2,1)S(1)}, bf16[1024,128]{1,0:T(8,128)(2,1)}, u32[]{:S(2)}) copy-start(bf16[1024,128]{1,0:T(8,128)(2,1)} %param.14) | copy-start | bytes 786436
  12.3 2.2 %copy-start.3 = (bf16[1024,128]{1,0:T(8,128)(2,1)S(1)}, bf16[1024,128]{1,0:T(8,128)(2,1)}, u32[]{:S(2)}) copy-start(bf16[1024,128]{1,0:T(8,128)(2,1)} %param.15) | copy-start | bytes 786436
  13.5 1.1 copy-start.5
  13.5 1.3 copy-start.8
  15.0 6.2 %collective-permute-start.1 = (bf16[1,272,128]{2,1,0:T(8,128)(2,1)S(1)}, bf16[1,272,128]{2,1,0:T(8,128)(2,1)S(1)}, u32[]{:S(2)}, u32[]{:S(2)}) collective-permute-start(bf16[1,272,128]{2,1,0:T(8,128)(2,1)S(1)} %bitcast.20), channel_id=1, source_target_pairs={{0,16},{16,0},{32,48},{48,32},{64,80},{80,64},{96,112},{112,96},{1... | collective-permute-start | bytes 208904 | tf_op jit(solution)/shard_map/ppermute | solution.py:62
  21.2 9.8 %collective-permute-start.2 = (bf16[2,272,128]{2,1,0:T(8,128)(2,1)S(1)}, bf16[2,272,128]{2,1,0:T(8,128)(2,1)S(1)}, u32[]{:S(2)}, u32[]{:S(2)}) collective-permute-start(bf16[2,272,128]{2,1,0:T(8,128)(2,1)S(1)} %pad_maximum_fusion.4), channel_id=1, source_target_pairs={{0,32},{16,48},{32,64},{48,80},{64,96},{80,112},{96,0},{112,16},{1... | collective-permute-start | bytes 417800 | tf_op jit(solution)/shard_map/ppermute | solution.py:40
  24.8 10.1 %collective-permute-start.3 = (bf16[2,272,128]{2,1,0:T(8,128)(2,1)S(1)}, bf16[2,272,128]{2,1,0:T(8,128)(2,1)S(1)}, u32[]{:S(2)}, u32[]{:S(2)}) collective-permute-start(bf16[2,272,128]{2,1,0:T(8,128)(2,1)S(1)} %pad_maximum_fusion.4), channel_id=1, source_target_pairs={{0,96},{16,112},{32,0},{48,16},{64,32},{80,48},{96,64},{112,80},{1... | collective-permute-start | bytes 417800 | tf_op jit(solution)/shard_map/ppermute | solution.py:40
  31.0 8.2 %collective-permute-start.4 = (bf16[1,272,128]{2,1,0:T(8,128)(2,1)S(1)}, bf16[1,272,128]{2,1,0:T(8,128)(2,1)S(1)}, u32[]{:S(2)}, u32[]{:S(2)}) collective-permute-start(bf16[1,272,128]{2,1,0:T(8,128)(2,1)S(1)} %slice.80), channel_id=1, source_target_pairs={{0,32},{16,48},{32,64},{48,80},{64,96},{80,112},{96,0},{112,16},{1... | collective-permute-start | bytes 208904 | tf_op jit(solution)/shard_map/ppermute | solution.py:40
  34.9 8.3 %collective-permute-start.5 = (bf16[1,272,128]{2,1,0:T(8,128)(2,1)S(1)}, bf16[1,272,128]{2,1,0:T(8,128)(2,1)S(1)}, u32[]{:S(2)}, u32[]{:S(2)}) collective-permute-start(bf16[1,272,128]{2,1,0:T(8,128)(2,1)S(1)} %slice.81), channel_id=1, source_target_pairs={{0,96},{16,112},{32,0},{48,16},{64,32},{80,48},{96,64},{112,80},{1... | collective-permute-start | bytes 208904 | tf_op jit(solution)/shard_map/ppermute | solution.py:40
  43.9 14.1 %collective-permute-start.6 = (bf16[8,272,128]{2,1,0:T(8,128)(2,1)}, bf16[8,272,128]{2,1,0:T(8,128)(2,1)S(1)}, u32[]{:S(2)}, u32[]{:S(2)}) collective-permute-start(bf16[8,272,128]{2,1,0:T(8,128)(2,1)} %get-tuple-element.22), channel_id=1, source_target_pairs={{0,128},{16,144},{32,160},{48,176},{64,192},{80,208},{96,224},{112... | collective-permute-start | bytes 1671176 | tf_op jit(solution)/shard_map/ppermute | solution.py:40
  47.1 14.3 %collective-permute-start.7 = (bf16[8,272,128]{2,1,0:T(8,128)(2,1)}, bf16[8,272,128]{2,1,0:T(8,128)(2,1)S(1)}, u32[]{:S(2)}, u32[]{:S(2)}) collective-permute-start(bf16[8,272,128]{2,1,0:T(8,128)(2,1)} %get-tuple-element.22), channel_id=1, source_target_pairs={{0,384},{16,400},{32,416},{48,432},{64,448},{80,464},{96,480},{112... | collective-permute-start | bytes 1671176 | tf_op jit(solution)/shard_map/ppermute | solution.py:40
  49.9 21.9 %copy-start.10 = (s32[32]{0:T(128)}, s32[32]{0:T(128)S(1)}, u32[]{:S(2)}) copy-start(s32[32]{0:T(128)S(1)} %concatenate.66.shards_ref) | copy-start | bytes 388
  58.0 8.4 %collective-permute-start.8 = (bf16[4,272,128]{2,1,0:T(8,128)(2,1)S(1)}, bf16[4,272,128]{2,1,0:T(8,128)(2,1)S(1)}, u32[]{:S(2)}, u32[]{:S(2)}) collective-permute-start(bf16[4,272,128]{2,1,0:T(8,128)(2,1)S(1)} %slice.82), channel_id=1, source_target_pairs={{0,128},{16,144},{32,160},{48,176},{64,192},{80,208},{96,224},{112... | collective-permute-start | bytes 835592 | tf_op jit(solution)/shard_map/ppermute | solution.py:40
  61.5 9.7 %collective-permute-start.9 = (bf16[4,272,128]{2,1,0:T(8,128)(2,1)S(1)}, bf16[4,272,128]{2,1,0:T(8,128)(2,1)S(1)}, u32[]{:S(2)}, u32[]{:S(2)}) collective-permute-start(bf16[4,272,128]{2,1,0:T(8,128)(2,1)S(1)} %slice.83), channel_id=1, source_target_pairs={{0,384},{16,400},{32,416},{48,432},{64,448},{80,464},{96,480},{112... | collective-permute-start | bytes 835592 | tf_op jit(solution)/shard_map/ppermute | solution.py:40
  74.6 20.2 %copy-start.2 = (bf16[1024,128]{1,0:T(8,128)(2,1)S(1)}, bf16[1024,128]{1,0:T(8,128)(2,1)}, u32[]{:S(2)}) copy-start(bf16[1024,128]{1,0:T(8,128)(2,1)} %param.14) | copy-start | bytes 786436
  74.6 20.2 %copy-start.4 = (bf16[1024,128]{1,0:T(8,128)(2,1)S(1)}, bf16[1024,128]{1,0:T(8,128)(2,1)}, u32[]{:S(2)}) copy-start(bf16[1024,128]{1,0:T(8,128)(2,1)} %param.15) | copy-start | bytes 786436
  74.6 20.3 %copy-start.6 = (bf16[1024,128]{1,0:T(8,128)(2,1)S(1)}, bf16[1024,128]{1,0:T(8,128)(2,1)}, u32[]{:S(2)}) copy-start(bf16[1024,128]{1,0:T(8,128)(2,1)} %param.16) | copy-start | bytes 786436
  92.6 31.9 %copy-start.9 = (bf16[64,128]{1,0:T(8,128)(2,1)S(1)}, bf16[64,128]{1,0:T(8,128)(2,1)}, u32[]{:S(2)}) copy-start(bf16[64,128]{1,0:T(8,128)(2,1)} %get-tuple-element.6) | copy-start | bytes 49156
  95.3 7.2 %collective-permute-start.10 = (bf16[64,1024]{1,0:T(8,128)(2,1)S(1)}, bf16[64,1024]{1,0:T(8,128)(2,1)S(1)}, u32[]{:S(2)}, u32[]{:S(2)}) collective-permute-start(bf16[64,1024]{1,0:T(8,128)(2,1)S(1)} %convolution_convert_fusion), channel_id=1, source_target_pairs={{0,2},{2,0},{4,6},{6,4},{8,10},{10,8},{12,14},{14,12},{1,3},{3,1},... | collective-permute-start | bytes 393224 | tf_op jit(solution)/shard_map/ppermute | solution.py:83
  102.5 11.6 %collective-permute-start.11 = (bf16[64,1024]{1,0:T(8,128)(2,1)S(1)}, bf16[64,1024]{1,0:T(8,128)(2,1)S(1)}, u32[]{:S(2)}, u32[]{:S(2)}) collective-permute-start(bf16[64,1024]{1,0:T(8,128)(2,1)S(1)} %add_convert_fusion.2), channel_id=1, source_target_pairs={{0,4},{2,6},{4,0},{6,2},{8,12},{10,14},{12,8},{14,10},{1,5},{3,7},... | collective-permute-start | bytes 393224 | tf_op jit(solution)/shard_map/ppermute | solution.py:83
  114.2 11.9 %collective-permute-start.12 = (bf16[64,1024]{1,0:T(8,128)(2,1)S(1)}, bf16[64,1024]{1,0:T(8,128)(2,1)S(1)}, u32[]{:S(2)}, u32[]{:S(2)}) collective-permute-start(bf16[64,1024]{1,0:T(8,128)(2,1)S(1)} %add_convert_fusion.1), channel_id=1, source_target_pairs={{14,0},{8,6},{6,8},{0,14},{15,1},{9,7},{7,9},{1,15},{30,16},{24,22... | collective-permute-start | bytes 393224 | tf_op jit(solution)/shard_map/ppermute | solution.py:91
  123.1 3.9 %collective-permute-start.13 = (bf16[64,1024]{1,0:T(8,128)(2,1)S(1)}, bf16[64,1024]{1,0:T(8,128)(2,1)S(1)}, u32[]{:S(2)}, u32[]{:S(2)}) collective-permute-start(bf16[64,1024]{1,0:T(8,128)(2,1)S(1)} %add_convert_fusion.1), channel_id=1, source_target_pairs={{14,2},{8,4},{6,10},{0,12},{15,3},{9,5},{7,11},{1,13},{30,18},{24,... | collective-permute-start | bytes 393224 | tf_op jit(solution)/shard_map/ppermute | solution.py:91
  128.5 6.8 %collective-permute-start.14 = (f32[3,1024]{1,0:T(4,128)S(1)}, f32[3,1024]{1,0:T(4,128)S(1)}, u32[]{:S(2)}, u32[]{:S(2)}) collective-permute-start(f32[3,1024]{1,0:T(4,128)S(1)} %fusion.8), channel_id=1, source_target_pairs={{16,0},{32,16},{48,32},{64,48},{80,64},{96,80},{112,96},{128,112},... | collective-permute-start | bytes 36872 | tf_op jit(solution)/shard_map/ppermute | solution.py:23

commit v15 on v14

--- a/solution.py
+++ b/solution.py
@@ -73,25 +73,41 @@
     return held, sources
 
 
+def nearest_exchange(value, axis, nearest):
+    devices = lax.axis_size(axis)
+
+    def distance(src, dst):
+        return min((dst - src) % devices, (src - dst) % devices)
+
+    got = None
+    for hops in sorted({distance(src, dst) for dst, src in nearest.items()}):
+        pairs = [(src, dst) for dst, src in nearest.items() if distance(src, dst) == hops]
+        part = lax.ppermute(value, axis, pairs).astype(jnp.float32)
+        got = part if got is None else got + part
+    return got
+
+
 def summed_over(partial, axis):
     devices = lax.axis_size(axis)
+    if devices == 8:
+        sent = partial.astype(jnp.bfloat16)
+        total = sent.astype(jnp.float32) + lax.ppermute(
+            sent, axis, [(i, i ^ 1) for i in range(devices)]
+        ).astype(jnp.float32)
+        for nearest in (
+            {0: 2, 1: 2, 2: 1, 3: 1, 4: 6, 5: 6, 6: 5, 7: 5},
+            {0: 7, 1: 7, 2: 4, 3: 4, 4: 3, 5: 3, 6: 0, 7: 0},
+        ):
+            sent = total.astype(jnp.bfloat16)
+            total = sent.astype(jnp.float32) + nearest_exchange(sent, axis, nearest)
+        return total
     total = partial
     step = 1
-    last = devices // 2 if devices == 8 else devices
-    while step < last:
+    while step < devices:
         sent = total.astype(jnp.bfloat16)
         got = lax.ppermute(sent, axis, [(i, i ^ step) for i in range(devices)])
         total = sent.astype(jnp.float32) + got.astype(jnp.float32)
         step *= 2
-    if devices == 8:
-        nearest = {0: 7, 1: 7, 2: 4, 3: 4, 4: 3, 5: 3, 6: 0, 7: 0}
-        sent = total.astype(jnp.bfloat16)
-        near = [(src, dst) for dst, src in nearest.items() if min((dst - src) % 8, (src - dst) % 8) == 1]
-        far = [(src, dst) for dst, src in nearest.items() if min((dst - src) % 8, (src - dst) % 8) == 2]
-        got = lax.ppermute(sent, axis, near).astype(jnp.float32) + lax.ppermute(
-            sent, axis, far
-        ).astype(jnp.float32)
-        total = sent.astype(jnp.float32) + got
     return total
 
 

time: 137 us -> 137 us (level)
  starting transfers between devices: 56.6 us -> 50.2 us
  waiting for transfers between devices: 33.7 us -> 39.9 us
    ppermute x4 -> x5, starting transfers between devices: 21.8 us -> 16.5 us  [the longest x4 12.3 us: nearest_exchange(): part = lax.ppermute(value, axis, pairs).astype(jnp.float32)]
    ppermute x4 -> x5, waiting for transfers between devices: 9.05 us -> 14.2 us  [the longest x4 11.2 us: nearest_exchange(): part = lax.ppermute(value, axis, pairs).astype(jnp.float32)]
  transfers between devices with their start and end apart: 15 -> 16, of which waited for: 11 -> 11; matrix products, arithmetic and copies ran while one was open for 7% -> 7% of each run, Pallas kernels for 0% -> 0%
where the time goes in v15:
time: 137 us; the launch traced here: 136 us
  starting transfers between devices  50.2 us (37%)
  waiting for transfers between devices  39.9 us (29%)
  Pallas kernels  17.9 us (13%)
  local copies, waits for them, and re-layouts  12.8 us (9%)
  other arithmetic  9.98 us (7%)
  matrix products  3.86 us (3%)
  between operations  1.74 us (1%)
    ppermute x8, starting transfers between devices, shifted(): return lax.ppermute(array, axis, pairs)  25.1 us
    pallas_call x1, Pallas kernels, attention_all(): pl.pallas_call(forward_kernel, grid_spec=grid_spec, out_shape=[jax.ShapeD...  17.9 us
    ppermute x8, waiting for transfers between devices, shifted(): return lax.ppermute(array, axis, pairs)  17.8 us
    ppermute x4, starting transfers between devices, nearest_exchange(): part = lax.ppermute(value, axis, pairs).astype(jnp.float32)  12.3 us
    ppermute x4, waiting for transfers between devices, nearest_exchange(): part = lax.ppermute(value, axis, pairs).astype(jnp.float32)  11.2 us
    ppermute x2, starting transfers between devices, passed_along(): return lax.ppermute(array, axis, pairs)  6.6 us
    unnamed x30, local copies, waits for them, and re-layouts  5.94 us
    ppermute x1, starting transfers between devices, summed_over(): lax.ppermute(sent, axis, [(i, i ^ 1) for i in range(devices)])  4.25 us
  transfers between devices with their start and end apart: 16, of which 11 were waited for; matrix products, arithmetic and copies ran while one was open for 7% of the time, Pallas kernels for 0%

profile of v15, /device:TPU:30, one launch (start us, length us, event | category | flops | bytes accessed | tf_op | source)
XLA Modules:
  0.0 136.3 jit_solution(15758640142720222094)
XLA Ops:
  0.6 0.9 slice.112
  1.5 4.7 %collective-permute-start = (bf16[3,1024]{1,0:T(4,128)(2,1)S(1)}, bf16[3,1024]{1,0:T(4,128)(2,1)S(1)}, u32[]{:S(2)}, u32[]{:S(2)}) collective-permute-start(bf16[3,1024]{1,0:T(4,128)(2,1)S(1)} %slice.112), channel_id=1, source_target_pairs={{0,16},{16,32},{32,48},{48,64},{64,80},{80,96},{96,112},{112,128},... | collective-permute-start | bytes 18440 | tf_op jit(solution)/shard_map/ppermute | solution.py:23
  6.2 0.7 iota_subtract_fusion
  7.1 0.9 fusion.51
  8.7 0.1 multiply_add_fusion.6
  8.8 1.5 %pad_maximum_fusion = bf16[515,1024]{1,0:T(8,128)(2,1)S(1)} fusion(bf16[512,1024]{1,0:T(8,128)(2,1)} %param.10, bf16[3,1024]{1,0:T(4,128)(2,1)S(1)} %collective-permute-done), kind=kLoop, calls=%fused_computation.10 | loop fusion | flops 2109440 | bytes 2109440 | tf_op jit(solution)/shard_map/concatenate | solution.py:222
  10.3 2.0 %gather_fusion = bf16[256,1024]{1,0:T(8,128)(2,1)} fusion(bf16[515,1024]{1,0:T(8,128)(2,1)S(1)} %pad_maximum_fusion, s32[1024]{0:T(1024)S(1)} %pad_clamp_fusion), kind=kCustom, calls=%fused_computation | custom fusion | bytes 1049600 | tf_op jit(solution)/shard_map/jit(_take)/gather | solution.py:224
  12.3 1.2 select_convert_fusion
  13.6 0.6 multiply_reduce_fusion.1
  14.2 0.1 multiply_convert_fusion
  14.3 0.2 fusion.2
  14.5 0.2 fusion.1
  14.7 0.2 fusion
  15.0 1.9 %collective-permute-start.1 = (bf16[1,272,128]{2,1,0:T(8,128)(2,1)S(1)}, bf16[1,272,128]{2,1,0:T(8,128)(2,1)S(1)}, u32[]{:S(2)}, u32[]{:S(2)}) collective-permute-start(bf16[1,272,128]{2,1,0:T(8,128)(2,1)S(1)} %bitcast.20), channel_id=1, source_target_pairs={{0,16},{16,0},{32,48},{48,32},{64,80},{80,64},{96,112},{112,96},{1... | collective-permute-start | bytes 208904 | tf_op jit(solution)/shard_map/ppermute | solution.py:62
  17.1 4.1 %collective-permute-done.1 = bf16[1,272,128]{2,1,0:T(8,128)(2,1)S(1)} collective-permute-done((bf16[1,272,128]{2,1,0:T(8,128)(2,1)S(1)}, bf16[1,272,128]{2,1,0:T(8,128)(2,1)S(1)}, u32[]{:S(2)}, u32[]{:S(2)}) %collective-permute-start.1) | collective-permute-done | bytes 69664 | tf_op jit(solution)/shard_map/ppermute | solution.py:62
  21.2 3.6 %collective-permute-start.2 = (bf16[2,272,128]{2,1,0:T(8,128)(2,1)S(1)}, bf16[2,272,128]{2,1,0:T(8,128)(2,1)S(1)}, u32[]{:S(2)}, u32[]{:S(2)}) collective-permute-start(bf16[2,272,128]{2,1,0:T(8,128)(2,1)S(1)} %pad_maximum_fusion.4), channel_id=1, source_target_pairs={{0,32},{16,48},{32,64},{48,80},{64,96},{80,112},{96,0},{112,16},{1... | collective-permute-start | bytes 417800 | tf_op jit(solution)/shard_map/ppermute | solution.py:40
  24.8 3.2 %collective-permute-start.3 = (bf16[2,272,128]{2,1,0:T(8,128)(2,1)S(1)}, bf16[2,272,128]{2,1,0:T(8,128)(2,1)S(1)}, u32[]{:S(2)}, u32[]{:S(2)}) collective-permute-start(bf16[2,272,128]{2,1,0:T(8,128)(2,1)S(1)} %pad_maximum_fusion.4), channel_id=1, source_target_pairs={{0,96},{16,112},{32,0},{48,16},{64,32},{80,48},{96,64},{112,80},{1... | collective-permute-start | bytes 417800 | tf_op jit(solution)/shard_map/ppermute | solution.py:40
  27.9 0.7 constant_dynamic-update-slice_fusion.7
  28.6 0.7 constant_dynamic-update-slice_fusion.6
  29.3 1.7 %collective-permute-done.2 = bf16[2,272,128]{2,1,0:T(8,128)(2,1)S(1)} collective-permute-done((bf16[2,272,128]{2,1,0:T(8,128)(2,1)S(1)}, bf16[2,272,128]{2,1,0:T(8,128)(2,1)S(1)}, u32[]{:S(2)}, u32[]{:S(2)}) %collective-permute-start.2) | collective-permute-done | bytes 139296 | tf_op jit(solution)/shard_map/ppermute | solution.py:40
  31.0 3.9 %collective-permute-start.4 = (bf16[1,272,128]{2,1,0:T(8,128)(2,1)S(1)}, bf16[1,272,128]{2,1,0:T(8,128)(2,1)S(1)}, u32[]{:S(2)}, u32[]{:S(2)}) collective-permute-start(bf16[1,272,128]{2,1,0:T(8,128)(2,1)S(1)} %slice.80), channel_id=1, source_target_pairs={{0,32},{16,48},{32,64},{48,80},{64,96},{80,112},{96,0},{112,16},{1... | collective-permute-start | bytes 208904 | tf_op jit(solution)/shard_map/ppermute | solution.py:40
  34.9 2.8 %collective-permute-start.5 = (bf16[1,272,128]{2,1,0:T(8,128)(2,1)S(1)}, bf16[1,272,128]{2,1,0:T(8,128)(2,1)S(1)}, u32[]{:S(2)}, u32[]{:S(2)}) collective-permute-start(bf16[1,272,128]{2,1,0:T(8,128)(2,1)S(1)} %slice.81), channel_id=1, source_target_pairs={{0,96},{16,112},{32,0},{48,16},{64,32},{80,48},{96,64},{112,80},{1... | collective-permute-start | bytes 208904 | tf_op jit(solution)/shard_map/ppermute | solution.py:40
  37.7 0.7 constant_dynamic-update-slice_fusion.5
  38.5 0.7 constant_dynamic-update-slice_fusion.4
  39.2 0.7 constant_dynamic-update-slice_fusion.3
  39.9 3.3 %collective-permute-done.5 = bf16[1,272,128]{2,1,0:T(8,128)(2,1)S(1)} collective-permute-done((bf16[1,272,128]{2,1,0:T(8,128)(2,1)S(1)}, bf16[1,272,128]{2,1,0:T(8,128)(2,1)S(1)}, u32[]{:S(2)}, u32[]{:S(2)}) %collective-permute-start.5) | collective-permute-done | bytes 69664 | tf_op jit(solution)/shard_map/ppermute | solution.py:40
  43.2 0.7 constant_dynamic-update-slice_fusion.2
  43.9 3.2 %collective-permute-start.6 = (bf16[8,272,128]{2,1,0:T(8,128)(2,1)}, bf16[8,272,128]{2,1,0:T(8,128)(2,1)S(1)}, u32[]{:S(2)}, u32[]{:S(2)}) collective-permute-start(bf16[8,272,128]{2,1,0:T(8,128)(2,1)} %get-tuple-element.22), channel_id=1, source_target_pairs={{0,128},{16,144},{32,160},{48,176},{64,192},{80,208},{96,224},{112... | collective-permute-start | bytes 1671176 | tf_op jit(solution)/shard_map/ppermute | solution.py:40
  47.1 2.6 %collective-permute-start.7 = (bf16[8,272,128]{2,1,0:T(8,128)(2,1)}, bf16[8,272,128]{2,1,0:T(8,128)(2,1)S(1)}, u32[]{:S(2)}, u32[]{:S(2)}) collective-permute-start(bf16[8,272,128]{2,1,0:T(8,128)(2,1)} %get-tuple-element.22), channel_id=1, source_target_pairs={{0,384},{16,400},{32,416},{48,432},{64,448},{80,464},{96,480},{112... | collective-permute-start | bytes 1671176 | tf_op jit(solution)/shard_map/ppermute | solution.py:40
  49.7 0.1 multiply_add_fusion.2
  49.9 8.0 %collective-permute-done.6 = bf16[8,272,128]{2,1,0:T(8,128)(2,1)S(1)} collective-permute-done((bf16[8,272,128]{2,1,0:T(8,128)(2,1)}, bf16[8,272,128]{2,1,0:T(8,128)(2,1)S(1)}, u32[]{:S(2)}, u32[]{:S(2)}) %collective-permute-start.6) | collective-permute-done | bytes 557088 | tf_op jit(solution)/shard_map/ppermute | solution.py:40
  58.0 3.4 %collective-permute-start.8 = (bf16[4,272,128]{2,1,0:T(8,128)(2,1)S(1)}, bf16[4,272,128]{2,1,0:T(8,128)(2,1)S(1)}, u32[]{:S(2)}, u32[]{:S(2)}) collective-permute-start(bf16[4,272,128]{2,1,0:T(8,128)(2,1)S(1)} %slice.82), channel_id=1, source_target_pairs={{0,128},{16,144},{32,160},{48,176},{64,192},{80,208},{96,224},{112... | collective-permute-start | bytes 835592 | tf_op jit(solution)/shard_map/ppermute | solution.py:40
  61.5 2.4 %collective-permute-start.9 = (bf16[4,272,128]{2,1,0:T(8,128)(2,1)S(1)}, bf16[4,272,128]{2,1,0:T(8,128)(2,1)S(1)}, u32[]{:S(2)}, u32[]{:S(2)}) collective-permute-start(bf16[4,272,128]{2,1,0:T(8,128)(2,1)S(1)} %slice.83), channel_id=1, source_target_pairs={{0,384},{16,400},{32,416},{48,432},{64,448},{80,464},{96,480},{112... | collective-permute-start | bytes 835592 | tf_op jit(solution)/shard_map/ppermute | solution.py:40
  63.9 0.9 constant_dynamic-update-slice_fusion.11
  64.7 0.8 constant_dynamic-update-slice_fusion.10
  65.6 0.8 collective-permute-done.8
  66.4 0.7 constant_dynamic-update-slice_fusion.9
  67.2 4.0 %collective-permute-done.9 = bf16[4,272,128]{2,1,0:T(8,128)(2,1)S(1)} collective-permute-done((bf16[4,272,128]{2,1,0:T(8,128)(2,1)S(1)}, bf16[4,272,128]{2,1,0:T(8,128)(2,1)S(1)}, u32[]{:S(2)}, u32[]{:S(2)}) %collective-permute-start.9) | collective-permute-done | bytes 278560 | tf_op jit(solution)/shard_map/ppermute | solution.py:40
  71.1 0.7 constant_dynamic-update-slice_fusion.8.q_ref.k_ref.v_ref.g_ref
  71.8 1.5 %fusion.28 = s32[32]{0:T(128)S(1)} fusion(bf16[32,272,128]{2,1,0:T(8,128)(2,1)} %constant_dynamic-update-slice_fusion.8.q_ref.k_ref.v_ref.g_ref), kind=kLoop, calls=%fused_computation.74 | loop fusion | flops 32 | bytes 192 | tf_op jit(solution)/shard_map/convert_element_type | solution.py:247
  73.4 0.7 select_n.205.key_code_ref
  74.1 0.6 slice.85.own_code_ref
  74.7 17.9 %shard_map.113 = (bf16[64,128]{1,0:T(8,128)(2,1)}, f32[64,128]{1,0:T(8,128)}, f32[64,128]{1,0:T(8,128)}, f32[64,128]{1,0:T(8,128)}) custom-call(s32[32]{0:T(128)} %copy-done.10, bf16[32,272,128]{2,1,0:T(8,128)(2,1)} %constant_dynamic-update-slice_fusion.8.q_ref.k_ref.v_ref.g_ref, ...), custom_call_target="tpu_custom_call" | custom-call | tf_op jit(solution)/shard_map/pallas_call | solution.py:193
  92.6 0.8 convert_element_type.100
  93.4 0.8 multiply_convert_fusion.1
  94.1 0.8 multiply_convert_fusion.2
  94.9 0.4 convolution_convert_fusion
  95.3 4.3 %collective-permute-start.10 = (bf16[64,1024]{1,0:T(8,128)(2,1)S(1)}, bf16[64,1024]{1,0:T(8,128)(2,1)S(1)}, u32[]{:S(2)}, u32[]{:S(2)}) collective-permute-start(bf16[64,1024]{1,0:T(8,128)(2,1)S(1)} %convolution_convert_fusion), channel_id=1, source_target_pairs={{0,2},{2,0},{4,6},{6,4},{8,10},{10,8},{12,14},{14,12},{1,3},{3,1},... | collective-permute-start | bytes 393224 | tf_op jit(solution)/shard_map/ppermute | solution.py:94
  99.5 2.9 %collective-permute-done.10 = bf16[64,1024]{1,0:T(8,128)(2,1)S(1)} collective-permute-done((bf16[64,1024]{1,0:T(8,128)(2,1)S(1)}, bf16[64,1024]{1,0:T(8,128)(2,1)S(1)}, u32[]{:S(2)}, u32[]{:S(2)}) %collective-permute-start.10) | collective-permute-done | bytes 131104 | tf_op jit(solution)/shard_map/ppermute | solution.py:94
  102.5 0.7 collective-permute-start.11
  103.2 1.3 collective-permute-start.12
  104.6 9.4 %collective-permute-done.12 = bf16[64,1024]{1,0:T(8,128)(2,1)S(1)} collective-permute-done((bf16[64,1024]{1,0:T(8,128)(2,1)S(1)}, bf16[64,1024]{1,0:T(8,128)(2,1)S(1)}, u32[]{:S(2)}, u32[]{:S(2)}) %collective-permute-start.12) | collective-permute-done | bytes 131104 | tf_op jit(solution)/shard_map/ppermute | solution.py:85
  114.0 9.0 %collective-permute-start.13 = (bf16[64,1024]{1,0:T(8,128)(2,1)S(1)}, bf16[64,1024]{1,0:T(8,128)(2,1)S(1)}, u32[]{:S(2)}, u32[]{:S(2)}) collective-permute-start(bf16[64,1024]{1,0:T(8,128)(2,1)S(1)} %add_convert_fusion.1), channel_id=1, source_target_pairs={{14,0},{8,6},{6,8},{0,14},{15,1},{9,7},{7,9},{1,15},{30,16},{24,22... | collective-permute-start | bytes 393224 | tf_op jit(solution)/shard_map/ppermute | solution.py:85
  123.0 1.3 collective-permute-start.14
  124.3 0.7 broadcast_select_fusion
  125.0 0.9 collective-permute-done.13
  125.9 0.9 collective-permute-done.14
  126.9 0.2 multiply_reduce_fusion
  127.1 0.8 multiply_add_fusion
  127.9 0.5 fusion.8
  128.4 1.9 %collective-permute-start.15 = (f32[3,1024]{1,0:T(4,128)S(1)}, f32[3,1024]{1,0:T(4,128)S(1)}, u32[]{:S(2)}, u32[]{:S(2)}) collective-permute-start(f32[3,1024]{1,0:T(4,128)S(1)} %fusion.8), channel_id=1, source_target_pairs={{16,0},{32,16},{48,32},{64,48},{80,64},{96,80},{112,96},{128,112},... | collective-permute-start | bytes 36872 | tf_op jit(solution)/shard_map/ppermute | solution.py:23
  130.3 1.1 fusion.9
  131.4 3.8 %collective-permute-done.15 = f32[3,1024]{1,0:T(4,128)S(1)} collective-permute-done((f32[3,1024]{1,0:T(4,128)S(1)}, f32[3,1024]{1,0:T(4,128)S(1)}, u32[]{:S(2)}, u32[]{:S(2)}) %collective-permute-start.15) | collective-permute-done | bytes 12320 | tf_op jit(solution)/shard_map/ppermute | solution.py:23
  135.2 1.1 add_convert_fusion
  (54 shorter events, 1.0 us)
Async XLA Ops:
  0.6 12.9 %copy-start = (bf16[1024,1024]{1,0:T(8,128)(2,1)S(1)}, bf16[1024,1024]{1,0:T(8,128)(2,1)}, u32[]{:S(2)}) copy-start(bf16[1024,1024]{1,0:T(8,128)(2,1)} %param.12) | copy-start | bytes 6291460
  1.5 7.3 %collective-permute-start = (bf16[3,1024]{1,0:T(4,128)(2,1)S(1)}, bf16[3,1024]{1,0:T(4,128)(2,1)S(1)}, u32[]{:S(2)}, u32[]{:S(2)}) collective-permute-start(bf16[3,1024]{1,0:T(4,128)(2,1)S(1)} %slice.112), channel_id=1, source_target_pairs={{0,16},{16,32},{32,48},{48,64},{64,80},{80,96},{96,112},{112,128},... | collective-permute-start | bytes 18440 | tf_op jit(solution)/shard_map/ppermute | solution.py:23
  12.3 1.9 %copy-start.7 = (f32[1024]{0:T(1024)S(1)}, f32[1024]{0:T(1024)}, u32[]{:S(2)}) copy-start(f32[1024]{0:T(1024)} %param.13) | copy-start | bytes 12292
  12.3 2.0 %copy-start.1 = (bf16[1024,128]{1,0:T(8,128)(2,1)S(1)}, bf16[1024,128]{1,0:T(8,128)(2,1)}, u32[]{:S(2)}) copy-start(bf16[1024,128]{1,0:T(8,128)(2,1)} %param.14) | copy-start | bytes 786436
  12.3 2.2 %copy-start.3 = (bf16[1024,128]{1,0:T(8,128)(2,1)S(1)}, bf16[1024,128]{1,0:T(8,128)(2,1)}, u32[]{:S(2)}) copy-start(bf16[1024,128]{1,0:T(8,128)(2,1)} %param.15) | copy-start | bytes 786436
  13.5 1.1 copy-start.5
  13.5 1.3 copy-start.8
  15.0 6.2 %collective-permute-start.1 = (bf16[1,272,128]{2,1,0:T(8,128)(2,1)S(1)}, bf16[1,272,128]{2,1,0:T(8,128)(2,1)S(1)}, u32[]{:S(2)}, u32[]{:S(2)}) collective-permute-start(bf16[1,272,128]{2,1,0:T(8,128)(2,1)S(1)} %bitcast.20), channel_id=1, source_target_pairs={{0,16},{16,0},{32,48},{48,32},{64,80},{80,64},{96,112},{112,96},{1... | collective-permute-start | bytes 208904 | tf_op jit(solution)/shard_map/ppermute | solution.py:62
  21.2 9.8 %collective-permute-start.2 = (bf16[2,272,128]{2,1,0:T(8,128)(2,1)S(1)}, bf16[2,272,128]{2,1,0:T(8,128)(2,1)S(1)}, u32[]{:S(2)}, u32[]{:S(2)}) collective-permute-start(bf16[2,272,128]{2,1,0:T(8,128)(2,1)S(1)} %pad_maximum_fusion.4), channel_id=1, source_target_pairs={{0,32},{16,48},{32,64},{48,80},{64,96},{80,112},{96,0},{112,16},{1... | collective-permute-start | bytes 417800 | tf_op jit(solution)/shard_map/ppermute | solution.py:40
  24.8 10.1 %collective-permute-start.3 = (bf16[2,272,128]{2,1,0:T(8,128)(2,1)S(1)}, bf16[2,272,128]{2,1,0:T(8,128)(2,1)S(1)}, u32[]{:S(2)}, u32[]{:S(2)}) collective-permute-start(bf16[2,272,128]{2,1,0:T(8,128)(2,1)S(1)} %pad_maximum_fusion.4), channel_id=1, source_target_pairs={{0,96},{16,112},{32,0},{48,16},{64,32},{80,48},{96,64},{112,80},{1... | collective-permute-start | bytes 417800 | tf_op jit(solution)/shard_map/ppermute | solution.py:40
  31.0 8.3 %collective-permute-start.4 = (bf16[1,272,128]{2,1,0:T(8,128)(2,1)S(1)}, bf16[1,272,128]{2,1,0:T(8,128)(2,1)S(1)}, u32[]{:S(2)}, u32[]{:S(2)}) collective-permute-start(bf16[1,272,128]{2,1,0:T(8,128)(2,1)S(1)} %slice.80), channel_id=1, source_target_pairs={{0,32},{16,48},{32,64},{48,80},{64,96},{80,112},{96,0},{112,16},{1... | collective-permute-start | bytes 208904 | tf_op jit(solution)/shard_map/ppermute | solution.py:40
  34.9 8.3 %collective-permute-start.5 = (bf16[1,272,128]{2,1,0:T(8,128)(2,1)S(1)}, bf16[1,272,128]{2,1,0:T(8,128)(2,1)S(1)}, u32[]{:S(2)}, u32[]{:S(2)}) collective-permute-start(bf16[1,272,128]{2,1,0:T(8,128)(2,1)S(1)} %slice.81), channel_id=1, source_target_pairs={{0,96},{16,112},{32,0},{48,16},{64,32},{80,48},{96,64},{112,80},{1... | collective-permute-start | bytes 208904 | tf_op jit(solution)/shard_map/ppermute | solution.py:40
  43.9 14.1 %collective-permute-start.6 = (bf16[8,272,128]{2,1,0:T(8,128)(2,1)}, bf16[8,272,128]{2,1,0:T(8,128)(2,1)S(1)}, u32[]{:S(2)}, u32[]{:S(2)}) collective-permute-start(bf16[8,272,128]{2,1,0:T(8,128)(2,1)} %get-tuple-element.22), channel_id=1, source_target_pairs={{0,128},{16,144},{32,160},{48,176},{64,192},{80,208},{96,224},{112... | collective-permute-start | bytes 1671176 | tf_op jit(solution)/shard_map/ppermute | solution.py:40
  47.1 14.3 %collective-permute-start.7 = (bf16[8,272,128]{2,1,0:T(8,128)(2,1)}, bf16[8,272,128]{2,1,0:T(8,128)(2,1)S(1)}, u32[]{:S(2)}, u32[]{:S(2)}) collective-permute-start(bf16[8,272,128]{2,1,0:T(8,128)(2,1)} %get-tuple-element.22), channel_id=1, source_target_pairs={{0,384},{16,400},{32,416},{48,432},{64,448},{80,464},{96,480},{112... | collective-permute-start | bytes 1671176 | tf_op jit(solution)/shard_map/ppermute | solution.py:40
  49.9 21.9 %copy-start.10 = (s32[32]{0:T(128)}, s32[32]{0:T(128)S(1)}, u32[]{:S(2)}) copy-start(s32[32]{0:T(128)S(1)} %concatenate.66.shards_ref) | copy-start | bytes 388
  58.0 8.4 %collective-permute-start.8 = (bf16[4,272,128]{2,1,0:T(8,128)(2,1)S(1)}, bf16[4,272,128]{2,1,0:T(8,128)(2,1)S(1)}, u32[]{:S(2)}, u32[]{:S(2)}) collective-permute-start(bf16[4,272,128]{2,1,0:T(8,128)(2,1)S(1)} %slice.82), channel_id=1, source_target_pairs={{0,128},{16,144},{32,160},{48,176},{64,192},{80,208},{96,224},{112... | collective-permute-start | bytes 835592 | tf_op jit(solution)/shard_map/ppermute | solution.py:40
  61.5 9.7 %collective-permute-start.9 = (bf16[4,272,128]{2,1,0:T(8,128)(2,1)S(1)}, bf16[4,272,128]{2,1,0:T(8,128)(2,1)S(1)}, u32[]{:S(2)}, u32[]{:S(2)}) collective-permute-start(bf16[4,272,128]{2,1,0:T(8,128)(2,1)S(1)} %slice.83), channel_id=1, source_target_pairs={{0,384},{16,400},{32,416},{48,432},{64,448},{80,464},{96,480},{112... | collective-permute-start | bytes 835592 | tf_op jit(solution)/shard_map/ppermute | solution.py:40
  74.7 20.2 %copy-start.2 = (bf16[1024,128]{1,0:T(8,128)(2,1)S(1)}, bf16[1024,128]{1,0:T(8,128)(2,1)}, u32[]{:S(2)}) copy-start(bf16[1024,128]{1,0:T(8,128)(2,1)} %param.14) | copy-start | bytes 786436
  74.7 20.2 %copy-start.4 = (bf16[1024,128]{1,0:T(8,128)(2,1)S(1)}, bf16[1024,128]{1,0:T(8,128)(2,1)}, u32[]{:S(2)}) copy-start(bf16[1024,128]{1,0:T(8,128)(2,1)} %param.15) | copy-start | bytes 786436
  74.7 20.2 %copy-start.6 = (bf16[1024,128]{1,0:T(8,128)(2,1)S(1)}, bf16[1024,128]{1,0:T(8,128)(2,1)}, u32[]{:S(2)}) copy-start(bf16[1024,128]{1,0:T(8,128)(2,1)} %param.16) | copy-start | bytes 786436
  92.6 31.7 %copy-start.9 = (bf16[64,128]{1,0:T(8,128)(2,1)S(1)}, bf16[64,128]{1,0:T(8,128)(2,1)}, u32[]{:S(2)}) copy-start(bf16[64,128]{1,0:T(8,128)(2,1)} %get-tuple-element.6) | copy-start | bytes 49156
  95.3 7.2 %collective-permute-start.10 = (bf16[64,1024]{1,0:T(8,128)(2,1)S(1)}, bf16[64,1024]{1,0:T(8,128)(2,1)S(1)}, u32[]{:S(2)}, u32[]{:S(2)}) collective-permute-start(bf16[64,1024]{1,0:T(8,128)(2,1)S(1)} %convolution_convert_fusion), channel_id=1, source_target_pairs={{0,2},{2,0},{4,6},{6,4},{8,10},{10,8},{12,14},{14,12},{1,3},{3,1},... | collective-permute-start | bytes 393224 | tf_op jit(solution)/shard_map/ppermute | solution.py:94
  102.5 2.1 %collective-permute-start.11 = (bf16[64,1024]{1,0:T(8,128)(2,1)S(1)}, bf16[64,1024]{1,0:T(8,128)(2,1)S(1)}, u32[]{:S(2)}, u32[]{:S(2)}) collective-permute-start(bf16[64,1024]{1,0:T(8,128)(2,1)S(1)} %add_convert_fusion.2), channel_id=1, source_target_pairs={{4,2},{2,4},{12,10},{10,12},{5,3},{3,5},{13,11},{11,13},{20,18},{1... | collective-permute-start | bytes 393224 | tf_op jit(solution)/shard_map/ppermute | solution.py:85
  103.2 10.7 %collective-permute-start.12 = (bf16[64,1024]{1,0:T(8,128)(2,1)S(1)}, bf16[64,1024]{1,0:T(8,128)(2,1)S(1)}, u32[]{:S(2)}, u32[]{:S(2)}) collective-permute-start(bf16[64,1024]{1,0:T(8,128)(2,1)S(1)} %add_convert_fusion.2), channel_id=1, source_target_pairs={{4,0},{2,6},{12,8},{10,14},{5,1},{3,7},{13,9},{11,15},{20,16},{18,... | collective-permute-start | bytes 393224 | tf_op jit(solution)/shard_map/ppermute | solution.py:85
  114.0 12.0 %collective-permute-start.13 = (bf16[64,1024]{1,0:T(8,128)(2,1)S(1)}, bf16[64,1024]{1,0:T(8,128)(2,1)S(1)}, u32[]{:S(2)}, u32[]{:S(2)}) collective-permute-start(bf16[64,1024]{1,0:T(8,128)(2,1)S(1)} %add_convert_fusion.1), channel_id=1, source_target_pairs={{14,0},{8,6},{6,8},{0,14},{15,1},{9,7},{7,9},{1,15},{30,16},{24,22... | collective-permute-start | bytes 393224 | tf_op jit(solution)/shard_map/ppermute | solution.py:85
  123.0 3.9 %collective-permute-start.14 = (bf16[64,1024]{1,0:T(8,128)(2,1)S(1)}, bf16[64,1024]{1,0:T(8,128)(2,1)S(1)}, u32[]{:S(2)}, u32[]{:S(2)}) collective-permute-start(bf16[64,1024]{1,0:T(8,128)(2,1)S(1)} %add_convert_fusion.1), channel_id=1, source_target_pairs={{14,2},{8,4},{6,10},{0,12},{15,3},{9,5},{7,11},{1,13},{30,18},{24,... | collective-permute-start | bytes 393224 | tf_op jit(solution)/shard_map/ppermute | solution.py:85
  128.4 6.8 %collective-permute-start.15 = (f32[3,1024]{1,0:T(4,128)S(1)}, f32[3,1024]{1,0:T(4,128)S(1)}, u32[]{:S(2)}, u32[]{:S(2)}) collective-permute-start(f32[3,1024]{1,0:T(4,128)S(1)} %fusion.8), channel_id=1, source_target_pairs={{16,0},{32,16},{48,32},{64,48},{80,64},{96,80},{112,96},{128,112},... | collective-permute-start | bytes 36872 | tf_op jit(solution)/shard_map/ppermute | solution.py:23

commit v16 on v14

--- a/solution.py
+++ b/solution.py
@@ -203,9 +203,10 @@
     first_slot = shard_index * slot_count
     own_ids = first_slot + jnp.arange(slot_count, dtype=jnp.int32)
     before_rim = neighbour(byte_states[row_count - (KCONV - 1) :].astype(jnp.float32), 1)
-    extended = jnp.concatenate([before_rim.astype(jnp.bfloat16), byte_states], axis=0)
-    tap_rows = (boundaries[None, :] + jnp.arange(KCONV - 1, -1, -1, dtype=jnp.int32)[:, None])
-    tapped = jnp.take(extended, tap_rows.reshape(-1), axis=0).astype(jnp.float32)
+    tap_rows = (boundaries[None, :] - jnp.arange(KCONV, dtype=jnp.int32)[:, None]).reshape(-1)
+    tapped = jnp.take(byte_states, jnp.maximum(tap_rows, 0), axis=0).astype(jnp.float32)
+    rim_tapped = jnp.take(before_rim, jnp.clip(tap_rows + (KCONV - 1), 0, KCONV - 2), axis=0)
+    tapped = jnp.where((tap_rows < 0)[:, None], rim_tapped, tapped)
     tapped = tapped.reshape(KCONV, slot_count, D)
     span_depth = conv_kernel[0] * tapped[0]
     for offset in range(1, KCONV):

time: 137 us -> 138 us (level)
  waiting for transfers between devices: 33.7 us -> 31.3 us
  local copies, waits for them, and re-layouts: 12.7 us -> 14.6 us
    gather x1 -> x2, local copies, waits for them, and re-layouts: 1.96 us -> 4.75 us  [the longest x1 3.71 us: per_device(): jnp.take(byte_states, jnp.maximum(tap_rows, 0), axis=0).astype(jnp.float32)]
    concatenate x1 -> x0, other arithmetic: 1.5 us -> none  [per_device(): jnp.concatenate([before_rim.astype(jnp.bfloat16), byte_states], axis=0)]
    ppermute x1, starting transfers between devices: 8.97 us -> 10.4 us  [summed_over(): lax.ppermute(sent, axis, near).astype(jnp.float32)]
  transfers between devices with their start and end apart: 15 -> 15, of which waited for: 11 -> 11; matrix products, arithmetic and copies ran while one was open for 7% -> 10% of each run, Pallas kernels for 0% -> 0%
where the time goes in v16:
time: 138 us; the launch traced here: 137 us
  starting transfers between devices  57.8 us (42%)
  waiting for transfers between devices  31.3 us (23%)
  Pallas kernels  17.9 us (13%)
  local copies, waits for them, and re-layouts  14.6 us (11%)
  other arithmetic  9.36 us (7%)
  matrix products  3.86 us (3%)
  between operations  1.72 us (1%)
    ppermute x8, starting transfers between devices, shifted(): return lax.ppermute(array, axis, pairs)  25.2 us
    pallas_call x1, Pallas kernels, attention_all(): pl.pallas_call(forward_kernel, grid_spec=grid_spec, out_shape=[jax.ShapeD...  17.9 us
    ppermute x8, waiting for transfers between devices, shifted(): return lax.ppermute(array, axis, pairs)  16.7 us
    ppermute x2, starting transfers between devices, summed_over(): got = lax.ppermute(sent, axis, [(i, i ^ step) for i in range(devices)])  11.4 us
    ppermute x1, starting transfers between devices, summed_over(): lax.ppermute(sent, axis, near).astype(jnp.float32)  10.4 us
    ppermute x2, starting transfers between devices, passed_along(): return lax.ppermute(array, axis, pairs)  7.55 us
    unnamed x30, local copies, waits for them, and re-layouts  5.93 us
    ppermute x2, waiting for transfers between devices, summed_over(): got = lax.ppermute(sent, axis, [(i, i ^ step) for i in range(devices)])  5.85 us
  transfers between devices with their start and end apart: 15, of which 11 were waited for; matrix products, arithmetic and copies ran while one was open for 10% of the time, Pallas kernels for 0%

profile of v16, /device:TPU:30, one launch (start us, length us, event | category | flops | bytes accessed | tf_op | source)
XLA Modules:
  0.0 136.6 jit_solution(11048200051632917632)
XLA Ops:
  0.6 0.9 slice_convert_fusion.1
  1.5 4.7 %collective-permute-start = (f32[3,1024]{1,0:T(4,128)S(1)}, f32[3,1024]{1,0:T(4,128)S(1)}, u32[]{:S(2)}, u32[]{:S(2)}) collective-permute-start(f32[3,1024]{1,0:T(4,128)S(1)} %slice_convert_fusion.1), channel_id=1, source_target_pairs={{0,16},{16,32},{32,48},{48,64},{64,80},{80,96},{96,112},{112,128},... | collective-permute-start | bytes 36872 | tf_op jit(solution)/shard_map/ppermute | solution.py:23
  6.2 0.7 iota_subtract_fusion
  7.1 0.9 fusion.52
  8.7 0.1 multiply_add_fusion.5
  8.8 3.7 %gather_fusion.1 = bf16[256,1024]{1,0:T(8,128)(2,1)} fusion(bf16[512,1024]{1,0:T(8,128)(2,1)} %param.10, s32[1024]{0:T(1024)S(1)} %get-tuple-element.46), kind=kCustom, calls=%fused_computation.1 | custom fusion | bytes 1049600 | tf_op jit(solution)/shard_map/jit(_take)/gather | solution.py:207
  12.5 1.0 gather_fusion
  13.6 1.3 convert_select_fusion
  15.0 0.6 multiply_reduce_fusion.1
  15.6 0.1 multiply_convert_fusion
  15.7 0.2 fusion.2
  15.9 0.2 fusion.1
  16.1 0.2 fusion
  16.3 0.1 constant_dynamic-update-slice_fusion.1
  16.4 1.9 %collective-permute-start.1 = (bf16[1,272,128]{2,1,0:T(8,128)(2,1)S(1)}, bf16[1,272,128]{2,1,0:T(8,128)(2,1)S(1)}, u32[]{:S(2)}, u32[]{:S(2)}) collective-permute-start(bf16[1,272,128]{2,1,0:T(8,128)(2,1)S(1)} %bitcast.20), channel_id=1, source_target_pairs={{0,16},{16,0},{32,48},{48,32},{64,80},{80,64},{96,112},{112,96},{1... | collective-permute-start | bytes 208904 | tf_op jit(solution)/shard_map/ppermute | solution.py:62
  18.5 4.1 %collective-permute-done.1 = bf16[1,272,128]{2,1,0:T(8,128)(2,1)S(1)} collective-permute-done((bf16[1,272,128]{2,1,0:T(8,128)(2,1)S(1)}, bf16[1,272,128]{2,1,0:T(8,128)(2,1)S(1)}, u32[]{:S(2)}, u32[]{:S(2)}) %collective-permute-start.1) | collective-permute-done | bytes 69664 | tf_op jit(solution)/shard_map/ppermute | solution.py:62
  22.6 2.7 %collective-permute-start.2 = (bf16[2,272,128]{2,1,0:T(8,128)(2,1)S(1)}, bf16[2,272,128]{2,1,0:T(8,128)(2,1)S(1)}, u32[]{:S(2)}, u32[]{:S(2)}) collective-permute-start(bf16[2,272,128]{2,1,0:T(8,128)(2,1)S(1)} %pad_maximum_fusion.3), channel_id=1, source_target_pairs={{0,32},{16,48},{32,64},{48,80},{64,96},{80,112},{96,0},{112,16},{1... | collective-permute-start | bytes 417800 | tf_op jit(solution)/shard_map/ppermute | solution.py:40
  25.3 4.0 %collective-permute-start.3 = (bf16[2,272,128]{2,1,0:T(8,128)(2,1)S(1)}, bf16[2,272,128]{2,1,0:T(8,128)(2,1)S(1)}, u32[]{:S(2)}, u32[]{:S(2)}) collective-permute-start(bf16[2,272,128]{2,1,0:T(8,128)(2,1)S(1)} %pad_maximum_fusion.3), channel_id=1, source_target_pairs={{0,96},{16,112},{32,0},{48,16},{64,32},{80,48},{96,64},{112,80},{1... | collective-permute-start | bytes 417800 | tf_op jit(solution)/shard_map/ppermute | solution.py:40
  29.3 0.7 constant_dynamic-update-slice_fusion.7
  30.0 0.7 constant_dynamic-update-slice_fusion.6
  30.7 1.5 %collective-permute-done.2 = bf16[2,272,128]{2,1,0:T(8,128)(2,1)S(1)} collective-permute-done((bf16[2,272,128]{2,1,0:T(8,128)(2,1)S(1)}, bf16[2,272,128]{2,1,0:T(8,128)(2,1)S(1)}, u32[]{:S(2)}, u32[]{:S(2)}) %collective-permute-start.2) | collective-permute-done | bytes 139296 | tf_op jit(solution)/shard_map/ppermute | solution.py:40
  32.1 3.7 %collective-permute-start.4 = (bf16[1,272,128]{2,1,0:T(8,128)(2,1)S(1)}, bf16[1,272,128]{2,1,0:T(8,128)(2,1)S(1)}, u32[]{:S(2)}, u32[]{:S(2)}) collective-permute-start(bf16[1,272,128]{2,1,0:T(8,128)(2,1)S(1)} %slice.82), channel_id=1, source_target_pairs={{0,32},{16,48},{32,64},{48,80},{64,96},{80,112},{96,0},{112,16},{1... | collective-permute-start | bytes 208904 | tf_op jit(solution)/shard_map/ppermute | solution.py:40
  35.9 3.0 %collective-permute-start.5 = (bf16[1,272,128]{2,1,0:T(8,128)(2,1)S(1)}, bf16[1,272,128]{2,1,0:T(8,128)(2,1)S(1)}, u32[]{:S(2)}, u32[]{:S(2)}) collective-permute-start(bf16[1,272,128]{2,1,0:T(8,128)(2,1)S(1)} %slice.83), channel_id=1, source_target_pairs={{0,96},{16,112},{32,0},{48,16},{64,32},{80,48},{96,64},{112,80},{1... | collective-permute-start | bytes 208904 | tf_op jit(solution)/shard_map/ppermute | solution.py:40
  39.0 0.7 constant_dynamic-update-slice_fusion.5
  39.7 0.7 constant_dynamic-update-slice_fusion.4
  40.4 0.7 constant_dynamic-update-slice_fusion.3
  41.1 3.2 %collective-permute-done.5 = bf16[1,272,128]{2,1,0:T(8,128)(2,1)S(1)} collective-permute-done((bf16[1,272,128]{2,1,0:T(8,128)(2,1)S(1)}, bf16[1,272,128]{2,1,0:T(8,128)(2,1)S(1)}, u32[]{:S(2)}, u32[]{:S(2)}) %collective-permute-start.5) | collective-permute-done | bytes 69664 | tf_op jit(solution)/shard_map/ppermute | solution.py:40
  44.3 0.7 constant_dynamic-update-slice_fusion.2
  45.0 2.9 %collective-permute-start.6 = (bf16[8,272,128]{2,1,0:T(8,128)(2,1)}, bf16[8,272,128]{2,1,0:T(8,128)(2,1)S(1)}, u32[]{:S(2)}, u32[]{:S(2)}) collective-permute-start(bf16[8,272,128]{2,1,0:T(8,128)(2,1)} %get-tuple-element.22), channel_id=1, source_target_pairs={{0,128},{16,144},{32,160},{48,176},{64,192},{80,208},{96,224},{112... | collective-permute-start | bytes 1671176 | tf_op jit(solution)/shard_map/ppermute | solution.py:40
  48.0 2.9 %collective-permute-start.7 = (bf16[8,272,128]{2,1,0:T(8,128)(2,1)}, bf16[8,272,128]{2,1,0:T(8,128)(2,1)S(1)}, u32[]{:S(2)}, u32[]{:S(2)}) collective-permute-start(bf16[8,272,128]{2,1,0:T(8,128)(2,1)} %get-tuple-element.22), channel_id=1, source_target_pairs={{0,384},{16,400},{32,416},{48,432},{64,448},{80,464},{96,480},{112... | collective-permute-start | bytes 1671176 | tf_op jit(solution)/shard_map/ppermute | solution.py:40
  50.8 0.1 multiply_add_fusion.1
  51.1 6.9 %collective-permute-done.6 = bf16[8,272,128]{2,1,0:T(8,128)(2,1)S(1)} collective-permute-done((bf16[8,272,128]{2,1,0:T(8,128)(2,1)}, bf16[8,272,128]{2,1,0:T(8,128)(2,1)S(1)}, u32[]{:S(2)}, u32[]{:S(2)}) %collective-permute-start.6) | collective-permute-done | bytes 557088 | tf_op jit(solution)/shard_map/ppermute | solution.py:40
  58.0 3.7 %collective-permute-start.8 = (bf16[4,272,128]{2,1,0:T(8,128)(2,1)S(1)}, bf16[4,272,128]{2,1,0:T(8,128)(2,1)S(1)}, u32[]{:S(2)}, u32[]{:S(2)}) collective-permute-start(bf16[4,272,128]{2,1,0:T(8,128)(2,1)S(1)} %slice.84), channel_id=1, source_target_pairs={{0,128},{16,144},{32,160},{48,176},{64,192},{80,208},{96,224},{112... | collective-permute-start | bytes 835592 | tf_op jit(solution)/shard_map/ppermute | solution.py:40
  61.7 2.1 %collective-permute-start.9 = (bf16[4,272,128]{2,1,0:T(8,128)(2,1)S(1)}, bf16[4,272,128]{2,1,0:T(8,128)(2,1)S(1)}, u32[]{:S(2)}, u32[]{:S(2)}) collective-permute-start(bf16[4,272,128]{2,1,0:T(8,128)(2,1)S(1)} %slice.85), channel_id=1, source_target_pairs={{0,384},{16,400},{32,416},{48,432},{64,448},{80,464},{96,480},{112... | collective-permute-start | bytes 835592 | tf_op jit(solution)/shard_map/ppermute | solution.py:40
  63.9 0.8 constant_dynamic-update-slice_fusion.11
  64.7 0.8 constant_dynamic-update-slice_fusion.10
  65.6 0.8 collective-permute-done.8
  66.4 0.7 constant_dynamic-update-slice_fusion.9
  67.1 4.2 %collective-permute-done.9 = bf16[4,272,128]{2,1,0:T(8,128)(2,1)S(1)} collective-permute-done((bf16[4,272,128]{2,1,0:T(8,128)(2,1)S(1)}, bf16[4,272,128]{2,1,0:T(8,128)(2,1)S(1)}, u32[]{:S(2)}, u32[]{:S(2)}) %collective-permute-start.9) | collective-permute-done | bytes 278560 | tf_op jit(solution)/shard_map/ppermute | solution.py:40
  71.4 0.7 constant_dynamic-update-slice_fusion.8.q_ref.k_ref.v_ref.g_ref
  72.1 1.5 %fusion.28 = s32[32]{0:T(128)S(1)} fusion(bf16[32,272,128]{2,1,0:T(8,128)(2,1)} %constant_dynamic-update-slice_fusion.8.q_ref.k_ref.v_ref.g_ref), kind=kLoop, calls=%fused_computation.74 | loop fusion | flops 32 | bytes 192 | tf_op jit(solution)/shard_map/convert_element_type | solution.py:232
  73.7 0.7 select_n.217.key_code_ref
  74.4 0.5 slice.87.own_code_ref
  74.9 17.9 %shard_map.113 = (bf16[64,128]{1,0:T(8,128)(2,1)}, f32[64,128]{1,0:T(8,128)}, f32[64,128]{1,0:T(8,128)}, f32[64,128]{1,0:T(8,128)}) custom-call(s32[32]{0:T(128)} %copy-done.10, bf16[32,272,128]{2,1,0:T(8,128)(2,1)} %constant_dynamic-update-slice_fusion.8.q_ref.k_ref.v_ref.g_ref, ...), custom_call_target="tpu_custom_call" | custom-call | tf_op jit(solution)/shard_map/pallas_call | solution.py:177
  92.8 0.8 convert_element_type.93
  93.6 0.8 multiply_convert_fusion.1
  94.4 0.8 multiply_convert_fusion.2
  95.1 0.4 convolution_convert_fusion
  95.5 4.5 %collective-permute-start.10 = (bf16[64,1024]{1,0:T(8,128)(2,1)S(1)}, bf16[64,1024]{1,0:T(8,128)(2,1)S(1)}, u32[]{:S(2)}, u32[]{:S(2)}) collective-permute-start(bf16[64,1024]{1,0:T(8,128)(2,1)S(1)} %convolution_convert_fusion), channel_id=1, source_target_pairs={{0,2},{2,0},{4,6},{6,4},{8,10},{10,8},{12,14},{14,12},{1,3},{3,1},... | collective-permute-start | bytes 393224 | tf_op jit(solution)/shard_map/ppermute | solution.py:83
  100.0 2.9 %collective-permute-done.10 = bf16[64,1024]{1,0:T(8,128)(2,1)S(1)} collective-permute-done((bf16[64,1024]{1,0:T(8,128)(2,1)S(1)}, bf16[64,1024]{1,0:T(8,128)(2,1)S(1)}, u32[]{:S(2)}, u32[]{:S(2)}) %collective-permute-start.10) | collective-permute-done | bytes 131104 | tf_op jit(solution)/shard_map/ppermute | solution.py:83
  103.0 6.9 %collective-permute-start.11 = (bf16[64,1024]{1,0:T(8,128)(2,1)S(1)}, bf16[64,1024]{1,0:T(8,128)(2,1)S(1)}, u32[]{:S(2)}, u32[]{:S(2)}) collective-permute-start(bf16[64,1024]{1,0:T(8,128)(2,1)S(1)} %add_convert_fusion.2), channel_id=1, source_target_pairs={{0,4},{2,6},{4,0},{6,2},{8,12},{10,14},{12,8},{14,10},{1,5},{3,7},... | collective-permute-start | bytes 393224 | tf_op jit(solution)/shard_map/ppermute | solution.py:83
  109.9 2.9 %collective-permute-done.11 = bf16[64,1024]{1,0:T(8,128)(2,1)S(1)} collective-permute-done((bf16[64,1024]{1,0:T(8,128)(2,1)S(1)}, bf16[64,1024]{1,0:T(8,128)(2,1)S(1)}, u32[]{:S(2)}, u32[]{:S(2)}) %collective-permute-start.11) | collective-permute-done | bytes 131104 | tf_op jit(solution)/shard_map/ppermute | solution.py:83
  112.9 10.4 %collective-permute-start.12 = (bf16[64,1024]{1,0:T(8,128)(2,1)S(1)}, bf16[64,1024]{1,0:T(8,128)(2,1)S(1)}, u32[]{:S(2)}, u32[]{:S(2)}) collective-permute-start(bf16[64,1024]{1,0:T(8,128)(2,1)S(1)} %add_convert_fusion.1), channel_id=1, source_target_pairs={{14,0},{8,6},{6,8},{0,14},{15,1},{9,7},{7,9},{1,15},{30,16},{24,22... | collective-permute-start | bytes 393224 | tf_op jit(solution)/shard_map/ppermute | solution.py:91
  123.3 1.3 collective-permute-start.13
  124.6 0.7 broadcast_select_fusion
  125.3 0.9 collective-permute-done.12
  126.2 0.9 collective-permute-done.13
  127.2 0.2 multiply_reduce_fusion
  127.3 0.8 multiply_add_fusion
  128.2 0.5 fusion.8
  128.6 2.9 %collective-permute-start.14 = (f32[3,1024]{1,0:T(4,128)S(1)}, f32[3,1024]{1,0:T(4,128)S(1)}, u32[]{:S(2)}, u32[]{:S(2)}) collective-permute-start(f32[3,1024]{1,0:T(4,128)S(1)} %fusion.8), channel_id=1, source_target_pairs={{16,0},{32,16},{48,32},{64,48},{80,64},{96,80},{112,96},{128,112},... | collective-permute-start | bytes 36872 | tf_op jit(solution)/shard_map/ppermute | solution.py:23
  131.5 1.1 fusion.9
  132.6 2.9 %collective-permute-done.14 = f32[3,1024]{1,0:T(4,128)S(1)} collective-permute-done((f32[3,1024]{1,0:T(4,128)S(1)}, f32[3,1024]{1,0:T(4,128)S(1)}, u32[]{:S(2)}, u32[]{:S(2)}) %collective-permute-start.14) | collective-permute-done | bytes 12320 | tf_op jit(solution)/shard_map/ppermute | solution.py:23
  135.5 1.1 add_convert_fusion
  (51 shorter events, 0.9 us)
Async XLA Ops:
  0.6 14.3 %copy-start = (bf16[1024,1024]{1,0:T(8,128)(2,1)S(1)}, bf16[1024,1024]{1,0:T(8,128)(2,1)}, u32[]{:S(2)}) copy-start(bf16[1024,1024]{1,0:T(8,128)(2,1)} %param.12) | copy-start | bytes 6291460
  1.5 11.0 %collective-permute-start = (f32[3,1024]{1,0:T(4,128)S(1)}, f32[3,1024]{1,0:T(4,128)S(1)}, u32[]{:S(2)}, u32[]{:S(2)}) collective-permute-start(f32[3,1024]{1,0:T(4,128)S(1)} %slice_convert_fusion.1), channel_id=1, source_target_pairs={{0,16},{16,32},{32,48},{48,64},{64,80},{80,96},{96,112},{112,128},... | collective-permute-start | bytes 36872 | tf_op jit(solution)/shard_map/ppermute | solution.py:23
  13.6 2.0 %copy-start.7 = (f32[1024]{0:T(1024)S(1)}, f32[1024]{0:T(1024)}, u32[]{:S(2)}) copy-start(f32[1024]{0:T(1024)} %param.13) | copy-start | bytes 12292
  13.6 2.1 %copy-start.1 = (bf16[1024,128]{1,0:T(8,128)(2,1)S(1)}, bf16[1024,128]{1,0:T(8,128)(2,1)}, u32[]{:S(2)}) copy-start(bf16[1024,128]{1,0:T(8,128)(2,1)} %param.14) | copy-start | bytes 786436
  14.9 1.0 copy-start.3
  14.9 1.1 copy-start.5
  14.9 1.3 copy-start.8
  16.4 6.2 %collective-permute-start.1 = (bf16[1,272,128]{2,1,0:T(8,128)(2,1)S(1)}, bf16[1,272,128]{2,1,0:T(8,128)(2,1)S(1)}, u32[]{:S(2)}, u32[]{:S(2)}) collective-permute-start(bf16[1,272,128]{2,1,0:T(8,128)(2,1)S(1)} %bitcast.20), channel_id=1, source_target_pairs={{0,16},{16,0},{32,48},{48,32},{64,80},{80,64},{96,112},{112,96},{1... | collective-permute-start | bytes 208904 | tf_op jit(solution)/shard_map/ppermute | solution.py:62
  22.6 9.6 %collective-permute-start.2 = (bf16[2,272,128]{2,1,0:T(8,128)(2,1)S(1)}, bf16[2,272,128]{2,1,0:T(8,128)(2,1)S(1)}, u32[]{:S(2)}, u32[]{:S(2)}) collective-permute-start(bf16[2,272,128]{2,1,0:T(8,128)(2,1)S(1)} %pad_maximum_fusion.3), channel_id=1, source_target_pairs={{0,32},{16,48},{32,64},{48,80},{64,96},{80,112},{96,0},{112,16},{1... | collective-permute-start | bytes 417800 | tf_op jit(solution)/shard_map/ppermute | solution.py:40
  25.3 10.6 %collective-permute-start.3 = (bf16[2,272,128]{2,1,0:T(8,128)(2,1)S(1)}, bf16[2,272,128]{2,1,0:T(8,128)(2,1)S(1)}, u32[]{:S(2)}, u32[]{:S(2)}) collective-permute-start(bf16[2,272,128]{2,1,0:T(8,128)(2,1)S(1)} %pad_maximum_fusion.3), channel_id=1, source_target_pairs={{0,96},{16,112},{32,0},{48,16},{64,32},{80,48},{96,64},{112,80},{1... | collective-permute-start | bytes 417800 | tf_op jit(solution)/shard_map/ppermute | solution.py:40
  32.1 8.3 %collective-permute-start.4 = (bf16[1,272,128]{2,1,0:T(8,128)(2,1)S(1)}, bf16[1,272,128]{2,1,0:T(8,128)(2,1)S(1)}, u32[]{:S(2)}, u32[]{:S(2)}) collective-permute-start(bf16[1,272,128]{2,1,0:T(8,128)(2,1)S(1)} %slice.82), channel_id=1, source_target_pairs={{0,32},{16,48},{32,64},{48,80},{64,96},{80,112},{96,0},{112,16},{1... | collective-permute-start | bytes 208904 | tf_op jit(solution)/shard_map/ppermute | solution.py:40
  35.9 8.4 %collective-permute-start.5 = (bf16[1,272,128]{2,1,0:T(8,128)(2,1)S(1)}, bf16[1,272,128]{2,1,0:T(8,128)(2,1)S(1)}, u32[]{:S(2)}, u32[]{:S(2)}) collective-permute-start(bf16[1,272,128]{2,1,0:T(8,128)(2,1)S(1)} %slice.83), channel_id=1, source_target_pairs={{0,96},{16,112},{32,0},{48,16},{64,32},{80,48},{96,64},{112,80},{1... | collective-permute-start | bytes 208904 | tf_op jit(solution)/shard_map/ppermute | solution.py:40
  45.0 13.0 %collective-permute-start.6 = (bf16[8,272,128]{2,1,0:T(8,128)(2,1)}, bf16[8,272,128]{2,1,0:T(8,128)(2,1)S(1)}, u32[]{:S(2)}, u32[]{:S(2)}) collective-permute-start(bf16[8,272,128]{2,1,0:T(8,128)(2,1)} %get-tuple-element.22), channel_id=1, source_target_pairs={{0,128},{16,144},{32,160},{48,176},{64,192},{80,208},{96,224},{112... | collective-permute-start | bytes 1671176 | tf_op jit(solution)/shard_map/ppermute | solution.py:40
  48.0 13.7 %collective-permute-start.7 = (bf16[8,272,128]{2,1,0:T(8,128)(2,1)}, bf16[8,272,128]{2,1,0:T(8,128)(2,1)S(1)}, u32[]{:S(2)}, u32[]{:S(2)}) collective-permute-start(bf16[8,272,128]{2,1,0:T(8,128)(2,1)} %get-tuple-element.22), channel_id=1, source_target_pairs={{0,384},{16,400},{32,416},{48,432},{64,448},{80,464},{96,480},{112... | collective-permute-start | bytes 1671176 | tf_op jit(solution)/shard_map/ppermute | solution.py:40
  51.0 21.1 %copy-start.10 = (s32[32]{0:T(128)}, s32[32]{0:T(128)S(1)}, u32[]{:S(2)}) copy-start(s32[32]{0:T(128)S(1)} %concatenate.63.shards_ref) | copy-start | bytes 388
  58.0 8.4 %collective-permute-start.8 = (bf16[4,272,128]{2,1,0:T(8,128)(2,1)S(1)}, bf16[4,272,128]{2,1,0:T(8,128)(2,1)S(1)}, u32[]{:S(2)}, u32[]{:S(2)}) collective-permute-start(bf16[4,272,128]{2,1,0:T(8,128)(2,1)S(1)} %slice.84), channel_id=1, source_target_pairs={{0,128},{16,144},{32,160},{48,176},{64,192},{80,208},{96,224},{112... | collective-permute-start | bytes 835592 | tf_op jit(solution)/shard_map/ppermute | solution.py:40
  61.7 9.7 %collective-permute-start.9 = (bf16[4,272,128]{2,1,0:T(8,128)(2,1)S(1)}, bf16[4,272,128]{2,1,0:T(8,128)(2,1)S(1)}, u32[]{:S(2)}, u32[]{:S(2)}) collective-permute-start(bf16[4,272,128]{2,1,0:T(8,128)(2,1)S(1)} %slice.85), channel_id=1, source_target_pairs={{0,384},{16,400},{32,416},{48,432},{64,448},{80,464},{96,480},{112... | collective-permute-start | bytes 835592 | tf_op jit(solution)/shard_map/ppermute | solution.py:40
  74.9 20.2 %copy-start.2 = (bf16[1024,128]{1,0:T(8,128)(2,1)S(1)}, bf16[1024,128]{1,0:T(8,128)(2,1)}, u32[]{:S(2)}) copy-start(bf16[1024,128]{1,0:T(8,128)(2,1)} %param.14) | copy-start | bytes 786436
  74.9 20.2 %copy-start.4 = (bf16[1024,128]{1,0:T(8,128)(2,1)S(1)}, bf16[1024,128]{1,0:T(8,128)(2,1)}, u32[]{:S(2)}) copy-start(bf16[1024,128]{1,0:T(8,128)(2,1)} %param.15) | copy-start | bytes 786436
  74.9 20.2 %copy-start.6 = (bf16[1024,128]{1,0:T(8,128)(2,1)S(1)}, bf16[1024,128]{1,0:T(8,128)(2,1)}, u32[]{:S(2)}) copy-start(bf16[1024,128]{1,0:T(8,128)(2,1)} %param.16) | copy-start | bytes 786436
  92.8 31.8 %copy-start.9 = (bf16[64,128]{1,0:T(8,128)(2,1)S(1)}, bf16[64,128]{1,0:T(8,128)(2,1)}, u32[]{:S(2)}) copy-start(bf16[64,128]{1,0:T(8,128)(2,1)} %get-tuple-element.6) | copy-start | bytes 49156
  95.5 7.4 %collective-permute-start.10 = (bf16[64,1024]{1,0:T(8,128)(2,1)S(1)}, bf16[64,1024]{1,0:T(8,128)(2,1)S(1)}, u32[]{:S(2)}, u32[]{:S(2)}) collective-permute-start(bf16[64,1024]{1,0:T(8,128)(2,1)S(1)} %convolution_convert_fusion), channel_id=1, source_target_pairs={{0,2},{2,0},{4,6},{6,4},{8,10},{10,8},{12,14},{14,12},{1,3},{3,1},... | collective-permute-start | bytes 393224 | tf_op jit(solution)/shard_map/ppermute | solution.py:83
  103.0 9.9 %collective-permute-start.11 = (bf16[64,1024]{1,0:T(8,128)(2,1)S(1)}, bf16[64,1024]{1,0:T(8,128)(2,1)S(1)}, u32[]{:S(2)}, u32[]{:S(2)}) collective-permute-start(bf16[64,1024]{1,0:T(8,128)(2,1)S(1)} %add_convert_fusion.2), channel_id=1, source_target_pairs={{0,4},{2,6},{4,0},{6,2},{8,12},{10,14},{12,8},{14,10},{1,5},{3,7},... | collective-permute-start | bytes 393224 | tf_op jit(solution)/shard_map/ppermute | solution.py:83
  112.9 13.4 %collective-permute-start.12 = (bf16[64,1024]{1,0:T(8,128)(2,1)S(1)}, bf16[64,1024]{1,0:T(8,128)(2,1)S(1)}, u32[]{:S(2)}, u32[]{:S(2)}) collective-permute-start(bf16[64,1024]{1,0:T(8,128)(2,1)S(1)} %add_convert_fusion.1), channel_id=1, source_target_pairs={{14,0},{8,6},{6,8},{0,14},{15,1},{9,7},{7,9},{1,15},{30,16},{24,22... | collective-permute-start | bytes 393224 | tf_op jit(solution)/shard_map/ppermute | solution.py:91
  123.3 3.9 %collective-permute-start.13 = (bf16[64,1024]{1,0:T(8,128)(2,1)S(1)}, bf16[64,1024]{1,0:T(8,128)(2,1)S(1)}, u32[]{:S(2)}, u32[]{:S(2)}) collective-permute-start(bf16[64,1024]{1,0:T(8,128)(2,1)S(1)} %add_convert_fusion.1), channel_id=1, source_target_pairs={{14,2},{8,4},{6,10},{0,12},{15,3},{9,5},{7,11},{1,13},{30,18},{24,... | collective-permute-start | bytes 393224 | tf_op jit(solution)/shard_map/ppermute | solution.py:91
  128.6 6.8 %collective-permute-start.14 = (f32[3,1024]{1,0:T(4,128)S(1)}, f32[3,1024]{1,0:T(4,128)S(1)}, u32[]{:S(2)}, u32[]{:S(2)}) collective-permute-start(f32[3,1024]{1,0:T(4,128)S(1)} %fusion.8), channel_id=1, source_target_pairs={{16,0},{32,16},{48,32},{64,48},{80,64},{96,80},{112,96},{128,112},... | collective-permute-start | bytes 36872 | tf_op jit(solution)/shard_map/ppermute | solution.py:23

commit v17 on v14

--- a/solution.py
+++ b/solution.py
@@ -96,7 +96,7 @@
 
 
 def forward_kernel(
-    shards_ref, q_ref, k_ref, v_ref, g_ref, key_code_ref, own_code_ref,
+    shards_ref, q_ref, k_ref, v_ref, g_ref, info_ref,
     att_ref, gq_ref, gk_ref, gv_ref,
 ):
     block_rows = q_ref.shape[1]
@@ -111,12 +111,22 @@
     scale = 1.0 / math.sqrt(HD)
     by_rows = (((1,), (1,)), ((), ()))
     by_cols = (((0,), (0,)), ((), ()))
+    blocks = k_ref.shape[0]
+    slots = blocks * block_rows
+    info = jnp.max(info_ref[...].astype(jnp.float32), axis=1)
+    column = lax.broadcasted_iota(jnp.int32, (blocks, slots), 1)
+    pick = (column // block_rows == lax.broadcasted_iota(jnp.int32, (blocks, slots), 0))
+    spread = lax.dot_general(info, pick.astype(jnp.float32), by_cols, preferred_element_type=jnp.float32)
+    lane = lax.broadcasted_iota(jnp.int32, (1, slots), 1) % block_rows
+    counts_row = spread[0:1].astype(jnp.int32)
+    sources_row = spread[info.shape[1] // 2 : info.shape[1] // 2 + 1].astype(jnp.int32)
+    key_code = jnp.where(lane < counts_row, sources_row * block_rows + lane, slots)
     queries = q_ref[...].reshape(rows, width)
     grads = g_ref[...].reshape(rows, width)
     keys = k_ref[...].reshape(-1, width)
     values = v_ref[...].reshape(-1, width)
     scores = lax.dot_general(queries, keys, by_rows, preferred_element_type=jnp.float32) * scale
-    scores = jnp.where(key_code_ref[...] <= q_ids, scores, masked_score)
+    scores = jnp.where(key_code <= q_ids, scores, masked_score)
     row_max = jnp.max(scores, axis=1, keepdims=True)
     softmax_part = jnp.exp(scores - row_max)
     row_sum = jnp.sum(softmax_part, axis=1, keepdims=True)
@@ -144,7 +154,7 @@
     own_scores = lax.dot_general(
         queries, k_ref[0], by_rows, preferred_element_type=jnp.float32
     ) * scale
-    own_scores = jnp.where(own_code_ref[...] <= q_ids, own_scores, masked_score)
+    own_scores = jnp.where(key_code[:, :own] <= q_ids, own_scores, masked_score)
     probs = jnp.exp(own_scores - log_total)
     gv_ref[...] += lax.dot_general(
         probs.astype(jnp.bfloat16), grads, by_cols, preferred_element_type=jnp.float32
@@ -154,10 +164,8 @@
     gk_ref[...] += lax.dot_general(grad_scores, queries, by_cols, preferred_element_type=jnp.float32)
 
 
-def attention_all(gathered, key_code, held_shards):
+def attention_all(gathered, held_shards, block_rows, info_rows):
     blocks, _, width = gathered.shape
-    block_rows = key_code.shape[0] // blocks
-    slots = blocks * block_rows
     step_spec = lambda part: pl.BlockSpec(
         (BLOCKS_PER_STEP, block_rows, width), lambda i, shards: (i, part, 0)
     )
@@ -169,8 +177,8 @@
         num_scalar_prefetch=1,
         grid=(blocks // BLOCKS_PER_STEP,),
         in_specs=[step_spec(0), all_spec(1), all_spec(2), step_spec(3),
-                  pl.BlockSpec((1, slots), lambda i, shards: (0, 0)),
-                  pl.BlockSpec((1, block_rows), lambda i, shards: (0, 0))],
+                  pl.BlockSpec((blocks, info_rows, width),
+                               lambda i, shards: (0, 4 * block_rows // info_rows, 0))],
         out_specs=[own_spec, own_spec, own_spec, own_spec],
     )
     own_grad = jax.ShapeDtypeStruct((block_rows, width), jnp.float32)
@@ -178,8 +186,7 @@
         forward_kernel,
         grid_spec=grid_spec,
         out_shape=[jax.ShapeDtypeStruct((block_rows, width), jnp.bfloat16), own_grad, own_grad, own_grad],
-    )(held_shards, gathered, gathered, gathered, gathered, key_code.reshape(1, slots),
-      key_code[:block_rows].reshape(1, block_rows))
+    )(held_shards, gathered, gathered, gathered, gathered, gathered)
 
 
 def per_device(
@@ -223,22 +230,18 @@
     )
     grad_rows = jnp.where(live_mask[:, None], grad_attended, jnp.zeros_like(grad_attended))
 
-    count_rows = jnp.broadcast_to(span_counts[0].astype(jnp.bfloat16), (16, head_width))
-    packed = jnp.concatenate([queries, key_rows, value_rows, grad_rows, count_rows], axis=0)
+    info_rows = jnp.concatenate(
+        [
+            jnp.broadcast_to(span_counts[0].astype(jnp.bfloat16), (16, head_width // 2)),
+            jnp.broadcast_to(shard_index.astype(jnp.bfloat16), (16, head_width // 2)),
+        ],
+        axis=1,
+    )
+    packed = jnp.concatenate([queries, key_rows, value_rows, grad_rows, info_rows], axis=0)
     gathered, held_shards = gather_blocks(packed, "seq")
     total_slots = shards * slot_count
 
-    all_counts = gathered[:, 4 * slot_count, 0].astype(jnp.int32)
-    all_live = (
-        jnp.arange(slot_count, dtype=jnp.int32)[None, :] < all_counts[:, None]
-    ).reshape(total_slots)
-    slot_ids = (
-        held_shards[:, None] * slot_count + jnp.arange(slot_count, dtype=jnp.int32)[None, :]
-    ).reshape(total_slots)
-
-    own_attended, query_grad, key_grad, value_grad = attention_all(
-        gathered, jnp.where(all_live, slot_ids, total_slots), held_shards
-    )
+    own_attended, query_grad, key_grad, value_grad = attention_all(gathered, held_shards, slot_count, 16)
     attended = jnp.where(live_mask[:, None], own_attended, jnp.bfloat16(0.0))
     query_grad_rows = (query_grad * score_scale).astype(jnp.bfloat16)
     key_grad_rows = (key_grad * score_scale).astype(jnp.bfloat16)

time: 137 us -> 137 us (level)
  other arithmetic: 9.96 us -> 8.39 us
    convert_element_type x1 -> x0, other arithmetic: 1.5 us -> none  [per_device(): all_counts = gathered[:, 4 * slot_count, 0].astype(jnp.int32)]
    unnamed x30 -> x28, local copies, waits for them, and re-layouts: 5.95 us -> 6.86 us
  transfers between devices with their start and end apart: 15 -> 15, of which waited for: 11 -> 11; matrix products, arithmetic and copies ran while one was open for 7% -> 9% of each run, Pallas kernels for 0% -> 0%
where the time goes in v17:
time: 137 us; the launch traced here: 136 us
  starting transfers between devices  55.5 us (41%)
  waiting for transfers between devices  33.9 us (25%)
  Pallas kernels  19.2 us (14%)
  local copies, waits for them, and re-layouts  13.7 us (10%)
  other arithmetic  8.39 us (6%)
  matrix products  3.86 us (3%)
  between operations  1.73 us (1%)
    ppermute x8, starting transfers between devices, shifted(): return lax.ppermute(array, axis, pairs)  25.1 us
    pallas_call x1, Pallas kernels, attention_all(): pl.pallas_call(forward_kernel, grid_spec=grid_spec, out_shape=[jax.ShapeD...  19.2 us
    ppermute x8, waiting for transfers between devices, shifted(): return lax.ppermute(array, axis, pairs)  16.9 us
    ppermute x2, starting transfers between devices, summed_over(): got = lax.ppermute(sent, axis, [(i, i ^ step) for i in range(devices)])  11.5 us
    ppermute x1, starting transfers between devices, summed_over(): lax.ppermute(sent, axis, near).astype(jnp.float32)  8.94 us
    ppermute x2, waiting for transfers between devices, summed_over(): got = lax.ppermute(sent, axis, [(i, i ^ step) for i in range(devices)])  7.18 us
    unnamed x28, local copies, waits for them, and re-layouts  6.86 us
    ppermute x2, starting transfers between devices, passed_along(): return lax.ppermute(array, axis, pairs)  6.66 us
  transfers between devices with their start and end apart: 15, of which 11 were waited for; matrix products, arithmetic and copies ran while one was open for 9% of the time, Pallas kernels for 0%

profile of v17, /device:TPU:30, one launch (start us, length us, event | category | flops | bytes accessed | tf_op | source)
XLA Modules:
  0.0 136.3 jit_solution(6817389329591900140)
XLA Ops:
  0.6 0.9 slice.98
  1.5 4.7 %collective-permute-start = (bf16[3,1024]{1,0:T(4,128)(2,1)S(1)}, bf16[3,1024]{1,0:T(4,128)(2,1)S(1)}, u32[]{:S(2)}, u32[]{:S(2)}) collective-permute-start(bf16[3,1024]{1,0:T(4,128)(2,1)S(1)} %slice.98), channel_id=1, source_target_pairs={{0,16},{16,32},{32,48},{48,64},{64,80},{80,96},{96,112},{112,128},... | collective-permute-start | bytes 18440 | tf_op jit(solution)/shard_map/ppermute | solution.py:23
  6.2 0.7 iota_subtract_fusion
  7.0 0.1 add.270
  7.1 0.9 fusion.50
  8.8 1.5 %pad_maximum_fusion = bf16[515,1024]{1,0:T(8,128)(2,1)S(1)} fusion(bf16[512,1024]{1,0:T(8,128)(2,1)} %param.10, bf16[3,1024]{1,0:T(4,128)(2,1)S(1)} %collective-permute-done), kind=kLoop, calls=%fused_computation.10 | loop fusion | flops 2109440 | bytes 2109440 | tf_op jit(solution)/shard_map/concatenate | solution.py:213
  10.3 2.0 %gather_fusion = bf16[256,1024]{1,0:T(8,128)(2,1)} fusion(bf16[515,1024]{1,0:T(8,128)(2,1)S(1)} %pad_maximum_fusion, s32[1024]{0:T(1024)S(1)} %pad_clamp_fusion), kind=kCustom, calls=%fused_computation | custom fusion | bytes 1049600 | tf_op jit(solution)/shard_map/jit(_take)/gather | solution.py:215
  12.2 1.2 select_convert_fusion
  13.5 0.6 multiply_reduce_fusion.1
  14.1 0.1 multiply_convert_fusion
  14.2 0.2 fusion.2
  14.4 0.2 fusion.1
  14.6 0.2 fusion
  14.8 0.1 constant_dynamic-update-slice_fusion.1
  14.9 1.9 %collective-permute-start.1 = (bf16[1,272,128]{2,1,0:T(8,128)(2,1)S(1)}, bf16[1,272,128]{2,1,0:T(8,128)(2,1)S(1)}, u32[]{:S(2)}, u32[]{:S(2)}) collective-permute-start(bf16[1,272,128]{2,1,0:T(8,128)(2,1)S(1)} %bitcast.20), channel_id=1, source_target_pairs={{0,16},{16,0},{32,48},{48,32},{64,80},{80,64},{96,112},{112,96},{1... | collective-permute-start | bytes 208904 | tf_op jit(solution)/shard_map/ppermute | solution.py:62
  16.8 0.1 multiply_add_fusion.6
  16.9 4.2 %collective-permute-done.1 = bf16[1,272,128]{2,1,0:T(8,128)(2,1)S(1)} collective-permute-done((bf16[1,272,128]{2,1,0:T(8,128)(2,1)S(1)}, bf16[1,272,128]{2,1,0:T(8,128)(2,1)S(1)}, u32[]{:S(2)}, u32[]{:S(2)}) %collective-permute-start.1) | collective-permute-done | bytes 69664 | tf_op jit(solution)/shard_map/ppermute | solution.py:62
  21.1 3.7 %collective-permute-start.2 = (bf16[2,272,128]{2,1,0:T(8,128)(2,1)S(1)}, bf16[2,272,128]{2,1,0:T(8,128)(2,1)S(1)}, u32[]{:S(2)}, u32[]{:S(2)}) collective-permute-start(bf16[2,272,128]{2,1,0:T(8,128)(2,1)S(1)} %pad_maximum_fusion.4), channel_id=1, source_target_pairs={{0,32},{16,48},{32,64},{48,80},{64,96},{80,112},{96,0},{112,16},{1... | collective-permute-start | bytes 417800 | tf_op jit(solution)/shard_map/ppermute | solution.py:40
  24.8 3.1 %collective-permute-start.3 = (bf16[2,272,128]{2,1,0:T(8,128)(2,1)S(1)}, bf16[2,272,128]{2,1,0:T(8,128)(2,1)S(1)}, u32[]{:S(2)}, u32[]{:S(2)}) collective-permute-start(bf16[2,272,128]{2,1,0:T(8,128)(2,1)S(1)} %pad_maximum_fusion.4), channel_id=1, source_target_pairs={{0,96},{16,112},{32,0},{48,16},{64,32},{80,48},{96,64},{112,80},{1... | collective-permute-start | bytes 417800 | tf_op jit(solution)/shard_map/ppermute | solution.py:40
  27.9 0.7 constant_dynamic-update-slice_fusion.7
  28.5 0.7 constant_dynamic-update-slice_fusion.6
  29.2 1.7 %collective-permute-done.2 = bf16[2,272,128]{2,1,0:T(8,128)(2,1)S(1)} collective-permute-done((bf16[2,272,128]{2,1,0:T(8,128)(2,1)S(1)}, bf16[2,272,128]{2,1,0:T(8,128)(2,1)S(1)}, u32[]{:S(2)}, u32[]{:S(2)}) %collective-permute-start.2) | collective-permute-done | bytes 139296 | tf_op jit(solution)/shard_map/ppermute | solution.py:40
  30.9 4.0 %collective-permute-start.4 = (bf16[1,272,128]{2,1,0:T(8,128)(2,1)S(1)}, bf16[1,272,128]{2,1,0:T(8,128)(2,1)S(1)}, u32[]{:S(2)}, u32[]{:S(2)}) collective-permute-start(bf16[1,272,128]{2,1,0:T(8,128)(2,1)S(1)} %slice.71), channel_id=1, source_target_pairs={{0,32},{16,48},{32,64},{48,80},{64,96},{80,112},{96,0},{112,16},{1... | collective-permute-start | bytes 208904 | tf_op jit(solution)/shard_map/ppermute | solution.py:40
  34.9 2.7 %collective-permute-start.5 = (bf16[1,272,128]{2,1,0:T(8,128)(2,1)S(1)}, bf16[1,272,128]{2,1,0:T(8,128)(2,1)S(1)}, u32[]{:S(2)}, u32[]{:S(2)}) collective-permute-start(bf16[1,272,128]{2,1,0:T(8,128)(2,1)S(1)} %slice.72), channel_id=1, source_target_pairs={{0,96},{16,112},{32,0},{48,16},{64,32},{80,48},{96,64},{112,80},{1... | collective-permute-start | bytes 208904 | tf_op jit(solution)/shard_map/ppermute | solution.py:40
  37.7 0.7 constant_dynamic-update-slice_fusion.5
  38.4 0.7 constant_dynamic-update-slice_fusion.4
  39.1 0.7 constant_dynamic-update-slice_fusion.3
  39.8 3.4 %collective-permute-done.5 = bf16[1,272,128]{2,1,0:T(8,128)(2,1)S(1)} collective-permute-done((bf16[1,272,128]{2,1,0:T(8,128)(2,1)S(1)}, bf16[1,272,128]{2,1,0:T(8,128)(2,1)S(1)}, u32[]{:S(2)}, u32[]{:S(2)}) %collective-permute-start.5) | collective-permute-done | bytes 69664 | tf_op jit(solution)/shard_map/ppermute | solution.py:40
  43.2 0.7 constant_dynamic-update-slice_fusion.2
  43.9 3.1 %collective-permute-start.6 = (bf16[8,272,128]{2,1,0:T(8,128)(2,1)}, bf16[8,272,128]{2,1,0:T(8,128)(2,1)S(1)}, u32[]{:S(2)}, u32[]{:S(2)}) collective-permute-start(bf16[8,272,128]{2,1,0:T(8,128)(2,1)} %get-tuple-element.22), channel_id=1, source_target_pairs={{0,128},{16,144},{32,160},{48,176},{64,192},{80,208},{96,224},{112... | collective-permute-start | bytes 1671176 | tf_op jit(solution)/shard_map/ppermute | solution.py:40
  47.2 2.7 %collective-permute-start.7 = (bf16[8,272,128]{2,1,0:T(8,128)(2,1)}, bf16[8,272,128]{2,1,0:T(8,128)(2,1)S(1)}, u32[]{:S(2)}, u32[]{:S(2)}) collective-permute-start(bf16[8,272,128]{2,1,0:T(8,128)(2,1)} %get-tuple-element.22), channel_id=1, source_target_pairs={{0,384},{16,400},{32,416},{48,432},{64,448},{80,464},{96,480},{112... | collective-permute-start | bytes 1671176 | tf_op jit(solution)/shard_map/ppermute | solution.py:40
  50.0 8.0 %collective-permute-done.6 = bf16[8,272,128]{2,1,0:T(8,128)(2,1)S(1)} collective-permute-done((bf16[8,272,128]{2,1,0:T(8,128)(2,1)}, bf16[8,272,128]{2,1,0:T(8,128)(2,1)S(1)}, u32[]{:S(2)}, u32[]{:S(2)}) %collective-permute-start.6) | collective-permute-done | bytes 557088 | tf_op jit(solution)/shard_map/ppermute | solution.py:40
  58.0 0.8 slice.73
  58.7 3.4 %collective-permute-start.8 = (bf16[4,272,128]{2,1,0:T(8,128)(2,1)}, bf16[4,272,128]{2,1,0:T(8,128)(2,1)}, u32[]{:S(2)}, u32[]{:S(2)}) collective-permute-start(bf16[4,272,128]{2,1,0:T(8,128)(2,1)} %slice.73), channel_id=1, source_target_pairs={{0,128},{16,144},{32,160},{48,176},{64,192},{80,208},{96,224},{112... | collective-permute-start | bytes 835592 | tf_op jit(solution)/shard_map/ppermute | solution.py:40
  62.1 0.1 multiply_add_fusion.2
  62.2 0.6 concatenate.55.shards_ref
  62.9 2.4 %collective-permute-start.9 = (bf16[4,272,128]{2,1,0:T(8,128)(2,1)S(1)}, bf16[4,272,128]{2,1,0:T(8,128)(2,1)S(1)}, u32[]{:S(2)}, u32[]{:S(2)}) collective-permute-start(bf16[4,272,128]{2,1,0:T(8,128)(2,1)S(1)} %slice.74), channel_id=1, source_target_pairs={{0,384},{16,400},{32,416},{48,432},{64,448},{80,464},{96,480},{112... | collective-permute-start | bytes 835592 | tf_op jit(solution)/shard_map/ppermute | solution.py:40
  65.3 0.8 constant_dynamic-update-slice_fusion.11
  66.2 0.8 constant_dynamic-update-slice_fusion.10
  67.0 0.4 collective-permute-done.8
  67.5 1.7 %constant_dynamic-update-slice_fusion.9 = bf16[32,272,128]{2,1,0:T(8,128)(2,1)} fusion(bf16[32,272,128]{2,1,0:T(8,128)(2,1)} %constant_dynamic-update-slice_fusion.10, bf16[4,272,128]{2,1,0:T(8,128)(2,1)} %collective-permute-done.8), kind=kLoop, calls=%fused_computation.62 | loop fusion | bytes 557056
  69.1 3.4 %collective-permute-done.9 = bf16[4,272,128]{2,1,0:T(8,128)(2,1)S(1)} collective-permute-done((bf16[4,272,128]{2,1,0:T(8,128)(2,1)S(1)}, bf16[4,272,128]{2,1,0:T(8,128)(2,1)S(1)}, u32[]{:S(2)}, u32[]{:S(2)}) %collective-permute-start.9) | collective-permute-done | bytes 278560 | tf_op jit(solution)/shard_map/ppermute | solution.py:40
  72.5 0.7 constant_dynamic-update-slice_fusion.8.q_ref.k_ref.v_ref.g_ref.info_ref
  73.3 19.2 %shard_map.113 = (bf16[64,128]{1,0:T(8,128)(2,1)}, f32[64,128]{1,0:T(8,128)}, f32[64,128]{1,0:T(8,128)}, f32[64,128]{1,0:T(8,128)}) custom-call(s32[32]{0:T(128)} %concatenate.55.shards_ref, bf16[32,272,128]{2,1,0:T(8,128)(2,1)} %constant_dynamic-update-slice_fusion.8.q_ref.k_ref.v_ref.g_ref.info_ref, ...), custom_call_target="tpu_custom_call" | custom-call | tf_op jit(solution)/shard_map/pallas_call | solution.py:185
  92.5 0.8 convert_element_type.89
  93.2 0.8 multiply_convert_fusion.1
  94.0 0.8 multiply_convert_fusion.2
  94.8 0.4 convolution_convert_fusion
  95.2 4.3 %collective-permute-start.10 = (bf16[64,1024]{1,0:T(8,128)(2,1)S(1)}, bf16[64,1024]{1,0:T(8,128)(2,1)S(1)}, u32[]{:S(2)}, u32[]{:S(2)}) collective-permute-start(bf16[64,1024]{1,0:T(8,128)(2,1)S(1)} %convolution_convert_fusion), channel_id=1, source_target_pairs={{0,2},{2,0},{4,6},{6,4},{8,10},{10,8},{12,14},{14,12},{1,3},{3,1},... | collective-permute-start | bytes 393224 | tf_op jit(solution)/shard_map/ppermute | solution.py:83
  99.5 2.9 %collective-permute-done.10 = bf16[64,1024]{1,0:T(8,128)(2,1)S(1)} collective-permute-done((bf16[64,1024]{1,0:T(8,128)(2,1)S(1)}, bf16[64,1024]{1,0:T(8,128)(2,1)S(1)}, u32[]{:S(2)}, u32[]{:S(2)}) %collective-permute-start.10) | collective-permute-done | bytes 131104 | tf_op jit(solution)/shard_map/ppermute | solution.py:83
  102.4 7.3 %collective-permute-start.11 = (bf16[64,1024]{1,0:T(8,128)(2,1)S(1)}, bf16[64,1024]{1,0:T(8,128)(2,1)S(1)}, u32[]{:S(2)}, u32[]{:S(2)}) collective-permute-start(bf16[64,1024]{1,0:T(8,128)(2,1)S(1)} %add_convert_fusion.2), channel_id=1, source_target_pairs={{0,4},{2,6},{4,0},{6,2},{8,12},{10,14},{12,8},{14,10},{1,5},{3,7},... | collective-permute-start | bytes 393224 | tf_op jit(solution)/shard_map/ppermute | solution.py:83
  109.8 4.2 %collective-permute-done.11 = bf16[64,1024]{1,0:T(8,128)(2,1)S(1)} collective-permute-done((bf16[64,1024]{1,0:T(8,128)(2,1)S(1)}, bf16[64,1024]{1,0:T(8,128)(2,1)S(1)}, u32[]{:S(2)}, u32[]{:S(2)}) %collective-permute-start.11) | collective-permute-done | bytes 131104 | tf_op jit(solution)/shard_map/ppermute | solution.py:83
  114.1 8.9 %collective-permute-start.12 = (bf16[64,1024]{1,0:T(8,128)(2,1)S(1)}, bf16[64,1024]{1,0:T(8,128)(2,1)S(1)}, u32[]{:S(2)}, u32[]{:S(2)}) collective-permute-start(bf16[64,1024]{1,0:T(8,128)(2,1)S(1)} %add_convert_fusion.1), channel_id=1, source_target_pairs={{14,0},{8,6},{6,8},{0,14},{15,1},{9,7},{7,9},{1,15},{30,16},{24,22... | collective-permute-start | bytes 393224 | tf_op jit(solution)/shard_map/ppermute | solution.py:91
  123.0 1.3 collective-permute-start.13
  124.3 0.7 broadcast_select_fusion
  125.0 0.9 collective-permute-done.12
  126.0 0.9 collective-permute-done.13
  126.9 0.2 multiply_reduce_fusion
  127.1 0.8 multiply_add_fusion
  127.9 0.5 fusion.8
  128.4 2.0 %collective-permute-start.14 = (f32[3,1024]{1,0:T(4,128)S(1)}, f32[3,1024]{1,0:T(4,128)S(1)}, u32[]{:S(2)}, u32[]{:S(2)}) collective-permute-start(f32[3,1024]{1,0:T(4,128)S(1)} %fusion.8), channel_id=1, source_target_pairs={{16,0},{32,16},{48,32},{64,48},{80,64},{96,80},{112,96},{128,112},... | collective-permute-start | bytes 36872 | tf_op jit(solution)/shard_map/ppermute | solution.py:23
  130.3 1.1 fusion.9
  131.4 3.8 %collective-permute-done.14 = f32[3,1024]{1,0:T(4,128)S(1)} collective-permute-done((f32[3,1024]{1,0:T(4,128)S(1)}, f32[3,1024]{1,0:T(4,128)S(1)}, u32[]{:S(2)}, u32[]{:S(2)}) %collective-permute-start.14) | collective-permute-done | bytes 12320 | tf_op jit(solution)/shard_map/ppermute | solution.py:23
  135.2 1.1 add_convert_fusion
  (47 shorter events, 0.6 us)
Async XLA Ops:
  0.6 12.9 %copy-start = (bf16[1024,1024]{1,0:T(8,128)(2,1)S(1)}, bf16[1024,1024]{1,0:T(8,128)(2,1)}, u32[]{:S(2)}) copy-start(bf16[1024,1024]{1,0:T(8,128)(2,1)} %param.12) | copy-start | bytes 6291460
  1.5 7.2 %collective-permute-start = (bf16[3,1024]{1,0:T(4,128)(2,1)S(1)}, bf16[3,1024]{1,0:T(4,128)(2,1)S(1)}, u32[]{:S(2)}, u32[]{:S(2)}) collective-permute-start(bf16[3,1024]{1,0:T(4,128)(2,1)S(1)} %slice.98), channel_id=1, source_target_pairs={{0,16},{16,32},{32,48},{48,64},{64,80},{80,96},{96,112},{112,128},... | collective-permute-start | bytes 18440 | tf_op jit(solution)/shard_map/ppermute | solution.py:23
  12.2 1.9 %copy-start.7 = (f32[1024]{0:T(1024)S(1)}, f32[1024]{0:T(1024)}, u32[]{:S(2)}) copy-start(f32[1024]{0:T(1024)} %param.13) | copy-start | bytes 12292
  12.2 2.0 %copy-start.1 = (bf16[1024,128]{1,0:T(8,128)(2,1)S(1)}, bf16[1024,128]{1,0:T(8,128)(2,1)}, u32[]{:S(2)}) copy-start(bf16[1024,128]{1,0:T(8,128)(2,1)} %param.14) | copy-start | bytes 786436
  12.2 2.2 %copy-start.3 = (bf16[1024,128]{1,0:T(8,128)(2,1)S(1)}, bf16[1024,128]{1,0:T(8,128)(2,1)}, u32[]{:S(2)}) copy-start(bf16[1024,128]{1,0:T(8,128)(2,1)} %param.15) | copy-start | bytes 786436
  13.5 1.1 copy-start.5
  13.5 1.3 copy-start.8
  14.9 6.2 %collective-permute-start.1 = (bf16[1,272,128]{2,1,0:T(8,128)(2,1)S(1)}, bf16[1,272,128]{2,1,0:T(8,128)(2,1)S(1)}, u32[]{:S(2)}, u32[]{:S(2)}) collective-permute-start(bf16[1,272,128]{2,1,0:T(8,128)(2,1)S(1)} %bitcast.20), channel_id=1, source_target_pairs={{0,16},{16,0},{32,48},{48,32},{64,80},{80,64},{96,112},{112,96},{1... | collective-permute-start | bytes 208904 | tf_op jit(solution)/shard_map/ppermute | solution.py:62
  21.1 9.8 %collective-permute-start.2 = (bf16[2,272,128]{2,1,0:T(8,128)(2,1)S(1)}, bf16[2,272,128]{2,1,0:T(8,128)(2,1)S(1)}, u32[]{:S(2)}, u32[]{:S(2)}) collective-permute-start(bf16[2,272,128]{2,1,0:T(8,128)(2,1)S(1)} %pad_maximum_fusion.4), channel_id=1, source_target_pairs={{0,32},{16,48},{32,64},{48,80},{64,96},{80,112},{96,0},{112,16},{1... | collective-permute-start | bytes 417800 | tf_op jit(solution)/shard_map/ppermute | solution.py:40
  24.8 10.1 %collective-permute-start.3 = (bf16[2,272,128]{2,1,0:T(8,128)(2,1)S(1)}, bf16[2,272,128]{2,1,0:T(8,128)(2,1)S(1)}, u32[]{:S(2)}, u32[]{:S(2)}) collective-permute-start(bf16[2,272,128]{2,1,0:T(8,128)(2,1)S(1)} %pad_maximum_fusion.4), channel_id=1, source_target_pairs={{0,96},{16,112},{32,0},{48,16},{64,32},{80,48},{96,64},{112,80},{1... | collective-permute-start | bytes 417800 | tf_op jit(solution)/shard_map/ppermute | solution.py:40
  30.9 8.2 %collective-permute-start.4 = (bf16[1,272,128]{2,1,0:T(8,128)(2,1)S(1)}, bf16[1,272,128]{2,1,0:T(8,128)(2,1)S(1)}, u32[]{:S(2)}, u32[]{:S(2)}) collective-permute-start(bf16[1,272,128]{2,1,0:T(8,128)(2,1)S(1)} %slice.71), channel_id=1, source_target_pairs={{0,32},{16,48},{32,64},{48,80},{64,96},{80,112},{96,0},{112,16},{1... | collective-permute-start | bytes 208904 | tf_op jit(solution)/shard_map/ppermute | solution.py:40
  34.9 8.3 %collective-permute-start.5 = (bf16[1,272,128]{2,1,0:T(8,128)(2,1)S(1)}, bf16[1,272,128]{2,1,0:T(8,128)(2,1)S(1)}, u32[]{:S(2)}, u32[]{:S(2)}) collective-permute-start(bf16[1,272,128]{2,1,0:T(8,128)(2,1)S(1)} %slice.72), channel_id=1, source_target_pairs={{0,96},{16,112},{32,0},{48,16},{64,32},{80,48},{96,64},{112,80},{1... | collective-permute-start | bytes 208904 | tf_op jit(solution)/shard_map/ppermute | solution.py:40
  43.9 14.1 %collective-permute-start.6 = (bf16[8,272,128]{2,1,0:T(8,128)(2,1)}, bf16[8,272,128]{2,1,0:T(8,128)(2,1)S(1)}, u32[]{:S(2)}, u32[]{:S(2)}) collective-permute-start(bf16[8,272,128]{2,1,0:T(8,128)(2,1)} %get-tuple-element.22), channel_id=1, source_target_pairs={{0,128},{16,144},{32,160},{48,176},{64,192},{80,208},{96,224},{112... | collective-permute-start | bytes 1671176 | tf_op jit(solution)/shard_map/ppermute | solution.py:40
  47.2 15.6 %collective-permute-start.7 = (bf16[8,272,128]{2,1,0:T(8,128)(2,1)}, bf16[8,272,128]{2,1,0:T(8,128)(2,1)S(1)}, u32[]{:S(2)}, u32[]{:S(2)}) collective-permute-start(bf16[8,272,128]{2,1,0:T(8,128)(2,1)} %get-tuple-element.22), channel_id=1, source_target_pairs={{0,384},{16,400},{32,416},{48,432},{64,448},{80,464},{96,480},{112... | collective-permute-start | bytes 1671176 | tf_op jit(solution)/shard_map/ppermute | solution.py:40
  58.7 8.7 %collective-permute-start.8 = (bf16[4,272,128]{2,1,0:T(8,128)(2,1)}, bf16[4,272,128]{2,1,0:T(8,128)(2,1)}, u32[]{:S(2)}, u32[]{:S(2)}) collective-permute-start(bf16[4,272,128]{2,1,0:T(8,128)(2,1)} %slice.73), channel_id=1, source_target_pairs={{0,128},{16,144},{32,160},{48,176},{64,192},{80,208},{96,224},{112... | collective-permute-start | bytes 835592 | tf_op jit(solution)/shard_map/ppermute | solution.py:40
  62.9 9.7 %collective-permute-start.9 = (bf16[4,272,128]{2,1,0:T(8,128)(2,1)S(1)}, bf16[4,272,128]{2,1,0:T(8,128)(2,1)S(1)}, u32[]{:S(2)}, u32[]{:S(2)}) collective-permute-start(bf16[4,272,128]{2,1,0:T(8,128)(2,1)S(1)} %slice.74), channel_id=1, source_target_pairs={{0,384},{16,400},{32,416},{48,432},{64,448},{80,464},{96,480},{112... | collective-permute-start | bytes 835592 | tf_op jit(solution)/shard_map/ppermute | solution.py:40
  73.3 21.5 %copy-start.2 = (bf16[1024,128]{1,0:T(8,128)(2,1)S(1)}, bf16[1024,128]{1,0:T(8,128)(2,1)}, u32[]{:S(2)}) copy-start(bf16[1024,128]{1,0:T(8,128)(2,1)} %param.14) | copy-start | bytes 786436
  73.3 21.5 %copy-start.4 = (bf16[1024,128]{1,0:T(8,128)(2,1)S(1)}, bf16[1024,128]{1,0:T(8,128)(2,1)}, u32[]{:S(2)}) copy-start(bf16[1024,128]{1,0:T(8,128)(2,1)} %param.15) | copy-start | bytes 786436
  73.3 21.5 %copy-start.6 = (bf16[1024,128]{1,0:T(8,128)(2,1)S(1)}, bf16[1024,128]{1,0:T(8,128)(2,1)}, u32[]{:S(2)}) copy-start(bf16[1024,128]{1,0:T(8,128)(2,1)} %param.16) | copy-start | bytes 786436
  92.5 31.9 %copy-start.9 = (bf16[64,128]{1,0:T(8,128)(2,1)S(1)}, bf16[64,128]{1,0:T(8,128)(2,1)}, u32[]{:S(2)}) copy-start(bf16[64,128]{1,0:T(8,128)(2,1)} %get-tuple-element.6) | copy-start | bytes 49156
  95.2 7.2 %collective-permute-start.10 = (bf16[64,1024]{1,0:T(8,128)(2,1)S(1)}, bf16[64,1024]{1,0:T(8,128)(2,1)S(1)}, u32[]{:S(2)}, u32[]{:S(2)}) collective-permute-start(bf16[64,1024]{1,0:T(8,128)(2,1)S(1)} %convolution_convert_fusion), channel_id=1, source_target_pairs={{0,2},{2,0},{4,6},{6,4},{8,10},{10,8},{12,14},{14,12},{1,3},{3,1},... | collective-permute-start | bytes 393224 | tf_op jit(solution)/shard_map/ppermute | solution.py:83
  102.4 11.6 %collective-permute-start.11 = (bf16[64,1024]{1,0:T(8,128)(2,1)S(1)}, bf16[64,1024]{1,0:T(8,128)(2,1)S(1)}, u32[]{:S(2)}, u32[]{:S(2)}) collective-permute-start(bf16[64,1024]{1,0:T(8,128)(2,1)S(1)} %add_convert_fusion.2), channel_id=1, source_target_pairs={{0,4},{2,6},{4,0},{6,2},{8,12},{10,14},{12,8},{14,10},{1,5},{3,7},... | collective-permute-start | bytes 393224 | tf_op jit(solution)/shard_map/ppermute | solution.py:83
  114.1 11.9 %collective-permute-start.12 = (bf16[64,1024]{1,0:T(8,128)(2,1)S(1)}, bf16[64,1024]{1,0:T(8,128)(2,1)S(1)}, u32[]{:S(2)}, u32[]{:S(2)}) collective-permute-start(bf16[64,1024]{1,0:T(8,128)(2,1)S(1)} %add_convert_fusion.1), channel_id=1, source_target_pairs={{14,0},{8,6},{6,8},{0,14},{15,1},{9,7},{7,9},{1,15},{30,16},{24,22... | collective-permute-start | bytes 393224 | tf_op jit(solution)/shard_map/ppermute | solution.py:91
  123.0 3.9 %collective-permute-start.13 = (bf16[64,1024]{1,0:T(8,128)(2,1)S(1)}, bf16[64,1024]{1,0:T(8,128)(2,1)S(1)}, u32[]{:S(2)}, u32[]{:S(2)}) collective-permute-start(bf16[64,1024]{1,0:T(8,128)(2,1)S(1)} %add_convert_fusion.1), channel_id=1, source_target_pairs={{14,2},{8,4},{6,10},{0,12},{15,3},{9,5},{7,11},{1,13},{30,18},{24,... | collective-permute-start | bytes 393224 | tf_op jit(solution)/shard_map/ppermute | solution.py:91
  128.4 6.8 %collective-permute-start.14 = (f32[3,1024]{1,0:T(4,128)S(1)}, f32[3,1024]{1,0:T(4,128)S(1)}, u32[]{:S(2)}, u32[]{:S(2)}) collective-permute-start(f32[3,1024]{1,0:T(4,128)S(1)} %fusion.8), channel_id=1, source_target_pairs={{16,0},{32,16},{48,32},{64,48},{80,64},{96,80},{112,96},{128,112},... | collective-permute-start | bytes 36872 | tf_op jit(solution)/shard_map/ppermute | solution.py:23

commit v18 on v14

--- a/solution.py
+++ b/solution.py
@@ -97,7 +97,7 @@
 
 def forward_kernel(
     shards_ref, q_ref, k_ref, v_ref, g_ref, key_code_ref, own_code_ref,
-    att_ref, gq_ref, gk_ref, gv_ref,
+    att_ref, grad_ref, gk_ref, gv_ref,
 ):
     block_rows = q_ref.shape[1]
     rows = q_ref.shape[0] * block_rows
@@ -136,7 +136,8 @@
             grads[:own], values, by_rows, preferred_element_type=jnp.float32
         )
         grad_scores = (probs * (grad_probs - delta[:own])).astype(jnp.bfloat16)
-        gq_ref[...] = jnp.dot(grad_scores, keys, preferred_element_type=jnp.float32)
+        query_grad = jnp.dot(grad_scores, keys, preferred_element_type=jnp.float32) * scale
+        grad_ref[:, :width] = query_grad.astype(jnp.bfloat16)
         att_ref[...] = attention[:own]
         gk_ref[...] = jnp.zeros_like(gk_ref)
         gv_ref[...] = jnp.zeros_like(gv_ref)
@@ -153,6 +154,11 @@
     grad_scores = (probs * (grad_probs - delta)).astype(jnp.bfloat16)
     gk_ref[...] += lax.dot_general(grad_scores, queries, by_cols, preferred_element_type=jnp.float32)
 
+    @pl.when(step == pl.num_programs(0) - 1)
+    def _():
+        grad_ref[:, width : 2 * width] = (gk_ref[...] * scale).astype(jnp.bfloat16)
+        grad_ref[:, 2 * width :] = gv_ref[...].astype(jnp.bfloat16)
+
 
 def attention_all(gathered, key_code, held_shards):
     blocks, _, width = gathered.shape
@@ -171,13 +177,16 @@
         in_specs=[step_spec(0), all_spec(1), all_spec(2), step_spec(3),
                   pl.BlockSpec((1, slots), lambda i, shards: (0, 0)),
                   pl.BlockSpec((1, block_rows), lambda i, shards: (0, 0))],
-        out_specs=[own_spec, own_spec, own_spec, own_spec],
-    )
-    own_grad = jax.ShapeDtypeStruct((block_rows, width), jnp.float32)
+        out_specs=[own_spec, pl.BlockSpec((block_rows, 3 * width), lambda i, shards: (0, 0))],
+        scratch_shapes=[pltpu.VMEM((block_rows, width), jnp.float32)] * 2,
+    )
     return pl.pallas_call(
         forward_kernel,
         grid_spec=grid_spec,
-        out_shape=[jax.ShapeDtypeStruct((block_rows, width), jnp.bfloat16), own_grad, own_grad, own_grad],
+        out_shape=[
+            jax.ShapeDtypeStruct((block_rows, width), jnp.bfloat16),
+            jax.ShapeDtypeStruct((block_rows, 3 * width), jnp.bfloat16),
+        ],
     )(held_shards, gathered, gathered, gathered, gathered, key_code.reshape(1, slots),
       key_code[:block_rows].reshape(1, block_rows))
 
@@ -236,17 +245,14 @@
         held_shards[:, None] * slot_count + jnp.arange(slot_count, dtype=jnp.int32)[None, :]
     ).reshape(total_slots)
 
-    own_attended, query_grad, key_grad, value_grad = attention_all(
+    own_attended, own_grads = attention_all(
         gathered, jnp.where(all_live, slot_ids, total_slots), held_shards
     )
     attended = jnp.where(live_mask[:, None], own_attended, jnp.bfloat16(0.0))
-    query_grad_rows = (query_grad * score_scale).astype(jnp.bfloat16)
-    key_grad_rows = (key_grad * score_scale).astype(jnp.bfloat16)
-    value_grad_rows = value_grad.astype(jnp.bfloat16)
 
     contract = (((1,), (1,)), ((), ()))
     partial_normed = lax.dot_general(
-        jnp.concatenate([query_grad_rows, key_grad_rows, value_grad_rows], axis=1),
+        own_grads,
         jnp.concatenate([query_weight, key_weight, value_weight], axis=1),
         contract,
         preferred_element_type=jnp.float32,

time: 137 us -> 136 us (level)
  other arithmetic: 9.96 us -> 7.66 us
    convert_element_type x3 -> x0, other arithmetic: 2.3 us -> none  [the longest x1 0.77 us: per_device(): value_grad_rows = value_grad.astype(jnp.bfloat16)]
where the time goes in v18:
time: 136 us; the launch traced here: 135 us
  starting transfers between devices  56.6 us (42%)
  waiting for transfers between devices  33.7 us (25%)
  Pallas kernels  18 us (13%)
  local copies, waits for them, and re-layouts  12.7 us (9%)
  other arithmetic  7.66 us (6%)
  matrix products  4.66 us (3%)
  between operations  1.74 us (1%)
    ppermute x8, starting transfers between devices, shifted(): return lax.ppermute(array, axis, pairs)  25.1 us
    pallas_call x1, Pallas kernels, attention_all(): pl.pallas_call(forward_kernel, grid_spec=grid_spec, out_shape=[jax.ShapeD...  18 us
    ppermute x8, waiting for transfers between devices, shifted(): return lax.ppermute(array, axis, pairs)  17.8 us
    ppermute x2, starting transfers between devices, summed_over(): got = lax.ppermute(sent, axis, [(i, i ^ step) for i in range(devices)])  11.5 us
    ppermute x1, starting transfers between devices, summed_over(): lax.ppermute(sent, axis, near).astype(jnp.float32)  8.99 us
    ppermute x2, starting transfers between devices, passed_along(): return lax.ppermute(array, axis, pairs)  7.67 us
    ppermute x2, waiting for transfers between devices, summed_over(): got = lax.ppermute(sent, axis, [(i, i ^ step) for i in range(devices)])  7.18 us
    unnamed x30, local copies, waits for them, and re-layouts  5.95 us
  transfers between devices with their start and end apart: 15, of which 11 were waited for; matrix products, arithmetic and copies ran while one was open for 7% of the time, Pallas kernels for 0%

profile of v18, /device:TPU:30, one launch (start us, length us, event | category | flops | bytes accessed | tf_op | source)
XLA Modules:
  0.0 135.0 jit_solution(11498826697371484864)
XLA Ops:
  0.6 0.9 slice.112
  1.5 4.7 %collective-permute-start = (bf16[3,1024]{1,0:T(4,128)(2,1)S(1)}, bf16[3,1024]{1,0:T(4,128)(2,1)S(1)}, u32[]{:S(2)}, u32[]{:S(2)}) collective-permute-start(bf16[3,1024]{1,0:T(4,128)(2,1)S(1)} %slice.112), channel_id=1, source_target_pairs={{0,16},{16,32},{32,48},{48,64},{64,80},{80,96},{96,112},{112,128},... | collective-permute-start | bytes 18440 | tf_op jit(solution)/shard_map/ppermute | solution.py:23
  6.2 0.7 iota_subtract_fusion
  7.0 0.1 add.349
  7.0 0.1 add.346
  7.1 0.9 fusion.46
  8.7 0.1 multiply_add_fusion.6
  8.8 1.5 %pad_maximum_fusion = bf16[515,1024]{1,0:T(8,128)(2,1)S(1)} fusion(bf16[512,1024]{1,0:T(8,128)(2,1)} %param.10, bf16[3,1024]{1,0:T(4,128)(2,1)S(1)} %collective-permute-done), kind=kLoop, calls=%fused_computation.10 | loop fusion | flops 2109440 | bytes 2109440 | tf_op jit(solution)/shard_map/concatenate | solution.py:215
  10.3 2.0 %gather_fusion = bf16[256,1024]{1,0:T(8,128)(2,1)} fusion(bf16[515,1024]{1,0:T(8,128)(2,1)S(1)} %pad_maximum_fusion, s32[1024]{0:T(1024)S(1)} %pad_clamp_fusion), kind=kCustom, calls=%fused_computation | custom fusion | bytes 1049600 | tf_op jit(solution)/shard_map/jit(_take)/gather | solution.py:217
  12.3 1.2 select_convert_fusion
  13.6 0.6 multiply_reduce_fusion.1
  14.2 0.1 multiply_convert_fusion
  14.3 0.2 fusion.2
  14.5 0.2 fusion.1
  14.7 0.2 fusion
  14.9 0.1 constant_dynamic-update-slice_fusion.1
  15.0 1.9 %collective-permute-start.1 = (bf16[1,272,128]{2,1,0:T(8,128)(2,1)S(1)}, bf16[1,272,128]{2,1,0:T(8,128)(2,1)S(1)}, u32[]{:S(2)}, u32[]{:S(2)}) collective-permute-start(bf16[1,272,128]{2,1,0:T(8,128)(2,1)S(1)} %bitcast.21), channel_id=1, source_target_pairs={{0,16},{16,0},{32,48},{48,32},{64,80},{80,64},{96,112},{112,96},{1... | collective-permute-start | bytes 208904 | tf_op jit(solution)/shard_map/ppermute | solution.py:62
  17.1 4.1 %collective-permute-done.1 = bf16[1,272,128]{2,1,0:T(8,128)(2,1)S(1)} collective-permute-done((bf16[1,272,128]{2,1,0:T(8,128)(2,1)S(1)}, bf16[1,272,128]{2,1,0:T(8,128)(2,1)S(1)}, u32[]{:S(2)}, u32[]{:S(2)}) %collective-permute-start.1) | collective-permute-done | bytes 69664 | tf_op jit(solution)/shard_map/ppermute | solution.py:62
  21.2 3.6 %collective-permute-start.2 = (bf16[2,272,128]{2,1,0:T(8,128)(2,1)S(1)}, bf16[2,272,128]{2,1,0:T(8,128)(2,1)S(1)}, u32[]{:S(2)}, u32[]{:S(2)}) collective-permute-start(bf16[2,272,128]{2,1,0:T(8,128)(2,1)S(1)} %pad_maximum_fusion.4), channel_id=1, source_target_pairs={{0,32},{16,48},{32,64},{48,80},{64,96},{80,112},{96,0},{112,16},{1... | collective-permute-start | bytes 417800 | tf_op jit(solution)/shard_map/ppermute | solution.py:40
  24.8 3.2 %collective-permute-start.3 = (bf16[2,272,128]{2,1,0:T(8,128)(2,1)S(1)}, bf16[2,272,128]{2,1,0:T(8,128)(2,1)S(1)}, u32[]{:S(2)}, u32[]{:S(2)}) collective-permute-start(bf16[2,272,128]{2,1,0:T(8,128)(2,1)S(1)} %pad_maximum_fusion.4), channel_id=1, source_target_pairs={{0,96},{16,112},{32,0},{48,16},{64,32},{80,48},{96,64},{112,80},{1... | collective-permute-start | bytes 417800 | tf_op jit(solution)/shard_map/ppermute | solution.py:40
  27.9 0.7 constant_dynamic-update-slice_fusion.7
  28.6 0.7 constant_dynamic-update-slice_fusion.6
  29.3 1.7 %collective-permute-done.2 = bf16[2,272,128]{2,1,0:T(8,128)(2,1)S(1)} collective-permute-done((bf16[2,272,128]{2,1,0:T(8,128)(2,1)S(1)}, bf16[2,272,128]{2,1,0:T(8,128)(2,1)S(1)}, u32[]{:S(2)}, u32[]{:S(2)}) %collective-permute-start.2) | collective-permute-done | bytes 139296 | tf_op jit(solution)/shard_map/ppermute | solution.py:40
  31.0 3.9 %collective-permute-start.4 = (bf16[1,272,128]{2,1,0:T(8,128)(2,1)S(1)}, bf16[1,272,128]{2,1,0:T(8,128)(2,1)S(1)}, u32[]{:S(2)}, u32[]{:S(2)}) collective-permute-start(bf16[1,272,128]{2,1,0:T(8,128)(2,1)S(1)} %slice.80), channel_id=1, source_target_pairs={{0,32},{16,48},{32,64},{48,80},{64,96},{80,112},{96,0},{112,16},{1... | collective-permute-start | bytes 208904 | tf_op jit(solution)/shard_map/ppermute | solution.py:40
  34.9 2.8 %collective-permute-start.5 = (bf16[1,272,128]{2,1,0:T(8,128)(2,1)S(1)}, bf16[1,272,128]{2,1,0:T(8,128)(2,1)S(1)}, u32[]{:S(2)}, u32[]{:S(2)}) collective-permute-start(bf16[1,272,128]{2,1,0:T(8,128)(2,1)S(1)} %slice.81), channel_id=1, source_target_pairs={{0,96},{16,112},{32,0},{48,16},{64,32},{80,48},{96,64},{112,80},{1... | collective-permute-start | bytes 208904 | tf_op jit(solution)/shard_map/ppermute | solution.py:40
  37.7 0.7 constant_dynamic-update-slice_fusion.5
  38.5 0.7 constant_dynamic-update-slice_fusion.4
  39.2 0.7 constant_dynamic-update-slice_fusion.3
  39.9 3.3 %collective-permute-done.5 = bf16[1,272,128]{2,1,0:T(8,128)(2,1)S(1)} collective-permute-done((bf16[1,272,128]{2,1,0:T(8,128)(2,1)S(1)}, bf16[1,272,128]{2,1,0:T(8,128)(2,1)S(1)}, u32[]{:S(2)}, u32[]{:S(2)}) %collective-permute-start.5) | collective-permute-done | bytes 69664 | tf_op jit(solution)/shard_map/ppermute | solution.py:40
  43.2 0.7 constant_dynamic-update-slice_fusion.2
  43.9 3.2 %collective-permute-start.6 = (bf16[8,272,128]{2,1,0:T(8,128)(2,1)}, bf16[8,272,128]{2,1,0:T(8,128)(2,1)S(1)}, u32[]{:S(2)}, u32[]{:S(2)}) collective-permute-start(bf16[8,272,128]{2,1,0:T(8,128)(2,1)} %get-tuple-element.18), channel_id=1, source_target_pairs={{0,128},{16,144},{32,160},{48,176},{64,192},{80,208},{96,224},{112... | collective-permute-start | bytes 1671176 | tf_op jit(solution)/shard_map/ppermute | solution.py:40
  47.1 2.6 %collective-permute-start.7 = (bf16[8,272,128]{2,1,0:T(8,128)(2,1)}, bf16[8,272,128]{2,1,0:T(8,128)(2,1)S(1)}, u32[]{:S(2)}, u32[]{:S(2)}) collective-permute-start(bf16[8,272,128]{2,1,0:T(8,128)(2,1)} %get-tuple-element.18), channel_id=1, source_target_pairs={{0,384},{16,400},{32,416},{48,432},{64,448},{80,464},{96,480},{112... | collective-permute-start | bytes 1671176 | tf_op jit(solution)/shard_map/ppermute | solution.py:40
  49.7 0.1 multiply_add_fusion.2
  50.0 8.0 %collective-permute-done.6 = bf16[8,272,128]{2,1,0:T(8,128)(2,1)S(1)} collective-permute-done((bf16[8,272,128]{2,1,0:T(8,128)(2,1)}, bf16[8,272,128]{2,1,0:T(8,128)(2,1)S(1)}, u32[]{:S(2)}, u32[]{:S(2)}) %collective-permute-start.6) | collective-permute-done | bytes 557088 | tf_op jit(solution)/shard_map/ppermute | solution.py:40
  58.0 3.4 %collective-permute-start.8 = (bf16[4,272,128]{2,1,0:T(8,128)(2,1)S(1)}, bf16[4,272,128]{2,1,0:T(8,128)(2,1)S(1)}, u32[]{:S(2)}, u32[]{:S(2)}) collective-permute-start(bf16[4,272,128]{2,1,0:T(8,128)(2,1)S(1)} %slice.82), channel_id=1, source_target_pairs={{0,128},{16,144},{32,160},{48,176},{64,192},{80,208},{96,224},{112... | collective-permute-start | bytes 835592 | tf_op jit(solution)/shard_map/ppermute | solution.py:40
  61.5 2.4 %collective-permute-start.9 = (bf16[4,272,128]{2,1,0:T(8,128)(2,1)S(1)}, bf16[4,272,128]{2,1,0:T(8,128)(2,1)S(1)}, u32[]{:S(2)}, u32[]{:S(2)}) collective-permute-start(bf16[4,272,128]{2,1,0:T(8,128)(2,1)S(1)} %slice.83), channel_id=1, source_target_pairs={{0,384},{16,400},{32,416},{48,432},{64,448},{80,464},{96,480},{112... | collective-permute-start | bytes 835592 | tf_op jit(solution)/shard_map/ppermute | solution.py:40
  63.9 0.9 constant_dynamic-update-slice_fusion.11
  64.8 0.8 constant_dynamic-update-slice_fusion.10
  65.6 0.8 collective-permute-done.8
  66.4 0.7 constant_dynamic-update-slice_fusion.9
  67.1 4.0 %collective-permute-done.9 = bf16[4,272,128]{2,1,0:T(8,128)(2,1)S(1)} collective-permute-done((bf16[4,272,128]{2,1,0:T(8,128)(2,1)S(1)}, bf16[4,272,128]{2,1,0:T(8,128)(2,1)S(1)}, u32[]{:S(2)}, u32[]{:S(2)}) %collective-permute-start.9) | collective-permute-done | bytes 278560 | tf_op jit(solution)/shard_map/ppermute | solution.py:40
  71.1 0.7 constant_dynamic-update-slice_fusion.8.q_ref.k_ref.v_ref.g_ref
  71.8 1.5 %fusion.23 = s32[32]{0:T(128)S(1)} fusion(bf16[32,272,128]{2,1,0:T(8,128)(2,1)} %constant_dynamic-update-slice_fusion.8.q_ref.k_ref.v_ref.g_ref), kind=kLoop, calls=%fused_computation.67 | loop fusion | flops 32 | bytes 192 | tf_op jit(solution)/shard_map/convert_element_type | solution.py:240
  73.4 0.7 select_n.205.key_code_ref
  74.1 0.5 slice.85.own_code_ref
  74.6 18.0 %shard_map.113 = (bf16[64,128]{1,0:T(8,128)(2,1)}, bf16[64,384]{1,0:T(8,128)(2,1)}) custom-call(s32[32]{0:T(128)} %copy-done.10, bf16[32,272,128]{2,1,0:T(8,128)(2,1)} %constant_dynamic-update-slice_fusion.8.q_ref.k_ref.v_ref.g_ref, bf16[32,272,128]{2,1,0:T(8,128)(2,1)} %constant_dynamic-update-slice_fusion.8.q_ref.k_ref.v_ref.g_ref, ...), custom_call_target="tpu_custom_call" | custom-call | tf_op jit(solution)/shard_map/pallas_call | solution.py:183
  92.6 1.2 convolution_convert_fusion
  93.8 4.3 %collective-permute-start.10 = (bf16[64,1024]{1,0:T(8,128)(2,1)S(1)}, bf16[64,1024]{1,0:T(8,128)(2,1)S(1)}, u32[]{:S(2)}, u32[]{:S(2)}) collective-permute-start(bf16[64,1024]{1,0:T(8,128)(2,1)S(1)} %convolution_convert_fusion), channel_id=1, source_target_pairs={{0,2},{2,0},{4,6},{6,4},{8,10},{10,8},{12,14},{14,12},{1,3},{3,1},... | collective-permute-start | bytes 393224 | tf_op jit(solution)/shard_map/ppermute | solution.py:83
  98.0 2.9 %collective-permute-done.10 = bf16[64,1024]{1,0:T(8,128)(2,1)S(1)} collective-permute-done((bf16[64,1024]{1,0:T(8,128)(2,1)S(1)}, bf16[64,1024]{1,0:T(8,128)(2,1)S(1)}, u32[]{:S(2)}, u32[]{:S(2)}) %collective-permute-start.10) | collective-permute-done | bytes 131104 | tf_op jit(solution)/shard_map/ppermute | solution.py:83
  101.0 7.3 %collective-permute-start.11 = (bf16[64,1024]{1,0:T(8,128)(2,1)S(1)}, bf16[64,1024]{1,0:T(8,128)(2,1)S(1)}, u32[]{:S(2)}, u32[]{:S(2)}) collective-permute-start(bf16[64,1024]{1,0:T(8,128)(2,1)S(1)} %add_convert_fusion.2), channel_id=1, source_target_pairs={{0,4},{2,6},{4,0},{6,2},{8,12},{10,14},{12,8},{14,10},{1,5},{3,7},... | collective-permute-start | bytes 393224 | tf_op jit(solution)/shard_map/ppermute | solution.py:83
  108.3 0.1 sub.97
  108.4 4.2 %collective-permute-done.11 = bf16[64,1024]{1,0:T(8,128)(2,1)S(1)} collective-permute-done((bf16[64,1024]{1,0:T(8,128)(2,1)S(1)}, bf16[64,1024]{1,0:T(8,128)(2,1)S(1)}, u32[]{:S(2)}, u32[]{:S(2)}) %collective-permute-start.11) | collective-permute-done | bytes 131104 | tf_op jit(solution)/shard_map/ppermute | solution.py:83
  112.7 9.0 %collective-permute-start.12 = (bf16[64,1024]{1,0:T(8,128)(2,1)S(1)}, bf16[64,1024]{1,0:T(8,128)(2,1)S(1)}, u32[]{:S(2)}, u32[]{:S(2)}) collective-permute-start(bf16[64,1024]{1,0:T(8,128)(2,1)S(1)} %add_convert_fusion.1), channel_id=1, source_target_pairs={{14,0},{8,6},{6,8},{0,14},{15,1},{9,7},{7,9},{1,15},{30,16},{24,22... | collective-permute-start | bytes 393224 | tf_op jit(solution)/shard_map/ppermute | solution.py:91
  121.7 1.3 collective-permute-start.13
  123.0 0.7 broadcast_select_fusion
  123.7 0.9 collective-permute-done.12
  124.6 0.9 collective-permute-done.13
  125.6 0.2 multiply_reduce_fusion
  125.7 0.8 multiply_add_fusion
  126.6 0.5 fusion.8
  127.0 3.0 %collective-permute-start.14 = (f32[3,1024]{1,0:T(4,128)S(1)}, f32[3,1024]{1,0:T(4,128)S(1)}, u32[]{:S(2)}, u32[]{:S(2)}) collective-permute-start(f32[3,1024]{1,0:T(4,128)S(1)} %fusion.8), channel_id=1, source_target_pairs={{16,0},{32,16},{48,32},{64,48},{80,64},{96,80},{112,96},{128,112},... | collective-permute-start | bytes 36872 | tf_op jit(solution)/shard_map/ppermute | solution.py:23
  130.0 1.1 fusion.9
  131.1 2.7 %collective-permute-done.14 = f32[3,1024]{1,0:T(4,128)S(1)} collective-permute-done((f32[3,1024]{1,0:T(4,128)S(1)}, f32[3,1024]{1,0:T(4,128)S(1)}, u32[]{:S(2)}, u32[]{:S(2)}) %collective-permute-start.14) | collective-permute-done | bytes 12320 | tf_op jit(solution)/shard_map/ppermute | solution.py:23
  133.9 1.1 add_convert_fusion
  (49 shorter events, 0.6 us)
Async XLA Ops:
  0.6 12.9 %copy-start = (bf16[1024,1024]{1,0:T(8,128)(2,1)S(1)}, bf16[1024,1024]{1,0:T(8,128)(2,1)}, u32[]{:S(2)}) copy-start(bf16[1024,1024]{1,0:T(8,128)(2,1)} %param.12) | copy-start | bytes 6291460
  1.5 7.3 %collective-permute-start = (bf16[3,1024]{1,0:T(4,128)(2,1)S(1)}, bf16[3,1024]{1,0:T(4,128)(2,1)S(1)}, u32[]{:S(2)}, u32[]{:S(2)}) collective-permute-start(bf16[3,1024]{1,0:T(4,128)(2,1)S(1)} %slice.112), channel_id=1, source_target_pairs={{0,16},{16,32},{32,48},{48,64},{64,80},{80,96},{96,112},{112,128},... | collective-permute-start | bytes 18440 | tf_op jit(solution)/shard_map/ppermute | solution.py:23
  12.3 1.9 %copy-start.7 = (f32[1024]{0:T(1024)S(1)}, f32[1024]{0:T(1024)}, u32[]{:S(2)}) copy-start(f32[1024]{0:T(1024)} %param.13) | copy-start | bytes 12292
  12.3 2.0 %copy-start.1 = (bf16[1024,128]{1,0:T(8,128)(2,1)S(1)}, bf16[1024,128]{1,0:T(8,128)(2,1)}, u32[]{:S(2)}) copy-start(bf16[1024,128]{1,0:T(8,128)(2,1)} %param.14) | copy-start | bytes 786436
  12.3 2.2 %copy-start.3 = (bf16[1024,128]{1,0:T(8,128)(2,1)S(1)}, bf16[1024,128]{1,0:T(8,128)(2,1)}, u32[]{:S(2)}) copy-start(bf16[1024,128]{1,0:T(8,128)(2,1)} %param.15) | copy-start | bytes 786436
  13.5 1.1 copy-start.5
  13.5 1.3 copy-start.8
  15.0 6.2 %collective-permute-start.1 = (bf16[1,272,128]{2,1,0:T(8,128)(2,1)S(1)}, bf16[1,272,128]{2,1,0:T(8,128)(2,1)S(1)}, u32[]{:S(2)}, u32[]{:S(2)}) collective-permute-start(bf16[1,272,128]{2,1,0:T(8,128)(2,1)S(1)} %bitcast.21), channel_id=1, source_target_pairs={{0,16},{16,0},{32,48},{48,32},{64,80},{80,64},{96,112},{112,96},{1... | collective-permute-start | bytes 208904 | tf_op jit(solution)/shard_map/ppermute | solution.py:62
  21.2 9.8 %collective-permute-start.2 = (bf16[2,272,128]{2,1,0:T(8,128)(2,1)S(1)}, bf16[2,272,128]{2,1,0:T(8,128)(2,1)S(1)}, u32[]{:S(2)}, u32[]{:S(2)}) collective-permute-start(bf16[2,272,128]{2,1,0:T(8,128)(2,1)S(1)} %pad_maximum_fusion.4), channel_id=1, source_target_pairs={{0,32},{16,48},{32,64},{48,80},{64,96},{80,112},{96,0},{112,16},{1... | collective-permute-start | bytes 417800 | tf_op jit(solution)/shard_map/ppermute | solution.py:40
  24.8 10.1 %collective-permute-start.3 = (bf16[2,272,128]{2,1,0:T(8,128)(2,1)S(1)}, bf16[2,272,128]{2,1,0:T(8,128)(2,1)S(1)}, u32[]{:S(2)}, u32[]{:S(2)}) collective-permute-start(bf16[2,272,128]{2,1,0:T(8,128)(2,1)S(1)} %pad_maximum_fusion.4), channel_id=1, source_target_pairs={{0,96},{16,112},{32,0},{48,16},{64,32},{80,48},{96,64},{112,80},{1... | collective-permute-start | bytes 417800 | tf_op jit(solution)/shard_map/ppermute | solution.py:40
  31.0 8.2 %collective-permute-start.4 = (bf16[1,272,128]{2,1,0:T(8,128)(2,1)S(1)}, bf16[1,272,128]{2,1,0:T(8,128)(2,1)S(1)}, u32[]{:S(2)}, u32[]{:S(2)}) collective-permute-start(bf16[1,272,128]{2,1,0:T(8,128)(2,1)S(1)} %slice.80), channel_id=1, source_target_pairs={{0,32},{16,48},{32,64},{48,80},{64,96},{80,112},{96,0},{112,16},{1... | collective-permute-start | bytes 208904 | tf_op jit(solution)/shard_map/ppermute | solution.py:40
  34.9 8.3 %collective-permute-start.5 = (bf16[1,272,128]{2,1,0:T(8,128)(2,1)S(1)}, bf16[1,272,128]{2,1,0:T(8,128)(2,1)S(1)}, u32[]{:S(2)}, u32[]{:S(2)}) collective-permute-start(bf16[1,272,128]{2,1,0:T(8,128)(2,1)S(1)} %slice.81), channel_id=1, source_target_pairs={{0,96},{16,112},{32,0},{48,16},{64,32},{80,48},{96,64},{112,80},{1... | collective-permute-start | bytes 208904 | tf_op jit(solution)/shard_map/ppermute | solution.py:40
  43.9 14.1 %collective-permute-start.6 = (bf16[8,272,128]{2,1,0:T(8,128)(2,1)}, bf16[8,272,128]{2,1,0:T(8,128)(2,1)S(1)}, u32[]{:S(2)}, u32[]{:S(2)}) collective-permute-start(bf16[8,272,128]{2,1,0:T(8,128)(2,1)} %get-tuple-element.18), channel_id=1, source_target_pairs={{0,128},{16,144},{32,160},{48,176},{64,192},{80,208},{96,224},{112... | collective-permute-start | bytes 1671176 | tf_op jit(solution)/shard_map/ppermute | solution.py:40
  47.1 14.3 %collective-permute-start.7 = (bf16[8,272,128]{2,1,0:T(8,128)(2,1)}, bf16[8,272,128]{2,1,0:T(8,128)(2,1)S(1)}, u32[]{:S(2)}, u32[]{:S(2)}) collective-permute-start(bf16[8,272,128]{2,1,0:T(8,128)(2,1)} %get-tuple-element.18), channel_id=1, source_target_pairs={{0,384},{16,400},{32,416},{48,432},{64,448},{80,464},{96,480},{112... | collective-permute-start | bytes 1671176 | tf_op jit(solution)/shard_map/ppermute | solution.py:40
  49.9 21.9 %copy-start.10 = (s32[32]{0:T(128)}, s32[32]{0:T(128)S(1)}, u32[]{:S(2)}) copy-start(s32[32]{0:T(128)S(1)} %concatenate.63.shards_ref) | copy-start | bytes 388
  58.0 8.4 %collective-permute-start.8 = (bf16[4,272,128]{2,1,0:T(8,128)(2,1)S(1)}, bf16[4,272,128]{2,1,0:T(8,128)(2,1)S(1)}, u32[]{:S(2)}, u32[]{:S(2)}) collective-permute-start(bf16[4,272,128]{2,1,0:T(8,128)(2,1)S(1)} %slice.82), channel_id=1, source_target_pairs={{0,128},{16,144},{32,160},{48,176},{64,192},{80,208},{96,224},{112... | collective-permute-start | bytes 835592 | tf_op jit(solution)/shard_map/ppermute | solution.py:40
  61.5 9.7 %collective-permute-start.9 = (bf16[4,272,128]{2,1,0:T(8,128)(2,1)S(1)}, bf16[4,272,128]{2,1,0:T(8,128)(2,1)S(1)}, u32[]{:S(2)}, u32[]{:S(2)}) collective-permute-start(bf16[4,272,128]{2,1,0:T(8,128)(2,1)S(1)} %slice.83), channel_id=1, source_target_pairs={{0,384},{16,400},{32,416},{48,432},{64,448},{80,464},{96,480},{112... | collective-permute-start | bytes 835592 | tf_op jit(solution)/shard_map/ppermute | solution.py:40
  74.6 18.0 %copy-start.2 = (bf16[1024,128]{1,0:T(8,128)(2,1)S(1)}, bf16[1024,128]{1,0:T(8,128)(2,1)}, u32[]{:S(2)}) copy-start(bf16[1024,128]{1,0:T(8,128)(2,1)} %param.14) | copy-start | bytes 786436
  74.6 18.0 %copy-start.4 = (bf16[1024,128]{1,0:T(8,128)(2,1)S(1)}, bf16[1024,128]{1,0:T(8,128)(2,1)}, u32[]{:S(2)}) copy-start(bf16[1024,128]{1,0:T(8,128)(2,1)} %param.15) | copy-start | bytes 786436
  74.6 18.0 %copy-start.6 = (bf16[1024,128]{1,0:T(8,128)(2,1)S(1)}, bf16[1024,128]{1,0:T(8,128)(2,1)}, u32[]{:S(2)}) copy-start(bf16[1024,128]{1,0:T(8,128)(2,1)} %param.16) | copy-start | bytes 786436
  92.6 30.4 %copy-start.9 = (bf16[64,128]{1,0:T(8,128)(2,1)S(1)}, bf16[64,128]{1,0:T(8,128)(2,1)}, u32[]{:S(2)}) copy-start(bf16[64,128]{1,0:T(8,128)(2,1)} %get-tuple-element.4) | copy-start | bytes 49156
  93.8 7.2 %collective-permute-start.10 = (bf16[64,1024]{1,0:T(8,128)(2,1)S(1)}, bf16[64,1024]{1,0:T(8,128)(2,1)S(1)}, u32[]{:S(2)}, u32[]{:S(2)}) collective-permute-start(bf16[64,1024]{1,0:T(8,128)(2,1)S(1)} %convolution_convert_fusion), channel_id=1, source_target_pairs={{0,2},{2,0},{4,6},{6,4},{8,10},{10,8},{12,14},{14,12},{1,3},{3,1},... | collective-permute-start | bytes 393224 | tf_op jit(solution)/shard_map/ppermute | solution.py:83
  101.0 11.6 %collective-permute-start.11 = (bf16[64,1024]{1,0:T(8,128)(2,1)S(1)}, bf16[64,1024]{1,0:T(8,128)(2,1)S(1)}, u32[]{:S(2)}, u32[]{:S(2)}) collective-permute-start(bf16[64,1024]{1,0:T(8,128)(2,1)S(1)} %add_convert_fusion.2), channel_id=1, source_target_pairs={{0,4},{2,6},{4,0},{6,2},{8,12},{10,14},{12,8},{14,10},{1,5},{3,7},... | collective-permute-start | bytes 393224 | tf_op jit(solution)/shard_map/ppermute | solution.py:83
  112.7 11.9 %collective-permute-start.12 = (bf16[64,1024]{1,0:T(8,128)(2,1)S(1)}, bf16[64,1024]{1,0:T(8,128)(2,1)S(1)}, u32[]{:S(2)}, u32[]{:S(2)}) collective-permute-start(bf16[64,1024]{1,0:T(8,128)(2,1)S(1)} %add_convert_fusion.1), channel_id=1, source_target_pairs={{14,0},{8,6},{6,8},{0,14},{15,1},{9,7},{7,9},{1,15},{30,16},{24,22... | collective-permute-start | bytes 393224 | tf_op jit(solution)/shard_map/ppermute | solution.py:91
  121.7 3.9 %collective-permute-start.13 = (bf16[64,1024]{1,0:T(8,128)(2,1)S(1)}, bf16[64,1024]{1,0:T(8,128)(2,1)S(1)}, u32[]{:S(2)}, u32[]{:S(2)}) collective-permute-start(bf16[64,1024]{1,0:T(8,128)(2,1)S(1)} %add_convert_fusion.1), channel_id=1, source_target_pairs={{14,2},{8,4},{6,10},{0,12},{15,3},{9,5},{7,11},{1,13},{30,18},{24,... | collective-permute-start | bytes 393224 | tf_op jit(solution)/shard_map/ppermute | solution.py:91
  127.0 6.8 %collective-permute-start.14 = (f32[3,1024]{1,0:T(4,128)S(1)}, f32[3,1024]{1,0:T(4,128)S(1)}, u32[]{:S(2)}, u32[]{:S(2)}) collective-permute-start(f32[3,1024]{1,0:T(4,128)S(1)} %fusion.8), channel_id=1, source_target_pairs={{16,0},{32,16},{48,32},{64,48},{80,64},{96,80},{112,96},{128,112},... | collective-permute-start | bytes 36872 | tf_op jit(solution)/shard_map/ppermute | solution.py:23

commit v19 on v18

--- a/solution.py
+++ b/solution.py
@@ -96,8 +96,8 @@
 
 
 def forward_kernel(
-    shards_ref, q_ref, k_ref, v_ref, g_ref, key_code_ref, own_code_ref,
-    att_ref, grad_ref, gk_ref, gv_ref,
+    shards_ref, q_ref, k_ref, v_ref, g_ref, key_code_ref, own_code_ref, w_ref,
+    att_ref, partial_ref, grad_ref, gk_ref, gv_ref,
 ):
     block_rows = q_ref.shape[1]
     rows = q_ref.shape[0] * block_rows
@@ -158,9 +158,12 @@
     def _():
         grad_ref[:, width : 2 * width] = (gk_ref[...] * scale).astype(jnp.bfloat16)
         grad_ref[:, 2 * width :] = gv_ref[...].astype(jnp.bfloat16)
-
-
-def attention_all(gathered, key_code, held_shards):
+        partial_ref[...] = lax.dot_general(
+            grad_ref[...], w_ref[...], by_rows, preferred_element_type=jnp.float32
+        ).astype(jnp.bfloat16)
+
+
+def attention_all(gathered, key_code, held_shards, weights):
     blocks, _, width = gathered.shape
     block_rows = key_code.shape[0] // blocks
     slots = blocks * block_rows
@@ -176,19 +179,21 @@
         grid=(blocks // BLOCKS_PER_STEP,),
         in_specs=[step_spec(0), all_spec(1), all_spec(2), step_spec(3),
                   pl.BlockSpec((1, slots), lambda i, shards: (0, 0)),
-                  pl.BlockSpec((1, block_rows), lambda i, shards: (0, 0))],
-        out_specs=[own_spec, pl.BlockSpec((block_rows, 3 * width), lambda i, shards: (0, 0))],
-        scratch_shapes=[pltpu.VMEM((block_rows, width), jnp.float32)] * 2,
+                  pl.BlockSpec((1, block_rows), lambda i, shards: (0, 0)),
+                  pl.BlockSpec(weights.shape, lambda i, shards: (0, 0))],
+        out_specs=[own_spec, pl.BlockSpec((block_rows, weights.shape[0]), lambda i, shards: (0, 0))],
+        scratch_shapes=[pltpu.VMEM((block_rows, 3 * width), jnp.bfloat16)]
+        + [pltpu.VMEM((block_rows, width), jnp.float32)] * 2,
     )
     return pl.pallas_call(
         forward_kernel,
         grid_spec=grid_spec,
         out_shape=[
             jax.ShapeDtypeStruct((block_rows, width), jnp.bfloat16),
-            jax.ShapeDtypeStruct((block_rows, 3 * width), jnp.bfloat16),
+            jax.ShapeDtypeStruct((block_rows, weights.shape[0]), jnp.bfloat16),
         ],
     )(held_shards, gathered, gathered, gathered, gathered, key_code.reshape(1, slots),
-      key_code[:block_rows].reshape(1, block_rows))
+      key_code[:block_rows].reshape(1, block_rows), weights)
 
 
 def per_device(
@@ -245,18 +250,13 @@
         held_shards[:, None] * slot_count + jnp.arange(slot_count, dtype=jnp.int32)[None, :]
     ).reshape(total_slots)
 
-    own_attended, own_grads = attention_all(
-        gathered, jnp.where(all_live, slot_ids, total_slots), held_shards
+    own_attended, partial_normed = attention_all(
+        gathered, jnp.where(all_live, slot_ids, total_slots), held_shards,
+        jnp.concatenate([query_weight, key_weight, value_weight], axis=1),
     )
     attended = jnp.where(live_mask[:, None], own_attended, jnp.bfloat16(0.0))
 
     contract = (((1,), (1,)), ((), ()))
-    partial_normed = lax.dot_general(
-        own_grads,
-        jnp.concatenate([query_weight, key_weight, value_weight], axis=1),
-        contract,
-        preferred_element_type=jnp.float32,
-    )
     grad_normed = summed_over(partial_normed, "head")
     scaled_grad = norm_gain * grad_normed
     cubed = inverse_rms * inverse_rms * inverse_rms

time: 136 us -> 138 us (1.015)
  other arithmetic: 7.66 us -> 11.4 us
    concatenate x0 -> x1, other arithmetic: none -> 2.1 us  [per_device(): jnp.concatenate([query_weight, key_weight, value_weight], axis=1)]
    unnamed x30 -> x22, local copies, waits for them, and re-layouts: 5.95 us -> 6.02 us
  transfers between devices with their start and end apart: 15 -> 15, of which waited for: 11 -> 9; matrix products, arithmetic and copies ran while one was open for 7% -> 9% of each run, Pallas kernels for 0% -> 0%
where the time goes in v19:
time: 138 us; the launch traced here: 137 us
  starting transfers between devices  56.5 us (41%)
  waiting for transfers between devices  32.6 us (24%)
  Pallas kernels  18.5 us (13%)
  local copies, waits for them, and re-layouts  12.8 us (9%)
  other arithmetic  11.4 us (8%)
  matrix products  3.5 us (3%)
  between operations  1.69 us (1%)
    ppermute x8, starting transfers between devices, shifted(): return lax.ppermute(array, axis, pairs)  25.1 us
    pallas_call x1, Pallas kernels, attention_all(): pl.pallas_call(forward_kernel, grid_spec=grid_spec, out_shape=[jax.ShapeD...  18.5 us
    ppermute x8, waiting for transfers between devices, shifted(): return lax.ppermute(array, axis, pairs)  17.2 us
    ppermute x2, starting transfers between devices, summed_over(): got = lax.ppermute(sent, axis, [(i, i ^ step) for i in range(devices)])  11.5 us
    ppermute x1, starting transfers between devices, summed_over(): lax.ppermute(sent, axis, near).astype(jnp.float32)  8.09 us
    ppermute x2, starting transfers between devices, passed_along(): return lax.ppermute(array, axis, pairs)  7.78 us
    ppermute x2, waiting for transfers between devices, summed_over(): got = lax.ppermute(sent, axis, [(i, i ^ step) for i in range(devices)])  7.39 us
    unnamed x22, local copies, waits for them, and re-layouts  6.02 us
  transfers between devices with their start and end apart: 15, of which 9 were waited for; matrix products, arithmetic and copies ran while one was open for 9% of the time, Pallas kernels for 0%

profile of v19, /device:TPU:30, one launch (start us, length us, event | category | flops | bytes accessed | tf_op | source)
XLA Modules:
  0.0 136.9 jit_solution(7615222330447335557)
XLA Ops:
  0.6 0.9 slice.112
  1.5 4.7 %collective-permute-start = (bf16[3,1024]{1,0:T(4,128)(2,1)S(1)}, bf16[3,1024]{1,0:T(4,128)(2,1)S(1)}, u32[]{:S(2)}, u32[]{:S(2)}) collective-permute-start(bf16[3,1024]{1,0:T(4,128)(2,1)S(1)} %slice.112), channel_id=1, source_target_pairs={{0,16},{16,32},{32,48},{48,64},{64,80},{80,96},{96,112},{112,128},... | collective-permute-start | bytes 18440 | tf_op jit(solution)/shard_map/ppermute | solution.py:23
  6.2 0.7 iota_subtract_fusion
  7.0 0.1 add.349
  7.0 0.1 add.346
  7.1 0.9 fusion.40
  8.7 0.1 multiply_add_fusion.6
  9.0 1.5 %pad_maximum_fusion = bf16[515,1024]{1,0:T(8,128)(2,1)S(1)} fusion(bf16[512,1024]{1,0:T(8,128)(2,1)} %param.10, bf16[3,1024]{1,0:T(4,128)(2,1)S(1)} %collective-permute-done), kind=kLoop, calls=%fused_computation.9 | loop fusion | flops 2109440 | bytes 2109440 | tf_op jit(solution)/shard_map/concatenate | solution.py:220
  10.5 2.0 %gather_fusion = bf16[256,1024]{1,0:T(8,128)(2,1)} fusion(bf16[515,1024]{1,0:T(8,128)(2,1)S(1)} %pad_maximum_fusion, s32[1024]{0:T(1024)S(1)} %pad_clamp_fusion), kind=kCustom, calls=%fused_computation | custom fusion | bytes 1049600 | tf_op jit(solution)/shard_map/jit(_take)/gather | solution.py:222
  12.5 1.2 select_convert_fusion
  13.8 0.6 multiply_reduce_fusion.1
  14.4 0.1 multiply_convert_fusion
  14.5 0.2 fusion.2
  14.7 0.2 fusion.1
  14.9 0.2 fusion
  15.1 0.1 constant_dynamic-update-slice_fusion.1
  15.2 1.9 %collective-permute-start.1 = (bf16[1,272,128]{2,1,0:T(8,128)(2,1)S(1)}, bf16[1,272,128]{2,1,0:T(8,128)(2,1)S(1)}, u32[]{:S(2)}, u32[]{:S(2)}) collective-permute-start(bf16[1,272,128]{2,1,0:T(8,128)(2,1)S(1)} %bitcast.20), channel_id=1, source_target_pairs={{0,16},{16,0},{32,48},{48,32},{64,80},{80,64},{96,112},{112,96},{1... | collective-permute-start | bytes 208904 | tf_op jit(solution)/shard_map/ppermute | solution.py:62
  17.1 4.2 %collective-permute-done.1 = bf16[1,272,128]{2,1,0:T(8,128)(2,1)S(1)} collective-permute-done((bf16[1,272,128]{2,1,0:T(8,128)(2,1)S(1)}, bf16[1,272,128]{2,1,0:T(8,128)(2,1)S(1)}, u32[]{:S(2)}, u32[]{:S(2)}) %collective-permute-start.1) | collective-permute-done | bytes 69664 | tf_op jit(solution)/shard_map/ppermute | solution.py:62
  21.4 3.4 %collective-permute-start.2 = (bf16[2,272,128]{2,1,0:T(8,128)(2,1)S(1)}, bf16[2,272,128]{2,1,0:T(8,128)(2,1)S(1)}, u32[]{:S(2)}, u32[]{:S(2)}) collective-permute-start(bf16[2,272,128]{2,1,0:T(8,128)(2,1)S(1)} %pad_maximum_fusion.5), channel_id=1, source_target_pairs={{0,32},{16,48},{32,64},{48,80},{64,96},{80,112},{96,0},{112,16},{1... | collective-permute-start | bytes 417800 | tf_op jit(solution)/shard_map/ppermute | solution.py:40
  24.8 3.4 %collective-permute-start.3 = (bf16[2,272,128]{2,1,0:T(8,128)(2,1)S(1)}, bf16[2,272,128]{2,1,0:T(8,128)(2,1)S(1)}, u32[]{:S(2)}, u32[]{:S(2)}) collective-permute-start(bf16[2,272,128]{2,1,0:T(8,128)(2,1)S(1)} %pad_maximum_fusion.5), channel_id=1, source_target_pairs={{0,96},{16,112},{32,0},{48,16},{64,32},{80,48},{96,64},{112,80},{1... | collective-permute-start | bytes 417800 | tf_op jit(solution)/shard_map/ppermute | solution.py:40
  28.1 0.7 constant_dynamic-update-slice_fusion.7
  28.8 0.7 constant_dynamic-update-slice_fusion.6
  29.5 1.6 %collective-permute-done.2 = bf16[2,272,128]{2,1,0:T(8,128)(2,1)S(1)} collective-permute-done((bf16[2,272,128]{2,1,0:T(8,128)(2,1)S(1)}, bf16[2,272,128]{2,1,0:T(8,128)(2,1)S(1)}, u32[]{:S(2)}, u32[]{:S(2)}) %collective-permute-start.2) | collective-permute-done | bytes 139296 | tf_op jit(solution)/shard_map/ppermute | solution.py:40
  31.2 3.7 %collective-permute-start.4 = (bf16[1,272,128]{2,1,0:T(8,128)(2,1)S(1)}, bf16[1,272,128]{2,1,0:T(8,128)(2,1)S(1)}, u32[]{:S(2)}, u32[]{:S(2)}) collective-permute-start(bf16[1,272,128]{2,1,0:T(8,128)(2,1)S(1)} %slice.80), channel_id=1, source_target_pairs={{0,32},{16,48},{32,64},{48,80},{64,96},{80,112},{96,0},{112,16},{1... | collective-permute-start | bytes 208904 | tf_op jit(solution)/shard_map/ppermute | solution.py:40
  34.9 3.0 %collective-permute-start.5 = (bf16[1,272,128]{2,1,0:T(8,128)(2,1)S(1)}, bf16[1,272,128]{2,1,0:T(8,128)(2,1)S(1)}, u32[]{:S(2)}, u32[]{:S(2)}) collective-permute-start(bf16[1,272,128]{2,1,0:T(8,128)(2,1)S(1)} %slice.81), channel_id=1, source_target_pairs={{0,96},{16,112},{32,0},{48,16},{64,32},{80,48},{96,64},{112,80},{1... | collective-permute-start | bytes 208904 | tf_op jit(solution)/shard_map/ppermute | solution.py:40
  37.9 0.8 constant_dynamic-update-slice_fusion.5
  38.7 0.7 constant_dynamic-update-slice_fusion.4
  39.4 0.7 constant_dynamic-update-slice_fusion.3
  40.1 3.1 %collective-permute-done.5 = bf16[1,272,128]{2,1,0:T(8,128)(2,1)S(1)} collective-permute-done((bf16[1,272,128]{2,1,0:T(8,128)(2,1)S(1)}, bf16[1,272,128]{2,1,0:T(8,128)(2,1)S(1)}, u32[]{:S(2)}, u32[]{:S(2)}) %collective-permute-start.5) | collective-permute-done | bytes 69664 | tf_op jit(solution)/shard_map/ppermute | solution.py:40
  43.2 0.7 constant_dynamic-update-slice_fusion.2
  43.9 3.4 %collective-permute-start.6 = (bf16[8,272,128]{2,1,0:T(8,128)(2,1)}, bf16[8,272,128]{2,1,0:T(8,128)(2,1)S(1)}, u32[]{:S(2)}, u32[]{:S(2)}) collective-permute-start(bf16[8,272,128]{2,1,0:T(8,128)(2,1)} %get-tuple-element.18), channel_id=1, source_target_pairs={{0,128},{16,144},{32,160},{48,176},{64,192},{80,208},{96,224},{112... | collective-permute-start | bytes 1671176 | tf_op jit(solution)/shard_map/ppermute | solution.py:40
  47.3 0.1 multiply_add_fusion.2
  47.5 2.4 %collective-permute-start.7 = (bf16[8,272,128]{2,1,0:T(8,128)(2,1)}, bf16[8,272,128]{2,1,0:T(8,128)(2,1)S(1)}, u32[]{:S(2)}, u32[]{:S(2)}) collective-permute-start(bf16[8,272,128]{2,1,0:T(8,128)(2,1)} %get-tuple-element.18), channel_id=1, source_target_pairs={{0,384},{16,400},{32,416},{48,432},{64,448},{80,464},{96,480},{112... | collective-permute-start | bytes 1671176 | tf_op jit(solution)/shard_map/ppermute | solution.py:40
  49.9 0.1 concatenate.63.shards_ref
  50.0 7.7 %collective-permute-done.6 = bf16[8,272,128]{2,1,0:T(8,128)(2,1)S(1)} collective-permute-done((bf16[8,272,128]{2,1,0:T(8,128)(2,1)}, bf16[8,272,128]{2,1,0:T(8,128)(2,1)S(1)}, u32[]{:S(2)}, u32[]{:S(2)}) %collective-permute-start.6) | collective-permute-done | bytes 557088 | tf_op jit(solution)/shard_map/ppermute | solution.py:40
  57.7 3.4 %collective-permute-start.8 = (bf16[4,272,128]{2,1,0:T(8,128)(2,1)S(1)}, bf16[4,272,128]{2,1,0:T(8,128)(2,1)S(1)}, u32[]{:S(2)}, u32[]{:S(2)}) collective-permute-start(bf16[4,272,128]{2,1,0:T(8,128)(2,1)S(1)} %slice.82), channel_id=1, source_target_pairs={{0,128},{16,144},{32,160},{48,176},{64,192},{80,208},{96,224},{112... | collective-permute-start | bytes 835592 | tf_op jit(solution)/shard_map/ppermute | solution.py:40
  61.1 2.1 %pad_maximum_fusion.2.w_ref = bf16[1024,384]{1,0:T(8,128)(2,1)} fusion(bf16[1024,128]{1,0:T(8,128)(2,1)} %param.16, bf16[1024,128]{1,0:T(8,128)(2,1)} %param.15, bf16[1024,128]{1,0:T(8,128)(2,1)} %param.14), kind=kLoop, calls=%fused_computation.11 | loop fusion | flops 2359296 | bytes 1572864 | tf_op jit(solution)/shard_map/concatenate | solution.py:255
  63.2 2.4 %collective-permute-start.9 = (bf16[4,272,128]{2,1,0:T(8,128)(2,1)S(1)}, bf16[4,272,128]{2,1,0:T(8,128)(2,1)S(1)}, u32[]{:S(2)}, u32[]{:S(2)}) collective-permute-start(bf16[4,272,128]{2,1,0:T(8,128)(2,1)S(1)} %slice.83), channel_id=1, source_target_pairs={{0,384},{16,400},{32,416},{48,432},{64,448},{80,464},{96,480},{112... | collective-permute-start | bytes 835592 | tf_op jit(solution)/shard_map/ppermute | solution.py:40
  65.7 0.9 constant_dynamic-update-slice_fusion.11
  66.5 0.8 constant_dynamic-update-slice_fusion.10
  67.4 0.8 constant_dynamic-update-slice_fusion.9
  68.1 4.7 %collective-permute-done.9 = bf16[4,272,128]{2,1,0:T(8,128)(2,1)S(1)} collective-permute-done((bf16[4,272,128]{2,1,0:T(8,128)(2,1)S(1)}, bf16[4,272,128]{2,1,0:T(8,128)(2,1)S(1)}, u32[]{:S(2)}, u32[]{:S(2)}) %collective-permute-start.9) | collective-permute-done | bytes 278560 | tf_op jit(solution)/shard_map/ppermute | solution.py:40
  72.9 0.7 constant_dynamic-update-slice_fusion.8.q_ref.k_ref.v_ref.g_ref
  73.6 1.5 %fusion.18 = s32[32]{0:T(128)S(1)} fusion(bf16[32,272,128]{2,1,0:T(8,128)(2,1)} %constant_dynamic-update-slice_fusion.8.q_ref.k_ref.v_ref.g_ref), kind=kLoop, calls=%fused_computation.62 | loop fusion | flops 32 | bytes 192 | tf_op jit(solution)/shard_map/convert_element_type | solution.py:245
  75.2 0.7 select_n.205.key_code_ref
  75.9 0.5 slice.85.own_code_ref
  76.3 18.5 %shard_map.113 = (bf16[64,128]{1,0:T(8,128)(2,1)}, bf16[64,1024]{1,0:T(8,128)(2,1)}) custom-call(s32[32]{0:T(128)} %copy-done.6, bf16[32,272,128]{2,1,0:T(8,128)(2,1)} %constant_dynamic-update-slice_fusion.8.q_ref.k_ref.v_ref.g_ref, bf16[32,272,128]{2,1,0:T(8,128)(2,1)} %constant_dynamic-update-slice_fusion.8.q_ref.k_ref.v_ref.g_ref, ...), custom_call_target="tpu_custom_call" | custom-call | tf_op jit(solution)/shard_map/pallas_call | solution.py:188
  94.8 4.3 %collective-permute-start.10 = (bf16[64,1024]{1,0:T(8,128)(2,1)}, bf16[64,1024]{1,0:T(8,128)(2,1)S(1)}, u32[]{:S(2)}, u32[]{:S(2)}) collective-permute-start(bf16[64,1024]{1,0:T(8,128)(2,1)} %get-tuple-element.5), channel_id=1, source_target_pairs={{0,2},{2,0},{4,6},{6,4},{8,10},{10,8},{12,14},{14,12},{1,3},{3,1},... | collective-permute-start | bytes 393224 | tf_op jit(solution)/shard_map/ppermute | solution.py:83
  99.1 3.1 %collective-permute-done.10 = bf16[64,1024]{1,0:T(8,128)(2,1)S(1)} collective-permute-done((bf16[64,1024]{1,0:T(8,128)(2,1)}, bf16[64,1024]{1,0:T(8,128)(2,1)S(1)}, u32[]{:S(2)}, u32[]{:S(2)}) %collective-permute-start.10) | collective-permute-done | bytes 131104 | tf_op jit(solution)/shard_map/ppermute | solution.py:83
  102.2 0.9 add_convert_fusion.2
  103.2 7.2 %collective-permute-start.11 = (bf16[64,1024]{1,0:T(8,128)(2,1)S(1)}, bf16[64,1024]{1,0:T(8,128)(2,1)S(1)}, u32[]{:S(2)}, u32[]{:S(2)}) collective-permute-start(bf16[64,1024]{1,0:T(8,128)(2,1)S(1)} %add_convert_fusion.2), channel_id=1, source_target_pairs={{0,4},{2,6},{4,0},{6,2},{8,12},{10,14},{12,8},{14,10},{1,5},{3,7},... | collective-permute-start | bytes 393224 | tf_op jit(solution)/shard_map/ppermute | solution.py:83
  110.4 0.1 sub.97
  110.5 4.2 %collective-permute-done.11 = bf16[64,1024]{1,0:T(8,128)(2,1)S(1)} collective-permute-done((bf16[64,1024]{1,0:T(8,128)(2,1)S(1)}, bf16[64,1024]{1,0:T(8,128)(2,1)S(1)}, u32[]{:S(2)}, u32[]{:S(2)}) %collective-permute-start.11) | collective-permute-done | bytes 131104 | tf_op jit(solution)/shard_map/ppermute | solution.py:83
  114.8 8.1 %collective-permute-start.12 = (bf16[64,1024]{1,0:T(8,128)(2,1)S(1)}, bf16[64,1024]{1,0:T(8,128)(2,1)S(1)}, u32[]{:S(2)}, u32[]{:S(2)}) collective-permute-start(bf16[64,1024]{1,0:T(8,128)(2,1)S(1)} %add_convert_fusion.1), channel_id=1, source_target_pairs={{14,0},{8,6},{6,8},{0,14},{15,1},{9,7},{7,9},{1,15},{30,16},{24,22... | collective-permute-start | bytes 393224 | tf_op jit(solution)/shard_map/ppermute | solution.py:91
  122.9 2.1 %collective-permute-start.13 = (bf16[64,1024]{1,0:T(8,128)(2,1)S(1)}, bf16[64,1024]{1,0:T(8,128)(2,1)S(1)}, u32[]{:S(2)}, u32[]{:S(2)}) collective-permute-start(bf16[64,1024]{1,0:T(8,128)(2,1)S(1)} %add_convert_fusion.1), channel_id=1, source_target_pairs={{14,2},{8,4},{6,10},{0,12},{15,3},{9,5},{7,11},{1,13},{30,18},{24,... | collective-permute-start | bytes 393224 | tf_op jit(solution)/shard_map/ppermute | solution.py:91
  125.0 1.4 %broadcast_select_fusion = bf16[64,128]{1,0:T(8,128)(2,1)} fusion(bf16[64,128]{1,0:T(8,128)(2,1)} %get-tuple-element.4, pred[64]{0:T(512)(128)(4,1)S(1)} %iota_compare_fusion.3), kind=kLoop, calls=%fused_computation.65 | loop fusion | flops 8192 | bytes 32832 | tf_op jit(solution)/shard_map/jit(_where)/select_n | solution.py:257
  126.4 1.1 collective-permute-done.13
  127.5 0.2 multiply_reduce_fusion
  127.7 0.8 multiply_add_fusion
  128.5 0.5 fusion.3
  129.0 3.1 %collective-permute-start.14 = (f32[3,1024]{1,0:T(4,128)S(1)}, f32[3,1024]{1,0:T(4,128)S(1)}, u32[]{:S(2)}, u32[]{:S(2)}) collective-permute-start(f32[3,1024]{1,0:T(4,128)S(1)} %fusion.3), channel_id=1, source_target_pairs={{16,0},{32,16},{48,32},{64,48},{80,64},{96,80},{112,96},{128,112},... | collective-permute-start | bytes 36872 | tf_op jit(solution)/shard_map/ppermute | solution.py:23
  132.1 1.1 fusion.4
  133.2 2.6 %collective-permute-done.14 = f32[3,1024]{1,0:T(4,128)S(1)} collective-permute-done((f32[3,1024]{1,0:T(4,128)S(1)}, f32[3,1024]{1,0:T(4,128)S(1)}, u32[]{:S(2)}, u32[]{:S(2)}) %collective-permute-start.14) | collective-permute-done | bytes 12320 | tf_op jit(solution)/shard_map/ppermute | solution.py:23
  135.8 1.1 add_convert_fusion
  (41 shorter events, 0.5 us)
Async XLA Ops:
  0.6 13.1 %copy-start = (bf16[1024,1024]{1,0:T(8,128)(2,1)S(1)}, bf16[1024,1024]{1,0:T(8,128)(2,1)}, u32[]{:S(2)}) copy-start(bf16[1024,1024]{1,0:T(8,128)(2,1)} %param.12) | copy-start | bytes 6291460
  1.5 7.5 %collective-permute-start = (bf16[3,1024]{1,0:T(4,128)(2,1)S(1)}, bf16[3,1024]{1,0:T(4,128)(2,1)S(1)}, u32[]{:S(2)}, u32[]{:S(2)}) collective-permute-start(bf16[3,1024]{1,0:T(4,128)(2,1)S(1)} %slice.112), channel_id=1, source_target_pairs={{0,16},{16,32},{32,48},{48,64},{64,80},{80,96},{96,112},{112,128},... | collective-permute-start | bytes 18440 | tf_op jit(solution)/shard_map/ppermute | solution.py:23
  12.5 1.9 %copy-start.4 = (f32[1024]{0:T(1024)S(1)}, f32[1024]{0:T(1024)}, u32[]{:S(2)}) copy-start(f32[1024]{0:T(1024)} %param.13) | copy-start | bytes 12292
  12.5 2.0 %copy-start.1 = (bf16[1024,128]{1,0:T(8,128)(2,1)S(1)}, bf16[1024,128]{1,0:T(8,128)(2,1)}, u32[]{:S(2)}) copy-start(bf16[1024,128]{1,0:T(8,128)(2,1)} %param.14) | copy-start | bytes 786436
  12.5 2.2 %copy-start.2 = (bf16[1024,128]{1,0:T(8,128)(2,1)S(1)}, bf16[1024,128]{1,0:T(8,128)(2,1)}, u32[]{:S(2)}) copy-start(bf16[1024,128]{1,0:T(8,128)(2,1)} %param.15) | copy-start | bytes 786436
  13.7 1.1 copy-start.3
  13.7 1.3 copy-start.5
  15.2 6.2 %collective-permute-start.1 = (bf16[1,272,128]{2,1,0:T(8,128)(2,1)S(1)}, bf16[1,272,128]{2,1,0:T(8,128)(2,1)S(1)}, u32[]{:S(2)}, u32[]{:S(2)}) collective-permute-start(bf16[1,272,128]{2,1,0:T(8,128)(2,1)S(1)} %bitcast.20), channel_id=1, source_target_pairs={{0,16},{16,0},{32,48},{48,32},{64,80},{80,64},{96,112},{112,96},{1... | collective-permute-start | bytes 208904 | tf_op jit(solution)/shard_map/ppermute | solution.py:62
  21.4 9.8 %collective-permute-start.2 = (bf16[2,272,128]{2,1,0:T(8,128)(2,1)S(1)}, bf16[2,272,128]{2,1,0:T(8,128)(2,1)S(1)}, u32[]{:S(2)}, u32[]{:S(2)}) collective-permute-start(bf16[2,272,128]{2,1,0:T(8,128)(2,1)S(1)} %pad_maximum_fusion.5), channel_id=1, source_target_pairs={{0,32},{16,48},{32,64},{48,80},{64,96},{80,112},{96,0},{112,16},{1... | collective-permute-start | bytes 417800 | tf_op jit(solution)/shard_map/ppermute | solution.py:40
  24.8 10.1 %collective-permute-start.3 = (bf16[2,272,128]{2,1,0:T(8,128)(2,1)S(1)}, bf16[2,272,128]{2,1,0:T(8,128)(2,1)S(1)}, u32[]{:S(2)}, u32[]{:S(2)}) collective-permute-start(bf16[2,272,128]{2,1,0:T(8,128)(2,1)S(1)} %pad_maximum_fusion.5), channel_id=1, source_target_pairs={{0,96},{16,112},{32,0},{48,16},{64,32},{80,48},{96,64},{112,80},{1... | collective-permute-start | bytes 417800 | tf_op jit(solution)/shard_map/ppermute | solution.py:40
  31.2 8.3 %collective-permute-start.4 = (bf16[1,272,128]{2,1,0:T(8,128)(2,1)S(1)}, bf16[1,272,128]{2,1,0:T(8,128)(2,1)S(1)}, u32[]{:S(2)}, u32[]{:S(2)}) collective-permute-start(bf16[1,272,128]{2,1,0:T(8,128)(2,1)S(1)} %slice.80), channel_id=1, source_target_pairs={{0,32},{16,48},{32,64},{48,80},{64,96},{80,112},{96,0},{112,16},{1... | collective-permute-start | bytes 208904 | tf_op jit(solution)/shard_map/ppermute | solution.py:40
  34.9 8.3 %collective-permute-start.5 = (bf16[1,272,128]{2,1,0:T(8,128)(2,1)S(1)}, bf16[1,272,128]{2,1,0:T(8,128)(2,1)S(1)}, u32[]{:S(2)}, u32[]{:S(2)}) collective-permute-start(bf16[1,272,128]{2,1,0:T(8,128)(2,1)S(1)} %slice.81), channel_id=1, source_target_pairs={{0,96},{16,112},{32,0},{48,16},{64,32},{80,48},{96,64},{112,80},{1... | collective-permute-start | bytes 208904 | tf_op jit(solution)/shard_map/ppermute | solution.py:40
  43.9 13.8 %collective-permute-start.6 = (bf16[8,272,128]{2,1,0:T(8,128)(2,1)}, bf16[8,272,128]{2,1,0:T(8,128)(2,1)S(1)}, u32[]{:S(2)}, u32[]{:S(2)}) collective-permute-start(bf16[8,272,128]{2,1,0:T(8,128)(2,1)} %get-tuple-element.18), channel_id=1, source_target_pairs={{0,128},{16,144},{32,160},{48,176},{64,192},{80,208},{96,224},{112... | collective-permute-start | bytes 1671176 | tf_op jit(solution)/shard_map/ppermute | solution.py:40
  47.5 15.8 %collective-permute-start.7 = (bf16[8,272,128]{2,1,0:T(8,128)(2,1)}, bf16[8,272,128]{2,1,0:T(8,128)(2,1)S(1)}, u32[]{:S(2)}, u32[]{:S(2)}) collective-permute-start(bf16[8,272,128]{2,1,0:T(8,128)(2,1)} %get-tuple-element.18), channel_id=1, source_target_pairs={{0,384},{16,400},{32,416},{48,432},{64,448},{80,464},{96,480},{112... | collective-permute-start | bytes 1671176 | tf_op jit(solution)/shard_map/ppermute | solution.py:40
  49.9 17.4 %copy-start.6 = (s32[32]{0:T(128)}, s32[32]{0:T(128)S(1)}, u32[]{:S(2)}) copy-start(s32[32]{0:T(128)S(1)} %concatenate.63.shards_ref) | copy-start | bytes 388
  57.7 9.7 %collective-permute-start.8 = (bf16[4,272,128]{2,1,0:T(8,128)(2,1)S(1)}, bf16[4,272,128]{2,1,0:T(8,128)(2,1)S(1)}, u32[]{:S(2)}, u32[]{:S(2)}) collective-permute-start(bf16[4,272,128]{2,1,0:T(8,128)(2,1)S(1)} %slice.82), channel_id=1, source_target_pairs={{0,128},{16,144},{32,160},{48,176},{64,192},{80,208},{96,224},{112... | collective-permute-start | bytes 835592 | tf_op jit(solution)/shard_map/ppermute | solution.py:40
  63.2 9.7 %collective-permute-start.9 = (bf16[4,272,128]{2,1,0:T(8,128)(2,1)S(1)}, bf16[4,272,128]{2,1,0:T(8,128)(2,1)S(1)}, u32[]{:S(2)}, u32[]{:S(2)}) collective-permute-start(bf16[4,272,128]{2,1,0:T(8,128)(2,1)S(1)} %slice.83), channel_id=1, source_target_pairs={{0,384},{16,400},{32,416},{48,432},{64,448},{80,464},{96,480},{112... | collective-permute-start | bytes 835592 | tf_op jit(solution)/shard_map/ppermute | solution.py:40
  94.8 7.4 %collective-permute-start.10 = (bf16[64,1024]{1,0:T(8,128)(2,1)}, bf16[64,1024]{1,0:T(8,128)(2,1)S(1)}, u32[]{:S(2)}, u32[]{:S(2)}) collective-permute-start(bf16[64,1024]{1,0:T(8,128)(2,1)} %get-tuple-element.5), channel_id=1, source_target_pairs={{0,2},{2,0},{4,6},{6,4},{8,10},{10,8},{12,14},{14,12},{1,3},{3,1},... | collective-permute-start | bytes 393224 | tf_op jit(solution)/shard_map/ppermute | solution.py:83
  103.2 11.6 %collective-permute-start.11 = (bf16[64,1024]{1,0:T(8,128)(2,1)S(1)}, bf16[64,1024]{1,0:T(8,128)(2,1)S(1)}, u32[]{:S(2)}, u32[]{:S(2)}) collective-permute-start(bf16[64,1024]{1,0:T(8,128)(2,1)S(1)} %add_convert_fusion.2), channel_id=1, source_target_pairs={{0,4},{2,6},{4,0},{6,2},{8,12},{10,14},{12,8},{14,10},{1,5},{3,7},... | collective-permute-start | bytes 393224 | tf_op jit(solution)/shard_map/ppermute | solution.py:83
  114.8 11.6 %collective-permute-start.12 = (bf16[64,1024]{1,0:T(8,128)(2,1)S(1)}, bf16[64,1024]{1,0:T(8,128)(2,1)S(1)}, u32[]{:S(2)}, u32[]{:S(2)}) collective-permute-start(bf16[64,1024]{1,0:T(8,128)(2,1)S(1)} %add_convert_fusion.1), channel_id=1, source_target_pairs={{14,0},{8,6},{6,8},{0,14},{15,1},{9,7},{7,9},{1,15},{30,16},{24,22... | collective-permute-start | bytes 393224 | tf_op jit(solution)/shard_map/ppermute | solution.py:91
  122.9 4.6 %collective-permute-start.13 = (bf16[64,1024]{1,0:T(8,128)(2,1)S(1)}, bf16[64,1024]{1,0:T(8,128)(2,1)S(1)}, u32[]{:S(2)}, u32[]{:S(2)}) collective-permute-start(bf16[64,1024]{1,0:T(8,128)(2,1)S(1)} %add_convert_fusion.1), channel_id=1, source_target_pairs={{14,2},{8,4},{6,10},{0,12},{15,3},{9,5},{7,11},{1,13},{30,18},{24,... | collective-permute-start | bytes 393224 | tf_op jit(solution)/shard_map/ppermute | solution.py:91
  129.0 6.8 %collective-permute-start.14 = (f32[3,1024]{1,0:T(4,128)S(1)}, f32[3,1024]{1,0:T(4,128)S(1)}, u32[]{:S(2)}, u32[]{:S(2)}) collective-permute-start(f32[3,1024]{1,0:T(4,128)S(1)} %fusion.3), channel_id=1, source_target_pairs={{16,0},{32,16},{48,32},{64,48},{80,64},{96,80},{112,96},{128,112},... | collective-permute-start | bytes 36872 | tf_op jit(solution)/shard_map/ppermute | solution.py:23

commit v20 on v18

--- a/solution.py
+++ b/solution.py
@@ -10,8 +10,8 @@
 D = 1024
 HD = 128
 KCONV = 4
-QBLOCK = 256
-BLOCKS_PER_STEP = 4
+QBLOCK = 128
+BLOCKS_PER_STEP = 2
 
 
 masked_score = -1e30

time: 136 us -> 140 us (1.029)
  Pallas kernels: 18 us -> 22.2 us
    pallas_call x1, Pallas kernels: 18 us -> 22.2 us  [attention_all(): pl.pallas_call(forward_kernel, grid_spec=grid_spec, out_shape=[jax.ShapeD...]
where the time goes in v20:
time: 140 us; the launch traced here: 139 us
  starting transfers between devices  56.6 us (40%)
  waiting for transfers between devices  33.7 us (24%)
  Pallas kernels  22.2 us (16%)
  local copies, waits for them, and re-layouts  12.7 us (9%)
  other arithmetic  7.66 us (5%)
  matrix products  4.66 us (3%)
  between operations  1.74 us (1%)
    ppermute x8, starting transfers between devices, shifted(): return lax.ppermute(array, axis, pairs)  25.1 us
    pallas_call x1, Pallas kernels, attention_all(): pl.pallas_call(forward_kernel, grid_spec=grid_spec, out_shape=[jax.ShapeD...  22.2 us
    ppermute x8, waiting for transfers between devices, shifted(): return lax.ppermute(array, axis, pairs)  17.8 us
    ppermute x2, starting transfers between devices, summed_over(): got = lax.ppermute(sent, axis, [(i, i ^ step) for i in range(devices)])  11.6 us
    ppermute x1, starting transfers between devices, summed_over(): lax.ppermute(sent, axis, near).astype(jnp.float32)  8.96 us
    ppermute x2, starting transfers between devices, passed_along(): return lax.ppermute(array, axis, pairs)  7.68 us
    ppermute x2, waiting for transfers between devices, summed_over(): got = lax.ppermute(sent, axis, [(i, i ^ step) for i in range(devices)])  7.18 us
    unnamed x30, local copies, waits for them, and re-layouts  5.95 us
  transfers between devices with their start and end apart: 15, of which 11 were waited for; matrix products, arithmetic and copies ran while one was open for 7% of the time, Pallas kernels for 0%

profile of v20, /device:TPU:30, one launch (start us, length us, event | category | flops | bytes accessed | tf_op | source)
XLA Modules:
  0.0 139.2 jit_solution(12384034075062918901)
XLA Ops:
  0.6 0.9 slice.112
  1.5 4.7 %collective-permute-start = (bf16[3,1024]{1,0:T(4,128)(2,1)S(1)}, bf16[3,1024]{1,0:T(4,128)(2,1)S(1)}, u32[]{:S(2)}, u32[]{:S(2)}) collective-permute-start(bf16[3,1024]{1,0:T(4,128)(2,1)S(1)} %slice.112), channel_id=1, source_target_pairs={{0,16},{16,32},{32,48},{48,64},{64,80},{80,96},{96,112},{112,128},... | collective-permute-start | bytes 18440 | tf_op jit(solution)/shard_map/ppermute | solution.py:23
  6.2 0.7 iota_subtract_fusion
  7.0 0.1 add.349
  7.0 0.1 add.346
  7.1 0.9 fusion.46
  8.7 0.1 multiply_add_fusion.6
  8.8 1.5 %pad_maximum_fusion = bf16[515,1024]{1,0:T(8,128)(2,1)S(1)} fusion(bf16[512,1024]{1,0:T(8,128)(2,1)} %param.10, bf16[3,1024]{1,0:T(4,128)(2,1)S(1)} %collective-permute-done), kind=kLoop, calls=%fused_computation.10 | loop fusion | flops 2109440 | bytes 2109440 | tf_op jit(solution)/shard_map/concatenate | solution.py:215
  10.3 2.0 %gather_fusion = bf16[256,1024]{1,0:T(8,128)(2,1)} fusion(bf16[515,1024]{1,0:T(8,128)(2,1)S(1)} %pad_maximum_fusion, s32[1024]{0:T(1024)S(1)} %pad_clamp_fusion), kind=kCustom, calls=%fused_computation | custom fusion | bytes 1049600 | tf_op jit(solution)/shard_map/jit(_take)/gather | solution.py:217
  12.3 1.2 select_convert_fusion
  13.6 0.6 multiply_reduce_fusion.1
  14.2 0.1 multiply_convert_fusion
  14.3 0.2 fusion.2
  14.5 0.2 fusion.1
  14.7 0.2 fusion
  14.9 0.1 constant_dynamic-update-slice_fusion.1
  15.0 1.9 %collective-permute-start.1 = (bf16[1,272,128]{2,1,0:T(8,128)(2,1)S(1)}, bf16[1,272,128]{2,1,0:T(8,128)(2,1)S(1)}, u32[]{:S(2)}, u32[]{:S(2)}) collective-permute-start(bf16[1,272,128]{2,1,0:T(8,128)(2,1)S(1)} %bitcast.21), channel_id=1, source_target_pairs={{0,16},{16,0},{32,48},{48,32},{64,80},{80,64},{96,112},{112,96},{1... | collective-permute-start | bytes 208904 | tf_op jit(solution)/shard_map/ppermute | solution.py:62
  17.1 4.1 %collective-permute-done.1 = bf16[1,272,128]{2,1,0:T(8,128)(2,1)S(1)} collective-permute-done((bf16[1,272,128]{2,1,0:T(8,128)(2,1)S(1)}, bf16[1,272,128]{2,1,0:T(8,128)(2,1)S(1)}, u32[]{:S(2)}, u32[]{:S(2)}) %collective-permute-start.1) | collective-permute-done | bytes 69664 | tf_op jit(solution)/shard_map/ppermute | solution.py:62
  21.2 3.6 %collective-permute-start.2 = (bf16[2,272,128]{2,1,0:T(8,128)(2,1)S(1)}, bf16[2,272,128]{2,1,0:T(8,128)(2,1)S(1)}, u32[]{:S(2)}, u32[]{:S(2)}) collective-permute-start(bf16[2,272,128]{2,1,0:T(8,128)(2,1)S(1)} %pad_maximum_fusion.4), channel_id=1, source_target_pairs={{0,32},{16,48},{32,64},{48,80},{64,96},{80,112},{96,0},{112,16},{1... | collective-permute-start | bytes 417800 | tf_op jit(solution)/shard_map/ppermute | solution.py:40
  24.8 3.2 %collective-permute-start.3 = (bf16[2,272,128]{2,1,0:T(8,128)(2,1)S(1)}, bf16[2,272,128]{2,1,0:T(8,128)(2,1)S(1)}, u32[]{:S(2)}, u32[]{:S(2)}) collective-permute-start(bf16[2,272,128]{2,1,0:T(8,128)(2,1)S(1)} %pad_maximum_fusion.4), channel_id=1, source_target_pairs={{0,96},{16,112},{32,0},{48,16},{64,32},{80,48},{96,64},{112,80},{1... | collective-permute-start | bytes 417800 | tf_op jit(solution)/shard_map/ppermute | solution.py:40
  27.9 0.7 constant_dynamic-update-slice_fusion.7
  28.6 0.7 constant_dynamic-update-slice_fusion.6
  29.3 1.7 %collective-permute-done.2 = bf16[2,272,128]{2,1,0:T(8,128)(2,1)S(1)} collective-permute-done((bf16[2,272,128]{2,1,0:T(8,128)(2,1)S(1)}, bf16[2,272,128]{2,1,0:T(8,128)(2,1)S(1)}, u32[]{:S(2)}, u32[]{:S(2)}) %collective-permute-start.2) | collective-permute-done | bytes 139296 | tf_op jit(solution)/shard_map/ppermute | solution.py:40
  31.0 3.9 %collective-permute-start.4 = (bf16[1,272,128]{2,1,0:T(8,128)(2,1)S(1)}, bf16[1,272,128]{2,1,0:T(8,128)(2,1)S(1)}, u32[]{:S(2)}, u32[]{:S(2)}) collective-permute-start(bf16[1,272,128]{2,1,0:T(8,128)(2,1)S(1)} %slice.80), channel_id=1, source_target_pairs={{0,32},{16,48},{32,64},{48,80},{64,96},{80,112},{96,0},{112,16},{1... | collective-permute-start | bytes 208904 | tf_op jit(solution)/shard_map/ppermute | solution.py:40
  34.9 2.8 %collective-permute-start.5 = (bf16[1,272,128]{2,1,0:T(8,128)(2,1)S(1)}, bf16[1,272,128]{2,1,0:T(8,128)(2,1)S(1)}, u32[]{:S(2)}, u32[]{:S(2)}) collective-permute-start(bf16[1,272,128]{2,1,0:T(8,128)(2,1)S(1)} %slice.81), channel_id=1, source_target_pairs={{0,96},{16,112},{32,0},{48,16},{64,32},{80,48},{96,64},{112,80},{1... | collective-permute-start | bytes 208904 | tf_op jit(solution)/shard_map/ppermute | solution.py:40
  37.7 0.7 constant_dynamic-update-slice_fusion.5
  38.5 0.7 constant_dynamic-update-slice_fusion.4
  39.2 0.7 constant_dynamic-update-slice_fusion.3
  39.9 3.3 %collective-permute-done.5 = bf16[1,272,128]{2,1,0:T(8,128)(2,1)S(1)} collective-permute-done((bf16[1,272,128]{2,1,0:T(8,128)(2,1)S(1)}, bf16[1,272,128]{2,1,0:T(8,128)(2,1)S(1)}, u32[]{:S(2)}, u32[]{:S(2)}) %collective-permute-start.5) | collective-permute-done | bytes 69664 | tf_op jit(solution)/shard_map/ppermute | solution.py:40
  43.2 0.7 constant_dynamic-update-slice_fusion.2
  43.9 3.2 %collective-permute-start.6 = (bf16[8,272,128]{2,1,0:T(8,128)(2,1)}, bf16[8,272,128]{2,1,0:T(8,128)(2,1)S(1)}, u32[]{:S(2)}, u32[]{:S(2)}) collective-permute-start(bf16[8,272,128]{2,1,0:T(8,128)(2,1)} %get-tuple-element.18), channel_id=1, source_target_pairs={{0,128},{16,144},{32,160},{48,176},{64,192},{80,208},{96,224},{112... | collective-permute-start | bytes 1671176 | tf_op jit(solution)/shard_map/ppermute | solution.py:40
  47.1 2.6 %collective-permute-start.7 = (bf16[8,272,128]{2,1,0:T(8,128)(2,1)}, bf16[8,272,128]{2,1,0:T(8,128)(2,1)S(1)}, u32[]{:S(2)}, u32[]{:S(2)}) collective-permute-start(bf16[8,272,128]{2,1,0:T(8,128)(2,1)} %get-tuple-element.18), channel_id=1, source_target_pairs={{0,384},{16,400},{32,416},{48,432},{64,448},{80,464},{96,480},{112... | collective-permute-start | bytes 1671176 | tf_op jit(solution)/shard_map/ppermute | solution.py:40
  49.7 0.1 multiply_add_fusion.2
  50.0 8.0 %collective-permute-done.6 = bf16[8,272,128]{2,1,0:T(8,128)(2,1)S(1)} collective-permute-done((bf16[8,272,128]{2,1,0:T(8,128)(2,1)}, bf16[8,272,128]{2,1,0:T(8,128)(2,1)S(1)}, u32[]{:S(2)}, u32[]{:S(2)}) %collective-permute-start.6) | collective-permute-done | bytes 557088 | tf_op jit(solution)/shard_map/ppermute | solution.py:40
  58.0 3.4 %collective-permute-start.8 = (bf16[4,272,128]{2,1,0:T(8,128)(2,1)S(1)}, bf16[4,272,128]{2,1,0:T(8,128)(2,1)S(1)}, u32[]{:S(2)}, u32[]{:S(2)}) collective-permute-start(bf16[4,272,128]{2,1,0:T(8,128)(2,1)S(1)} %slice.82), channel_id=1, source_target_pairs={{0,128},{16,144},{32,160},{48,176},{64,192},{80,208},{96,224},{112... | collective-permute-start | bytes 835592 | tf_op jit(solution)/shard_map/ppermute | solution.py:40
  61.5 2.4 %collective-permute-start.9 = (bf16[4,272,128]{2,1,0:T(8,128)(2,1)S(1)}, bf16[4,272,128]{2,1,0:T(8,128)(2,1)S(1)}, u32[]{:S(2)}, u32[]{:S(2)}) collective-permute-start(bf16[4,272,128]{2,1,0:T(8,128)(2,1)S(1)} %slice.83), channel_id=1, source_target_pairs={{0,384},{16,400},{32,416},{48,432},{64,448},{80,464},{96,480},{112... | collective-permute-start | bytes 835592 | tf_op jit(solution)/shard_map/ppermute | solution.py:40
  63.9 0.9 constant_dynamic-update-slice_fusion.11
  64.8 0.8 constant_dynamic-update-slice_fusion.10
  65.6 0.8 collective-permute-done.8
  66.4 0.7 constant_dynamic-update-slice_fusion.9
  67.1 4.0 %collective-permute-done.9 = bf16[4,272,128]{2,1,0:T(8,128)(2,1)S(1)} collective-permute-done((bf16[4,272,128]{2,1,0:T(8,128)(2,1)S(1)}, bf16[4,272,128]{2,1,0:T(8,128)(2,1)S(1)}, u32[]{:S(2)}, u32[]{:S(2)}) %collective-permute-start.9) | collective-permute-done | bytes 278560 | tf_op jit(solution)/shard_map/ppermute | solution.py:40
  71.1 0.7 constant_dynamic-update-slice_fusion.8.q_ref.k_ref.v_ref.g_ref
  71.8 1.5 %fusion.23 = s32[32]{0:T(128)S(1)} fusion(bf16[32,272,128]{2,1,0:T(8,128)(2,1)} %constant_dynamic-update-slice_fusion.8.q_ref.k_ref.v_ref.g_ref), kind=kLoop, calls=%fused_computation.67 | loop fusion | flops 32 | bytes 192 | tf_op jit(solution)/shard_map/convert_element_type | solution.py:240
  73.4 0.7 select_n.205.key_code_ref
  74.1 0.5 slice.85.own_code_ref
  74.6 22.2 %shard_map.113 = (bf16[64,128]{1,0:T(8,128)(2,1)}, bf16[64,384]{1,0:T(8,128)(2,1)}) custom-call(s32[32]{0:T(128)} %copy-done.10, bf16[32,272,128]{2,1,0:T(8,128)(2,1)} %constant_dynamic-update-slice_fusion.8.q_ref.k_ref.v_ref.g_ref, bf16[32,272,128]{2,1,0:T(8,128)(2,1)} %constant_dynamic-update-slice_fusion.8.q_ref.k_ref.v_ref.g_ref, ...), custom_call_target="tpu_custom_call" | custom-call | tf_op jit(solution)/shard_map/pallas_call | solution.py:183
  96.8 1.2 convolution_convert_fusion
  98.0 4.3 %collective-permute-start.10 = (bf16[64,1024]{1,0:T(8,128)(2,1)S(1)}, bf16[64,1024]{1,0:T(8,128)(2,1)S(1)}, u32[]{:S(2)}, u32[]{:S(2)}) collective-permute-start(bf16[64,1024]{1,0:T(8,128)(2,1)S(1)} %convolution_convert_fusion), channel_id=1, source_target_pairs={{0,2},{2,0},{4,6},{6,4},{8,10},{10,8},{12,14},{14,12},{1,3},{3,1},... | collective-permute-start | bytes 393224 | tf_op jit(solution)/shard_map/ppermute | solution.py:83
  102.2 2.9 %collective-permute-done.10 = bf16[64,1024]{1,0:T(8,128)(2,1)S(1)} collective-permute-done((bf16[64,1024]{1,0:T(8,128)(2,1)S(1)}, bf16[64,1024]{1,0:T(8,128)(2,1)S(1)}, u32[]{:S(2)}, u32[]{:S(2)}) %collective-permute-start.10) | collective-permute-done | bytes 131104 | tf_op jit(solution)/shard_map/ppermute | solution.py:83
  105.2 7.3 %collective-permute-start.11 = (bf16[64,1024]{1,0:T(8,128)(2,1)S(1)}, bf16[64,1024]{1,0:T(8,128)(2,1)S(1)}, u32[]{:S(2)}, u32[]{:S(2)}) collective-permute-start(bf16[64,1024]{1,0:T(8,128)(2,1)S(1)} %add_convert_fusion.2), channel_id=1, source_target_pairs={{0,4},{2,6},{4,0},{6,2},{8,12},{10,14},{12,8},{14,10},{1,5},{3,7},... | collective-permute-start | bytes 393224 | tf_op jit(solution)/shard_map/ppermute | solution.py:83
  112.5 0.1 sub.97
  112.6 4.2 %collective-permute-done.11 = bf16[64,1024]{1,0:T(8,128)(2,1)S(1)} collective-permute-done((bf16[64,1024]{1,0:T(8,128)(2,1)S(1)}, bf16[64,1024]{1,0:T(8,128)(2,1)S(1)}, u32[]{:S(2)}, u32[]{:S(2)}) %collective-permute-start.11) | collective-permute-done | bytes 131104 | tf_op jit(solution)/shard_map/ppermute | solution.py:83
  116.9 9.0 %collective-permute-start.12 = (bf16[64,1024]{1,0:T(8,128)(2,1)S(1)}, bf16[64,1024]{1,0:T(8,128)(2,1)S(1)}, u32[]{:S(2)}, u32[]{:S(2)}) collective-permute-start(bf16[64,1024]{1,0:T(8,128)(2,1)S(1)} %add_convert_fusion.1), channel_id=1, source_target_pairs={{14,0},{8,6},{6,8},{0,14},{15,1},{9,7},{7,9},{1,15},{30,16},{24,22... | collective-permute-start | bytes 393224 | tf_op jit(solution)/shard_map/ppermute | solution.py:91
  125.9 1.3 collective-permute-start.13
  127.2 0.7 broadcast_select_fusion
  127.9 0.9 collective-permute-done.12
  128.8 0.9 collective-permute-done.13
  129.7 0.2 multiply_reduce_fusion
  129.9 0.8 multiply_add_fusion
  130.7 0.5 fusion.8
  131.2 3.0 %collective-permute-start.14 = (f32[3,1024]{1,0:T(4,128)S(1)}, f32[3,1024]{1,0:T(4,128)S(1)}, u32[]{:S(2)}, u32[]{:S(2)}) collective-permute-start(f32[3,1024]{1,0:T(4,128)S(1)} %fusion.8), channel_id=1, source_target_pairs={{16,0},{32,16},{48,32},{64,48},{80,64},{96,80},{112,96},{128,112},... | collective-permute-start | bytes 36872 | tf_op jit(solution)/shard_map/ppermute | solution.py:23
  134.2 1.1 fusion.9
  135.3 2.7 %collective-permute-done.14 = f32[3,1024]{1,0:T(4,128)S(1)} collective-permute-done((f32[3,1024]{1,0:T(4,128)S(1)}, f32[3,1024]{1,0:T(4,128)S(1)}, u32[]{:S(2)}, u32[]{:S(2)}) %collective-permute-start.14) | collective-permute-done | bytes 12320 | tf_op jit(solution)/shard_map/ppermute | solution.py:23
  138.0 1.1 add_convert_fusion
  (49 shorter events, 0.6 us)
Async XLA Ops:
  0.6 12.9 %copy-start = (bf16[1024,1024]{1,0:T(8,128)(2,1)S(1)}, bf16[1024,1024]{1,0:T(8,128)(2,1)}, u32[]{:S(2)}) copy-start(bf16[1024,1024]{1,0:T(8,128)(2,1)} %param.12) | copy-start | bytes 6291460
  1.5 7.3 %collective-permute-start = (bf16[3,1024]{1,0:T(4,128)(2,1)S(1)}, bf16[3,1024]{1,0:T(4,128)(2,1)S(1)}, u32[]{:S(2)}, u32[]{:S(2)}) collective-permute-start(bf16[3,1024]{1,0:T(4,128)(2,1)S(1)} %slice.112), channel_id=1, source_target_pairs={{0,16},{16,32},{32,48},{48,64},{64,80},{80,96},{96,112},{112,128},... | collective-permute-start | bytes 18440 | tf_op jit(solution)/shard_map/ppermute | solution.py:23
  12.3 1.9 %copy-start.7 = (f32[1024]{0:T(1024)S(1)}, f32[1024]{0:T(1024)}, u32[]{:S(2)}) copy-start(f32[1024]{0:T(1024)} %param.13) | copy-start | bytes 12292
  12.3 2.0 %copy-start.1 = (bf16[1024,128]{1,0:T(8,128)(2,1)S(1)}, bf16[1024,128]{1,0:T(8,128)(2,1)}, u32[]{:S(2)}) copy-start(bf16[1024,128]{1,0:T(8,128)(2,1)} %param.14) | copy-start | bytes 786436
  12.3 2.2 %copy-start.3 = (bf16[1024,128]{1,0:T(8,128)(2,1)S(1)}, bf16[1024,128]{1,0:T(8,128)(2,1)}, u32[]{:S(2)}) copy-start(bf16[1024,128]{1,0:T(8,128)(2,1)} %param.15) | copy-start | bytes 786436
  13.5 1.1 copy-start.5
  13.5 1.3 copy-start.8
  15.0 6.2 %collective-permute-start.1 = (bf16[1,272,128]{2,1,0:T(8,128)(2,1)S(1)}, bf16[1,272,128]{2,1,0:T(8,128)(2,1)S(1)}, u32[]{:S(2)}, u32[]{:S(2)}) collective-permute-start(bf16[1,272,128]{2,1,0:T(8,128)(2,1)S(1)} %bitcast.21), channel_id=1, source_target_pairs={{0,16},{16,0},{32,48},{48,32},{64,80},{80,64},{96,112},{112,96},{1... | collective-permute-start | bytes 208904 | tf_op jit(solution)/shard_map/ppermute | solution.py:62
  21.2 9.8 %collective-permute-start.2 = (bf16[2,272,128]{2,1,0:T(8,128)(2,1)S(1)}, bf16[2,272,128]{2,1,0:T(8,128)(2,1)S(1)}, u32[]{:S(2)}, u32[]{:S(2)}) collective-permute-start(bf16[2,272,128]{2,1,0:T(8,128)(2,1)S(1)} %pad_maximum_fusion.4), channel_id=1, source_target_pairs={{0,32},{16,48},{32,64},{48,80},{64,96},{80,112},{96,0},{112,16},{1... | collective-permute-start | bytes 417800 | tf_op jit(solution)/shard_map/ppermute | solution.py:40
  24.8 10.1 %collective-permute-start.3 = (bf16[2,272,128]{2,1,0:T(8,128)(2,1)S(1)}, bf16[2,272,128]{2,1,0:T(8,128)(2,1)S(1)}, u32[]{:S(2)}, u32[]{:S(2)}) collective-permute-start(bf16[2,272,128]{2,1,0:T(8,128)(2,1)S(1)} %pad_maximum_fusion.4), channel_id=1, source_target_pairs={{0,96},{16,112},{32,0},{48,16},{64,32},{80,48},{96,64},{112,80},{1... | collective-permute-start | bytes 417800 | tf_op jit(solution)/shard_map/ppermute | solution.py:40
  31.0 8.2 %collective-permute-start.4 = (bf16[1,272,128]{2,1,0:T(8,128)(2,1)S(1)}, bf16[1,272,128]{2,1,0:T(8,128)(2,1)S(1)}, u32[]{:S(2)}, u32[]{:S(2)}) collective-permute-start(bf16[1,272,128]{2,1,0:T(8,128)(2,1)S(1)} %slice.80), channel_id=1, source_target_pairs={{0,32},{16,48},{32,64},{48,80},{64,96},{80,112},{96,0},{112,16},{1... | collective-permute-start | bytes 208904 | tf_op jit(solution)/shard_map/ppermute | solution.py:40
  34.9 8.3 %collective-permute-start.5 = (bf16[1,272,128]{2,1,0:T(8,128)(2,1)S(1)}, bf16[1,272,128]{2,1,0:T(8,128)(2,1)S(1)}, u32[]{:S(2)}, u32[]{:S(2)}) collective-permute-start(bf16[1,272,128]{2,1,0:T(8,128)(2,1)S(1)} %slice.81), channel_id=1, source_target_pairs={{0,96},{16,112},{32,0},{48,16},{64,32},{80,48},{96,64},{112,80},{1... | collective-permute-start | bytes 208904 | tf_op jit(solution)/shard_map/ppermute | solution.py:40
  43.9 14.1 %collective-permute-start.6 = (bf16[8,272,128]{2,1,0:T(8,128)(2,1)}, bf16[8,272,128]{2,1,0:T(8,128)(2,1)S(1)}, u32[]{:S(2)}, u32[]{:S(2)}) collective-permute-start(bf16[8,272,128]{2,1,0:T(8,128)(2,1)} %get-tuple-element.18), channel_id=1, source_target_pairs={{0,128},{16,144},{32,160},{48,176},{64,192},{80,208},{96,224},{112... | collective-permute-start | bytes 1671176 | tf_op jit(solution)/shard_map/ppermute | solution.py:40
  47.1 14.3 %collective-permute-start.7 = (bf16[8,272,128]{2,1,0:T(8,128)(2,1)}, bf16[8,272,128]{2,1,0:T(8,128)(2,1)S(1)}, u32[]{:S(2)}, u32[]{:S(2)}) collective-permute-start(bf16[8,272,128]{2,1,0:T(8,128)(2,1)} %get-tuple-element.18), channel_id=1, source_target_pairs={{0,384},{16,400},{32,416},{48,432},{64,448},{80,464},{96,480},{112... | collective-permute-start | bytes 1671176 | tf_op jit(solution)/shard_map/ppermute | solution.py:40
  49.9 21.9 %copy-start.10 = (s32[32]{0:T(128)}, s32[32]{0:T(128)S(1)}, u32[]{:S(2)}) copy-start(s32[32]{0:T(128)S(1)} %concatenate.63.shards_ref) | copy-start | bytes 388
  58.0 8.4 %collective-permute-start.8 = (bf16[4,272,128]{2,1,0:T(8,128)(2,1)S(1)}, bf16[4,272,128]{2,1,0:T(8,128)(2,1)S(1)}, u32[]{:S(2)}, u32[]{:S(2)}) collective-permute-start(bf16[4,272,128]{2,1,0:T(8,128)(2,1)S(1)} %slice.82), channel_id=1, source_target_pairs={{0,128},{16,144},{32,160},{48,176},{64,192},{80,208},{96,224},{112... | collective-permute-start | bytes 835592 | tf_op jit(solution)/shard_map/ppermute | solution.py:40
  61.5 9.7 %collective-permute-start.9 = (bf16[4,272,128]{2,1,0:T(8,128)(2,1)S(1)}, bf16[4,272,128]{2,1,0:T(8,128)(2,1)S(1)}, u32[]{:S(2)}, u32[]{:S(2)}) collective-permute-start(bf16[4,272,128]{2,1,0:T(8,128)(2,1)S(1)} %slice.83), channel_id=1, source_target_pairs={{0,384},{16,400},{32,416},{48,432},{64,448},{80,464},{96,480},{112... | collective-permute-start | bytes 835592 | tf_op jit(solution)/shard_map/ppermute | solution.py:40
  74.6 22.2 %copy-start.2 = (bf16[1024,128]{1,0:T(8,128)(2,1)S(1)}, bf16[1024,128]{1,0:T(8,128)(2,1)}, u32[]{:S(2)}) copy-start(bf16[1024,128]{1,0:T(8,128)(2,1)} %param.14) | copy-start | bytes 786436
  74.6 22.2 %copy-start.4 = (bf16[1024,128]{1,0:T(8,128)(2,1)S(1)}, bf16[1024,128]{1,0:T(8,128)(2,1)}, u32[]{:S(2)}) copy-start(bf16[1024,128]{1,0:T(8,128)(2,1)} %param.15) | copy-start | bytes 786436
  74.6 22.2 %copy-start.6 = (bf16[1024,128]{1,0:T(8,128)(2,1)S(1)}, bf16[1024,128]{1,0:T(8,128)(2,1)}, u32[]{:S(2)}) copy-start(bf16[1024,128]{1,0:T(8,128)(2,1)} %param.16) | copy-start | bytes 786436
  96.8 30.4 %copy-start.9 = (bf16[64,128]{1,0:T(8,128)(2,1)S(1)}, bf16[64,128]{1,0:T(8,128)(2,1)}, u32[]{:S(2)}) copy-start(bf16[64,128]{1,0:T(8,128)(2,1)} %get-tuple-element.4) | copy-start | bytes 49156
  98.0 7.2 %collective-permute-start.10 = (bf16[64,1024]{1,0:T(8,128)(2,1)S(1)}, bf16[64,1024]{1,0:T(8,128)(2,1)S(1)}, u32[]{:S(2)}, u32[]{:S(2)}) collective-permute-start(bf16[64,1024]{1,0:T(8,128)(2,1)S(1)} %convolution_convert_fusion), channel_id=1, source_target_pairs={{0,2},{2,0},{4,6},{6,4},{8,10},{10,8},{12,14},{14,12},{1,3},{3,1},... | collective-permute-start | bytes 393224 | tf_op jit(solution)/shard_map/ppermute | solution.py:83
  105.2 11.6 %collective-permute-start.11 = (bf16[64,1024]{1,0:T(8,128)(2,1)S(1)}, bf16[64,1024]{1,0:T(8,128)(2,1)S(1)}, u32[]{:S(2)}, u32[]{:S(2)}) collective-permute-start(bf16[64,1024]{1,0:T(8,128)(2,1)S(1)} %add_convert_fusion.2), channel_id=1, source_target_pairs={{0,4},{2,6},{4,0},{6,2},{8,12},{10,14},{12,8},{14,10},{1,5},{3,7},... | collective-permute-start | bytes 393224 | tf_op jit(solution)/shard_map/ppermute | solution.py:83
  116.9 11.9 %collective-permute-start.12 = (bf16[64,1024]{1,0:T(8,128)(2,1)S(1)}, bf16[64,1024]{1,0:T(8,128)(2,1)S(1)}, u32[]{:S(2)}, u32[]{:S(2)}) collective-permute-start(bf16[64,1024]{1,0:T(8,128)(2,1)S(1)} %add_convert_fusion.1), channel_id=1, source_target_pairs={{14,0},{8,6},{6,8},{0,14},{15,1},{9,7},{7,9},{1,15},{30,16},{24,22... | collective-permute-start | bytes 393224 | tf_op jit(solution)/shard_map/ppermute | solution.py:91
  125.9 3.9 %collective-permute-start.13 = (bf16[64,1024]{1,0:T(8,128)(2,1)S(1)}, bf16[64,1024]{1,0:T(8,128)(2,1)S(1)}, u32[]{:S(2)}, u32[]{:S(2)}) collective-permute-start(bf16[64,1024]{1,0:T(8,128)(2,1)S(1)} %add_convert_fusion.1), channel_id=1, source_target_pairs={{14,2},{8,4},{6,10},{0,12},{15,3},{9,5},{7,11},{1,13},{30,18},{24,... | collective-permute-start | bytes 393224 | tf_op jit(solution)/shard_map/ppermute | solution.py:91
  131.2 6.8 %collective-permute-start.14 = (f32[3,1024]{1,0:T(4,128)S(1)}, f32[3,1024]{1,0:T(4,128)S(1)}, u32[]{:S(2)}, u32[]{:S(2)}) collective-permute-start(f32[3,1024]{1,0:T(4,128)S(1)} %fusion.8), channel_id=1, source_target_pairs={{16,0},{32,16},{48,32},{64,48},{80,64},{96,80},{112,96},{128,112},... | collective-permute-start | bytes 36872 | tf_op jit(solution)/shard_map/ppermute | solution.py:23
